TPU v7x, 32 devices: a whole 2x2x4 slice. The times are simulated.
32 devices in a mesh: dp: 8 (over z, x), fsdp: 4 (over y, core).
Axes of the slice: x: 2, y: 2, z: 4, core: 2. Of those that a mesh axis runs over, the one named last changes fastest.
Arguments:
- dec_hidden: bfloat16 [1024, 4096], P('dp'), may hold values from -18 to 18
- w_query: bfloat16 [4096, 2048], P(None, 'fsdp'), may hold values from -0.01171875 to 0.01171875
- enc_states: bfloat16 [2, 1536, 2048], P(None, 'dp', 'fsdp')
- w_out: bfloat16 [2048, 4096], P('fsdp'), may hold values from -0.5 to 0.5
- norm_gain: float32 [4096], replicated, may hold values from 0.25 to 1.75
- w_vocab: bfloat16 [4096, 16384], P(None, 'fsdp'), may hold values from -1 to 1
- enc_segment: int32 [1536], replicated, may hold values from 0 to 3, as said below
- dec_segment: int32 [1024], P('dp'), may hold values from 0 to 3, as said below
- seg_map: int32 [8, 4], replicated, may hold values from 0 to 31, as said below
- targets: int32 [1024], P('dp'), may hold values from 0 to 16383
- loss_mask: int32 [1024], P('dp'), may hold values from 0 to 1, as said below
Outputs:
- mean_loss: float32 [], replicated
- grad_hidden: bfloat16 [1024, 4096], P('dp', 'fsdp')
- grad_gain: float32 [4096], P('fsdp')
Inputs may be any that keep to these rules, and one draw needn't show every extreme that they name: `enc_segment`: each encoder row of 192 tokens holds 4 segments numbered in order, never falling, each nonempty and at most 80 tokens long; one segment of every row is exactly 80 long. `dec_segment`: each decoder row of 128 tokens holds 4 segments numbered in order, never falling, each nonempty and at most 56 tokens long; one segment of every row is exactly 56 long. seg_map[b, j] names the encoder segment (encoder row times 4 plus its number in that row) read by segment j of decoder row b. Every encoder segment is named exactly once. The encoder row read in column j is (b + o_j) mod 8, with offsets o_j that are the same for every decoder row and differ between columns; one of them is 4 and one is 7. The segments of one encoder row go to different decoder rows. `loss_mask`: the first token of every decoder row has mask 1.
All inputs are finite; a program needn't handle non-finite values.
Results may differ from a plain program's by a relative error of at most 0.0086.
Values may be sent and summed in bfloat16 or wider, within the bound.
No kernel may reach another device: no remote copies, remote signals or barrier semaphores. Data moves between devices by JAX's collectives and lax.ppermute only.
A program may use at most 128 MiB of HBM per device.

v0:
```python
import jax
import jax.numpy as jnp
from jax import lax
from jax.sharding import PartitionSpec as P

HEAD_DIM = 64


def joined(x, axis, combine):
    everything = jax.tree.map(lambda part: lax.all_gather(part, axis), x)
    leading = jax.tree.map(lambda part: part[0], everything)

    def turn(k, so_far):
        return combine(so_far, jax.tree.map(lambda part: part[k], everything))

    return lax.fori_loop(1, lax.axis_size(axis), turn, leading)


def merge_totals(first_set, second_set):
    larger = jnp.maximum(first_set[0], second_set[0])
    combined = first_set[1] * jnp.exp(first_set[0] - larger) + second_set[1] * jnp.exp(
        second_set[0] - larger
    )
    return (larger, combined, first_set[2] + second_set[2])


def attend(carry, block, block_ids, queries, sources):
    run_max, run_sum, run_acc = carry
    block_rows = block.shape[1]
    heads_here = queries.shape[1]
    keys_block = block[0].astype(jnp.float32).reshape(block_rows, heads_here, HEAD_DIM)
    values_block = block[1].astype(jnp.float32).reshape(block_rows, heads_here, HEAD_DIM)
    scores = jnp.einsum("ihd,jhd->hij", queries, keys_block)
    allowed = (sources[:, None] == block_ids[None, :])[None]
    new_max = jnp.maximum(run_max, jnp.max(jnp.where(allowed, scores, jnp.float32(-1e30)), 2))
    weights = jnp.where(allowed, jnp.exp(scores - new_max[:, :, None]), 0.0)
    run_sum = jnp.sum(weights, 2)
    run_acc = jnp.einsum("hij,jhd->hid", weights, values_block)
    return (new_max, run_sum, run_acc)


def body(
    dec_hidden,
    w_query,
    enc_states,
    w_out,
    norm_gain,
    w_vocab,
    enc_segment,
    dec_segment,
    seg_map,
    targets,
    loss_mask,
):
    dp_index = lax.axis_index("dp")
    fsdp_index = lax.axis_index("fsdp")
    dp_count = lax.axis_size("dp")
    dec_len, width = dec_hidden.shape
    enc_len = enc_states.shape[1]
    heads_here = w_query.shape[1] // HEAD_DIM
    segments = seg_map.shape[1]
    feature_count = width // lax.axis_size("fsdp")
    vocab_here = w_vocab.shape[1]
    map_row = lax.dynamic_index_in_dim(seg_map, dp_index, 0, keepdims=False)
    segment_picks = dec_segment[:, None] == jnp.arange(segments)[None, :]
    sources = jnp.sum(jnp.where(segment_picks, map_row[None, :], 0), 1)
    query_proj = jnp.dot(dec_hidden, w_query, preferred_element_type=jnp.float32).astype(
        jnp.bfloat16
    )
    queries = (
        lax.optimization_barrier(query_proj)
        .astype(jnp.float32)
        .reshape(dec_len, heads_here, HEAD_DIM)
    )
    start_state = (
        jnp.full((heads_here, dec_len), -1e30, jnp.float32),
        jnp.zeros((heads_here, dec_len), jnp.float32),
        jnp.zeros((heads_here, dec_len, HEAD_DIM), jnp.float32),
    )
    global_ids = jnp.arange(dp_count * enc_len) // enc_len * segments + enc_segment
    state = attend(
        start_state,
        lax.all_gather(enc_states, "dp", axis=1, tiled=True),
        global_ids,
        queries,
        sources,
    )
    run_max, run_sum, run_acc = state
    attended = (
        (run_acc / run_sum[:, :, None])
        .transpose(1, 0, 2)
        .reshape(dec_len, heads_here * HEAD_DIM)
        .astype(jnp.bfloat16)
    )
    feature_start = fsdp_index * feature_count
    gain_part = lax.dynamic_slice_in_dim(norm_gain, feature_start, feature_count, 0)
    summed_full = lax.psum(
        jnp.dot(attended, w_out, preferred_element_type=jnp.float32), "fsdp"
    ) + dec_hidden.astype(jnp.float32)
    inv_root = lax.rsqrt(jnp.sum(summed_full * summed_full, 1) / width + 1e-06)
    unit_full = summed_full * inv_root[:, None]
    normed_full = (unit_full * norm_gain).astype(jnp.bfloat16)
    logits = jnp.dot(normed_full, w_vocab, preferred_element_type=jnp.float32)
    unit_part = lax.dynamic_slice_in_dim(unit_full, feature_start, feature_count, 1)
    local_target = targets - fsdp_index * vocab_here
    picked = jnp.arange(vocab_here)[None, :] == local_target[:, None]
    local_top = jnp.max(logits, 1)
    local_total = jnp.sum(jnp.exp(logits - local_top[:, None]), 1)
    local_pick = jnp.sum(jnp.where(picked, logits, 0.0), 1)
    row_top, row_total, target_logit = joined(
        (local_top, local_total, local_pick), "fsdp", merge_totals
    )
    log_total = row_top + jnp.log(row_total)
    mask_float = loss_mask.astype(jnp.float32)
    grad_logits = (
        mask_float[:, None] * (jnp.exp(logits - log_total[:, None]) - picked.astype(jnp.float32))
    ).astype(jnp.bfloat16)
    grad_normed = lax.psum_scatter(
        lax.dot_general(
            w_vocab, grad_logits, (((1,), (1,)), ((), ())), preferred_element_type=jnp.float32
        ),
        "fsdp",
        scatter_dimension=0,
        tiled=True,
    ).T
    grad_unit = grad_normed * gain_part
    inner_total = lax.psum(jnp.sum(grad_unit * unit_part, 1), "fsdp")
    grad_summed = inv_root[:, None] * (grad_unit - unit_part * (inner_total / width)[:, None])
    gain_local = jnp.sum(grad_normed * unit_part, 0)
    token_count, loss_total, gain_total = lax.psum(
        (jnp.sum(mask_float), jnp.sum(mask_float * (log_total - target_logit)), gain_local), "dp"
    )
    return (
        loss_total / token_count,
        (grad_summed / token_count).astype(jnp.bfloat16),
        gain_total / token_count,
    )


def solution(mesh):
    in_specs = (
        P("dp", None),
        P(None, "fsdp"),
        P(None, "dp", "fsdp"),
        P("fsdp", None),
        P(),
        P(None, "fsdp"),
        P(),
        P("dp"),
        P(),
        P("dp"),
        P("dp"),
    )
    out_specs = (P(), P("dp", "fsdp"), P("fsdp"))
    return jax.shard_map(body, mesh=mesh, in_specs=in_specs, out_specs=out_specs, check_vma=False)
```

profile of v0, /device:TPU:0, one launch (start us, length us, event | category | flops | bytes accessed | tf_op | source)
XLA Modules:
  0.0 266.7 jit_solution(12701368455562883856)
XLA Ops:
  7.2 0.0 copy-start
  7.2 0.0 all-gather.8.cloned.1.call-start
  7.2 0.7 all-gather.8.cloned.1.call-update
  7.9 0.0 all-reduce.3.cloned.1.call-start
  8.0 0.0 copy-start.11
  8.0 0.0 copy-start.9
  8.0 3.2 %convolution_convert_fusion = bf16[128,512]{1,0:T(8,128)(2,1)S(1)} fusion(bf16[128,4096]{1,0:T(8,128)(2,1)} %param.13, bf16[4096,512]{1,0:T(8,128)(2,1)} %param.14), kind=kOutput, calls=%fused_computation.27 | convolution fusion | flops 536936448 | bytes 5373952 | tf_op jit(solution)/shard_map/dot_general | solution.py:67
  11.2 0.1 copy.23
  11.4 0.0 copy-done
  11.4 0.2 dynamic-slice_reduce_fusion
  11.6 0.0 copy-done.11
  11.6 0.1 select_reduce_fusion.2
  11.6 0.0 copy-done.9
  11.7 0.2 broadcast_compare_fusion
  11.8 61.6 %all-gather.8.cloned.1.call-done = bf16[2,1536,512]{2,1,0:T(8,128)(2,1)} async-done(((bf16[2,192,512]{2,1,0:T(8,128)(2,1)}), bf16[2,1536,512]{2,1,0:T(8,128)(2,1)}) %all-gather.8.cloned.1.call-update) | async-done | bytes 3145744 | tf_op jit(solution)/shard_map/all_gather | solution.py:83
  73.4 3.2 %fusion.29 = (bf16[1,1536,512]{2,1,0:T(8,128)(2,1)}, bf16[1,1536,512]{2,1,0:T(8,128)(2,1)S(1)}) fusion(bf16[2,1536,512]{2,1,0:T(8,128)(2,1)} %all-gather.8.cloned.1.call-done), kind=kLoop, calls=%fused_computation.65 | loop fusion | bytes 6291456 | tf_op jit(solution)/shard_map/slice | solution.py:31
  76.6 1.7 copy.24
  78.3 3.8 %select_reduce_fusion = (f32[8,128]{1,0:T(8,128)S(1)}, f32[8,128,1536]{2,1,0:T(8,128)}) fusion(pred[128,1536]{1,0:T(8,128)(4,1)S(1)} %broadcast_compare_fusion, bf16[128,8,64]{0,2,1:T(8,128)(2,1)S(1)} %bitcast.64, bf16[1536,8,64]{0,2,1:T(8,128)(2,1)S(1)} %bitcast.62), kind=kOutput, calls=%fused_computation.11 | convolution fusion | flops 204471296 | bytes 8196096 | tf_op jit(solution)/shard_map/ihd,jhd->hij/dot_general | solution.py:33
  82.1 0.7 copy.25
  82.9 4.3 %fusion.7 = f32[8,128]{1,0:T(8,128)S(1)} fusion(f32[8,128,1536]{2,1,0:T(8,128)} %get-tuple-element.214, f32[8,128]{1,0:T(8,128)S(1)} %broadcast_maximum_fusion, pred[128,1536]{1,0:T(8,128)(4,1)S(1)} %broadcast_compare_fusion), kind=kLoop, calls=%fused_computation.12 | loop fusion | flops 4717568 | bytes 6496256 | tf_op jit(solution)/shard_map/reduce_sum | solution.py:37
  87.1 0.3 copy-done.2
  87.5 1.4 fusion.15
  88.8 0.8 copy-done.7
  89.6 2.0 fusion.31
  91.7 0.0 all-reduce.3.cloned.1.call-update
  91.7 0.0 reduce-scatter.2.cloned.1.call-start
  91.8 0.6 copy-done.10
  92.3 0.0 copy-done.12
  92.3 49.5 %all-reduce.3.cloned.1.call-done = f32[128,4096]{1,0:T(8,128)} async-done(((f32[128,4096]{1,0:T(8,128)}), f32[128,4096]{1,0:T(8,128)}) %all-reduce.3.cloned.1.call-update) | async-done | bytes 2097168 | tf_op jit(solution)/shard_map/psum | solution.py:97
  141.9 2.1 multiply_reduce_fusion
  144.0 0.1 copy-done.6
  144.1 0.4 fusion.12
  144.5 0.3 copy-done.8
  144.8 13.7 %fusion.30 = (f32[128]{0:T(128)S(1)}, f32[128,4096]{1,0:T(8,128)S(1)}) fusion(bf16[4096,4096]{1,0:T(8,128)(2,1)} %param.18, f32[128,4096]{1,0:T(8,128)S(1)} %fusion.12, f32[4096]{0:T(1024)S(1)} %copy-done.8), kind=kOutput, calls=%fused_computation.66 | convolution fusion | flops 4296540160 | bytes 37765632 | tf_op jit(solution)/shard_map/dot_general | solution.py:103
  158.6 0.7 select_reduce_fusion.1
  159.3 5.0 %all-gather.5 = f32[4,1,128]{2,1,0:T(1,128)S(1)} all-gather(f32[1,1,128]{2,1,0:T(1,128)S(1)} %bitcast.72), channel_id=4, replica_groups=mesh['dp'=8,'fsdp'=4] {'fsdp'}, dimensions={0}, use_global_device_ids=true | all-gather | bytes 2560 | tf_op jit(solution)/shard_map/all_gather | solution.py:10
  164.3 5.0 %all-gather.4 = f32[4,1,128]{2,1,0:T(1,128)S(1)} all-gather(f32[1,1,128]{2,1,0:T(1,128)S(1)} %bitcast.71), channel_id=3, replica_groups=mesh['dp'=8,'fsdp'=4] {'fsdp'}, dimensions={0}, use_global_device_ids=true | all-gather | bytes 2560 | tf_op jit(solution)/shard_map/all_gather | solution.py:10
  169.3 5.2 %all-gather.3 = f32[4,1,128]{2,1,0:T(1,128)S(1)} all-gather(f32[1,1,128]{2,1,0:T(1,128)S(1)} %bitcast.69), channel_id=2, replica_groups=mesh['dp'=8,'fsdp'=4] {'fsdp'}, dimensions={0}, use_global_device_ids=true | all-gather | bytes 2560 | tf_op jit(solution)/shard_map/all_gather | solution.py:10
  174.5 0.1 while.19
  174.7 0.6 convert_reduce_fusion
  175.3 17.3 %convolution_bitcast_fusion = f32[4096,128]{0,1:T(8,128)} fusion(bf16[4096,4096]{1,0:T(8,128)(2,1)} %param.18, f32[128,4096]{1,0:T(8,128)S(1)} %get-tuple-element.216, f32[128]{0:T(128)S(1)} %get-tuple-element.209, f32[128]{0:T(128)S(1)} %convert_element_type.30, s32[128]{0:T(128)S(1)} %broadcast_subtract_fusion), kind=kOutput, calls=%fused_computation.14 | convolution fusion | flops 4298113024 | bytes 37750272 | tf_op jit(solution)/shard_map/dot_general | solution.py:119
  192.6 0.0 reduce-scatter.2.cloned.1.call-update
  192.6 31.7 %reduce-scatter.2.cloned.1.call-done = f32[1024,128]{0,1:T(8,128)} async-done(((f32[4096,128]{0,1:T(8,128)}), f32[1024,128]{0,1:T(8,128)}) %reduce-scatter.2.cloned.1.call-update) | async-done | bytes 524304 | tf_op jit(solution)/shard_map/reduce_scatter | solution.py:118
  224.3 1.2 fusion.21
  225.5 5.8 %psum.38 = f32[128]{0:T(128)S(1)} all-reduce(f32[128]{0:T(128)S(1)} %get-tuple-element.185), channel_id=1, replica_groups=mesh['dp'=8,'fsdp'=4] {'fsdp'}, use_global_device_ids=true, to_apply=%region_16.17 | all-reduce | flops 128 | bytes 1024 | tf_op jit(solution)/shard_map/psum | solution.py:127
  231.2 22.5 %all-reduce = (f32[]{:T(128)}, f32[]{:T(128)}, f32[1024]{0:T(1024)S(1)}) all-reduce(f32[]{:T(128)} %get-tuple-element.189, f32[]{:T(128)} %get-tuple-element.188, f32[1024]{0:T(1024)S(1)} %get-tuple-element.184), channel_id=1, replica_groups=mesh['dp'=8,'fsdp'=4] {'dp'}, use_global_device_ids=true, to_apply=%region_11.12 | all-reduce | flops 1026 | bytes 8208 | tf_op jit(solution)/shard_map/psum | solution.py:130
  253.8 1.3 broadcast_divide_fusion
  256.4 2.6 divide_convert_fusion
  (27 shorter events, 0.2 us)
Async XLA Ops:
  7.2 4.2 %copy-start = (s32[8,4]{0,1:T(4,128)S(1)}, s32[8,4]{0,1:T(4,128)}, u32[]{:S(2)}) copy-start(s32[8,4]{0,1:T(4,128)} %param.21) | copy-start | bytes 388
  7.2 66.2 %all-gather.8.cloned.1.call-start = ((), (), s32[]{:S(2)}) async-start(), calls=%async_computation.1 | async-start | bytes 3538944 | tf_op jit(solution)/shard_map/all_gather | solution.py:83
  7.9 133.9 %all-reduce.3.cloned.1.call-start = ((), (), s32[]{:S(2)}) async-start(), calls=%async_computation.2 | async-start | bytes 4194304 | tf_op jit(solution)/shard_map/psum | solution.py:97
  8.0 3.6 %copy-start.11 = (s32[128]{0:T(128)S(1)}, s32[128]{0:T(128)}, u32[]{:S(2)}) copy-start(s32[128]{0:T(128)} %param.20) | copy-start | bytes 1540
  8.0 3.7 %copy-start.9 = (s32[1536]{0:T(1024)S(1)}, s32[1536]{0:T(1024)}, u32[]{:S(2)}) copy-start(s32[1536]{0:T(1024)} %param.19) | copy-start | bytes 18436
  82.8 4.6 %copy-start.2 = (f32[8,128,1536]{2,1,0:T(8,128)S(1)}, f32[8,128,1536]{2,1,0:T(8,128)}, u32[]{:S(2)}) copy-start(f32[8,128,1536]{2,1,0:T(8,128)} %get-tuple-element.214) | copy-start | bytes 18874372
  87.4 2.2 copy-start.7
  91.7 0.7 copy-start.10
  91.7 0.7 copy-start.12
  91.7 50.2 %copy-start.5 = (bf16[128,4096]{1,0:T(8,128)(2,1)S(1)}, bf16[128,4096]{1,0:T(8,128)(2,1)}, u32[]{:S(2)}) copy-start(bf16[128,4096]{1,0:T(8,128)(2,1)} %param.13) | copy-start | bytes 3145732
  91.7 132.6 %reduce-scatter.2.cloned.1.call-start = ((), (), s32[]{:S(2)}) async-start(), calls=%async_computation.3 | async-start | bytes 2621440 | tf_op jit(solution)/shard_map/reduce_scatter | solution.py:118
  141.9 2.2 copy-start.6
  144.1 0.7 copy-start.8
  144.8 13.8 %copy-start.3 = (f32[128,4096]{1,0:T(8,128)}, f32[128,4096]{1,0:T(8,128)S(1)}, u32[]{:S(2)}) copy-start(f32[128,4096]{1,0:T(8,128)S(1)} %fusion.12) | copy-start | bytes 6291460
  192.6 31.7 %copy-start.4 = (f32[128,4096]{1,0:T(8,128)S(1)}, f32[128,4096]{1,0:T(8,128)}, u32[]{:S(2)}) copy-start(f32[128,4096]{1,0:T(8,128)} %copy-done.3) | copy-start | bytes 6291460
  192.6 66.5 %copy-start.1 = (s32[8,4]{0,1:T(4,128)S(1)}, s32[8,4]{0,1:T(4,128)}, u32[]{:S(2)}) copy-start(s32[8,4]{0,1:T(4,128)} %param.21) | copy-start | bytes 388
Sparse Core Ops, SparseCore 0:
  10.2 63.1 all-gather.7
  91.8 49.9 all-reduce.2
  192.7 31.5 reduce-scatter.1
where the time goes:
time: 267 us
  waiting for transfers between devices  143 us (54%)
  blocking collectives  43.5 us (16%)
  matrix products  41.5 us (16%)
  between operations  16.4 us (6%)
  other arithmetic  13.6 us (5%)
  local copies, waits for them, and re-layouts  8.11 us (3%)
    all_gather x1, waiting for transfers between devices, body(): lax.all_gather(enc_states, 'dp', axis=1, tiled=True)  61.6 us
    psum x1, waiting for transfers between devices, body(): lax.psum(jnp.dot(attended, w_out, preferred_element_type=jnp.float32), 'f...  49.5 us
    reduce_scatter x1, waiting for transfers between devices, body(): lax.psum_scatter(lax.dot_general(w_vocab, grad_logits, (((1,), (1,)), (()...  31.7 us
    psum x1, blocking collectives, body(): lax.psum((jnp.sum(mask_float), jnp.sum(mask_float * (log_total - target_l...  22.5 us
    dot_general x1, matrix products, body(): lax.dot_general(w_vocab, grad_logits, (((1,), (1,)), ((), ())), preferred...  17.3 us
    all_gather x3, blocking collectives, joined(): everything = jax.tree.map(lambda part: lax.all_gather(part, axis), x)  15.3 us
    dot_general x1, matrix products, body(): logits = jnp.dot(normed_full, w_vocab, preferred_element_type=jnp.float32)  13.7 us
    psum x1, blocking collectives, body(): inner_total = lax.psum(jnp.sum(grad_unit * unit_part, 1), 'fsdp')  5.75 us
  transfers between devices with their start and end apart: 3, of which 3 were waited for; matrix products, arithmetic and copies ran while one was open for 1% of the time, Pallas kernels for 0%

commit v1 on v0

v1 whole, which is shorter than its diff:
```python
import jax
import jax.numpy as jnp
from jax import lax
from jax.sharding import PartitionSpec as P

HEAD_DIM = 64
ENC_MOST = 80


def is_power_of_two(n):
    return n & (n - 1) == 0


def exchange(x, axis, bit):
    size = lax.axis_size(axis)
    return lax.ppermute(x, axis, [(i, i ^ (1 << bit)) for i in range(size)])


def scatter_sum(x, axis, dim):
    size = lax.axis_size(axis)
    if not is_power_of_two(size):
        return lax.psum_scatter(x, axis, scatter_dimension=dim, tiled=True)
    me = lax.axis_index(axis)
    head, width, tail = x.shape[:dim], x.shape[dim] // size, x.shape[dim + 1 :]
    cur = x
    chunks, bit = size, 0
    while chunks > 1:
        cur = cur.reshape(head + (chunks // 2, 2, width) + tail)
        side = (me >> bit) & 1
        keep = lax.dynamic_index_in_dim(cur, side, dim + 1, keepdims=False)
        send = lax.dynamic_index_in_dim(cur, 1 - side, dim + 1, keepdims=False)
        cur = keep + exchange(send, axis, bit)
        chunks //= 2
        bit += 1
    return cur.reshape(head + (width,) + tail)


def gather_all(x, axis, dim):
    size = lax.axis_size(axis)
    if not is_power_of_two(size):
        return lax.all_gather(x, axis, axis=dim, tiled=True)
    me = lax.axis_index(axis)
    head, width, tail = x.shape[:dim], x.shape[dim], x.shape[dim + 1 :]
    cur = x.reshape(head + (1, width) + tail)
    chunks = 1
    bit = size.bit_length() - 2
    while bit >= 0:
        got = exchange(cur, axis, bit)
        low = (me >> bit) & 1 == 0
        first = jnp.where(low, cur, got)
        second = jnp.where(low, got, cur)
        cur = jnp.stack([first, second], dim + 1).reshape(head + (chunks * 2, width) + tail)
        chunks *= 2
        bit -= 1
    return cur.reshape(head + (chunks * width,) + tail)


def sum_all(x, axis):
    size = lax.axis_size(axis)
    if not is_power_of_two(size):
        return lax.psum(x, axis)
    for bit in range(size.bit_length() - 1):
        x = x + exchange(x, axis, bit)
    return x


def merge_totals(first_set, second_set):
    larger = jnp.maximum(first_set[0], second_set[0])
    combined = first_set[1] * jnp.exp(first_set[0] - larger) + second_set[1] * jnp.exp(
        second_set[0] - larger
    )
    return jnp.stack([larger, combined, first_set[2] + second_set[2]])


def merge_all(stats, axis):
    size = lax.axis_size(axis)
    if is_power_of_two(size):
        for bit in range(size.bit_length() - 1):
            stats = merge_totals(stats, exchange(stats, axis, bit))
        return stats
    everything = lax.all_gather(stats, axis)
    return lax.fori_loop(1, size, lambda k, so_far: merge_totals(so_far, everything[k]), everything[0])


def body(
    dec_hidden,
    w_query,
    enc_states,
    w_out,
    norm_gain,
    w_vocab,
    enc_segment,
    dec_segment,
    seg_map,
    targets,
    loss_mask,
):
    dp_index = lax.axis_index("dp")
    fsdp_index = lax.axis_index("fsdp")
    dp_count = lax.axis_size("dp")
    dec_len, width = dec_hidden.shape
    enc_len = enc_states.shape[1]
    heads_here = w_query.shape[1] // HEAD_DIM
    segments = seg_map.shape[1]
    feature_count = width // lax.axis_size("fsdp")
    vocab_here = w_vocab.shape[1]
    window = min(ENC_MOST, enc_len)

    map_row = lax.dynamic_index_in_dim(seg_map, dp_index, 0, keepdims=False)
    segment_picks = dec_segment[:, None] == jnp.arange(segments)[None, :]
    sources = jnp.sum(jnp.where(segment_picks, map_row[None, :], 0), 1)

    offsets = (seg_map[0] // segments) % dp_count
    column_hits = offsets[None, :] == jnp.arange(dp_count)[:, None]
    shift_used = jnp.any(column_hits, 1)
    shift_column = jnp.argmax(column_hits, 1)
    enc_rows = enc_segment.reshape(dp_count, enc_len)
    seg_starts = jnp.sum(enc_rows[:, None, :] < jnp.arange(segments)[None, :, None], 2)
    win_starts = jnp.clip(seg_starts, 0, enc_len - window)
    global_ids = jnp.arange(dp_count * enc_len) // enc_len * segments + enc_segment

    key_blocks = []
    id_blocks = []
    for shift in range(dp_count):
        column = shift_column[shift]
        reader = (dp_index - shift) % dp_count
        send_segment = seg_map[reader, column] % segments
        send_start = win_starts[dp_index, send_segment]
        block = lax.dynamic_slice_in_dim(enc_states, send_start, window, 1)
        if shift:
            block = lax.ppermute(
                block, "dp", [(i, (i - shift) % dp_count) for i in range(dp_count)]
            )
        owner = (dp_index + shift) % dp_count
        recv_segment = map_row[column] % segments
        recv_start = win_starts[owner, recv_segment]
        ids = lax.dynamic_slice_in_dim(global_ids, owner * enc_len + recv_start, window, 0)
        key_blocks.append(block)
        id_blocks.append(jnp.where(shift_used[shift], ids, -1))
    gathered = jnp.concatenate(key_blocks, 1)
    key_ids = jnp.concatenate(id_blocks, 0)
    key_count = gathered.shape[1]

    query_proj = jnp.dot(dec_hidden, w_query, preferred_element_type=jnp.float32).astype(
        jnp.bfloat16
    )
    queries = lax.optimization_barrier(query_proj).reshape(dec_len, heads_here, HEAD_DIM)
    keys_all = gathered[0].reshape(key_count, heads_here, HEAD_DIM)
    values_all = gathered[1].astype(jnp.float32).reshape(key_count, heads_here, HEAD_DIM)
    scores = jnp.einsum(
        "ihd,jhd->hij", queries, keys_all, preferred_element_type=jnp.float32
    )
    allowed = (sources[:, None] == key_ids[None, :])[None]
    top = jnp.max(jnp.where(allowed, scores, jnp.float32(-1e30)), 2)
    weights = jnp.where(allowed, jnp.exp(scores - top[:, :, None]), 0.0)
    run_sum = jnp.sum(weights, 2)
    run_acc = jnp.einsum("hij,jhd->hid", weights, values_all)
    attended = (
        (run_acc / run_sum[:, :, None])
        .transpose(1, 0, 2)
        .reshape(dec_len, heads_here * HEAD_DIM)
        .astype(jnp.bfloat16)
    )

    feature_start = fsdp_index * feature_count
    gain_part = lax.dynamic_slice_in_dim(norm_gain, feature_start, feature_count, 0)
    hidden_part = lax.dynamic_slice_in_dim(dec_hidden, feature_start, feature_count, 1)
    summed_part = scatter_sum(
        jnp.dot(attended, w_out, preferred_element_type=jnp.float32), "fsdp", 1
    ) + hidden_part.astype(jnp.float32)
    summed_full = gather_all(summed_part, "fsdp", 1)
    inv_root = lax.rsqrt(jnp.sum(summed_full * summed_full, 1) / width + 1e-06)
    unit_full = summed_full * inv_root[:, None]
    normed_full = (unit_full * norm_gain).astype(jnp.bfloat16)
    logits = jnp.dot(normed_full, w_vocab, preferred_element_type=jnp.float32)
    unit_part = summed_part * inv_root[:, None]
    local_target = targets - fsdp_index * vocab_here
    picked = jnp.arange(vocab_here)[None, :] == local_target[:, None]
    local_top = jnp.max(logits, 1)
    local_total = jnp.sum(jnp.exp(logits - local_top[:, None]), 1)
    local_pick = jnp.sum(jnp.where(picked, logits, 0.0), 1)
    row_top, row_total, target_logit = merge_all(
        jnp.stack([local_top, local_total, local_pick]), "fsdp"
    )
    log_total = row_top + jnp.log(row_total)
    mask_float = loss_mask.astype(jnp.float32)
    grad_logits = (
        mask_float[:, None] * (jnp.exp(logits - log_total[:, None]) - picked.astype(jnp.float32))
    ).astype(jnp.bfloat16)
    grad_normed = scatter_sum(
        lax.dot_general(
            w_vocab, grad_logits, (((1,), (1,)), ((), ())), preferred_element_type=jnp.float32
        ),
        "fsdp",
        0,
    ).T
    grad_unit = grad_normed * gain_part
    inner_total = sum_all(jnp.sum(grad_unit * unit_part, 1), "fsdp")
    grad_summed = inv_root[:, None] * (grad_unit - unit_part * (inner_total / width)[:, None])
    gain_local = jnp.sum(grad_normed * unit_part, 0)
    packed = jnp.concatenate(
        [jnp.stack([jnp.sum(mask_float), jnp.sum(mask_float * (log_total - target_logit))]), gain_local]
    )
    packed = sum_all(packed, "dp")
    token_count, loss_total, gain_total = packed[0], packed[1], packed[2:]
    return (
        loss_total / token_count,
        (grad_summed / token_count).astype(jnp.bfloat16),
        gain_total / token_count,
    )


def solution(mesh):
    in_specs = (
        P("dp", None),
        P(None, "fsdp"),
        P(None, "dp", "fsdp"),
        P("fsdp", None),
        P(),
        P(None, "fsdp"),
        P(),
        P("dp"),
        P(),
        P("dp"),
        P("dp"),
    )
    out_specs = (P(), P("dp", "fsdp"), P("fsdp"))
    return jax.shard_map(body, mesh=mesh, in_specs=in_specs, out_specs=out_specs, check_vma=False)
```

time: 267 us -> 244 us (0.914)
  waiting for transfers between devices: 143 us -> 60.7 us
  between operations: 16.4 us -> 69.5 us
  blocking collectives: 43.5 us -> 0 us
  local copies, waits for them, and re-layouts: 8.11 us -> 35.8 us
  starting transfers between devices: 0.12 us -> 21.9 us
  matrix products: 41.5 us -> 35 us
  other arithmetic: 13.6 us -> 19.4 us
    all_gather x1 -> x0, waiting for transfers between devices: 61.6 us -> none  [body(): lax.all_gather(enc_states, 'dp', axis=1, tiled=True)]
    ppermute x0 -> x20, waiting for transfers between devices: none -> 60.7 us  [the longest x13 56.9 us: exchange(): return lax.ppermute(x, axis, [(i, i ^ 1 << bit) for i in range(size)])]
    psum x1 -> x0, waiting for transfers between devices: 49.5 us -> none  [body(): lax.psum(jnp.dot(attended, w_out, preferred_element_type=jnp.float32), 'f...]
    reduce_scatter x1 -> x0, waiting for transfers between devices: 31.7 us -> none  [body(): lax.psum_scatter(lax.dot_general(w_vocab, grad_logits, (((1,), (1,)), (()...]
    psum x2 -> x0, blocking collectives: 28.3 us -> none  [the longest x1 22.5 us: body(): lax.psum((jnp.sum(mask_float), jnp.sum(mask_float * (log_total - target_l...]
    ppermute x0 -> x20, starting transfers between devices: none -> 21.9 us  [the longest x7 12.4 us: body(): lax.ppermute(block, 'dp', [(i, (i - shift) % dp_count) for i in range(dp_...]
    all_gather x3 -> x0, blocking collectives: 15.3 us -> none  [joined(): everything = jax.tree.map(lambda part: lax.all_gather(part, axis), x)]
    dynamic_slice x1 -> x7, local copies, waits for them, and re-layouts: 0.19 us -> 12.2 us  [the longest x1 4.38 us: scatter_sum(): keep = lax.dynamic_index_in_dim(cur, side, dim + 1, keepdims=False)]
  transfers between devices with their start and end apart: 3 -> 20, of which waited for: 3 -> 14; matrix products, arithmetic and copies ran while one was open for 1% -> 9% of each run, Pallas kernels for 0% -> 0%
where the time goes in v1:
time: 244 us; the launch traced here: 242 us
  between operations  69.5 us (28%)
  waiting for transfers between devices  60.7 us (25%)
  local copies, waits for them, and re-layouts  35.8 us (15%)
  matrix products  35 us (14%)
  starting transfers between devices  21.9 us (9%)
  other arithmetic  19.4 us (8%)
    ppermute x13, waiting for transfers between devices, exchange(): return lax.ppermute(x, axis, [(i, i ^ 1 << bit) for i in range(size)])  56.9 us
    dot_general x1, matrix products, body(): lax.dot_general(w_vocab, grad_logits, (((1,), (1,)), ((), ())), preferred...  16.1 us
    dot_general x1, matrix products, body(): logits = jnp.dot(normed_full, w_vocab, preferred_element_type=jnp.float32)  13 us
    ppermute x7, starting transfers between devices, body(): lax.ppermute(block, 'dp', [(i, (i - shift) % dp_count) for i in range(dp_...  12.4 us
    ppermute x13, starting transfers between devices, exchange(): return lax.ppermute(x, axis, [(i, i ^ 1 << bit) for i in range(size)])  9.44 us
    unnamed x22, local copies, waits for them, and re-layouts  7.05 us
    dot_general x1, local copies, waits for them, and re-layouts, body(): jnp.dot(attended, w_out, preferred_element_type=jnp.float32)  6.47 us
    select_n x1, other arithmetic, body(): id_blocks.append(jnp.where(shift_used[shift], ids, -1))  5.14 us
  transfers between devices with their start and end apart: 20, of which 14 were waited for; matrix products, arithmetic and copies ran while one was open for 9% of the time, Pallas kernels for 0%

profile of v1, /device:TPU:0, one launch (start us, length us, event | category | flops | bytes accessed | tf_op | source)
XLA Modules:
  0.0 242.3 jit_solution(4375656122165141085)
XLA Ops:
  0.7 1.0 fusion.22
  18.3 1.9 fusion.45
  35.2 1.5 fusion.47
  61.2 2.7 %constant_dynamic-slice_fusion.4 = (bf16[2,80,512]{2,1,0:T(8,128)(2,1)S(1)}, bf16[2,80,512]{2,1,0:T(8,128)(2,1)S(1)}, bf16[2,80,512]{2,1,0:T(8,128)(2,1)S(1)}, b...) fusion(bf16[2,192,512]{2,1,0:T(8,128)(2,1)} %param.13, ...), kind=kLoop, calls=%fused_computation.64 | loop fusion | bytes 2621472 | tf_op jit(solution)/shard_map/dynamic_slice | solution.py:129
  63.9 5.9 %collective-permute-start = (bf16[2,80,512]{2,1,0:T(8,128)(2,1)}, bf16[2,80,512]{2,1,0:T(8,128)(2,1)}, u32[]{:S(2)}, u32[]{:S(2)}) collective-permute-start(bf16[2,80,512]{2,1,0:T(8,128)(2,1)} %get-tuple-element.33), channel_id=1, source_target_pairs={{0,28},{4,0},{8,4},{12,8},{16,12},{20,16},{24,20},{28,24},{1,29},{... | collective-permute-start | bytes 491528 | tf_op jit(solution)/shard_map/ppermute | solution.py:131
  70.3 3.1 %collective-permute-start.3 = (bf16[2,80,512]{2,1,0:T(8,128)(2,1)S(1)}, bf16[2,80,512]{2,1,0:T(8,128)(2,1)}, u32[]{:S(2)}, u32[]{:S(2)}) collective-permute-start(bf16[2,80,512]{2,1,0:T(8,128)(2,1)S(1)} %get-tuple-element.30), channel_id=1, source_target_pairs={{0,16},{4,20},{8,24},{12,28},{16,0},{20,4},{24,8},{28,12},{1,17},{... | collective-permute-start | bytes 491528 | tf_op jit(solution)/shard_map/ppermute | solution.py:131
  87.7 2.9 %convolution_convert_fusion = bf16[128,512]{1,0:T(8,128)(2,1)S(1)} fusion(bf16[128,4096]{1,0:T(8,128)(2,1)S(1)} %copy-done.2, bf16[4096,512]{1,0:T(8,128)(2,1)} %param.12), kind=kOutput, calls=%fused_computation.19 | convolution fusion | flops 536936448 | bytes 5373952 | tf_op jit(solution)/shard_map/dot_general | solution.py:144
  90.6 5.1 %broadcast_select_fusion = (s32[80]{0:T(128)S(1)}, s32[80]{0:T(128)S(1)}, s32[80]{0:T(128)S(1)}, s32[80]{0:T(128)S(1)}, s32[80]{0:T(128)S(1)}, /*index=5*/s32[80]{0:T(128)S(1)}, s32[80]{0:T(128)S(1)}, s32[80]{0:T(128)S(1)}) fusion(pred[]{:T(512)} %bitcast.29, s32[1536]{0:T(1024)S(1)} %fusion.15, s32[]{:T(128)S(6)} %select_n.547, s32[]{:T(128)S(6)} %select_n.538, ...), kind=kLoop, calls=%fused_computation.94 | loop fusion | flops 640 | bytes 5160 | tf_op jit(solution)/shard_map/jit(_where)/select_n | solution.py:139
  96.1 6.5 %copy.49 = bf16[4096,512]{1,0:T(8,128)(2,1)} copy(bf16[4096,512]{0,1:T(8,128)(2,1)} %bitcast.203) | data formatting | bytes 8388608 | tf_op jit(solution)/shard_map/dot_general | solution.py:169
  102.6 1.6 collective-permute-start.5
  105.2 1.3 collective-permute-start.6
  107.4 0.9 constant_dynamic-update-slice_fusion.4
  108.4 0.9 constant_dynamic-update-slice_fusion.3
  109.3 0.9 constant_dynamic-update-slice_fusion.2
  110.6 3.4 %collective-permute-done.6 = bf16[2,80,512]{2,1,0:T(8,128)(2,1)S(1)} collective-permute-done((bf16[2,80,512]{2,1,0:T(8,128)(2,1)S(1)}, bf16[2,80,512]{2,1,0:T(8,128)(2,1)S(1)}, u32[]{:S(2)}, u32[]{:S(2)}) %collective-permute-start.6) | collective-permute-done | bytes 163872 | tf_op jit(solution)/shard_map/ppermute | solution.py:131
  117.0 1.4 copy-done
  118.4 1.5 fusion.51
  120.1 2.8 %collective-permute-done.7 = f32[128,2,1024]{2,0,1:T(8,128)} collective-permute-done((f32[128,2,1024]{2,0,1:T(8,128)S(1)}, f32[128,2,1024]{2,0,1:T(8,128)}, u32[]{:S(2)}, u32[]{:S(2)}) %collective-permute-start.7) | collective-permute-done | bytes 1048608 | tf_op jit(solution)/shard_map/ppermute | solution.py:16
  122.9 1.4 bitcast_add_fusion.1
  124.3 1.0 copy-done.1
  125.3 1.6 collective-permute-start.8
  126.9 12.4 %collective-permute-done.8 = f32[128,1,1024]{2,0,1:T(8,128)S(1)} collective-permute-done((f32[128,1,1024]{2,0,1:T(8,128)S(1)}, f32[128,1,1024]{2,0,1:T(8,128)S(1)}, u32[]{:S(2)}, u32[]{:S(2)}) %collective-permute-start.8) | collective-permute-done | bytes 524320 | tf_op jit(solution)/shard_map/ppermute | solution.py:16
  139.3 1.2 bitcast_add_fusion.2
  140.5 1.6 collective-permute-start.9
  142.1 11.6 %collective-permute-done.9 = f32[128,1,1024]{2,0,1:T(8,128)S(1)} collective-permute-done((f32[128,1,1024]{2,0,1:T(8,128)S(1)}, f32[128,1,1024]{2,0,1:T(8,128)S(1)}, u32[]{:S(2)}, u32[]{:S(2)}) %collective-permute-start.9) | collective-permute-done | bytes 524320 | tf_op jit(solution)/shard_map/ppermute | solution.py:16
  153.8 1.1 maximum_bitcast_fusion
  154.9 2.9 %collective-permute-done.10 = f32[128,2,1024]{2,0,1:T(8,128)S(1)} collective-permute-done((f32[128,2,1024]{2,0,1:T(8,128)}, f32[128,2,1024]{2,0,1:T(8,128)S(1)}, u32[]{:S(2)}, u32[]{:S(2)}) %collective-permute-start.10) | collective-permute-done | bytes 1048608 | tf_op jit(solution)/shard_map/ppermute | solution.py:16
  158.5 2.1 copy.44
  160.6 1.9 fusion.3
  162.5 13.0 %fusion.50 = (f32[128]{0:T(128)S(1)}, f32[128,4096]{1,0:T(8,128)S(1)}) fusion(bf16[128,4096]{0,1:T(8,128)(2,1)S(1)} %fusion.3, bf16[4096,4096]{1,0:T(8,128)(2,1)} %param.16), kind=kOutput, calls=%fused_computation.141 | convolution fusion | flops 4295491584 | bytes 36700672 | tf_op jit(solution)/shard_map/dot_general | solution.py:175
  176.5 1.0 collective-permute-done.11
  177.5 1.6 collective-permute-start.12
  179.1 2.1 collective-permute-done.12
  181.8 16.1 %convolution_bitcast_fusion = f32[4096,128]{0,1:T(8,128)S(1)} fusion(bf16[4096,4096]{1,0:T(8,128)(2,1)} %param.16, f32[128,4096]{1,0:T(8,128)S(1)} %get-tuple-element.100, f32[128]{0:T(128)S(1)} %get-tuple-element.17, f32[128]{0:T(128)S(1)} %convert_element_type.31, s32[128]{0:T(128)S(1)} %broadcast_subtract_fusion), kind=kOutput, calls=%fused_computation | convolution fusion | flops 4298113024 | bytes 37750272 | tf_op jit(solution)/shard_map/dot_general | solution.py:191
  197.9 2.8 %reshape.153 = f32[2,2,1024,128]{2,1,0,3:T(2,128)} reshape(f32[4096,128]{0,1:T(8,128)S(1)} %convolution_bitcast_fusion) | data formatting | bytes 4194304 | tf_op jit(solution)/shard_map/reshape | solution.py:28
  200.7 4.4 %constant_dynamic-slice_fusion.2 = (f32[2,1,1024,128]{2,1,0,3:T(1,128)S(1)}, f32[2,1,1024,128]{2,1,0,3:T(1,128)S(1)}) fusion(f32[2,2,1024,128]{2,1,0,3:T(2,128)} %reshape.153, s32[]{:T(128)S(6)} %select_n.589, s32[]{:T(128)S(6)} %select_n.590), kind=kLoop, calls=%fused_computation.62 | loop fusion | bytes 4194312 | tf_op jit(solution)/shard_map/jit(dynamic_index_in_dim)/dynamic_slice | solution.py:30
  205.5 2.6 %collective-permute-done.13 = f32[2,1024,128]{1,2,0:T(8,128)S(1)} collective-permute-done((f32[2,1024,128]{1,2,0:T(8,128)S(1)}, f32[2,1024,128]{1,2,0:T(8,128)S(1)}, u32[]{:S(2)}, u32[]{:S(2)}) %collective-permute-start.13) | collective-permute-done | bytes 1048608 | tf_op jit(solution)/shard_map/ppermute | solution.py:16
  208.7 1.6 collective-permute-start.14
  210.3 12.4 %collective-permute-done.14 = f32[1,1024,128]{1,2,0:T(8,128)S(1)} collective-permute-done((f32[1,1024,128]{1,2,0:T(8,128)S(1)}, f32[1,1024,128]{1,2,0:T(8,128)S(1)}, u32[]{:S(2)}, u32[]{:S(2)}) %collective-permute-start.14) | collective-permute-done | bytes 524320 | tf_op jit(solution)/shard_map/ppermute | solution.py:16
  223.1 1.4 concatenate.11
  224.4 3.6 %collective-permute-done.15 = f32[1026]{0:T(1024)S(1)} collective-permute-done((f32[1026]{0:T(1024)S(1)}, f32[1026]{0:T(1024)S(1)}, u32[]{:S(2)}, u32[]{:S(2)}) %collective-permute-start.15) | collective-permute-done | bytes 4136 | tf_op jit(solution)/shard_map/ppermute | solution.py:16
  228.1 1.1 collective-permute-done.18
  229.2 1.5 collective-permute-start.19
  230.7 1.0 collective-permute-done.16
  231.7 1.2 collective-permute-start.17
  233.0 3.3 %collective-permute-done.17 = f32[1026]{0:T(1024)S(1)} collective-permute-done((f32[1026]{0:T(1024)S(1)}, f32[1026]{0:T(1024)S(1)}, u32[]{:S(2)}, u32[]{:S(2)}) %collective-permute-start.17) | collective-permute-done | bytes 4136 | tf_op jit(solution)/shard_map/ppermute | solution.py:16
  236.9 1.4 slice_divide_fusion
  239.6 1.6 divide_convert_fusion
  (79 shorter events, 14.9 us)
Async XLA Ops:
  0.6 86.3 %copy-start.3 = (s32[1536]{0:T(1024)S(1)}, s32[1536]{0:T(1024)}, u32[]{:S(2)}) copy-start(s32[1536]{0:T(1024)} %param.17) | copy-start | bytes 18436
  0.6 87.0 %copy-start.6 = (s32[128]{0:T(128)S(1)}, s32[128]{0:T(128)}, u32[]{:S(2)}) copy-start(s32[128]{0:T(128)} %param.18) | copy-start | bytes 1540
  0.7 87.1 %copy-start.2 = (bf16[128,4096]{1,0:T(8,128)(2,1)S(1)}, bf16[128,4096]{1,0:T(8,128)(2,1)}, u32[]{:S(2)}) copy-start(bf16[128,4096]{1,0:T(8,128)(2,1)} %param.11) | copy-start | bytes 3145732
  63.9 38.7 %collective-permute-start = (bf16[2,80,512]{2,1,0:T(8,128)(2,1)}, bf16[2,80,512]{2,1,0:T(8,128)(2,1)}, u32[]{:S(2)}, u32[]{:S(2)}) collective-permute-start(bf16[2,80,512]{2,1,0:T(8,128)(2,1)} %get-tuple-element.33), channel_id=1, source_target_pairs={{0,28},{4,0},{8,4},{12,8},{16,12},{20,16},{24,20},{28,24},{1,29},{... | collective-permute-start | bytes 491528 | tf_op jit(solution)/shard_map/ppermute | solution.py:131
  69.9 35.3 %collective-permute-start.1 = (bf16[2,80,512]{2,1,0:T(8,128)(2,1)}, bf16[2,80,512]{2,1,0:T(8,128)(2,1)}, u32[]{:S(2)}, u32[]{:S(2)}) collective-permute-start(bf16[2,80,512]{2,1,0:T(8,128)(2,1)} %get-tuple-element.32), channel_id=1, source_target_pairs={{0,24},{4,28},{8,0},{12,4},{16,8},{20,12},{24,16},{28,20},{1,25},{... | collective-permute-start | bytes 491528 | tf_op jit(solution)/shard_map/ppermute | solution.py:131
  70.3 37.1 %collective-permute-start.2 = (bf16[2,80,512]{2,1,0:T(8,128)(2,1)}, bf16[2,80,512]{2,1,0:T(8,128)(2,1)}, u32[]{:S(2)}, u32[]{:S(2)}) collective-permute-start(bf16[2,80,512]{2,1,0:T(8,128)(2,1)} %get-tuple-element.31), channel_id=1, source_target_pairs={{0,20},{4,24},{8,28},{12,0},{16,4},{20,8},{24,12},{28,16},{1,21},{... | collective-permute-start | bytes 491528 | tf_op jit(solution)/shard_map/ppermute | solution.py:131
  70.3 38.1 %collective-permute-start.3 = (bf16[2,80,512]{2,1,0:T(8,128)(2,1)S(1)}, bf16[2,80,512]{2,1,0:T(8,128)(2,1)}, u32[]{:S(2)}, u32[]{:S(2)}) collective-permute-start(bf16[2,80,512]{2,1,0:T(8,128)(2,1)S(1)} %get-tuple-element.30), channel_id=1, source_target_pairs={{0,16},{4,20},{8,24},{12,28},{16,0},{20,4},{24,8},{28,12},{1,17},{... | collective-permute-start | bytes 491528 | tf_op jit(solution)/shard_map/ppermute | solution.py:131
  73.4 35.9 %collective-permute-start.4 = (bf16[2,80,512]{2,1,0:T(8,128)(2,1)S(1)}, bf16[2,80,512]{2,1,0:T(8,128)(2,1)}, u32[]{:S(2)}, u32[]{:S(2)}) collective-permute-start(bf16[2,80,512]{2,1,0:T(8,128)(2,1)S(1)} %get-tuple-element.29), channel_id=1, source_target_pairs={{0,12},{4,16},{8,20},{12,24},{16,28},{20,0},{24,4},{28,8},{1,13},{... | collective-permute-start | bytes 491528 | tf_op jit(solution)/shard_map/ppermute | solution.py:131
  102.6 8.0 %collective-permute-start.5 = (bf16[2,80,512]{2,1,0:T(8,128)(2,1)S(1)}, bf16[2,80,512]{2,1,0:T(8,128)(2,1)S(1)}, u32[]{:S(2)}, u32[]{:S(2)}) collective-permute-start(bf16[2,80,512]{2,1,0:T(8,128)(2,1)S(1)} %get-tuple-element.35), channel_id=1, source_target_pairs={{0,8},{4,12},{8,16},{12,20},{16,24},{20,28},{24,0},{28,4},{1,9},{5... | collective-permute-start | bytes 491528 | tf_op jit(solution)/shard_map/ppermute | solution.py:131
  105.2 8.8 %collective-permute-start.6 = (bf16[2,80,512]{2,1,0:T(8,128)(2,1)S(1)}, bf16[2,80,512]{2,1,0:T(8,128)(2,1)S(1)}, u32[]{:S(2)}, u32[]{:S(2)}) collective-permute-start(bf16[2,80,512]{2,1,0:T(8,128)(2,1)S(1)} %get-tuple-element.28), channel_id=1, source_target_pairs={{0,4},{4,8},{8,12},{12,16},{16,20},{20,24},{24,28},{28,0},{1,5},{5... | collective-permute-start | bytes 491528 | tf_op jit(solution)/shard_map/ppermute | solution.py:131
  116.2 2.2 copy-start
  120.1 2.9 %collective-permute-start.7 = (f32[128,2,1024]{2,0,1:T(8,128)S(1)}, f32[128,2,1024]{2,0,1:T(8,128)}, u32[]{:S(2)}, u32[]{:S(2)}) collective-permute-start(f32[128,2,1024]{2,0,1:T(8,128)S(1)} %dynamic-slice_bitcast_fusion), channel_id=1, source_target_pairs={{0,1},{1,0},{2,3},{3,2},{4,5},{5,4},{6,7},{7,6},{8,9},{9,8},{10,11... | collective-permute-start | bytes 3145736 | tf_op jit(solution)/shard_map/ppermute | solution.py:16
  124.3 1.0 copy-start.1
  125.3 14.0 %collective-permute-start.8 = (f32[128,1,1024]{2,0,1:T(8,128)S(1)}, f32[128,1,1024]{2,0,1:T(8,128)S(1)}, u32[]{:S(2)}, u32[]{:S(2)}) collective-permute-start(f32[128,1,1024]{2,0,1:T(8,128)S(1)} %constant_dynamic-slice_fusion.3), channel_id=1, source_target_pairs={{0,2},{1,3},{2,0},{3,1},{4,6},{5,7},{6,4},{7,5},{8,10},{9,11},{10,... | collective-permute-start | bytes 1572872 | tf_op jit(solution)/shard_map/ppermute | solution.py:16
  140.5 13.2 %collective-permute-start.9 = (f32[128,1,1024]{2,0,1:T(8,128)S(1)}, f32[128,1,1024]{2,0,1:T(8,128)S(1)}, u32[]{:S(2)}, u32[]{:S(2)}) collective-permute-start(f32[128,1,1024]{2,0,1:T(8,128)S(1)} %bitcast.202), channel_id=1, source_target_pairs={{0,2},{1,3},{2,0},{3,1},{4,6},{5,7},{6,4},{7,5},{8,10},{9,11},{10,... | collective-permute-start | bytes 1572872 | tf_op jit(solution)/shard_map/ppermute | solution.py:16
  142.1 12.8 %copy-start.7 = (s32[128]{0:T(128)S(1)}, s32[128]{0:T(128)}, u32[]{:S(2)}) copy-start(s32[128]{0:T(128)} %param.20) | copy-start | bytes 1540
  154.9 2.9 %collective-permute-start.10 = (f32[128,2,1024]{2,0,1:T(8,128)}, f32[128,2,1024]{2,0,1:T(8,128)S(1)}, u32[]{:S(2)}, u32[]{:S(2)}) collective-permute-start(f32[128,2,1024]{2,0,1:T(8,128)} %maximum_bitcast_fusion), channel_id=1, source_target_pairs={{0,1},{1,0},{2,3},{3,2},{4,5},{5,4},{6,7},{7,6},{8,9},{9,8},{10,11... | collective-permute-start | bytes 3145736 | tf_op jit(solution)/shard_map/ppermute | solution.py:16
  158.5 2.1 copy-start.4
  175.5 3.6 %copy-start.5 = (s32[128]{0:T(128)S(1)}, s32[128]{0:T(128)}, u32[]{:S(2)}) copy-start(s32[128]{0:T(128)} %param.21) | copy-start | bytes 1540
  176.3 1.2 collective-permute-start.11
  177.5 3.7 %collective-permute-start.12 = (f32[3,128]{1,0:T(4,128)S(1)}, f32[3,128]{1,0:T(4,128)S(1)}, u32[]{:S(2)}, u32[]{:S(2)}) collective-permute-start(f32[3,128]{1,0:T(4,128)S(1)} %pad_maximum_fusion.2), channel_id=1, source_target_pairs={{0,2},{1,3},{2,0},{3,1},{4,6},{5,7},{6,4},{7,5},{8,10},{9,11},{10,... | collective-permute-start | bytes 4616 | tf_op jit(solution)/shard_map/ppermute | solution.py:16
  205.5 2.7 %collective-permute-start.13 = (f32[2,1024,128]{1,2,0:T(8,128)S(1)}, f32[2,1024,128]{1,2,0:T(8,128)S(1)}, u32[]{:S(2)}, u32[]{:S(2)}) collective-permute-start(f32[2,1024,128]{1,2,0:T(8,128)S(1)} %bitcast.205), channel_id=1, source_target_pairs={{0,1},{1,0},{2,3},{3,2},{4,5},{5,4},{6,7},{7,6},{8,9},{9,8},{10,11... | collective-permute-start | bytes 3145736 | tf_op jit(solution)/shard_map/ppermute | solution.py:16
  208.7 14.0 %collective-permute-start.14 = (f32[1,1024,128]{1,2,0:T(8,128)S(1)}, f32[1,1024,128]{1,2,0:T(8,128)S(1)}, u32[]{:S(2)}, u32[]{:S(2)}) collective-permute-start(f32[1,1024,128]{1,2,0:T(8,128)S(1)} %constant_dynamic-slice_fusion), channel_id=1, source_target_pairs={{0,2},{1,3},{2,0},{3,1},{4,6},{5,7},{6,4},{7,5},{8,10},{9,11},{10,... | collective-permute-start | bytes 1572872 | tf_op jit(solution)/shard_map/ppermute | solution.py:16
  224.4 3.7 %collective-permute-start.15 = (f32[1026]{0:T(1024)S(1)}, f32[1026]{0:T(1024)S(1)}, u32[]{:S(2)}, u32[]{:S(2)}) collective-permute-start(f32[1026]{0:T(1024)S(1)} %concatenate.11), channel_id=1, source_target_pairs={{0,4},{4,0},{8,12},{12,8},{16,20},{20,16},{24,28},{28,24},{1,5},{5... | collective-permute-start | bytes 12320 | tf_op jit(solution)/shard_map/ppermute | solution.py:16
  228.1 3.7 %collective-permute-start.16 = (f32[1026]{0:T(1024)S(1)}, f32[1026]{0:T(1024)S(1)}, u32[]{:S(2)}, u32[]{:S(2)}) collective-permute-start(f32[1026]{0:T(1024)S(1)} %add.584), channel_id=1, source_target_pairs={{0,8},{4,12},{8,0},{12,4},{16,24},{20,28},{24,16},{28,20},{1,9},{5... | collective-permute-start | bytes 12320 | tf_op jit(solution)/shard_map/ppermute | solution.py:16
  228.1 1.1 collective-permute-start.18
  229.2 3.8 %collective-permute-start.19 = (f32[128]{0:T(128)S(1)}, f32[128]{0:T(128)S(1)}, u32[]{:S(2)}, u32[]{:S(2)}) collective-permute-start(f32[128]{0:T(128)S(1)} %add.587), channel_id=1, source_target_pairs={{0,2},{1,3},{2,0},{3,1},{4,6},{5,7},{6,4},{7,5},{8,10},{9,11},{10,... | collective-permute-start | bytes 1544 | tf_op jit(solution)/shard_map/ppermute | solution.py:16
  231.7 4.5 %collective-permute-start.17 = (f32[1026]{0:T(1024)S(1)}, f32[1026]{0:T(1024)S(1)}, u32[]{:S(2)}, u32[]{:S(2)}) collective-permute-start(f32[1026]{0:T(1024)S(1)} %add.585), channel_id=1, source_target_pairs={{0,16},{4,20},{8,24},{12,28},{16,0},{20,4},{24,8},{28,12},{1,17},{... | collective-permute-start | bytes 12320 | tf_op jit(solution)/shard_map/ppermute | solution.py:16

commit v2 on v1

v2 whole, which is shorter than its diff:
```python
import jax
import jax.numpy as jnp
from jax import lax
from jax.sharding import PartitionSpec as P

HEAD_DIM = 64
ENC_MOST = 80


def is_power_of_two(n):
    return n & (n - 1) == 0


def exchange(x, axis, bit):
    size = lax.axis_size(axis)
    return lax.ppermute(x, axis, [(i, i ^ (1 << bit)) for i in range(size)])


def scatter_bits(x, axis, dim, levels):
    me = lax.axis_index(axis)
    chunks = 1 << levels
    head, width, tail = x.shape[:dim], x.shape[dim] // chunks, x.shape[dim + 1 :]
    cur = x
    bit = 0
    while chunks > 1:
        cur = cur.reshape(head + (chunks // 2, 2, width) + tail)
        side = (me >> bit) & 1
        keep = lax.dynamic_index_in_dim(cur, side, dim + 1, keepdims=False)
        send = lax.dynamic_index_in_dim(cur, 1 - side, dim + 1, keepdims=False)
        cur = keep + exchange(send, axis, bit)
        chunks //= 2
        bit += 1
    return cur.reshape(head + (width,) + tail)


def gather_bits(x, axis, dim, levels):
    me = lax.axis_index(axis)
    head, width, tail = x.shape[:dim], x.shape[dim], x.shape[dim + 1 :]
    cur = x.reshape(head + (1, width) + tail)
    chunks = 1
    for bit in range(levels):
        got = exchange(cur, axis, bit)
        low = (me >> bit) & 1 == 0
        first = jnp.where(low, cur, got)
        second = jnp.where(low, got, cur)
        cur = jnp.stack([first, second], dim).reshape(head + (chunks * 2, width) + tail)
        chunks *= 2
    return cur.reshape(head + (chunks * width,) + tail)


def sum_all(x, axis):
    size = lax.axis_size(axis)
    if not is_power_of_two(size):
        return lax.psum(x, axis)
    for bit in range(size.bit_length() - 1):
        x = x + exchange(x, axis, bit)
    return x


def merge_totals(first_set, second_set):
    larger = jnp.maximum(first_set[0], second_set[0])
    combined = first_set[1] * jnp.exp(first_set[0] - larger) + second_set[1] * jnp.exp(
        second_set[0] - larger
    )
    return jnp.stack([larger, combined, first_set[2] + second_set[2]])


def merge_all(stats, axis):
    size = lax.axis_size(axis)
    if is_power_of_two(size):
        for bit in range(size.bit_length() - 1):
            stats = merge_totals(stats, exchange(stats, axis, bit))
        return stats
    everything = lax.all_gather(stats, axis)
    return lax.fori_loop(1, size, lambda k, so_far: merge_totals(so_far, everything[k]), everything[0])


def body(
    dec_hidden,
    w_query,
    enc_states,
    w_out,
    norm_gain,
    w_vocab,
    enc_segment,
    dec_segment,
    seg_map,
    targets,
    loss_mask,
):
    dp_index = lax.axis_index("dp")
    fsdp_index = lax.axis_index("fsdp")
    dp_count = lax.axis_size("dp")
    fsdp_count = lax.axis_size("fsdp")
    dec_len, width = dec_hidden.shape
    enc_len = enc_states.shape[1]
    heads_here = w_query.shape[1] // HEAD_DIM
    segments = seg_map.shape[1]
    feature_count = width // fsdp_count
    vocab_here = w_vocab.shape[1]
    window = min(ENC_MOST, enc_len)
    split_fsdp = is_power_of_two(fsdp_count) and fsdp_count > 1
    levels = fsdp_count.bit_length() - 1

    rows = jnp.arange(dp_count)
    seg_ids = jnp.arange(segments)
    map_row = jnp.sum(jnp.where((rows == dp_index)[:, None], seg_map, 0), 0)
    sources = jnp.sum(
        jnp.where(dec_segment[:, None] == seg_ids[None, :], map_row[None, :], 0), 1
    )
    offsets = (seg_map[0] // segments) % dp_count
    hits = offsets[None, :] == rows[:, None]
    used = jnp.any(hits, 1)
    enc_rows = enc_segment.reshape(dp_count, enc_len)
    all_starts = jnp.sum(enc_rows[:, None, :] < seg_ids[None, :, None], 2)
    reader_hot = ((dp_index - rows) % dp_count)[:, None] == rows[None, :]
    reader_maps = jnp.sum(jnp.where(reader_hot[:, :, None], seg_map[None], 0), 1)
    send_seg = jnp.sum(jnp.where(hits, reader_maps, 0), 1) % segments
    my_starts = jnp.sum(jnp.where((rows == dp_index)[:, None], all_starts, 0), 0)
    send_start = jnp.clip(
        jnp.sum(jnp.where(send_seg[:, None] == seg_ids[None, :], my_starts[None, :], 0), 1),
        0,
        enc_len - window,
    )
    token_at = jnp.arange(enc_len)[None, None, :]
    send_pos = send_start[:, None] + jnp.arange(window)[None, :]
    pick = (token_at == send_pos[:, :, None]).astype(jnp.bfloat16)
    windows = jnp.einsum(
        "str,crf->sctf", pick, enc_states, preferred_element_type=jnp.float32
    ).astype(jnp.bfloat16)
    owner_hot = ((dp_index + rows) % dp_count)[:, None] == rows[None, :]
    owner_rows = jnp.sum(jnp.where(owner_hot[:, :, None], enc_rows[None], 0), 1)
    owner_starts = jnp.sum(jnp.where(owner_hot[:, :, None], all_starts[None], 0), 1)
    served = jnp.sum(jnp.where(hits, map_row[None, :], 0), 1)
    served_local = served % segments
    recv_start = jnp.clip(
        jnp.sum(jnp.where(served_local[:, None] == seg_ids[None, :], owner_starts, 0), 1),
        0,
        enc_len - window,
    )
    recv_pos = recv_start[:, None] + jnp.arange(window)[None, :]
    seg_at = jnp.sum(jnp.where(token_at == recv_pos[:, :, None], owner_rows[:, None, :], 0), 2)
    key_ids = jnp.where(used[:, None] & (seg_at == served_local[:, None]), served[:, None], -1)

    query_proj = jnp.dot(dec_hidden, w_query, preferred_element_type=jnp.float32).astype(
        jnp.bfloat16
    )
    queries = lax.optimization_barrier(query_proj).reshape(dec_len, heads_here, HEAD_DIM)
    run_sum = jnp.zeros((heads_here, dec_len), jnp.float32)
    run_acc = jnp.zeros((heads_here, dec_len, HEAD_DIM), jnp.float32)
    for shift in range(dp_count):
        block = windows[shift]
        if shift:
            block = lax.ppermute(
                block, "dp", [(i, (i - shift) % dp_count) for i in range(dp_count)]
            )
        keys_here = block[0].reshape(window, heads_here, HEAD_DIM)
        values_here = block[1].astype(jnp.float32).reshape(window, heads_here, HEAD_DIM)
        scores = jnp.einsum(
            "ihd,jhd->hij", queries, keys_here, preferred_element_type=jnp.float32
        )
        allowed = (sources[:, None] == key_ids[shift][None, :])[None]
        top = jnp.max(jnp.where(allowed, scores, jnp.float32(-1e30)), 2)
        weights = jnp.where(allowed, jnp.exp(scores - top[:, :, None]), 0.0)
        run_sum = run_sum + jnp.sum(weights, 2)
        run_acc = run_acc + jnp.einsum("hij,jhd->hid", weights, values_here)
    attended = (
        (run_acc / run_sum[:, :, None])
        .transpose(1, 0, 2)
        .reshape(dec_len, heads_here * HEAD_DIM)
        .astype(jnp.bfloat16)
    )

    feature_start = fsdp_index * feature_count
    gain_part = lax.dynamic_slice_in_dim(norm_gain, feature_start, feature_count, 0)
    hidden_part = lax.dynamic_slice_in_dim(dec_hidden, feature_start, feature_count, 1)
    projected = jnp.dot(attended, w_out, preferred_element_type=jnp.float32)
    if split_fsdp:
        projected = scatter_bits(projected, "fsdp", 1, levels)
    else:
        projected = lax.psum_scatter(projected, "fsdp", scatter_dimension=1, tiled=True)
    summed_part = projected + hidden_part.astype(jnp.float32)
    square_total = sum_all(jnp.sum(summed_part * summed_part, 1), "fsdp")
    inv_root = lax.rsqrt(square_total / width + 1e-06)
    unit_part = summed_part * inv_root[:, None]
    normed_part = (unit_part * gain_part).astype(jnp.bfloat16)
    if split_fsdp:
        half = width // 2
        top_side = (fsdp_index >> (levels - 1)) & 1
        near_rows = lax.dynamic_slice_in_dim(w_vocab, top_side * half, half, 0)
        far_rows = lax.dynamic_slice_in_dim(w_vocab, (1 - top_side) * half, half, 0)
        near_normed = gather_bits(normed_part, "fsdp", 1, levels - 1)
        far_normed = exchange(near_normed, "fsdp", levels - 1)
        logits = jnp.dot(near_normed, near_rows, preferred_element_type=jnp.float32) + jnp.dot(
            far_normed, far_rows, preferred_element_type=jnp.float32
        )
    else:
        normed_full = lax.all_gather(normed_part, "fsdp", axis=1, tiled=True)
        logits = jnp.dot(normed_full, w_vocab, preferred_element_type=jnp.float32)
    local_target = targets - fsdp_index * vocab_here
    picked = jnp.arange(vocab_here)[None, :] == local_target[:, None]
    local_top = jnp.max(logits, 1)
    local_total = jnp.sum(jnp.exp(logits - local_top[:, None]), 1)
    local_pick = jnp.sum(jnp.where(picked, logits, 0.0), 1)
    row_top, row_total, target_logit = merge_all(
        jnp.stack([local_top, local_total, local_pick]), "fsdp"
    )
    log_total = row_top + jnp.log(row_total)
    mask_float = loss_mask.astype(jnp.float32)
    grad_logits = (
        mask_float[:, None] * (jnp.exp(logits - log_total[:, None]) - picked.astype(jnp.float32))
    ).astype(jnp.bfloat16)
    contract = (((1,), (1,)), ((), ()))
    if split_fsdp:
        far_grad = lax.dot_general(
            far_rows, grad_logits, contract, preferred_element_type=jnp.float32
        )
        far_grad = exchange(scatter_bits(far_grad, "fsdp", 0, levels - 1), "fsdp", levels - 1)
        near_grad = lax.dot_general(
            near_rows, grad_logits, contract, preferred_element_type=jnp.float32
        )
        grad_normed = (scatter_bits(near_grad, "fsdp", 0, levels - 1) + far_grad).T
    else:
        grad_normed = lax.psum_scatter(
            lax.dot_general(w_vocab, grad_logits, contract, preferred_element_type=jnp.float32),
            "fsdp",
            scatter_dimension=0,
            tiled=True,
        ).T
    grad_unit = grad_normed * gain_part
    inner_total = sum_all(jnp.sum(grad_unit * unit_part, 1), "fsdp")
    grad_summed = inv_root[:, None] * (grad_unit - unit_part * (inner_total / width)[:, None])
    gain_local = jnp.sum(grad_normed * unit_part, 0)
    packed = jnp.concatenate(
        [jnp.stack([jnp.sum(mask_float), jnp.sum(mask_float * (log_total - target_logit))]), gain_local]
    )
    packed = sum_all(packed, "dp")
    token_count, loss_total, gain_total = packed[0], packed[1], packed[2:]
    return (
        loss_total / token_count,
        (grad_summed / token_count).astype(jnp.bfloat16),
        gain_total / token_count,
    )


def solution(mesh):
    in_specs = (
        P("dp", None),
        P(None, "fsdp"),
        P(None, "dp", "fsdp"),
        P("fsdp", None),
        P(),
        P(None, "fsdp"),
        P(),
        P("dp"),
        P(),
        P("dp"),
        P("dp"),
    )
    out_specs = (P(), P("dp", "fsdp"), P("fsdp"))
    return jax.shard_map(body, mesh=mesh, in_specs=in_specs, out_specs=out_specs, check_vma=False)
```

time: 244 us -> 160 us (0.66)
  between operations: 69.5 us -> 3.84 us
  local copies, waits for them, and re-layouts: 35.8 us -> 18.4 us
  other arithmetic: 19.4 us -> 13.2 us
  matrix products: 35 us -> 40.8 us
  starting transfers between devices: 21.9 us -> 26.4 us
  waiting for transfers between devices: 60.7 us -> 56.8 us
    ppermute x13 -> x16, waiting for transfers between devices: 56.9 us -> 45.6 us  [exchange(): return lax.ppermute(x, axis, [(i, i ^ 1 << bit) for i in range(size)])]
    dynamic_slice x7 -> x6, local copies, waits for them, and re-layouts: 12.2 us -> 4.41 us  [the longest x2 3.05 us: scatter_bits(): send = lax.dynamic_index_in_dim(cur, 1 - side, dim + 1, keepdims=False)]
    ppermute x7, waiting for transfers between devices: 3.77 us -> 11.2 us  [body(): lax.ppermute(block, 'dp', [(i, (i - shift) % dp_count) for i in range(dp_...]
    dot_general x5 -> x22, matrix products: 32.1 us -> 38.8 us  [the longest x1 8.36 us: body(): lax.dot_general(far_rows, grad_logits, contract, preferred_element_type=j...]
    unnamed x22 -> x14, local copies, waits for them, and re-layouts: 7.05 us -> 1.35 us
    ppermute x13 -> x16, starting transfers between devices: 9.44 us -> 13.7 us  [exchange(): return lax.ppermute(x, axis, [(i, i ^ 1 << bit) for i in range(size)])]
    select_n x1 -> x6, other arithmetic: 5.14 us -> 0.93 us  [the longest x1 0.82 us: body(): offsets = seg_map[0] // segments % dp_count]
    reduce_sum x4 -> x18, other arithmetic: 1.5 us -> 4.33 us  [the longest x1 1.12 us: body(): square_total = sum_all(jnp.sum(summed_part * summed_part, 1), 'fsdp')]
  transfers between devices with their start and end apart: 20 -> 23, of which waited for: 14 -> 15; matrix products, arithmetic and copies ran while one was open for 9% -> 19% of each run, Pallas kernels for 0% -> 0%
where the time goes in v2:
time: 160 us; the launch traced here: 159 us
  waiting for transfers between devices  56.8 us (36%)
  matrix products  40.8 us (25%)
  starting transfers between devices  26.4 us (16%)
  local copies, waits for them, and re-layouts  18.4 us (11%)
  other arithmetic  13.2 us (8%)
  between operations  3.84 us (2%)
    ppermute x16, waiting for transfers between devices, exchange(): return lax.ppermute(x, axis, [(i, i ^ 1 << bit) for i in range(size)])  45.6 us
    ppermute x16, starting transfers between devices, exchange(): return lax.ppermute(x, axis, [(i, i ^ 1 << bit) for i in range(size)])  13.7 us
    ppermute x7, starting transfers between devices, body(): lax.ppermute(block, 'dp', [(i, (i - shift) % dp_count) for i in range(dp_...  12.7 us
    ppermute x7, waiting for transfers between devices, body(): lax.ppermute(block, 'dp', [(i, (i - shift) % dp_count) for i in range(dp_...  11.2 us
    dot_general x1, matrix products, body(): lax.dot_general(far_rows, grad_logits, contract, preferred_element_type=j...  8.36 us
    dot_general x1, matrix products, body(): lax.dot_general(near_rows, grad_logits, contract, preferred_element_type=...  8.36 us
    dot_general x1, matrix products, body(): jnp.dot(far_normed, far_rows, preferred_element_type=jnp.float32)  8.27 us
    dot_general x1, matrix products, body(): jnp.dot(near_normed, near_rows, preferred_element_type=jnp.float32)  8.13 us
  transfers between devices with their start and end apart: 23, of which 15 were waited for; matrix products, arithmetic and copies ran while one was open for 19% of the time, Pallas kernels for 0%

profile of v2, /device:TPU:0, one launch (start us, length us, event | category | flops | bytes accessed | tf_op | source)
XLA Modules:
  0.0 159.4 jit_solution(999721000557680514)
XLA Ops:
  0.7 0.8 lt.71
  1.7 0.8 fusion.71
  2.5 0.8 select_reduce_fusion.11
  3.4 0.8 select_reduce_fusion.19
  5.4 6.0 %collective-permute-start = (bf16[2,80,512]{2,1,0:T(8,128)(2,1)S(1)}, bf16[2,80,512]{2,1,0:T(8,128)(2,1)S(1)}, u32[]{:S(2)}, u32[]{:S(2)}) collective-permute-start(bf16[2,80,512]{2,1,0:T(8,128)(2,1)S(1)} %get-tuple-element.26), channel_id=1, source_target_pairs={{0,28},{4,0},{8,4},{12,8},{16,12},{20,16},{24,20},{28,24},{1,29},{... | collective-permute-start | bytes 491528 | tf_op jit(solution)/shard_map/ppermute | solution.py:154
  11.9 3.0 %collective-permute-start.3 = (bf16[2,80,512]{2,1,0:T(8,128)(2,1)S(1)}, bf16[2,80,512]{2,1,0:T(8,128)(2,1)S(1)}, u32[]{:S(2)}, u32[]{:S(2)}) collective-permute-start(bf16[2,80,512]{2,1,0:T(8,128)(2,1)S(1)} %get-tuple-element.24), channel_id=1, source_target_pairs={{0,16},{4,20},{8,24},{12,28},{16,0},{20,4},{24,8},{28,12},{1,17},{... | collective-permute-start | bytes 491528 | tf_op jit(solution)/shard_map/ppermute | solution.py:154
  15.7 2.0 %convolution_convert_fusion.1 = bf16[128,512]{1,0:T(8,128)(2,1)S(1)} fusion(bf16[128,4096]{1,0:T(8,128)(2,1)} %param.11, bf16[4096,512]{1,0:T(8,128)(2,1)S(1)} %copy-done.3), kind=kOutput, calls=%fused_computation.24 | convolution fusion | flops 536936448 | bytes 5373952 | tf_op jit(solution)/shard_map/dot_general | solution.py:145
  18.7 6.5 %copy.139 = bf16[4096,512]{1,0:T(8,128)(2,1)} copy(bf16[4096,512]{0,1:T(8,128)(2,1)} %bitcast.231) | data formatting | bytes 8388608 | tf_op jit(solution)/shard_map/dot_general | solution.py:177
  25.3 1.9 %collective-permute-start.5 = (bf16[2,80,512]{2,1,0:T(8,128)(2,1)S(1)}, bf16[2,80,512]{2,1,0:T(8,128)(2,1)S(1)}, u32[]{:S(2)}, u32[]{:S(2)}) collective-permute-start(bf16[2,80,512]{2,1,0:T(8,128)(2,1)S(1)} %get-tuple-element.22), channel_id=1, source_target_pairs={{0,8},{4,12},{8,16},{12,20},{16,24},{20,28},{24,0},{28,4},{1,9},{5... | collective-permute-start | bytes 491528 | tf_op jit(solution)/shard_map/ppermute | solution.py:154
  27.3 1.4 collective-permute-start.6
  28.9 10.4 %collective-permute-done.3 = bf16[2,80,512]{2,1,0:T(8,128)(2,1)S(1)} collective-permute-done((bf16[2,80,512]{2,1,0:T(8,128)(2,1)S(1)}, bf16[2,80,512]{2,1,0:T(8,128)(2,1)S(1)}, u32[]{:S(2)}, u32[]{:S(2)}) %collective-permute-start.3) | collective-permute-done | bytes 163872 | tf_op jit(solution)/shard_map/ppermute | solution.py:154
  39.5 0.7 collective-permute-done.4
  45.4 1.3 copy-done.2
  46.7 1.5 fusion.112
  48.4 2.8 %collective-permute-done.7 = f32[128,2,1024]{2,0,1:T(8,128)} collective-permute-done((f32[128,2,1024]{2,0,1:T(8,128)S(1)}, f32[128,2,1024]{2,0,1:T(8,128)}, u32[]{:S(2)}, u32[]{:S(2)}) %collective-permute-start.7) | collective-permute-done | bytes 1048608 | tf_op jit(solution)/shard_map/ppermute | solution.py:16
  51.2 1.4 bitcast_add_fusion
  52.6 1.6 collective-permute-start.8
  54.2 12.4 %collective-permute-done.8 = f32[128,1,1024]{2,0,1:T(8,128)S(1)} collective-permute-done((f32[128,1,1024]{2,0,1:T(8,128)S(1)}, f32[128,1,1024]{2,0,1:T(8,128)S(1)}, u32[]{:S(2)}, u32[]{:S(2)}) %collective-permute-start.8) | collective-permute-done | bytes 524320 | tf_op jit(solution)/shard_map/ppermute | solution.py:16
  66.6 1.1 multiply_reduce_fusion.1
  67.8 1.1 collective-permute-done.9
  68.9 1.5 collective-permute-start.10
  70.5 0.7 dynamic_slice.38
  71.2 1.3 collective-permute-done.10
  72.7 1.5 collective-permute-done.11
  74.8 1.6 collective-permute-start.12
  76.3 8.1 %fusion.6 = f32[128,4096]{1,0:T(8,128)S(1)} fusion(bf16[128,2048]{0,1:T(8,128)(2,1)S(1)} %bitcast.246, bf16[4096,4096]{1,0:T(8,128)(2,1)} %param.16, s32[]{:T(128)S(6)} %select_n.229), kind=kOutput, calls=%fused_computation.6 | convolution fusion | flops 2147483648 | bytes 19398660 | tf_op jit(solution)/shard_map/dot_general | solution.py:194
  84.5 4.3 %collective-permute-done.12 = bf16[128,2048]{0,1:T(8,128)(2,1)S(1)} collective-permute-done((bf16[128,2048]{0,1:T(8,128)(2,1)S(1)}, bf16[128,2048]{0,1:T(8,128)(2,1)S(1)}, u32[]{:S(2)}, u32[]{:S(2)}) %collective-permute-start.12) | collective-permute-done | bytes 524320 | tf_op jit(solution)/shard_map/ppermute | solution.py:16
  88.8 8.3 %fusion.111 = (f32[128]{0:T(128)S(1)}, f32[128,4096]{1,0:T(8,128)S(1)}) fusion(f32[128,4096]{1,0:T(8,128)S(1)} %fusion.6, bf16[128,2048]{0,1:T(8,128)(2,1)S(1)} %collective-permute-done.12, bf16[4096,4096]{1,0:T(8,128)(2,1)} %param.16, s32[]{:T(128)S(6)} %select_n.230), kind=kOutput, calls=%fused_computation.240 | convolution fusion | flops 2148532224 | bytes 21496324 | tf_op jit(solution)/shard_map/dot_general | solution.py:194
  97.1 0.7 select_reduce_fusion
  97.9 1.1 collective-permute-done.13
  99.0 1.6 collective-permute-start.14
  100.6 2.1 %collective-permute-done.14 = f32[3,128]{1,0:T(4,128)S(1)} collective-permute-done((f32[3,128]{1,0:T(4,128)S(1)}, f32[3,128]{1,0:T(4,128)S(1)}, u32[]{:S(2)}, u32[]{:S(2)}) %collective-permute-start.14) | collective-permute-done | bytes 1568 | tf_op jit(solution)/shard_map/ppermute | solution.py:16
  103.3 8.4 %fusion = f32[2048,128]{1,0:T(8,128)S(1)} fusion(bf16[4096,4096]{1,0:T(8,128)(2,1)} %param.16, s32[]{:T(128)S(6)} %select_n.230, f32[128,4096]{1,0:T(8,128)S(1)} %get-tuple-element.87, f32[128]{0:T(128)S(1)} %get-tuple-element.17, f32[128]{0:T(128)S(1)} %convert_element_type.45, s32[128]{0:T(128)S(1)} %broadcast_subtract_fusion), kind=kOutput, calls=%fused_computation | convolution fusion | flops 2150629376 | bytes 19924484 | tf_op jit(solution)/shard_map/dot_general | solution.py:215
  111.7 0.9 constant_dynamic-slice_fusion
  112.6 2.0 %copy.119 = f32[1,1,1024,128]{2,3,1,0:T(8,128)} copy(f32[1,1,1024,128]{3,2,1,0:T(8,128)} %get-tuple-element.32) | data formatting | bytes 1048576 | tf_op jit(solution)/shard_map/jit(dynamic_index_in_dim)/dynamic_slice | solution.py:29
  114.6 8.4 %fusion.4 = f32[2048,128]{1,0:T(8,128)S(1)} fusion(bf16[4096,4096]{1,0:T(8,128)(2,1)} %param.16, s32[]{:T(128)S(6)} %select_n.229, f32[128,4096]{1,0:T(8,128)S(1)} %get-tuple-element.87, f32[128]{0:T(128)S(1)} %get-tuple-element.17, f32[128]{0:T(128)S(1)} %convert_element_type.45, s32[128]{0:T(128)S(1)} %broadcast_subtract_fusion), kind=kOutput, calls=%fused_computation.4 | convolution fusion | flops 2150629376 | bytes 19924484 | tf_op jit(solution)/shard_map/dot_general | solution.py:219
  123.0 1.0 copy.117
  124.8 1.1 fusion.23
  125.9 1.6 collective-permute-start.17
  127.7 12.1 %collective-permute-done.17 = f32[1024,128]{0,1:T(8,128)S(1)} collective-permute-done((f32[1024,128]{0,1:T(8,128)S(1)}, f32[1024,128]{0,1:T(8,128)S(1)}, u32[]{:S(2)}, u32[]{:S(2)}) %collective-permute-start.17) | collective-permute-done | bytes 524320 | tf_op jit(solution)/shard_map/ppermute | solution.py:16
  140.1 1.4 concatenate.3
  141.5 3.6 %collective-permute-done.18 = f32[1026]{0:T(1024)S(1)} collective-permute-done((f32[1026]{0:T(1024)S(1)}, f32[1026]{0:T(1024)S(1)}, u32[]{:S(2)}, u32[]{:S(2)}) %collective-permute-start.18) | collective-permute-done | bytes 4136 | tf_op jit(solution)/shard_map/ppermute | solution.py:16
  145.7 1.1 collective-permute-done.21
  146.9 1.5 collective-permute-start.22
  148.8 2.9 %collective-permute-start.20 = (f32[1026]{0:T(1024)S(1)}, f32[1026]{0:T(1024)S(1)}, u32[]{:S(2)}, u32[]{:S(2)}) collective-permute-start(f32[1026]{0:T(1024)S(1)} %add.347), channel_id=1, source_target_pairs={{0,16},{4,20},{8,24},{12,28},{16,0},{20,4},{24,8},{28,12},{1,17},{... | collective-permute-start | bytes 12320 | tf_op jit(solution)/shard_map/ppermute | solution.py:16
  151.6 1.7 %collective-permute-done.20 = f32[1026]{0:T(1024)S(1)} collective-permute-done((f32[1026]{0:T(1024)S(1)}, f32[1026]{0:T(1024)S(1)}, u32[]{:S(2)}, u32[]{:S(2)}) %collective-permute-start.20) | collective-permute-done | bytes 4136 | tf_op jit(solution)/shard_map/ppermute | solution.py:16
  153.9 1.4 slice_divide_fusion
  156.6 1.6 divide_convert_fusion
  (132 shorter events, 13.7 us)
Async XLA Ops:
  0.6 4.1 %copy-start = (bf16[2,192,512]{2,1,0:T(8,128)(2,1)S(1)}, bf16[2,192,512]{2,1,0:T(8,128)(2,1)}, u32[]{:S(2)}) copy-start(bf16[2,192,512]{2,1,0:T(8,128)(2,1)} %param.13) | copy-start | bytes 1179652
  4.7 10.9 %copy-start.5 = (s32[128]{0:T(128)S(1)}, s32[128]{0:T(128)}, u32[]{:S(2)}) copy-start(s32[128]{0:T(128)} %param.18) | copy-start | bytes 1540
  4.7 11.0 %copy-start.3 = (bf16[4096,512]{1,0:T(8,128)(2,1)S(1)}, bf16[4096,512]{1,0:T(8,128)(2,1)}, u32[]{:S(2)}) copy-start(bf16[4096,512]{1,0:T(8,128)(2,1)} %param.12) | copy-start | bytes 12582916
  5.4 19.9 %collective-permute-start = (bf16[2,80,512]{2,1,0:T(8,128)(2,1)S(1)}, bf16[2,80,512]{2,1,0:T(8,128)(2,1)S(1)}, u32[]{:S(2)}, u32[]{:S(2)}) collective-permute-start(bf16[2,80,512]{2,1,0:T(8,128)(2,1)S(1)} %get-tuple-element.26), channel_id=1, source_target_pairs={{0,28},{4,0},{8,4},{12,8},{16,12},{20,16},{24,20},{28,24},{1,29},{... | collective-permute-start | bytes 491528 | tf_op jit(solution)/shard_map/ppermute | solution.py:154
  11.4 15.9 %collective-permute-start.1 = (bf16[2,80,512]{2,1,0:T(8,128)(2,1)S(1)}, bf16[2,80,512]{2,1,0:T(8,128)(2,1)S(1)}, u32[]{:S(2)}, u32[]{:S(2)}) collective-permute-start(bf16[2,80,512]{2,1,0:T(8,128)(2,1)S(1)} %get-tuple-element.20), channel_id=1, source_target_pairs={{0,24},{4,28},{8,0},{12,4},{16,8},{20,12},{24,16},{28,20},{1,25},{... | collective-permute-start | bytes 491528 | tf_op jit(solution)/shard_map/ppermute | solution.py:154
  11.9 16.9 %collective-permute-start.2 = (bf16[2,80,512]{2,1,0:T(8,128)(2,1)S(1)}, bf16[2,80,512]{2,1,0:T(8,128)(2,1)S(1)}, u32[]{:S(2)}, u32[]{:S(2)}) collective-permute-start(bf16[2,80,512]{2,1,0:T(8,128)(2,1)S(1)} %get-tuple-element.25), channel_id=1, source_target_pairs={{0,20},{4,24},{8,28},{12,0},{16,4},{20,8},{24,12},{28,16},{1,21},{... | collective-permute-start | bytes 491528 | tf_op jit(solution)/shard_map/ppermute | solution.py:154
  11.9 27.5 %collective-permute-start.3 = (bf16[2,80,512]{2,1,0:T(8,128)(2,1)S(1)}, bf16[2,80,512]{2,1,0:T(8,128)(2,1)S(1)}, u32[]{:S(2)}, u32[]{:S(2)}) collective-permute-start(bf16[2,80,512]{2,1,0:T(8,128)(2,1)S(1)} %get-tuple-element.24), channel_id=1, source_target_pairs={{0,16},{4,20},{8,24},{12,28},{16,0},{20,4},{24,8},{28,12},{1,17},{... | collective-permute-start | bytes 491528 | tf_op jit(solution)/shard_map/ppermute | solution.py:154
  14.9 25.4 %collective-permute-start.4 = (bf16[2,80,512]{2,1,0:T(8,128)(2,1)S(1)}, bf16[2,80,512]{2,1,0:T(8,128)(2,1)S(1)}, u32[]{:S(2)}, u32[]{:S(2)}) collective-permute-start(bf16[2,80,512]{2,1,0:T(8,128)(2,1)S(1)} %get-tuple-element.23), channel_id=1, source_target_pairs={{0,12},{4,16},{8,20},{12,24},{16,28},{20,0},{24,4},{28,8},{1,13},{... | collective-permute-start | bytes 491528 | tf_op jit(solution)/shard_map/ppermute | solution.py:154
  25.3 15.1 %collective-permute-start.5 = (bf16[2,80,512]{2,1,0:T(8,128)(2,1)S(1)}, bf16[2,80,512]{2,1,0:T(8,128)(2,1)S(1)}, u32[]{:S(2)}, u32[]{:S(2)}) collective-permute-start(bf16[2,80,512]{2,1,0:T(8,128)(2,1)S(1)} %get-tuple-element.22), channel_id=1, source_target_pairs={{0,8},{4,12},{8,16},{12,20},{16,24},{20,28},{24,0},{28,4},{1,9},{5... | collective-permute-start | bytes 491528 | tf_op jit(solution)/shard_map/ppermute | solution.py:154
  27.3 13.2 %collective-permute-start.6 = (bf16[2,80,512]{2,1,0:T(8,128)(2,1)S(1)}, bf16[2,80,512]{2,1,0:T(8,128)(2,1)S(1)}, u32[]{:S(2)}, u32[]{:S(2)}) collective-permute-start(bf16[2,80,512]{2,1,0:T(8,128)(2,1)S(1)} %get-tuple-element.21), channel_id=1, source_target_pairs={{0,4},{4,8},{8,12},{12,16},{16,20},{20,24},{24,28},{28,0},{1,5},{5... | collective-permute-start | bytes 491528 | tf_op jit(solution)/shard_map/ppermute | solution.py:154
  44.5 2.2 %copy-start.2 = (bf16[4096,512]{1,0:T(8,128)(2,1)S(1)}, bf16[4096,512]{1,0:T(8,128)(2,1)}, u32[]{:S(2)}) copy-start(bf16[4096,512]{1,0:T(8,128)(2,1)} %copy.139) | copy-start | bytes 12582916
  48.3 2.9 %collective-permute-start.7 = (f32[128,2,1024]{2,0,1:T(8,128)S(1)}, f32[128,2,1024]{2,0,1:T(8,128)}, u32[]{:S(2)}, u32[]{:S(2)}) collective-permute-start(f32[128,2,1024]{2,0,1:T(8,128)S(1)} %dynamic-slice_bitcast_fusion), channel_id=1, source_target_pairs={{0,1},{1,0},{2,3},{3,2},{4,5},{5,4},{6,7},{7,6},{8,9},{9,8},{10,11... | collective-permute-start | bytes 3145736 | tf_op jit(solution)/shard_map/ppermute | solution.py:16
  52.6 14.0 %collective-permute-start.8 = (f32[128,1,1024]{2,0,1:T(8,128)S(1)}, f32[128,1,1024]{2,0,1:T(8,128)S(1)}, u32[]{:S(2)}, u32[]{:S(2)}) collective-permute-start(f32[128,1,1024]{2,0,1:T(8,128)S(1)} %constant_dynamic-slice_fusion.3), channel_id=1, source_target_pairs={{0,2},{1,3},{2,0},{3,1},{4,6},{5,7},{6,4},{7,5},{8,10},{9,11},{10,... | collective-permute-start | bytes 1572872 | tf_op jit(solution)/shard_map/ppermute | solution.py:16
  67.8 1.2 collective-permute-start.9
  68.9 3.5 %collective-permute-start.10 = (f32[128]{0:T(128)S(1)}, f32[128]{0:T(128)S(1)}, u32[]{:S(2)}, u32[]{:S(2)}) collective-permute-start(f32[128]{0:T(128)S(1)} %add.329), channel_id=1, source_target_pairs={{0,2},{1,3},{2,0},{3,1},{4,6},{5,7},{6,4},{7,5},{8,10},{9,11},{10,... | collective-permute-start | bytes 1544 | tf_op jit(solution)/shard_map/ppermute | solution.py:16
  72.5 3.8 %copy-start.6 = (s32[128]{0:T(128)S(1)}, s32[128]{0:T(128)}, u32[]{:S(2)}) copy-start(s32[128]{0:T(128)} %param.20) | copy-start | bytes 1540
  72.6 1.6 %collective-permute-start.11 = (bf16[128,1,1024]{2,0,1:T(8,128)(2,1)S(1)}, bf16[128,1,1024]{2,0,1:T(8,128)(2,1)S(1)}, u32[]{:S(2)}, u32[]{:S(2)}) collective-permute-start(bf16[128,1,1024]{2,0,1:T(8,128)(2,1)S(1)} %fusion.40), channel_id=1, source_target_pairs={{0,1},{1,0},{2,3},{3,2},{4,5},{5,4},{6,7},{7,6},{8,9},{9,8},{10,11... | collective-permute-start | bytes 786440 | tf_op jit(solution)/shard_map/ppermute | solution.py:16
  74.8 14.0 %collective-permute-start.12 = (bf16[128,2048]{0,1:T(8,128)(2,1)S(1)}, bf16[128,2048]{0,1:T(8,128)(2,1)S(1)}, u32[]{:S(2)}, u32[]{:S(2)}) collective-permute-start(bf16[128,2048]{0,1:T(8,128)(2,1)S(1)} %bitcast.245), channel_id=1, source_target_pairs={{0,2},{1,3},{2,0},{3,1},{4,6},{5,7},{6,4},{7,5},{8,10},{9,11},{10,... | collective-permute-start | bytes 1572872 | tf_op jit(solution)/shard_map/ppermute | solution.py:16
  97.0 3.6 %copy-start.4 = (s32[128]{0:T(128)S(1)}, s32[128]{0:T(128)}, u32[]{:S(2)}) copy-start(s32[128]{0:T(128)} %param.21) | copy-start | bytes 1540
  97.8 1.2 collective-permute-start.13
  99.0 3.7 %collective-permute-start.14 = (f32[3,128]{1,0:T(4,128)S(1)}, f32[3,128]{1,0:T(4,128)S(1)}, u32[]{:S(2)}, u32[]{:S(2)}) collective-permute-start(f32[3,128]{1,0:T(4,128)S(1)} %pad_maximum_fusion.2), channel_id=1, source_target_pairs={{0,2},{1,3},{2,0},{3,1},{4,6},{5,7},{6,4},{7,5},{8,10},{9,11},{10,... | collective-permute-start | bytes 4616 | tf_op jit(solution)/shard_map/ppermute | solution.py:16
  114.6 10.2 %collective-permute-start.16 = (f32[1,1024,128]{1,2,0:T(8,128)}, f32[1,1024,128]{1,2,0:T(8,128)}, u32[]{:S(2)}, u32[]{:S(2)}) collective-permute-start(f32[1,1024,128]{1,2,0:T(8,128)} %bitcast.247), channel_id=1, source_target_pairs={{0,1},{1,0},{2,3},{3,2},{4,5},{5,4},{6,7},{7,6},{8,9},{9,8},{10,11... | collective-permute-start | bytes 1572872 | tf_op jit(solution)/shard_map/ppermute | solution.py:16
  124.1 3.6 %collective-permute-start.15 = (f32[1,1024,128]{1,2,0:T(8,128)}, f32[1,1024,128]{1,2,0:T(8,128)S(1)}, u32[]{:S(2)}, u32[]{:S(2)}) collective-permute-start(f32[1,1024,128]{1,2,0:T(8,128)} %bitcast.62), channel_id=1, source_target_pairs={{0,1},{1,0},{2,3},{3,2},{4,5},{5,4},{6,7},{7,6},{8,9},{9,8},{10,11... | collective-permute-start | bytes 1572872 | tf_op jit(solution)/shard_map/ppermute | solution.py:16
  125.9 13.9 %collective-permute-start.17 = (f32[1024,128]{0,1:T(8,128)S(1)}, f32[1024,128]{0,1:T(8,128)S(1)}, u32[]{:S(2)}, u32[]{:S(2)}) collective-permute-start(f32[1024,128]{0,1:T(8,128)S(1)} %fusion.23), channel_id=1, source_target_pairs={{0,2},{1,3},{2,0},{3,1},{4,6},{5,7},{6,4},{7,5},{8,10},{9,11},{10,... | collective-permute-start | bytes 1572872 | tf_op jit(solution)/shard_map/ppermute | solution.py:16
  127.5 30.7 %copy-start.1 = (bf16[2,192,512]{2,1,0:T(8,128)(2,1)S(1)}, bf16[2,192,512]{2,1,0:T(8,128)(2,1)}, u32[]{:S(2)}) copy-start(bf16[2,192,512]{2,1,0:T(8,128)(2,1)} %param.13) | copy-start | bytes 1179652
  141.4 3.7 %collective-permute-start.18 = (f32[1026]{0:T(1024)S(1)}, f32[1026]{0:T(1024)S(1)}, u32[]{:S(2)}, u32[]{:S(2)}) collective-permute-start(f32[1026]{0:T(1024)S(1)} %concatenate.3), channel_id=1, source_target_pairs={{0,4},{4,0},{8,12},{12,8},{16,20},{20,16},{24,28},{28,24},{1,5},{5... | collective-permute-start | bytes 12320 | tf_op jit(solution)/shard_map/ppermute | solution.py:16
  145.1 3.7 %collective-permute-start.19 = (f32[1026]{0:T(1024)S(1)}, f32[1026]{0:T(1024)S(1)}, u32[]{:S(2)}, u32[]{:S(2)}) collective-permute-start(f32[1026]{0:T(1024)S(1)} %add.346), channel_id=1, source_target_pairs={{0,8},{4,12},{8,0},{12,4},{16,24},{20,28},{24,16},{28,20},{1,9},{5... | collective-permute-start | bytes 12320 | tf_op jit(solution)/shard_map/ppermute | solution.py:16
  145.7 1.1 collective-permute-start.21
  146.9 4.8 %collective-permute-start.22 = (f32[128]{0:T(128)S(1)}, f32[128]{0:T(128)S(1)}, u32[]{:S(2)}, u32[]{:S(2)}) collective-permute-start(f32[128]{0:T(128)S(1)} %add.349), channel_id=1, source_target_pairs={{0,2},{1,3},{2,0},{3,1},{4,6},{5,7},{6,4},{7,5},{8,10},{9,11},{10,... | collective-permute-start | bytes 1544 | tf_op jit(solution)/shard_map/ppermute | solution.py:16
  148.8 4.5 %collective-permute-start.20 = (f32[1026]{0:T(1024)S(1)}, f32[1026]{0:T(1024)S(1)}, u32[]{:S(2)}, u32[]{:S(2)}) collective-permute-start(f32[1026]{0:T(1024)S(1)} %add.347), channel_id=1, source_target_pairs={{0,16},{4,20},{8,24},{12,28},{16,0},{20,4},{24,8},{28,12},{1,17},{... | collective-permute-start | bytes 12320 | tf_op jit(solution)/shard_map/ppermute | solution.py:16

commit v3 on v2

--- a/solution.py
+++ b/solution.py
@@ -16,7 +16,7 @@
     return lax.ppermute(x, axis, [(i, i ^ (1 << bit)) for i in range(size)])
 
 
-def scatter_bits(x, axis, dim, levels):
+def scatter_bits(x, axis, dim, levels, last_wire=None):
     me = lax.axis_index(axis)
     chunks = 1 << levels
     head, width, tail = x.shape[:dim], x.shape[dim] // chunks, x.shape[dim + 1 :]
@@ -27,7 +27,10 @@
         side = (me >> bit) & 1
         keep = lax.dynamic_index_in_dim(cur, side, dim + 1, keepdims=False)
         send = lax.dynamic_index_in_dim(cur, 1 - side, dim + 1, keepdims=False)
-        cur = keep + exchange(send, axis, bit)
+        if last_wire is not None and chunks == 2:
+            cur = keep + exchange(send.astype(last_wire), axis, bit).astype(keep.dtype)
+        else:
+            cur = keep + exchange(send, axis, bit)
         chunks //= 2
         bit += 1
     return cur.reshape(head + (width,) + tail)
@@ -174,9 +177,11 @@
     feature_start = fsdp_index * feature_count
     gain_part = lax.dynamic_slice_in_dim(norm_gain, feature_start, feature_count, 0)
     hidden_part = lax.dynamic_slice_in_dim(dec_hidden, feature_start, feature_count, 1)
-    projected = jnp.dot(attended, w_out, preferred_element_type=jnp.float32)
+    projected = lax.optimization_barrier(
+        jnp.dot(attended, w_out, preferred_element_type=jnp.float32)
+    )
     if split_fsdp:
-        projected = scatter_bits(projected, "fsdp", 1, levels)
+        projected = scatter_bits(projected, "fsdp", 1, levels, jnp.bfloat16)
     else:
         projected = lax.psum_scatter(projected, "fsdp", scatter_dimension=1, tiled=True)
     summed_part = projected + hidden_part.astype(jnp.float32)
@@ -215,9 +220,14 @@
         far_grad = lax.dot_general(
             far_rows, grad_logits, contract, preferred_element_type=jnp.float32
         )
-        far_grad = exchange(scatter_bits(far_grad, "fsdp", 0, levels - 1), "fsdp", levels - 1)
+        far_grad, near_logits = lax.optimization_barrier(
+            (scatter_bits(far_grad, "fsdp", 0, levels - 1), grad_logits)
+        )
+        far_grad = exchange(far_grad.astype(jnp.bfloat16), "fsdp", levels - 1).astype(
+            jnp.float32
+        )
         near_grad = lax.dot_general(
-            near_rows, grad_logits, contract, preferred_element_type=jnp.float32
+            near_rows, near_logits, contract, preferred_element_type=jnp.float32
         )
         grad_normed = (scatter_bits(near_grad, "fsdp", 0, levels - 1) + far_grad).T
     else:

time: 160 us -> 158 us (0.988)
  waiting for transfers between devices: 56.8 us -> 41.4 us
  local copies, waits for them, and re-layouts: 18.4 us -> 25.5 us
  starting transfers between devices: 26.4 us -> 33.4 us
    ppermute x16, waiting for transfers between devices: 45.6 us -> 34.9 us  [exchange(): return lax.ppermute(x, axis, [(i, i ^ 1 << bit) for i in range(size)])]
    dot_general x1 -> x0, local copies, waits for them, and re-layouts: 6.47 us -> none  [body(): projected = jnp.dot(attended, w_out, preferred_element_type=jnp.float32)]
    slice x8, local copies, waits for them, and re-layouts: 0.1 us -> 5.66 us  [body(): keys_here = block[0].reshape(window, heads_here, HEAD_DIM)]
    ppermute x16, starting transfers between devices: 13.7 us -> 19.2 us  [exchange(): return lax.ppermute(x, axis, [(i, i ^ 1 << bit) for i in range(size)])]
    ppermute x7, waiting for transfers between devices: 11.2 us -> 6.5 us  [body(): lax.ppermute(block, 'dp', [(i, (i - shift) % dp_count) for i in range(dp_...]
    dynamic_slice x4 -> x2, local copies, waits for them, and re-layouts: 1.35 us -> 5.13 us  [scatter_bits(): keep = lax.dynamic_index_in_dim(cur, side, dim + 1, keepdims=False)]
    reshape x0 -> x1, local copies, waits for them, and re-layouts: none -> 3.02 us  [scatter_bits(): cur = cur.reshape(head + (chunks // 2, 2, width) + tail)]
    unnamed x14 -> x26, local copies, waits for them, and re-layouts: 1.35 us -> 3.37 us
  transfers between devices with their start and end apart: 23 -> 23, of which waited for: 15 -> 15; matrix products, arithmetic and copies ran while one was open for 19% -> 12% of each run, Pallas kernels for 0% -> 0%
where the time goes in v3:
time: 158 us; the launch traced here: 157 us
  waiting for transfers between devices  41.4 us (26%)
  matrix products  39.6 us (25%)
  starting transfers between devices  33.4 us (21%)
  local copies, waits for them, and re-layouts  25.5 us (16%)
  other arithmetic  13.6 us (9%)
  between operations  3.86 us (2%)
    ppermute x16, waiting for transfers between devices, exchange(): return lax.ppermute(x, axis, [(i, i ^ 1 << bit) for i in range(size)])  34.9 us
    ppermute x16, starting transfers between devices, exchange(): return lax.ppermute(x, axis, [(i, i ^ 1 << bit) for i in range(size)])  19.2 us
    ppermute x7, starting transfers between devices, body(): lax.ppermute(block, 'dp', [(i, (i - shift) % dp_count) for i in range(dp_...  14.2 us
    dot_general x1, matrix products, body(): lax.dot_general(far_rows, grad_logits, contract, preferred_element_type=j...  8.35 us
    dot_general x1, matrix products, body(): jnp.dot(far_normed, far_rows, preferred_element_type=jnp.float32)  8.27 us
    dot_general x1, matrix products, body(): lax.dot_general(near_rows, near_logits, contract, preferred_element_type=...  8.13 us
    dot_general x1, matrix products, body(): jnp.dot(near_normed, near_rows, preferred_element_type=jnp.float32)  8.13 us
    ppermute x7, waiting for transfers between devices, body(): lax.ppermute(block, 'dp', [(i, (i - shift) % dp_count) for i in range(dp_...  6.5 us
  transfers between devices with their start and end apart: 23, of which 15 were waited for; matrix products, arithmetic and copies ran while one was open for 12% of the time, Pallas kernels for 0%

profile of v3, /device:TPU:0, one launch (start us, length us, event | category | flops | bytes accessed | tf_op | source)
XLA Modules:
  0.0 157.4 jit_solution(4515735529542164692)
XLA Ops:
  4.8 1.7 %fusion.11 = bf16[8,2,80,512]{3,2,1,0:T(8,128)(2,1)S(1)} fusion(bf16[2,192,512]{2,1,0:T(8,128)(2,1)} %param.13, s32[8,80]{1,0:T(8,128)S(1)} %iota_add_fusion), kind=kOutput, calls=%fused_computation.14 | convolution fusion | flops 252436480 | bytes 1706496 | tf_op jit(solution)/shard_map/str,crf->sctf/dot_general | solution.py:131
  7.2 5.0 %collective-permute-start.1 = (bf16[2,80,512]{2,1,0:T(8,128)(2,1)S(1)}, bf16[2,80,512]{2,1,0:T(8,128)(2,1)}, u32[]{:S(2)}, u32[]{:S(2)}) collective-permute-start(bf16[2,80,512]{2,1,0:T(8,128)(2,1)S(1)} %get-tuple-element.29), channel_id=1, source_target_pairs={{0,24},{4,28},{8,0},{12,4},{16,8},{20,12},{24,16},{28,20},{1,25},{... | collective-permute-start | bytes 491528 | tf_op jit(solution)/shard_map/ppermute | solution.py:157
  12.3 1.5 collective-permute-start.6
  13.8 1.0 collective-permute-start.4
  14.8 2.8 %collective-permute-start.3 = (bf16[2,80,512]{2,1,0:T(8,128)(2,1)S(1)}, bf16[2,80,512]{2,1,0:T(8,128)(2,1)S(1)}, u32[]{:S(2)}, u32[]{:S(2)}) collective-permute-start(bf16[2,80,512]{2,1,0:T(8,128)(2,1)S(1)} %get-tuple-element.33), channel_id=1, source_target_pairs={{0,16},{4,20},{8,24},{12,28},{16,0},{20,4},{24,8},{28,12},{1,17},{... | collective-permute-start | bytes 491528 | tf_op jit(solution)/shard_map/ppermute | solution.py:157
  21.5 1.0 collective-permute-start.2
  22.5 0.9 fusion.103
  23.7 2.9 %collective-permute-start = (bf16[2,80,512]{2,1,0:T(8,128)(2,1)S(1)}, bf16[2,80,512]{2,1,0:T(8,128)(2,1)}, u32[]{:S(2)}, u32[]{:S(2)}) collective-permute-start(bf16[2,80,512]{2,1,0:T(8,128)(2,1)S(1)} %get-tuple-element.35), channel_id=1, source_target_pairs={{0,28},{4,0},{8,4},{12,8},{16,12},{20,16},{24,20},{28,24},{1,29},{... | collective-permute-start | bytes 491528 | tf_op jit(solution)/shard_map/ppermute | solution.py:157
  27.8 0.9 fusion.108
  28.9 6.5 %collective-permute-done.4 = bf16[2,80,512]{2,1,0:T(8,128)(2,1)} collective-permute-done((bf16[2,80,512]{2,1,0:T(8,128)(2,1)S(1)}, bf16[2,80,512]{2,1,0:T(8,128)(2,1)}, u32[]{:S(2)}, u32[]{:S(2)}) %collective-permute-start.4) | collective-permute-done | bytes 163872 | tf_op jit(solution)/shard_map/ppermute | solution.py:157
  35.4 0.9 fusion.107
  36.9 0.9 fusion.105
  38.1 0.9 fusion.104
  43.2 1.3 copy-done.3
  45.2 3.0 %reshape.535 = f32[128,2,2,1024]{3,2,1,0:T(2,128)} reshape(f32[128,4096]{1,0:T(8,128)S(1)} %fusion.112) | data formatting | bytes 4194304 | tf_op jit(solution)/shard_map/reshape | solution.py:26
  48.3 4.4 %constant_dynamic-slice_fusion.2 = (f32[128,2,1,1024]{3,2,1,0:T(1,128)S(1)}, f32[128,2,1,1024]{3,2,1,0:T(1,128)S(1)}) fusion(f32[128,2,2,1024]{3,2,1,0:T(2,128)} %reshape.535, s32[]{:T(128)S(6)} %select_n.222, s32[]{:T(128)S(6)} %select_n.223), kind=kLoop, calls=%fused_computation.144 | loop fusion | bytes 4194312 | tf_op jit(solution)/shard_map/jit(dynamic_index_in_dim)/dynamic_slice | solution.py:28
  52.6 2.0 %copy.88 = f32[128,2,1,1024]{0,3,1,2:T(8,128)} copy(f32[128,2,1,1024]{3,2,1,0:T(1,128)S(1)} %get-tuple-element.28) | data formatting | bytes 2097152 | tf_op jit(solution)/shard_map/jit(dynamic_index_in_dim)/dynamic_slice | solution.py:29
  55.4 2.2 %collective-permute-done.7 = f32[128,2,1024]{0,2,1:T(8,128)} collective-permute-done((f32[128,2,1024]{0,2,1:T(8,128)}, f32[128,2,1024]{0,2,1:T(8,128)}, u32[]{:S(2)}, u32[]{:S(2)}) %collective-permute-start.7) | collective-permute-done | bytes 1048608 | tf_op jit(solution)/shard_map/ppermute | solution.py:16
  57.6 1.3 bitcast_add_fusion
  59.0 1.0 copy-done.4
  60.0 1.6 %collective-permute-start.8 = (bf16[128,1,1024]{0,2,1:T(8,128)(2,1)S(1)}, bf16[128,1,1024]{0,2,1:T(8,128)(2,1)S(1)}, u32[]{:S(2)}, u32[]{:S(2)}) collective-permute-start(bf16[128,1,1024]{0,2,1:T(8,128)(2,1)S(1)} %dynamic-slice_convert_fusion), channel_id=1, source_target_pairs={{0,2},{1,3},{2,0},{3,1},{4,6},{5,7},{6,4},{7,5},{8,10},{9,11},{10,... | collective-permute-start | bytes 786440 | tf_op jit(solution)/shard_map/ppermute | solution.py:16
  61.8 6.6 %collective-permute-done.8 = bf16[128,1,1024]{0,2,1:T(8,128)(2,1)S(1)} collective-permute-done((bf16[128,1,1024]{0,2,1:T(8,128)(2,1)S(1)}, bf16[128,1,1024]{0,2,1:T(8,128)(2,1)S(1)}, u32[]{:S(2)}, u32[]{:S(2)}) %collective-permute-start.8) | collective-permute-done | bytes 262176 | tf_op jit(solution)/shard_map/ppermute | solution.py:16
  68.4 1.2 multiply_reduce_fusion.1
  69.7 1.1 collective-permute-done.9
  70.8 1.5 collective-permute-start.10
  73.0 1.3 collective-permute-done.10
  74.6 1.5 collective-permute-done.11
  76.4 1.6 %collective-permute-start.12 = (bf16[128,2048]{0,1:T(8,128)(2,1)S(1)}, bf16[128,2048]{0,1:T(8,128)(2,1)S(1)}, u32[]{:S(2)}, u32[]{:S(2)}) collective-permute-start(bf16[128,2048]{0,1:T(8,128)(2,1)S(1)} %bitcast.247), channel_id=1, source_target_pairs={{0,2},{1,3},{2,0},{3,1},{4,6},{5,7},{6,4},{7,5},{8,10},{9,11},{10,... | collective-permute-start | bytes 1572872 | tf_op jit(solution)/shard_map/ppermute | solution.py:16
  78.0 8.1 %fusion.6 = f32[128,4096]{1,0:T(8,128)S(1)} fusion(bf16[128,2048]{0,1:T(8,128)(2,1)S(1)} %bitcast.248, bf16[4096,4096]{1,0:T(8,128)(2,1)} %param.16, s32[]{:T(128)S(6)} %select_n.229), kind=kOutput, calls=%fused_computation.6 | convolution fusion | flops 2147483648 | bytes 19398660 | tf_op jit(solution)/shard_map/dot_general | solution.py:199
  86.1 4.3 %collective-permute-done.12 = bf16[128,2048]{0,1:T(8,128)(2,1)S(1)} collective-permute-done((bf16[128,2048]{0,1:T(8,128)(2,1)S(1)}, bf16[128,2048]{0,1:T(8,128)(2,1)S(1)}, u32[]{:S(2)}, u32[]{:S(2)}) %collective-permute-start.12) | collective-permute-done | bytes 524320 | tf_op jit(solution)/shard_map/ppermute | solution.py:16
  90.4 8.3 %fusion.111 = (f32[128]{0:T(128)S(1)}, f32[128,4096]{1,0:T(8,128)S(1)}) fusion(f32[128,4096]{1,0:T(8,128)S(1)} %fusion.6, bf16[128,2048]{0,1:T(8,128)(2,1)S(1)} %collective-permute-done.12, bf16[4096,4096]{1,0:T(8,128)(2,1)} %param.16, s32[]{:T(128)S(6)} %select_n.230), kind=kOutput, calls=%fused_computation.240 | convolution fusion | flops 2148532224 | bytes 21496324 | tf_op jit(solution)/shard_map/dot_general | solution.py:199
  99.5 1.1 collective-permute-done.13
  100.7 1.6 %collective-permute-start.14 = (f32[3,128]{1,0:T(4,128)S(1)}, f32[3,128]{1,0:T(4,128)S(1)}, u32[]{:S(2)}, u32[]{:S(2)}) collective-permute-start(f32[3,128]{1,0:T(4,128)S(1)} %pad_maximum_fusion.2), channel_id=1, source_target_pairs={{0,2},{1,3},{2,0},{3,1},{4,6},{5,7},{6,4},{7,5},{8,10},{9,11},{10,... | collective-permute-start | bytes 4616 | tf_op jit(solution)/shard_map/ppermute | solution.py:16
  102.3 2.1 %collective-permute-done.14 = f32[3,128]{1,0:T(4,128)S(1)} collective-permute-done((f32[3,128]{1,0:T(4,128)S(1)}, f32[3,128]{1,0:T(4,128)S(1)}, u32[]{:S(2)}, u32[]{:S(2)}) %collective-permute-start.14) | collective-permute-done | bytes 1568 | tf_op jit(solution)/shard_map/ppermute | solution.py:16
  105.6 8.3 %fusion = f32[2048,128]{1,0:T(8,128)S(1)} fusion(bf16[128,4096]{1,0:T(8,128)(2,1)S(1)} %multiply_convert_fusion, bf16[4096,4096]{1,0:T(8,128)(2,1)} %param.16, s32[]{:T(128)S(6)} %select_n.230), kind=kOutput, calls=%fused_computation | convolution fusion | flops 2147483648 | bytes 18874372 | tf_op jit(solution)/shard_map/dot_general | solution.py:220
  114.1 1.9 %collective-permute-done.15 = f32[1,1024,128]{2,1,0:T(8,128)S(1)} collective-permute-done((f32[1,1024,128]{2,1,0:T(8,128)S(1)}, f32[1,1024,128]{2,1,0:T(8,128)S(1)}, u32[]{:S(2)}, u32[]{:S(2)}) %collective-permute-start.15) | collective-permute-done | bytes 524320 | tf_op jit(solution)/shard_map/ppermute | solution.py:16
  116.1 8.1 %fusion.4 = f32[2048,128]{1,0:T(8,128)S(1)} fusion(bf16[128,4096]{1,0:T(8,128)(2,1)S(1)} %multiply_convert_fusion, bf16[4096,4096]{1,0:T(8,128)(2,1)} %param.16, s32[]{:T(128)S(6)} %select_n.229), kind=kOutput, calls=%fused_computation.4 | convolution fusion | flops 2147483648 | bytes 18874372 | tf_op jit(solution)/shard_map/dot_general | solution.py:229
  124.5 1.5 collective-permute-start.17
  126.0 7.0 %collective-permute-done.17 = bf16[1024,128]{1,0:T(8,128)(2,1)S(1)} collective-permute-done((bf16[1024,128]{1,0:T(8,128)(2,1)S(1)}, bf16[1024,128]{1,0:T(8,128)(2,1)S(1)}, u32[]{:S(2)}, u32[]{:S(2)}) %collective-permute-start.17) | collective-permute-done | bytes 262176 | tf_op jit(solution)/shard_map/ppermute | solution.py:16
  133.4 1.4 concatenate.3
  134.8 3.3 %collective-permute-start.18 = (f32[1026]{0:T(1024)S(1)}, f32[1026]{0:T(1024)S(1)}, u32[]{:S(2)}, u32[]{:S(2)}) collective-permute-start(f32[1026]{0:T(1024)S(1)} %concatenate.3), channel_id=1, source_target_pairs={{0,4},{4,0},{8,12},{12,8},{16,20},{20,16},{24,28},{28,24},{1,5},{5... | collective-permute-start | bytes 12320 | tf_op jit(solution)/shard_map/ppermute | solution.py:16
  138.1 1.6 %collective-permute-done.18 = f32[1026]{0:T(1024)S(1)} collective-permute-done((f32[1026]{0:T(1024)S(1)}, f32[1026]{0:T(1024)S(1)}, u32[]{:S(2)}, u32[]{:S(2)}) %collective-permute-start.18) | collective-permute-done | bytes 4136 | tf_op jit(solution)/shard_map/ppermute | solution.py:16
  139.7 4.4 %collective-permute-start.19 = (f32[1026]{0:T(1024)S(1)}, f32[1026]{0:T(1024)S(1)}, u32[]{:S(2)}, u32[]{:S(2)}) collective-permute-start(f32[1026]{0:T(1024)S(1)} %add.346), channel_id=1, source_target_pairs={{0,8},{4,12},{8,0},{12,4},{16,24},{20,28},{24,16},{28,20},{1,9},{5... | collective-permute-start | bytes 12320 | tf_op jit(solution)/shard_map/ppermute | solution.py:16
  144.1 1.1 collective-permute-done.21
  145.2 1.5 collective-permute-start.22
  146.8 1.7 %collective-permute-start.20 = (f32[1026]{0:T(1024)S(1)}, f32[1026]{0:T(1024)S(1)}, u32[]{:S(2)}, u32[]{:S(2)}) collective-permute-start(f32[1026]{0:T(1024)S(1)} %add.347), channel_id=1, source_target_pairs={{0,16},{4,20},{8,24},{12,28},{16,0},{20,4},{24,8},{28,12},{1,17},{... | collective-permute-start | bytes 12320 | tf_op jit(solution)/shard_map/ppermute | solution.py:16
  148.8 2.5 %collective-permute-done.20 = f32[1026]{0:T(1024)S(1)} collective-permute-done((f32[1026]{0:T(1024)S(1)}, f32[1026]{0:T(1024)S(1)}, u32[]{:S(2)}, u32[]{:S(2)}) %collective-permute-start.20) | collective-permute-done | bytes 4136 | tf_op jit(solution)/shard_map/ppermute | solution.py:16
  151.9 1.3 slice_divide_fusion
  (143 shorter events, 23.4 us)
Async XLA Ops:
  0.6 17.8 %copy-start = (bf16[128,4096]{1,0:T(8,128)(2,1)S(1)}, bf16[128,4096]{1,0:T(8,128)(2,1)}, u32[]{:S(2)}) copy-start(bf16[128,4096]{1,0:T(8,128)(2,1)} %param.11) | copy-start | bytes 3145732
  4.8 13.1 %copy-start.10 = (s32[128]{0:T(128)S(1)}, s32[128]{0:T(128)}, u32[]{:S(2)}) copy-start(s32[128]{0:T(128)} %param.18) | copy-start | bytes 1540
  4.8 13.7 %copy-start.2 = (bf16[4096,512]{1,0:T(8,128)(2,1)S(1)}, bf16[4096,512]{1,0:T(8,128)(2,1)}, u32[]{:S(2)}) copy-start(bf16[4096,512]{1,0:T(8,128)(2,1)} %param.12) | copy-start | bytes 12582916
  7.2 14.2 %collective-permute-start.1 = (bf16[2,80,512]{2,1,0:T(8,128)(2,1)S(1)}, bf16[2,80,512]{2,1,0:T(8,128)(2,1)}, u32[]{:S(2)}, u32[]{:S(2)}) collective-permute-start(bf16[2,80,512]{2,1,0:T(8,128)(2,1)S(1)} %get-tuple-element.29), channel_id=1, source_target_pairs={{0,24},{4,28},{8,0},{12,4},{16,8},{20,12},{24,16},{28,20},{1,25},{... | collective-permute-start | bytes 491528 | tf_op jit(solution)/shard_map/ppermute | solution.py:157
  12.3 11.4 %collective-permute-start.6 = (bf16[2,80,512]{2,1,0:T(8,128)(2,1)S(1)}, bf16[2,80,512]{2,1,0:T(8,128)(2,1)}, u32[]{:S(2)}, u32[]{:S(2)}) collective-permute-start(bf16[2,80,512]{2,1,0:T(8,128)(2,1)S(1)} %get-tuple-element.30), channel_id=1, source_target_pairs={{0,4},{4,8},{8,12},{12,16},{16,20},{20,24},{24,28},{28,0},{1,5},{5... | collective-permute-start | bytes 491528 | tf_op jit(solution)/shard_map/ppermute | solution.py:157
  13.8 14.0 %collective-permute-start.5 = (bf16[2,80,512]{2,1,0:T(8,128)(2,1)S(1)}, bf16[2,80,512]{2,1,0:T(8,128)(2,1)}, u32[]{:S(2)}, u32[]{:S(2)}) collective-permute-start(bf16[2,80,512]{2,1,0:T(8,128)(2,1)S(1)} %get-tuple-element.31), channel_id=1, source_target_pairs={{0,8},{4,12},{8,16},{12,20},{16,24},{20,28},{24,0},{28,4},{1,9},{5... | collective-permute-start | bytes 491528 | tf_op jit(solution)/shard_map/ppermute | solution.py:157
  13.8 21.7 %collective-permute-start.4 = (bf16[2,80,512]{2,1,0:T(8,128)(2,1)S(1)}, bf16[2,80,512]{2,1,0:T(8,128)(2,1)}, u32[]{:S(2)}, u32[]{:S(2)}) collective-permute-start(bf16[2,80,512]{2,1,0:T(8,128)(2,1)S(1)} %get-tuple-element.32), channel_id=1, source_target_pairs={{0,12},{4,16},{8,20},{12,24},{16,28},{20,0},{24,4},{28,8},{1,13},{... | collective-permute-start | bytes 491528 | tf_op jit(solution)/shard_map/ppermute | solution.py:157
  14.8 21.9 %collective-permute-start.3 = (bf16[2,80,512]{2,1,0:T(8,128)(2,1)S(1)}, bf16[2,80,512]{2,1,0:T(8,128)(2,1)S(1)}, u32[]{:S(2)}, u32[]{:S(2)}) collective-permute-start(bf16[2,80,512]{2,1,0:T(8,128)(2,1)S(1)} %get-tuple-element.33), channel_id=1, source_target_pairs={{0,16},{4,20},{8,24},{12,28},{16,0},{20,4},{24,8},{28,12},{1,17},{... | collective-permute-start | bytes 491528 | tf_op jit(solution)/shard_map/ppermute | solution.py:157
  21.5 15.5 %collective-permute-start.2 = (bf16[2,80,512]{2,1,0:T(8,128)(2,1)}, bf16[2,80,512]{2,1,0:T(8,128)(2,1)}, u32[]{:S(2)}, u32[]{:S(2)}) collective-permute-start(bf16[2,80,512]{2,1,0:T(8,128)(2,1)} %get-tuple-element.34), channel_id=1, source_target_pairs={{0,20},{4,24},{8,28},{12,0},{16,4},{20,8},{24,12},{28,16},{1,21},{... | collective-permute-start | bytes 491528 | tf_op jit(solution)/shard_map/ppermute | solution.py:157
  23.7 14.5 %collective-permute-start = (bf16[2,80,512]{2,1,0:T(8,128)(2,1)S(1)}, bf16[2,80,512]{2,1,0:T(8,128)(2,1)}, u32[]{:S(2)}, u32[]{:S(2)}) collective-permute-start(bf16[2,80,512]{2,1,0:T(8,128)(2,1)S(1)} %get-tuple-element.35), channel_id=1, source_target_pairs={{0,28},{4,0},{8,4},{12,8},{16,12},{20,16},{24,20},{28,24},{1,29},{... | collective-permute-start | bytes 491528 | tf_op jit(solution)/shard_map/ppermute | solution.py:157
  27.5 11.9 %copy-start.7 = (pred[128,80]{0,1:T(8,128)(4,1)S(1)}, pred[128,80]{0,1:T(8,128)(4,1)}, u32[]{:S(2)}) copy-start(pred[128,80]{0,1:T(8,128)(4,1)} %get-tuple-element.69) | copy-start | bytes 30724
  36.5 3.4 %copy-start.6 = (pred[128,80]{0,1:T(8,128)(4,1)S(1)}, pred[128,80]{0,1:T(8,128)(4,1)}, u32[]{:S(2)}) copy-start(pred[128,80]{0,1:T(8,128)(4,1)} %get-tuple-element.70) | copy-start | bytes 30724
  38.1 2.3 %copy-start.5 = (pred[128,80]{0,1:T(8,128)(4,1)S(1)}, pred[128,80]{0,1:T(8,128)(4,1)}, u32[]{:S(2)}) copy-start(pred[128,80]{0,1:T(8,128)(4,1)} %get-tuple-element.71) | copy-start | bytes 30724
  41.8 1.2 copy-start.8
  42.3 2.2 %copy-start.3 = (bf16[512,4096]{1,0:T(8,128)(2,1)S(1)}, bf16[512,4096]{1,0:T(8,128)(2,1)}, u32[]{:S(2)}) copy-start(bf16[512,4096]{1,0:T(8,128)(2,1)} %param.14) | copy-start | bytes 12582916
  54.6 3.0 %collective-permute-start.7 = (f32[128,2,1024]{0,2,1:T(8,128)}, f32[128,2,1024]{0,2,1:T(8,128)}, u32[]{:S(2)}, u32[]{:S(2)}) collective-permute-start(f32[128,2,1024]{0,2,1:T(8,128)} %bitcast.235), channel_id=1, source_target_pairs={{0,1},{1,0},{2,3},{3,2},{4,5},{5,4},{6,7},{7,6},{8,9},{9,8},{10,11... | collective-permute-start | bytes 3145736 | tf_op jit(solution)/shard_map/ppermute | solution.py:16
  59.0 1.0 copy-start.4
  60.0 8.4 %collective-permute-start.8 = (bf16[128,1,1024]{0,2,1:T(8,128)(2,1)S(1)}, bf16[128,1,1024]{0,2,1:T(8,128)(2,1)S(1)}, u32[]{:S(2)}, u32[]{:S(2)}) collective-permute-start(bf16[128,1,1024]{0,2,1:T(8,128)(2,1)S(1)} %dynamic-slice_convert_fusion), channel_id=1, source_target_pairs={{0,2},{1,3},{2,0},{3,1},{4,6},{5,7},{6,4},{7,5},{8,10},{9,11},{10,... | collective-permute-start | bytes 786440 | tf_op jit(solution)/shard_map/ppermute | solution.py:16
  61.8 16.2 %copy-start.11 = (s32[128]{0:T(128)S(1)}, s32[128]{0:T(128)}, u32[]{:S(2)}) copy-start(s32[128]{0:T(128)} %param.20) | copy-start | bytes 1540
  69.6 1.2 collective-permute-start.9
  70.8 3.5 %collective-permute-start.10 = (f32[128]{0:T(128)S(1)}, f32[128]{0:T(128)S(1)}, u32[]{:S(2)}, u32[]{:S(2)}) collective-permute-start(f32[128]{0:T(128)S(1)} %add.329), channel_id=1, source_target_pairs={{0,2},{1,3},{2,0},{3,1},{4,6},{5,7},{6,4},{7,5},{8,10},{9,11},{10,... | collective-permute-start | bytes 1544 | tf_op jit(solution)/shard_map/ppermute | solution.py:16
  74.5 1.6 %collective-permute-start.11 = (bf16[128,1,1024]{0,2,1:T(8,128)(2,1)S(1)}, bf16[128,1,1024]{0,2,1:T(8,128)(2,1)S(1)}, u32[]{:S(2)}, u32[]{:S(2)}) collective-permute-start(bf16[128,1,1024]{0,2,1:T(8,128)(2,1)S(1)} %fusion.40), channel_id=1, source_target_pairs={{0,1},{1,0},{2,3},{3,2},{4,5},{5,4},{6,7},{7,6},{8,9},{9,8},{10,11... | collective-permute-start | bytes 786440 | tf_op jit(solution)/shard_map/ppermute | solution.py:16
  76.4 14.0 %collective-permute-start.12 = (bf16[128,2048]{0,1:T(8,128)(2,1)S(1)}, bf16[128,2048]{0,1:T(8,128)(2,1)S(1)}, u32[]{:S(2)}, u32[]{:S(2)}) collective-permute-start(bf16[128,2048]{0,1:T(8,128)(2,1)S(1)} %bitcast.247), channel_id=1, source_target_pairs={{0,2},{1,3},{2,0},{3,1},{4,6},{5,7},{6,4},{7,5},{8,10},{9,11},{10,... | collective-permute-start | bytes 1572872 | tf_op jit(solution)/shard_map/ppermute | solution.py:16
  98.7 3.6 %copy-start.9 = (s32[128]{0:T(128)S(1)}, s32[128]{0:T(128)}, u32[]{:S(2)}) copy-start(s32[128]{0:T(128)} %param.21) | copy-start | bytes 1540
  99.4 1.2 collective-permute-start.13
  100.7 3.7 %collective-permute-start.14 = (f32[3,128]{1,0:T(4,128)S(1)}, f32[3,128]{1,0:T(4,128)S(1)}, u32[]{:S(2)}, u32[]{:S(2)}) collective-permute-start(f32[3,128]{1,0:T(4,128)S(1)} %pad_maximum_fusion.2), channel_id=1, source_target_pairs={{0,2},{1,3},{2,0},{3,1},{4,6},{5,7},{6,4},{7,5},{8,10},{9,11},{10,... | collective-permute-start | bytes 4616 | tf_op jit(solution)/shard_map/ppermute | solution.py:16
  114.0 2.0 %collective-permute-start.15 = (f32[1,1024,128]{2,1,0:T(8,128)S(1)}, f32[1,1024,128]{2,1,0:T(8,128)S(1)}, u32[]{:S(2)}, u32[]{:S(2)}) collective-permute-start(f32[1,1024,128]{2,1,0:T(8,128)S(1)} %dynamic-slice_bitcast_fusion.1), channel_id=1, source_target_pairs={{0,1},{1,0},{2,3},{3,2},{4,5},{5,4},{6,7},{7,6},{8,9},{9,8},{10,11... | collective-permute-start | bytes 1572872 | tf_op jit(solution)/shard_map/ppermute | solution.py:16
  124.2 32.1 %copy-start.1 = (bf16[128,4096]{1,0:T(8,128)(2,1)S(1)}, bf16[128,4096]{1,0:T(8,128)(2,1)}, u32[]{:S(2)}) copy-start(bf16[128,4096]{1,0:T(8,128)(2,1)} %param.11) | copy-start | bytes 3145732
  124.3 8.8 %collective-permute-start.16 = (f32[1,1024,128]{2,1,0:T(8,128)S(1)}, f32[1,1024,128]{2,1,0:T(8,128)S(1)}, u32[]{:S(2)}, u32[]{:S(2)}) collective-permute-start(f32[1,1024,128]{2,1,0:T(8,128)S(1)} %dynamic-slice_bitcast_fusion), channel_id=1, source_target_pairs={{0,1},{1,0},{2,3},{3,2},{4,5},{5,4},{6,7},{7,6},{8,9},{9,8},{10,11... | collective-permute-start | bytes 1572872 | tf_op jit(solution)/shard_map/ppermute | solution.py:16
  124.5 8.6 %collective-permute-start.17 = (bf16[1024,128]{1,0:T(8,128)(2,1)S(1)}, bf16[1024,128]{1,0:T(8,128)(2,1)S(1)}, u32[]{:S(2)}, u32[]{:S(2)}) collective-permute-start(bf16[1024,128]{1,0:T(8,128)(2,1)S(1)} %fusion.23), channel_id=1, source_target_pairs={{0,2},{1,3},{2,0},{3,1},{4,6},{5,7},{6,4},{7,5},{8,10},{9,11},{10,... | collective-permute-start | bytes 786440 | tf_op jit(solution)/shard_map/ppermute | solution.py:16
  134.8 4.9 %collective-permute-start.18 = (f32[1026]{0:T(1024)S(1)}, f32[1026]{0:T(1024)S(1)}, u32[]{:S(2)}, u32[]{:S(2)}) collective-permute-start(f32[1026]{0:T(1024)S(1)} %concatenate.3), channel_id=1, source_target_pairs={{0,4},{4,0},{8,12},{12,8},{16,20},{20,16},{24,28},{28,24},{1,5},{5... | collective-permute-start | bytes 12320 | tf_op jit(solution)/shard_map/ppermute | solution.py:16
  139.7 7.0 %collective-permute-start.19 = (f32[1026]{0:T(1024)S(1)}, f32[1026]{0:T(1024)S(1)}, u32[]{:S(2)}, u32[]{:S(2)}) collective-permute-start(f32[1026]{0:T(1024)S(1)} %add.346), channel_id=1, source_target_pairs={{0,8},{4,12},{8,0},{12,4},{16,24},{20,28},{24,16},{28,20},{1,9},{5... | collective-permute-start | bytes 12320 | tf_op jit(solution)/shard_map/ppermute | solution.py:16
  144.1 1.1 collective-permute-start.21
  145.2 3.5 %collective-permute-start.22 = (f32[128]{0:T(128)S(1)}, f32[128]{0:T(128)S(1)}, u32[]{:S(2)}, u32[]{:S(2)}) collective-permute-start(f32[128]{0:T(128)S(1)} %add.349), channel_id=1, source_target_pairs={{0,2},{1,3},{2,0},{3,1},{4,6},{5,7},{6,4},{7,5},{8,10},{9,11},{10,... | collective-permute-start | bytes 1544 | tf_op jit(solution)/shard_map/ppermute | solution.py:16
  146.8 4.6 %collective-permute-start.20 = (f32[1026]{0:T(1024)S(1)}, f32[1026]{0:T(1024)S(1)}, u32[]{:S(2)}, u32[]{:S(2)}) collective-permute-start(f32[1026]{0:T(1024)S(1)} %add.347), channel_id=1, source_target_pairs={{0,16},{4,20},{8,24},{12,28},{16,0},{20,4},{24,8},{28,12},{1,17},{... | collective-permute-start | bytes 12320 | tf_op jit(solution)/shard_map/ppermute | solution.py:16

commit v4 on v3

--- a/solution.py
+++ b/solution.py
@@ -24,9 +24,11 @@
     bit = 0
     while chunks > 1:
         cur = cur.reshape(head + (chunks // 2, 2, width) + tail)
-        side = (me >> bit) & 1
-        keep = lax.dynamic_index_in_dim(cur, side, dim + 1, keepdims=False)
-        send = lax.dynamic_index_in_dim(cur, 1 - side, dim + 1, keepdims=False)
+        low = (me >> bit) & 1 == 0
+        first = lax.index_in_dim(cur, 0, dim + 1, keepdims=False)
+        second = lax.index_in_dim(cur, 1, dim + 1, keepdims=False)
+        keep = jnp.where(low, first, second)
+        send = jnp.where(low, second, first)
         if last_wire is not None and chunks == 2:
             cur = keep + exchange(send.astype(last_wire), axis, bit).astype(keep.dtype)
         else:
@@ -177,12 +179,13 @@
     feature_start = fsdp_index * feature_count
     gain_part = lax.dynamic_slice_in_dim(norm_gain, feature_start, feature_count, 0)
     hidden_part = lax.dynamic_slice_in_dim(dec_hidden, feature_start, feature_count, 1)
-    projected = lax.optimization_barrier(
-        jnp.dot(attended, w_out, preferred_element_type=jnp.float32)
-    )
     if split_fsdp:
-        projected = scatter_bits(projected, "fsdp", 1, levels, jnp.bfloat16)
+        projected = lax.dot_general(
+            w_out, attended, (((0,), (1,)), ((), ())), preferred_element_type=jnp.float32
+        )
+        projected = scatter_bits(projected, "fsdp", 0, levels, jnp.bfloat16).T
     else:
+        projected = jnp.dot(attended, w_out, preferred_element_type=jnp.float32)
         projected = lax.psum_scatter(projected, "fsdp", scatter_dimension=1, tiled=True)
     summed_part = projected + hidden_part.astype(jnp.float32)
     square_total = sum_all(jnp.sum(summed_part * summed_part, 1), "fsdp")

time: 158 us -> 161 us (1.019)
    dynamic_slice x3 -> x0, local copies, waits for them, and re-layouts: 7.1 us -> none  [the longest x2 5.13 us: scatter_bits(): keep = lax.dynamic_index_in_dim(cur, side, dim + 1, keepdims=False)]
    slice x0 -> x1, local copies, waits for them, and re-layouts: none -> 5.36 us  [scatter_bits(): first = lax.index_in_dim(cur, 0, dim + 1, keepdims=False)]
    unnamed x26 -> x28, local copies, waits for them, and re-layouts: 3.37 us -> 6.45 us
where the time goes in v4:
time: 161 us
  waiting for transfers between devices  41.9 us (26%)
  matrix products  39.7 us (25%)
  starting transfers between devices  33.4 us (21%)
  local copies, waits for them, and re-layouts  26.8 us (17%)
  other arithmetic  15.1 us (9%)
  between operations  3.84 us (2%)
    ppermute x16, waiting for transfers between devices, exchange(): return lax.ppermute(x, axis, [(i, i ^ 1 << bit) for i in range(size)])  35.6 us
    ppermute x16, starting transfers between devices, exchange(): return lax.ppermute(x, axis, [(i, i ^ 1 << bit) for i in range(size)])  19.2 us
    ppermute x7, starting transfers between devices, body(): lax.ppermute(block, 'dp', [(i, (i - shift) % dp_count) for i in range(dp_...  14.2 us
    dot_general x1, matrix products, body(): lax.dot_general(far_rows, grad_logits, contract, preferred_element_type=j...  8.35 us
    dot_general x1, matrix products, body(): jnp.dot(far_normed, far_rows, preferred_element_type=jnp.float32)  8.28 us
    dot_general x1, matrix products, body(): jnp.dot(near_normed, near_rows, preferred_element_type=jnp.float32)  8.13 us
    dot_general x1, matrix products, body(): lax.dot_general(near_rows, near_logits, contract, preferred_element_type=...  8.13 us
    unnamed x28, local copies, waits for them, and re-layouts  6.45 us
  transfers between devices with their start and end apart: 23, of which 15 were waited for; matrix products, arithmetic and copies ran while one was open for 12% of the time, Pallas kernels for 0%

profile of v4, /device:TPU:0, one launch (start us, length us, event | category | flops | bytes accessed | tf_op | source)
XLA Modules:
  0.0 160.7 jit_solution(12589871346236945838)
XLA Ops:
  4.5 1.7 %fusion.11 = bf16[8,2,80,512]{3,2,1,0:T(8,128)(2,1)S(1)} fusion(bf16[2,192,512]{2,1,0:T(8,128)(2,1)} %param.13, s32[8,80]{1,0:T(8,128)S(1)} %iota_add_fusion), kind=kOutput, calls=%fused_computation.15 | convolution fusion | flops 252436480 | bytes 1706496 | tf_op jit(solution)/shard_map/str,crf->sctf/dot_general | solution.py:133
  7.0 5.0 %collective-permute-start.1 = (bf16[2,80,512]{2,1,0:T(8,128)(2,1)S(1)}, bf16[2,80,512]{2,1,0:T(8,128)(2,1)}, u32[]{:S(2)}, u32[]{:S(2)}) collective-permute-start(bf16[2,80,512]{2,1,0:T(8,128)(2,1)S(1)} %get-tuple-element.29), channel_id=1, source_target_pairs={{0,24},{4,28},{8,0},{12,4},{16,8},{20,12},{24,16},{28,20},{1,25},{... | collective-permute-start | bytes 491528 | tf_op jit(solution)/shard_map/ppermute | solution.py:159
  12.0 1.5 collective-permute-start.6
  13.5 1.0 collective-permute-start.4
  14.5 2.8 %collective-permute-start.3 = (bf16[2,80,512]{2,1,0:T(8,128)(2,1)S(1)}, bf16[2,80,512]{2,1,0:T(8,128)(2,1)S(1)}, u32[]{:S(2)}, u32[]{:S(2)}) collective-permute-start(bf16[2,80,512]{2,1,0:T(8,128)(2,1)S(1)} %get-tuple-element.33), channel_id=1, source_target_pairs={{0,16},{4,20},{8,24},{12,28},{16,0},{20,4},{24,8},{28,12},{1,17},{... | collective-permute-start | bytes 491528 | tf_op jit(solution)/shard_map/ppermute | solution.py:159
  21.5 1.0 collective-permute-start.2
  23.7 2.9 %collective-permute-start = (bf16[2,80,512]{2,1,0:T(8,128)(2,1)S(1)}, bf16[2,80,512]{2,1,0:T(8,128)(2,1)}, u32[]{:S(2)}, u32[]{:S(2)}) collective-permute-start(bf16[2,80,512]{2,1,0:T(8,128)(2,1)S(1)} %get-tuple-element.35), channel_id=1, source_target_pairs={{0,28},{4,0},{8,4},{12,8},{16,12},{20,16},{24,20},{28,24},{1,29},{... | collective-permute-start | bytes 491528 | tf_op jit(solution)/shard_map/ppermute | solution.py:159
  27.8 0.9 fusion.111
  29.0 6.2 %collective-permute-done.4 = bf16[2,80,512]{2,1,0:T(8,128)(2,1)} collective-permute-done((bf16[2,80,512]{2,1,0:T(8,128)(2,1)S(1)}, bf16[2,80,512]{2,1,0:T(8,128)(2,1)}, u32[]{:S(2)}, u32[]{:S(2)}) %collective-permute-start.4) | collective-permute-done | bytes 163872 | tf_op jit(solution)/shard_map/ppermute | solution.py:159
  35.2 0.9 fusion.110
  36.7 0.9 fusion.108
  37.9 0.9 fusion.107
  42.9 1.3 copy-done.4
  45.0 3.0 %reshape.672 = f32[2,2,1024,128]{2,1,0,3:T(2,128)} reshape(f32[4096,128]{0,1:T(8,128)S(1)} %convolution_bitcast_fusion) | data formatting | bytes 4194304 | tf_op jit(solution)/shard_map/reshape | solution.py:26
  48.0 5.4 %fusion.104 = (f32[2,1,1024,128]{2,1,0,3:T(1,128)S(1)}, f32[2,1,1024,128]{2,1,0,3:T(1,128)}) fusion(f32[2,2,1024,128]{2,1,0,3:T(2,128)} %reshape.672), kind=kLoop, calls=%fused_computation.234 | loop fusion | bytes 4194304 | tf_op jit(solution)/shard_map/slice | solution.py:28
  54.1 2.3 %copy.110 = f32[2,1,1024,128]{3,2,0,1:T(8,128)S(1)} copy(f32[2,1,1024,128]{2,1,0,3:T(1,128)} %get-tuple-element.28) | data formatting | bytes 2097152
  56.5 1.1 select_bitcast_fusion
  57.6 3.0 %collective-permute-done.7 = f32[2,1024,128]{2,1,0:T(8,128)} collective-permute-done((f32[2,1024,128]{2,1,0:T(8,128)}, f32[2,1024,128]{2,1,0:T(8,128)}, u32[]{:S(2)}, u32[]{:S(2)}) %collective-permute-start.7) | collective-permute-done | bytes 1048608 | tf_op jit(solution)/shard_map/ppermute | solution.py:16
  60.6 1.4 fusion.20
  61.9 1.0 copy-done.2
  63.0 1.6 collective-permute-start.8
  64.8 6.6 %collective-permute-done.8 = bf16[1,1024,128]{2,1,0:T(8,128)(2,1)S(1)} collective-permute-done((bf16[1,1024,128]{2,1,0:T(8,128)(2,1)S(1)}, bf16[1,1024,128]{2,1,0:T(8,128)(2,1)S(1)}, u32[]{:S(2)}, u32[]{:S(2)}) %collective-permute-start.8) | collective-permute-done | bytes 262176 | tf_op jit(solution)/shard_map/ppermute | solution.py:16
  71.4 1.4 multiply_reduce_fusion.1
  72.8 1.1 collective-permute-done.9
  73.9 1.5 collective-permute-start.10
  76.2 1.3 collective-permute-done.10
  77.8 1.5 collective-permute-done.11
  79.6 1.6 collective-permute-start.12
  81.2 8.1 %fusion.6 = f32[128,4096]{1,0:T(8,128)S(1)} fusion(bf16[128,2048]{0,1:T(8,128)(2,1)S(1)} %bitcast.265, bf16[4096,4096]{1,0:T(8,128)(2,1)} %param.16, s32[]{:T(128)S(6)} %select_n.327), kind=kOutput, calls=%fused_computation.6 | convolution fusion | flops 2147483648 | bytes 19398660 | tf_op jit(solution)/shard_map/dot_general | solution.py:202
  89.3 4.3 %collective-permute-done.12 = bf16[128,2048]{0,1:T(8,128)(2,1)S(1)} collective-permute-done((bf16[128,2048]{0,1:T(8,128)(2,1)S(1)}, bf16[128,2048]{0,1:T(8,128)(2,1)S(1)}, u32[]{:S(2)}, u32[]{:S(2)}) %collective-permute-start.12) | collective-permute-done | bytes 524320 | tf_op jit(solution)/shard_map/ppermute | solution.py:16
  93.6 8.3 %fusion.114 = (f32[128]{0:T(128)S(1)}, f32[128,4096]{1,0:T(8,128)S(1)}) fusion(f32[128,4096]{1,0:T(8,128)S(1)} %fusion.6, bf16[128,2048]{0,1:T(8,128)(2,1)S(1)} %collective-permute-done.12, bf16[4096,4096]{1,0:T(8,128)(2,1)} %param.16, s32[]{:T(128)S(6)} %select_n.328), kind=kOutput, calls=%fused_computation.244 | convolution fusion | flops 2148532224 | bytes 21496324 | tf_op jit(solution)/shard_map/dot_general | solution.py:202
  102.7 1.1 collective-permute-done.13
  103.9 1.6 collective-permute-start.14
  105.4 2.1 %collective-permute-done.14 = f32[3,128]{1,0:T(4,128)S(1)} collective-permute-done((f32[3,128]{1,0:T(4,128)S(1)}, f32[3,128]{1,0:T(4,128)S(1)}, u32[]{:S(2)}, u32[]{:S(2)}) %collective-permute-start.14) | collective-permute-done | bytes 1568 | tf_op jit(solution)/shard_map/ppermute | solution.py:16
  108.8 8.4 %fusion = f32[2048,128]{1,0:T(8,128)S(1)} fusion(bf16[128,4096]{1,0:T(8,128)(2,1)S(1)} %multiply_convert_fusion, bf16[4096,4096]{1,0:T(8,128)(2,1)} %param.16, s32[]{:T(128)S(6)} %select_n.328), kind=kOutput, calls=%fused_computation | convolution fusion | flops 2147483648 | bytes 18874372 | tf_op jit(solution)/shard_map/dot_general | solution.py:223
  117.3 1.9 %collective-permute-done.15 = f32[1,1024,128]{2,1,0:T(8,128)S(1)} collective-permute-done((f32[1,1024,128]{2,1,0:T(8,128)S(1)}, f32[1,1024,128]{2,1,0:T(8,128)S(1)}, u32[]{:S(2)}, u32[]{:S(2)}) %collective-permute-start.15) | collective-permute-done | bytes 524320 | tf_op jit(solution)/shard_map/ppermute | solution.py:16
  119.3 8.1 %fusion.4 = f32[2048,128]{1,0:T(8,128)S(1)} fusion(bf16[128,4096]{1,0:T(8,128)(2,1)S(1)} %multiply_convert_fusion, bf16[4096,4096]{1,0:T(8,128)(2,1)} %param.16, s32[]{:T(128)S(6)} %select_n.327), kind=kOutput, calls=%fused_computation.4 | convolution fusion | flops 2147483648 | bytes 18874372 | tf_op jit(solution)/shard_map/dot_general | solution.py:232
  127.7 1.5 collective-permute-start.17
  129.3 7.1 %collective-permute-done.17 = bf16[1024,128]{1,0:T(8,128)(2,1)S(1)} collective-permute-done((bf16[1024,128]{1,0:T(8,128)(2,1)S(1)}, bf16[1024,128]{1,0:T(8,128)(2,1)S(1)}, u32[]{:S(2)}, u32[]{:S(2)}) %collective-permute-start.17) | collective-permute-done | bytes 262176 | tf_op jit(solution)/shard_map/ppermute | solution.py:16
  136.7 1.4 concatenate.3
  138.1 3.3 %collective-permute-start.18 = (f32[1026]{0:T(1024)S(1)}, f32[1026]{0:T(1024)S(1)}, u32[]{:S(2)}, u32[]{:S(2)}) collective-permute-start(f32[1026]{0:T(1024)S(1)} %concatenate.3), channel_id=1, source_target_pairs={{0,4},{4,0},{8,12},{12,8},{16,20},{20,16},{24,28},{28,24},{1,5},{5... | collective-permute-start | bytes 12320 | tf_op jit(solution)/shard_map/ppermute | solution.py:16
  141.4 1.6 %collective-permute-done.18 = f32[1026]{0:T(1024)S(1)} collective-permute-done((f32[1026]{0:T(1024)S(1)}, f32[1026]{0:T(1024)S(1)}, u32[]{:S(2)}, u32[]{:S(2)}) %collective-permute-start.18) | collective-permute-done | bytes 4136 | tf_op jit(solution)/shard_map/ppermute | solution.py:16
  143.0 4.4 %collective-permute-start.19 = (f32[1026]{0:T(1024)S(1)}, f32[1026]{0:T(1024)S(1)}, u32[]{:S(2)}, u32[]{:S(2)}) collective-permute-start(f32[1026]{0:T(1024)S(1)} %add.321), channel_id=1, source_target_pairs={{0,8},{4,12},{8,0},{12,4},{16,24},{20,28},{24,16},{28,20},{1,9},{5... | collective-permute-start | bytes 12320 | tf_op jit(solution)/shard_map/ppermute | solution.py:16
  147.4 1.1 collective-permute-done.21
  148.5 1.5 collective-permute-start.22
  150.0 1.7 %collective-permute-start.20 = (f32[1026]{0:T(1024)S(1)}, f32[1026]{0:T(1024)S(1)}, u32[]{:S(2)}, u32[]{:S(2)}) collective-permute-start(f32[1026]{0:T(1024)S(1)} %add.322), channel_id=1, source_target_pairs={{0,16},{4,20},{8,24},{12,28},{16,0},{20,4},{24,8},{28,12},{1,17},{... | collective-permute-start | bytes 12320 | tf_op jit(solution)/shard_map/ppermute | solution.py:16
  152.0 2.5 %collective-permute-done.20 = f32[1026]{0:T(1024)S(1)} collective-permute-done((f32[1026]{0:T(1024)S(1)}, f32[1026]{0:T(1024)S(1)}, u32[]{:S(2)}, u32[]{:S(2)}) %collective-permute-start.20) | collective-permute-done | bytes 4136 | tf_op jit(solution)/shard_map/ppermute | solution.py:16
  155.2 1.3 slice_divide_fusion
  (144 shorter events, 24.5 us)
Async XLA Ops:
  0.6 17.8 %copy-start = (bf16[128,4096]{1,0:T(8,128)(2,1)S(1)}, bf16[128,4096]{1,0:T(8,128)(2,1)}, u32[]{:S(2)}) copy-start(bf16[128,4096]{1,0:T(8,128)(2,1)} %param.11) | copy-start | bytes 3145732
  4.5 13.3 %copy-start.10 = (s32[128]{0:T(128)S(1)}, s32[128]{0:T(128)}, u32[]{:S(2)}) copy-start(s32[128]{0:T(128)} %param.18) | copy-start | bytes 1540
  4.5 13.9 %copy-start.3 = (bf16[4096,512]{1,0:T(8,128)(2,1)S(1)}, bf16[4096,512]{1,0:T(8,128)(2,1)}, u32[]{:S(2)}) copy-start(bf16[4096,512]{1,0:T(8,128)(2,1)} %param.12) | copy-start | bytes 12582916
  7.0 14.5 %collective-permute-start.1 = (bf16[2,80,512]{2,1,0:T(8,128)(2,1)S(1)}, bf16[2,80,512]{2,1,0:T(8,128)(2,1)}, u32[]{:S(2)}, u32[]{:S(2)}) collective-permute-start(bf16[2,80,512]{2,1,0:T(8,128)(2,1)S(1)} %get-tuple-element.29), channel_id=1, source_target_pairs={{0,24},{4,28},{8,0},{12,4},{16,8},{20,12},{24,16},{28,20},{1,25},{... | collective-permute-start | bytes 491528 | tf_op jit(solution)/shard_map/ppermute | solution.py:159
  12.0 11.6 %collective-permute-start.6 = (bf16[2,80,512]{2,1,0:T(8,128)(2,1)S(1)}, bf16[2,80,512]{2,1,0:T(8,128)(2,1)}, u32[]{:S(2)}, u32[]{:S(2)}) collective-permute-start(bf16[2,80,512]{2,1,0:T(8,128)(2,1)S(1)} %get-tuple-element.30), channel_id=1, source_target_pairs={{0,4},{4,8},{8,12},{12,16},{16,20},{20,24},{24,28},{28,0},{1,5},{5... | collective-permute-start | bytes 491528 | tf_op jit(solution)/shard_map/ppermute | solution.py:159
  13.5 14.2 %collective-permute-start.5 = (bf16[2,80,512]{2,1,0:T(8,128)(2,1)S(1)}, bf16[2,80,512]{2,1,0:T(8,128)(2,1)}, u32[]{:S(2)}, u32[]{:S(2)}) collective-permute-start(bf16[2,80,512]{2,1,0:T(8,128)(2,1)S(1)} %get-tuple-element.31), channel_id=1, source_target_pairs={{0,8},{4,12},{8,16},{12,20},{16,24},{20,28},{24,0},{28,4},{1,9},{5... | collective-permute-start | bytes 491528 | tf_op jit(solution)/shard_map/ppermute | solution.py:159
  13.5 21.7 %collective-permute-start.4 = (bf16[2,80,512]{2,1,0:T(8,128)(2,1)S(1)}, bf16[2,80,512]{2,1,0:T(8,128)(2,1)}, u32[]{:S(2)}, u32[]{:S(2)}) collective-permute-start(bf16[2,80,512]{2,1,0:T(8,128)(2,1)S(1)} %get-tuple-element.32), channel_id=1, source_target_pairs={{0,12},{4,16},{8,20},{12,24},{16,28},{20,0},{24,4},{28,8},{1,13},{... | collective-permute-start | bytes 491528 | tf_op jit(solution)/shard_map/ppermute | solution.py:159
  14.5 21.9 %collective-permute-start.3 = (bf16[2,80,512]{2,1,0:T(8,128)(2,1)S(1)}, bf16[2,80,512]{2,1,0:T(8,128)(2,1)S(1)}, u32[]{:S(2)}, u32[]{:S(2)}) collective-permute-start(bf16[2,80,512]{2,1,0:T(8,128)(2,1)S(1)} %get-tuple-element.33), channel_id=1, source_target_pairs={{0,16},{4,20},{8,24},{12,28},{16,0},{20,4},{24,8},{28,12},{1,17},{... | collective-permute-start | bytes 491528 | tf_op jit(solution)/shard_map/ppermute | solution.py:159
  21.5 15.2 %collective-permute-start.2 = (bf16[2,80,512]{2,1,0:T(8,128)(2,1)}, bf16[2,80,512]{2,1,0:T(8,128)(2,1)}, u32[]{:S(2)}, u32[]{:S(2)}) collective-permute-start(bf16[2,80,512]{2,1,0:T(8,128)(2,1)} %get-tuple-element.34), channel_id=1, source_target_pairs={{0,20},{4,24},{8,28},{12,0},{16,4},{20,8},{24,12},{28,16},{1,21},{... | collective-permute-start | bytes 491528 | tf_op jit(solution)/shard_map/ppermute | solution.py:159
  23.7 14.2 %collective-permute-start = (bf16[2,80,512]{2,1,0:T(8,128)(2,1)S(1)}, bf16[2,80,512]{2,1,0:T(8,128)(2,1)}, u32[]{:S(2)}, u32[]{:S(2)}) collective-permute-start(bf16[2,80,512]{2,1,0:T(8,128)(2,1)S(1)} %get-tuple-element.35), channel_id=1, source_target_pairs={{0,28},{4,0},{8,4},{12,8},{16,12},{20,16},{24,20},{28,24},{1,29},{... | collective-permute-start | bytes 491528 | tf_op jit(solution)/shard_map/ppermute | solution.py:159
  27.5 11.6 %copy-start.7 = (pred[128,80]{0,1:T(8,128)(4,1)S(1)}, pred[128,80]{0,1:T(8,128)(4,1)}, u32[]{:S(2)}) copy-start(pred[128,80]{0,1:T(8,128)(4,1)} %get-tuple-element.69) | copy-start | bytes 30724
  36.2 3.4 %copy-start.6 = (pred[128,80]{0,1:T(8,128)(4,1)S(1)}, pred[128,80]{0,1:T(8,128)(4,1)}, u32[]{:S(2)}) copy-start(pred[128,80]{0,1:T(8,128)(4,1)} %get-tuple-element.70) | copy-start | bytes 30724
  37.9 2.3 %copy-start.5 = (pred[128,80]{0,1:T(8,128)(4,1)S(1)}, pred[128,80]{0,1:T(8,128)(4,1)}, u32[]{:S(2)}) copy-start(pred[128,80]{0,1:T(8,128)(4,1)} %get-tuple-element.71) | copy-start | bytes 30724
  41.5 1.2 copy-start.8
  42.1 2.2 %copy-start.4 = (bf16[512,4096]{1,0:T(8,128)(2,1)S(1)}, bf16[512,4096]{1,0:T(8,128)(2,1)}, u32[]{:S(2)}) copy-start(bf16[512,4096]{1,0:T(8,128)(2,1)} %param.14) | copy-start | bytes 12582916
  57.6 3.0 %collective-permute-start.7 = (f32[2,1024,128]{2,1,0:T(8,128)}, f32[2,1024,128]{2,1,0:T(8,128)}, u32[]{:S(2)}, u32[]{:S(2)}) collective-permute-start(f32[2,1024,128]{2,1,0:T(8,128)} %select_bitcast_fusion), channel_id=1, source_target_pairs={{0,1},{1,0},{2,3},{3,2},{4,5},{5,4},{6,7},{7,6},{8,9},{9,8},{10,11... | collective-permute-start | bytes 3145736 | tf_op jit(solution)/shard_map/ppermute | solution.py:16
  61.9 1.0 copy-start.2
  63.0 8.4 %collective-permute-start.8 = (bf16[1,1024,128]{2,1,0:T(8,128)(2,1)S(1)}, bf16[1,1024,128]{2,1,0:T(8,128)(2,1)S(1)}, u32[]{:S(2)}, u32[]{:S(2)}) collective-permute-start(bf16[1,1024,128]{2,1,0:T(8,128)(2,1)S(1)} %fusion.41), channel_id=1, source_target_pairs={{0,2},{1,3},{2,0},{3,1},{4,6},{5,7},{6,4},{7,5},{8,10},{9,11},{10,... | collective-permute-start | bytes 786440 | tf_op jit(solution)/shard_map/ppermute | solution.py:16
  72.7 8.4 %copy-start.11 = (s32[128]{0:T(128)S(1)}, s32[128]{0:T(128)}, u32[]{:S(2)}) copy-start(s32[128]{0:T(128)} %param.20) | copy-start | bytes 1540
  72.7 1.2 collective-permute-start.9
  73.9 3.5 %collective-permute-start.10 = (f32[128]{0:T(128)S(1)}, f32[128]{0:T(128)S(1)}, u32[]{:S(2)}, u32[]{:S(2)}) collective-permute-start(f32[128]{0:T(128)S(1)} %add.304), channel_id=1, source_target_pairs={{0,2},{1,3},{2,0},{3,1},{4,6},{5,7},{6,4},{7,5},{8,10},{9,11},{10,... | collective-permute-start | bytes 1544 | tf_op jit(solution)/shard_map/ppermute | solution.py:16
  77.7 1.6 collective-permute-start.11
  79.6 14.0 %collective-permute-start.12 = (bf16[128,2048]{0,1:T(8,128)(2,1)S(1)}, bf16[128,2048]{0,1:T(8,128)(2,1)S(1)}, u32[]{:S(2)}, u32[]{:S(2)}) collective-permute-start(bf16[128,2048]{0,1:T(8,128)(2,1)S(1)} %bitcast.264), channel_id=1, source_target_pairs={{0,2},{1,3},{2,0},{3,1},{4,6},{5,7},{6,4},{7,5},{8,10},{9,11},{10,... | collective-permute-start | bytes 1572872 | tf_op jit(solution)/shard_map/ppermute | solution.py:16
  101.9 3.6 %copy-start.9 = (s32[128]{0:T(128)S(1)}, s32[128]{0:T(128)}, u32[]{:S(2)}) copy-start(s32[128]{0:T(128)} %param.21) | copy-start | bytes 1540
  102.6 1.2 collective-permute-start.13
  103.9 3.7 %collective-permute-start.14 = (f32[3,128]{1,0:T(4,128)S(1)}, f32[3,128]{1,0:T(4,128)S(1)}, u32[]{:S(2)}, u32[]{:S(2)}) collective-permute-start(f32[3,128]{1,0:T(4,128)S(1)} %pad_maximum_fusion.2), channel_id=1, source_target_pairs={{0,2},{1,3},{2,0},{3,1},{4,6},{5,7},{6,4},{7,5},{8,10},{9,11},{10,... | collective-permute-start | bytes 4616 | tf_op jit(solution)/shard_map/ppermute | solution.py:16
  117.2 2.0 %collective-permute-start.15 = (f32[1,1024,128]{2,1,0:T(8,128)S(1)}, f32[1,1024,128]{2,1,0:T(8,128)S(1)}, u32[]{:S(2)}, u32[]{:S(2)}) collective-permute-start(f32[1,1024,128]{2,1,0:T(8,128)S(1)} %select_bitcast_fusion.2), channel_id=1, source_target_pairs={{0,1},{1,0},{2,3},{3,2},{4,5},{5,4},{6,7},{7,6},{8,9},{9,8},{10,11... | collective-permute-start | bytes 1572872 | tf_op jit(solution)/shard_map/ppermute | solution.py:16
  127.5 32.1 %copy-start.1 = (bf16[128,4096]{1,0:T(8,128)(2,1)S(1)}, bf16[128,4096]{1,0:T(8,128)(2,1)}, u32[]{:S(2)}) copy-start(bf16[128,4096]{1,0:T(8,128)(2,1)} %param.11) | copy-start | bytes 3145732
  127.5 8.8 %collective-permute-start.16 = (f32[1,1024,128]{2,1,0:T(8,128)S(1)}, f32[1,1024,128]{2,1,0:T(8,128)S(1)}, u32[]{:S(2)}, u32[]{:S(2)}) collective-permute-start(f32[1,1024,128]{2,1,0:T(8,128)S(1)} %select_bitcast_fusion.1), channel_id=1, source_target_pairs={{0,1},{1,0},{2,3},{3,2},{4,5},{5,4},{6,7},{7,6},{8,9},{9,8},{10,11... | collective-permute-start | bytes 1572872 | tf_op jit(solution)/shard_map/ppermute | solution.py:16
  127.7 8.6 %collective-permute-start.17 = (bf16[1024,128]{1,0:T(8,128)(2,1)S(1)}, bf16[1024,128]{1,0:T(8,128)(2,1)S(1)}, u32[]{:S(2)}, u32[]{:S(2)}) collective-permute-start(bf16[1024,128]{1,0:T(8,128)(2,1)S(1)} %fusion.24), channel_id=1, source_target_pairs={{0,2},{1,3},{2,0},{3,1},{4,6},{5,7},{6,4},{7,5},{8,10},{9,11},{10,... | collective-permute-start | bytes 786440 | tf_op jit(solution)/shard_map/ppermute | solution.py:16
  138.1 4.9 %collective-permute-start.18 = (f32[1026]{0:T(1024)S(1)}, f32[1026]{0:T(1024)S(1)}, u32[]{:S(2)}, u32[]{:S(2)}) collective-permute-start(f32[1026]{0:T(1024)S(1)} %concatenate.3), channel_id=1, source_target_pairs={{0,4},{4,0},{8,12},{12,8},{16,20},{20,16},{24,28},{28,24},{1,5},{5... | collective-permute-start | bytes 12320 | tf_op jit(solution)/shard_map/ppermute | solution.py:16
  143.0 7.0 %collective-permute-start.19 = (f32[1026]{0:T(1024)S(1)}, f32[1026]{0:T(1024)S(1)}, u32[]{:S(2)}, u32[]{:S(2)}) collective-permute-start(f32[1026]{0:T(1024)S(1)} %add.321), channel_id=1, source_target_pairs={{0,8},{4,12},{8,0},{12,4},{16,24},{20,28},{24,16},{28,20},{1,9},{5... | collective-permute-start | bytes 12320 | tf_op jit(solution)/shard_map/ppermute | solution.py:16
  147.4 1.1 collective-permute-start.21
  148.5 3.5 %collective-permute-start.22 = (f32[128]{0:T(128)S(1)}, f32[128]{0:T(128)S(1)}, u32[]{:S(2)}, u32[]{:S(2)}) collective-permute-start(f32[128]{0:T(128)S(1)} %add.324), channel_id=1, source_target_pairs={{0,2},{1,3},{2,0},{3,1},{4,6},{5,7},{6,4},{7,5},{8,10},{9,11},{10,... | collective-permute-start | bytes 1544 | tf_op jit(solution)/shard_map/ppermute | solution.py:16
  150.0 4.6 %collective-permute-start.20 = (f32[1026]{0:T(1024)S(1)}, f32[1026]{0:T(1024)S(1)}, u32[]{:S(2)}, u32[]{:S(2)}) collective-permute-start(f32[1026]{0:T(1024)S(1)} %add.322), channel_id=1, source_target_pairs={{0,16},{4,20},{8,24},{12,28},{16,0},{20,4},{24,8},{28,12},{1,17},{... | collective-permute-start | bytes 12320 | tf_op jit(solution)/shard_map/ppermute | solution.py:16

commit v5 on v3

--- a/solution.py
+++ b/solution.py
@@ -154,9 +154,13 @@
     for shift in range(dp_count):
         block = windows[shift]
         if shift:
-            block = lax.ppermute(
-                block, "dp", [(i, (i - shift) % dp_count) for i in range(dp_count)]
-            )
+            pairs = [(i, (i - shift) % dp_count) for i in range(dp_count)]
+            if shift in (dp_count // 2, dp_count - 1):
+                block = lax.ppermute(block, "dp", pairs)
+            else:
+                block = lax.cond(
+                    used[shift], lambda b: lax.ppermute(b, "dp", pairs), lambda b: b, block
+                )
         keys_here = block[0].reshape(window, heads_here, HEAD_DIM)
         values_here = block[1].astype(jnp.float32).reshape(window, heads_here, HEAD_DIM)
         scores = jnp.einsum(

time: 158 us -> 168 us (1.063)
  starting transfers between devices: 33.4 us -> 21.9 us
  waiting for transfers between devices: 41.4 us -> 50.9 us
  local copies, waits for them, and re-layouts: 25.5 us -> 33 us
  between operations: 3.86 us -> 6.97 us
  matrix products: 39.6 us -> 41.6 us
    ppermute x7 -> x4, waiting for transfers between devices: 6.5 us -> 16.1 us  [the longest x2 16.1 us: body(): lax.ppermute(b, 'dp', pairs)]
    ppermute x7 -> x4, starting transfers between devices: 14.2 us -> 6.65 us  [the longest x2 5.53 us: body(): block = lax.ppermute(block, 'dp', pairs)]
    ppermute x16, starting transfers between devices: 19.2 us -> 15.3 us  [exchange(): return lax.ppermute(x, axis, [(i, i ^ 1 << bit) for i in range(size)])]
    slice x8 -> x13, local copies, waits for them, and re-layouts: 5.66 us -> 8.45 us  [body(): keys_here = block[0].reshape(window, heads_here, HEAD_DIM)]
    slice x0 -> x6, local copies, waits for them, and re-layouts: none -> 2.15 us  [the longest x5 1.49 us: body(): block[1].astype(jnp.float32).reshape(window, heads_here, HEAD_DIM)]
    dot_general x1, matrix products: 0.77 us -> 2.91 us  [body(): jnp.dot(dec_hidden, w_query, preferred_element_type=jnp.float32)]
    squeeze x1 -> x6, local copies, waits for them, and re-layouts: 0.78 us -> 2.78 us  [body(): block = windows[shift]]
    unnamed x26 -> x16, local copies, waits for them, and re-layouts: 3.37 us -> 3.27 us
  transfers between devices with their start and end apart: 23 -> 20, of which waited for: 15 -> 16; matrix products, arithmetic and copies ran while one was open for 12% -> 18% of each run, Pallas kernels for 0% -> 0%
where the time goes in v5:
time: 168 us; the launch traced here: 167 us
  waiting for transfers between devices  50.9 us (30%)
  matrix products  41.6 us (25%)
  local copies, waits for them, and re-layouts  33 us (20%)
  starting transfers between devices  21.9 us (13%)
  other arithmetic  12.4 us (7%)
  between operations  6.97 us (4%)
    ppermute x16, waiting for transfers between devices, exchange(): return lax.ppermute(x, axis, [(i, i ^ 1 << bit) for i in range(size)])  34.8 us
    ppermute x2, waiting for transfers between devices, body(): lax.ppermute(b, 'dp', pairs)  16.1 us
    ppermute x16, starting transfers between devices, exchange(): return lax.ppermute(x, axis, [(i, i ^ 1 << bit) for i in range(size)])  15.3 us
    slice x13, local copies, waits for them, and re-layouts, body(): keys_here = block[0].reshape(window, heads_here, HEAD_DIM)  8.45 us
    dot_general x1, matrix products, body(): lax.dot_general(far_rows, grad_logits, contract, preferred_element_type=j...  8.35 us
    dot_general x1, matrix products, body(): jnp.dot(far_normed, far_rows, preferred_element_type=jnp.float32)  8.27 us
    dot_general x1, matrix products, body(): jnp.dot(near_normed, near_rows, preferred_element_type=jnp.float32)  8.13 us
    dot_general x1, matrix products, body(): lax.dot_general(near_rows, near_logits, contract, preferred_element_type=...  8.13 us
  transfers between devices with their start and end apart: 20, of which 16 were waited for; matrix products, arithmetic and copies ran while one was open for 18% of the time, Pallas kernels for 0%

profile of v5, /device:TPU:0, one launch (start us, length us, event | category | flops | bytes accessed | tf_op | source)
XLA Modules:
  0.0 166.8 jit_solution(12498830625085537773)
XLA Ops:
  4.8 1.5 fusion.11
  7.0 2.9 %collective-permute-start.6 = (bf16[2,80,512]{2,1,0:T(8,128)(2,1)}, bf16[2,80,512]{2,1,0:T(8,128)(2,1)}, u32[]{:S(2)}, u32[]{:S(2)}) collective-permute-start(bf16[2,80,512]{2,1,0:T(8,128)(2,1)} %get-tuple-element.79), channel_id=1, source_target_pairs={{0,4},{4,8},{8,12},{12,16},{16,20},{20,24},{24,28},{28,0},{1,5},{5... | collective-permute-start | bytes 491528 | tf_op jit(solution)/shard_map/ppermute | solution.py:159
  10.0 2.6 %collective-permute-start.5 = (bf16[2,80,512]{2,1,0:T(8,128)(2,1)}, bf16[2,80,512]{2,1,0:T(8,128)(2,1)}, u32[]{:S(2)}, u32[]{:S(2)}) collective-permute-start(bf16[2,80,512]{2,1,0:T(8,128)(2,1)} %get-tuple-element.80), channel_id=1, source_target_pairs={{0,16},{4,20},{8,24},{12,28},{16,0},{20,4},{24,8},{28,12},{1,17},{... | collective-permute-start | bytes 491528 | tf_op jit(solution)/shard_map/ppermute | solution.py:159
  17.9 2.9 %convolution_convert_fusion.1 = bf16[128,512]{1,0:T(8,128)(2,1)S(1)} fusion(bf16[128,4096]{1,0:T(8,128)(2,1)S(1)} %copy-done, bf16[4096,512]{1,0:T(8,128)(2,1)} %param.22), kind=kOutput, calls=%fused_computation.35 | convolution fusion | flops 536936448 | bytes 5373952 | tf_op jit(solution)/shard_map/dot_general | solution.py:148
  22.7 10.9 %conditional.8 = (bf16[2,80,512]{2,1,0:T(8,128)(2,1)}) conditional(s32[]{:T(128)} %bitcast.36, (bf16[8,2,80,512]{3,2,1,0:T(8,128)(2,1)S(1)}) %tuple.41, (bf16[8,2,80,512]{3,2,1,0:T(8,128)(2,1)S(1)}) %tuple.41), branch_computations={%region_25.26_spmd, %region_26.27_spmd} | conditional | bytes 983088 | solution.py:161
  22.7 1.1 collective-permute-start.3
  23.8 9.8 %collective-permute-done.3 = bf16[2,80,512]{2,1,0:T(8,128)(2,1)} collective-permute-done((bf16[2,80,512]{2,1,0:T(8,128)(2,1)S(1)}, bf16[2,80,512]{2,1,0:T(8,128)(2,1)}, u32[]{:S(2)}, u32[]{:S(2)}) %collective-permute-start.3) | collective-permute-done | bytes 163872 | tf_op jit(solution)/shard_map/cond/branch_1_fun/ppermute | solution.py:162
  34.8 6.4 %conditional.7 = (bf16[2,80,512]{2,1,0:T(8,128)(2,1)}) conditional(s32[]{:T(128)} %bitcast.28, (bf16[8,2,80,512]{3,2,1,0:T(8,128)(2,1)S(1)}) %tuple.41, (bf16[8,2,80,512]{3,2,1,0:T(8,128)(2,1)S(1)}) %tuple.41), branch_computations={%region_21.22_spmd, %region_22.23_spmd} | conditional | bytes 983088 | solution.py:161
  34.9 6.3 %collective-permute-done.2 = bf16[2,80,512]{2,1,0:T(8,128)(2,1)} collective-permute-done((bf16[2,80,512]{2,1,0:T(8,128)(2,1)S(1)}, bf16[2,80,512]{2,1,0:T(8,128)(2,1)}, u32[]{:S(2)}, u32[]{:S(2)}) %collective-permute-start.2) | collective-permute-done | bytes 163872 | tf_op jit(solution)/shard_map/cond/branch_1_fun/ppermute | solution.py:162
  43.1 1.6 fusion.99
  44.8 1.0 copy.76
  47.7 1.0 copy.93
  48.7 1.0 copy.94
  56.7 1.2 copy-done.2
  58.7 3.0 %reshape.545 = f32[128,2,2,1024]{3,2,1,0:T(2,128)} reshape(f32[128,4096]{1,0:T(8,128)S(1)} %fusion.105) | data formatting | bytes 4194304 | tf_op jit(solution)/shard_map/reshape | solution.py:26
  61.7 4.4 %constant_dynamic-slice_fusion.2 = (f32[128,2,1,1024]{3,2,1,0:T(1,128)S(1)}, f32[128,2,1,1024]{3,2,1,0:T(1,128)S(1)}) fusion(f32[128,2,2,1024]{3,2,1,0:T(2,128)} %reshape.545, s32[]{:T(128)S(6)} %select_n.222, s32[]{:T(128)S(6)} %select_n.223), kind=kLoop, calls=%fused_computation.145 | loop fusion | bytes 4194312 | tf_op jit(solution)/shard_map/jit(dynamic_index_in_dim)/dynamic_slice | solution.py:28
  66.1 2.0 %copy.88 = f32[128,2,1,1024]{0,3,1,2:T(8,128)} copy(f32[128,2,1,1024]{3,2,1,0:T(1,128)S(1)} %get-tuple-element.78) | data formatting | bytes 2097152 | tf_op jit(solution)/shard_map/jit(dynamic_index_in_dim)/dynamic_slice | solution.py:29
  68.8 2.2 %collective-permute-done.7 = f32[128,2,1024]{0,2,1:T(8,128)} collective-permute-done((f32[128,2,1024]{0,2,1:T(8,128)}, f32[128,2,1024]{0,2,1:T(8,128)}, u32[]{:S(2)}, u32[]{:S(2)}) %collective-permute-start.7) | collective-permute-done | bytes 1048608 | tf_op jit(solution)/shard_map/ppermute | solution.py:16
  71.1 1.3 bitcast_add_fusion
  72.4 1.0 copy-done.3
  73.4 1.6 collective-permute-start.8
  75.2 6.6 %collective-permute-done.8 = bf16[128,1,1024]{0,2,1:T(8,128)(2,1)S(1)} collective-permute-done((bf16[128,1,1024]{0,2,1:T(8,128)(2,1)S(1)}, bf16[128,1,1024]{0,2,1:T(8,128)(2,1)S(1)}, u32[]{:S(2)}, u32[]{:S(2)}) %collective-permute-start.8) | collective-permute-done | bytes 262176 | tf_op jit(solution)/shard_map/ppermute | solution.py:16
  81.8 1.2 multiply_reduce_fusion.1
  83.1 1.1 collective-permute-done.9
  84.2 1.5 collective-permute-start.10
  86.4 1.3 collective-permute-done.10
  88.1 1.5 collective-permute-done.11
  89.8 1.6 collective-permute-start.12
  91.4 8.1 %fusion.6 = f32[128,4096]{1,0:T(8,128)S(1)} fusion(bf16[128,2048]{0,1:T(8,128)(2,1)S(1)} %bitcast.265, bf16[4096,4096]{1,0:T(8,128)(2,1)} %param.26, s32[]{:T(128)S(6)} %select_n.229), kind=kOutput, calls=%fused_computation.16 | convolution fusion | flops 2147483648 | bytes 19398660 | tf_op jit(solution)/shard_map/dot_general | solution.py:203
  99.6 4.3 %collective-permute-done.12 = bf16[128,2048]{0,1:T(8,128)(2,1)S(1)} collective-permute-done((bf16[128,2048]{0,1:T(8,128)(2,1)S(1)}, bf16[128,2048]{0,1:T(8,128)(2,1)S(1)}, u32[]{:S(2)}, u32[]{:S(2)}) %collective-permute-start.12) | collective-permute-done | bytes 524320 | tf_op jit(solution)/shard_map/ppermute | solution.py:16
  103.9 8.3 %fusion.104 = (f32[128]{0:T(128)S(1)}, f32[128,4096]{1,0:T(8,128)S(1)}) fusion(f32[128,4096]{1,0:T(8,128)S(1)} %fusion.6, bf16[128,2048]{0,1:T(8,128)(2,1)S(1)} %collective-permute-done.12, bf16[4096,4096]{1,0:T(8,128)(2,1)} %param.26, s32[]{:T(128)S(6)} %select_n.230), kind=kOutput, calls=%fused_computation.242 | convolution fusion | flops 2148532224 | bytes 21496324 | tf_op jit(solution)/shard_map/dot_general | solution.py:203
  112.9 1.1 collective-permute-done.13
  114.1 1.6 collective-permute-start.14
  115.7 2.1 %collective-permute-done.14 = f32[3,128]{1,0:T(4,128)S(1)} collective-permute-done((f32[3,128]{1,0:T(4,128)S(1)}, f32[3,128]{1,0:T(4,128)S(1)}, u32[]{:S(2)}, u32[]{:S(2)}) %collective-permute-start.14) | collective-permute-done | bytes 1568 | tf_op jit(solution)/shard_map/ppermute | solution.py:16
  119.1 8.3 %fusion = f32[2048,128]{1,0:T(8,128)S(1)} fusion(bf16[128,4096]{1,0:T(8,128)(2,1)S(1)} %multiply_convert_fusion, bf16[4096,4096]{1,0:T(8,128)(2,1)} %param.26, s32[]{:T(128)S(6)} %select_n.230), kind=kOutput, calls=%fused_computation.10 | convolution fusion | flops 2147483648 | bytes 18874372 | tf_op jit(solution)/shard_map/dot_general | solution.py:224
  127.5 1.9 %collective-permute-done.15 = f32[1,1024,128]{2,1,0:T(8,128)S(1)} collective-permute-done((f32[1,1024,128]{2,1,0:T(8,128)S(1)}, f32[1,1024,128]{2,1,0:T(8,128)S(1)}, u32[]{:S(2)}, u32[]{:S(2)}) %collective-permute-start.15) | collective-permute-done | bytes 524320 | tf_op jit(solution)/shard_map/ppermute | solution.py:16
  129.5 8.1 %fusion.4 = f32[2048,128]{1,0:T(8,128)S(1)} fusion(bf16[128,4096]{1,0:T(8,128)(2,1)S(1)} %multiply_convert_fusion, bf16[4096,4096]{1,0:T(8,128)(2,1)} %param.26, s32[]{:T(128)S(6)} %select_n.229), kind=kOutput, calls=%fused_computation.14 | convolution fusion | flops 2147483648 | bytes 18874372 | tf_op jit(solution)/shard_map/dot_general | solution.py:233
  137.9 1.5 collective-permute-start.17
  139.4 7.0 %collective-permute-done.17 = bf16[1024,128]{1,0:T(8,128)(2,1)S(1)} collective-permute-done((bf16[1024,128]{1,0:T(8,128)(2,1)S(1)}, bf16[1024,128]{1,0:T(8,128)(2,1)S(1)}, u32[]{:S(2)}, u32[]{:S(2)}) %collective-permute-start.17) | collective-permute-done | bytes 262176 | tf_op jit(solution)/shard_map/ppermute | solution.py:16
  146.9 1.4 concatenate.3
  148.3 2.7 %collective-permute-start.18 = (f32[1026]{0:T(1024)S(1)}, f32[1026]{0:T(1024)S(1)}, u32[]{:S(2)}, u32[]{:S(2)}) collective-permute-start(f32[1026]{0:T(1024)S(1)} %concatenate.3), channel_id=1, source_target_pairs={{0,4},{4,0},{8,12},{12,8},{16,20},{20,16},{24,28},{28,24},{1,5},{5... | collective-permute-start | bytes 12320 | tf_op jit(solution)/shard_map/ppermute | solution.py:16
  150.9 1.6 collective-permute-done.18
  152.6 1.1 collective-permute-done.21
  153.7 1.5 collective-permute-start.22
  155.2 1.0 collective-permute-done.19
  156.2 2.8 %collective-permute-start.20 = (f32[1026]{0:T(1024)S(1)}, f32[1026]{0:T(1024)S(1)}, u32[]{:S(2)}, u32[]{:S(2)}) collective-permute-start(f32[1026]{0:T(1024)S(1)} %add.347), channel_id=1, source_target_pairs={{0,16},{4,20},{8,24},{12,28},{16,0},{20,4},{24,8},{28,12},{1,17},{... | collective-permute-start | bytes 12320 | tf_op jit(solution)/shard_map/ppermute | solution.py:16
  159.0 1.7 %collective-permute-done.20 = f32[1026]{0:T(1024)S(1)} collective-permute-done((f32[1026]{0:T(1024)S(1)}, f32[1026]{0:T(1024)S(1)}, u32[]{:S(2)}, u32[]{:S(2)}) %collective-permute-start.20) | collective-permute-done | bytes 4136 | tf_op jit(solution)/shard_map/ppermute | solution.py:16
  161.3 1.3 slice_divide_fusion
  (138 shorter events, 30.9 us)
Async XLA Ops:
  0.6 17.2 %copy-start = (bf16[128,4096]{1,0:T(8,128)(2,1)S(1)}, bf16[128,4096]{1,0:T(8,128)(2,1)}, u32[]{:S(2)}) copy-start(bf16[128,4096]{1,0:T(8,128)(2,1)} %param.21) | copy-start | bytes 3145732
  0.6 16.6 %copy-start.5 = (s32[128]{0:T(128)S(1)}, s32[128]{0:T(128)}, u32[]{:S(2)}) copy-start(s32[128]{0:T(128)} %param.28) | copy-start | bytes 1540
  7.0 46.0 %collective-permute-start.6 = (bf16[2,80,512]{2,1,0:T(8,128)(2,1)}, bf16[2,80,512]{2,1,0:T(8,128)(2,1)}, u32[]{:S(2)}, u32[]{:S(2)}) collective-permute-start(bf16[2,80,512]{2,1,0:T(8,128)(2,1)} %get-tuple-element.79), channel_id=1, source_target_pairs={{0,4},{4,8},{8,12},{12,16},{16,20},{20,24},{24,28},{28,0},{1,5},{5... | collective-permute-start | bytes 491528 | tf_op jit(solution)/shard_map/ppermute | solution.py:159
  10.0 44.2 %collective-permute-start.5 = (bf16[2,80,512]{2,1,0:T(8,128)(2,1)}, bf16[2,80,512]{2,1,0:T(8,128)(2,1)}, u32[]{:S(2)}, u32[]{:S(2)}) collective-permute-start(bf16[2,80,512]{2,1,0:T(8,128)(2,1)} %get-tuple-element.80), channel_id=1, source_target_pairs={{0,16},{4,20},{8,24},{12,28},{16,0},{20,4},{24,8},{28,12},{1,17},{... | collective-permute-start | bytes 491528 | tf_op jit(solution)/shard_map/ppermute | solution.py:159
  22.7 10.8 %collective-permute-start.3 = (bf16[2,80,512]{2,1,0:T(8,128)(2,1)S(1)}, bf16[2,80,512]{2,1,0:T(8,128)(2,1)}, u32[]{:S(2)}, u32[]{:S(2)}) collective-permute-start(bf16[2,80,512]{2,1,0:T(8,128)(2,1)S(1)} %slice_bitcast_fusion.7), channel_id=1, source_target_pairs={{0,12},{4,16},{8,20},{12,24},{16,28},{20,0},{24,4},{28,8},{1,13},{... | collective-permute-start | bytes 491528 | tf_op jit(solution)/shard_map/cond/branch_1_fun/ppermute | solution.py:162
  34.8 6.4 %collective-permute-start.2 = (bf16[2,80,512]{2,1,0:T(8,128)(2,1)S(1)}, bf16[2,80,512]{2,1,0:T(8,128)(2,1)}, u32[]{:S(2)}, u32[]{:S(2)}) collective-permute-start(bf16[2,80,512]{2,1,0:T(8,128)(2,1)S(1)} %slice_bitcast_fusion.5), channel_id=1, source_target_pairs={{0,20},{4,24},{8,28},{12,0},{16,4},{20,8},{24,12},{28,16},{1,21},{... | collective-permute-start | bytes 491528 | tf_op jit(solution)/shard_map/cond/branch_1_fun/ppermute | solution.py:162
  55.7 2.2 %copy-start.2 = (bf16[512,4096]{1,0:T(8,128)(2,1)S(1)}, bf16[512,4096]{1,0:T(8,128)(2,1)}, u32[]{:S(2)}) copy-start(bf16[512,4096]{1,0:T(8,128)(2,1)} %param.24) | copy-start | bytes 12582916
  68.1 3.0 %collective-permute-start.7 = (f32[128,2,1024]{0,2,1:T(8,128)}, f32[128,2,1024]{0,2,1:T(8,128)}, u32[]{:S(2)}, u32[]{:S(2)}) collective-permute-start(f32[128,2,1024]{0,2,1:T(8,128)} %bitcast.250), channel_id=1, source_target_pairs={{0,1},{1,0},{2,3},{3,2},{4,5},{5,4},{6,7},{7,6},{8,9},{9,8},{10,11... | collective-permute-start | bytes 3145736 | tf_op jit(solution)/shard_map/ppermute | solution.py:16
  72.4 1.0 copy-start.3
  73.4 8.4 %collective-permute-start.8 = (bf16[128,1,1024]{0,2,1:T(8,128)(2,1)S(1)}, bf16[128,1,1024]{0,2,1:T(8,128)(2,1)S(1)}, u32[]{:S(2)}, u32[]{:S(2)}) collective-permute-start(bf16[128,1,1024]{0,2,1:T(8,128)(2,1)S(1)} %dynamic-slice_convert_fusion), channel_id=1, source_target_pairs={{0,2},{1,3},{2,0},{3,1},{4,6},{5,7},{6,4},{7,5},{8,10},{9,11},{10,... | collective-permute-start | bytes 786440 | tf_op jit(solution)/shard_map/ppermute | solution.py:16
  75.2 16.2 %copy-start.6 = (s32[128]{0:T(128)S(1)}, s32[128]{0:T(128)}, u32[]{:S(2)}) copy-start(s32[128]{0:T(128)} %param.30) | copy-start | bytes 1540
  83.0 1.2 collective-permute-start.9
  84.2 3.5 %collective-permute-start.10 = (f32[128]{0:T(128)S(1)}, f32[128]{0:T(128)S(1)}, u32[]{:S(2)}, u32[]{:S(2)}) collective-permute-start(f32[128]{0:T(128)S(1)} %add.329), channel_id=1, source_target_pairs={{0,2},{1,3},{2,0},{3,1},{4,6},{5,7},{6,4},{7,5},{8,10},{9,11},{10,... | collective-permute-start | bytes 1544 | tf_op jit(solution)/shard_map/ppermute | solution.py:16
  88.0 1.6 collective-permute-start.11
  89.8 14.0 %collective-permute-start.12 = (bf16[128,2048]{0,1:T(8,128)(2,1)S(1)}, bf16[128,2048]{0,1:T(8,128)(2,1)S(1)}, u32[]{:S(2)}, u32[]{:S(2)}) collective-permute-start(bf16[128,2048]{0,1:T(8,128)(2,1)S(1)} %bitcast.264), channel_id=1, source_target_pairs={{0,2},{1,3},{2,0},{3,1},{4,6},{5,7},{6,4},{7,5},{8,10},{9,11},{10,... | collective-permute-start | bytes 1572872 | tf_op jit(solution)/shard_map/ppermute | solution.py:16
  112.1 3.6 %copy-start.4 = (s32[128]{0:T(128)S(1)}, s32[128]{0:T(128)}, u32[]{:S(2)}) copy-start(s32[128]{0:T(128)} %param.31) | copy-start | bytes 1540
  112.9 1.2 collective-permute-start.13
  114.1 3.7 %collective-permute-start.14 = (f32[3,128]{1,0:T(4,128)S(1)}, f32[3,128]{1,0:T(4,128)S(1)}, u32[]{:S(2)}, u32[]{:S(2)}) collective-permute-start(f32[3,128]{1,0:T(4,128)S(1)} %pad_maximum_fusion.2), channel_id=1, source_target_pairs={{0,2},{1,3},{2,0},{3,1},{4,6},{5,7},{6,4},{7,5},{8,10},{9,11},{10,... | collective-permute-start | bytes 4616 | tf_op jit(solution)/shard_map/ppermute | solution.py:16
  127.5 2.0 %collective-permute-start.15 = (f32[1,1024,128]{2,1,0:T(8,128)S(1)}, f32[1,1024,128]{2,1,0:T(8,128)S(1)}, u32[]{:S(2)}, u32[]{:S(2)}) collective-permute-start(f32[1,1024,128]{2,1,0:T(8,128)S(1)} %dynamic-slice_bitcast_fusion.1), channel_id=1, source_target_pairs={{0,1},{1,0},{2,3},{3,2},{4,5},{5,4},{6,7},{7,6},{8,9},{9,8},{10,11... | collective-permute-start | bytes 1572872 | tf_op jit(solution)/shard_map/ppermute | solution.py:16
  137.6 28.1 %copy-start.1 = (bf16[128,4096]{1,0:T(8,128)(2,1)S(1)}, bf16[128,4096]{1,0:T(8,128)(2,1)}, u32[]{:S(2)}) copy-start(bf16[128,4096]{1,0:T(8,128)(2,1)} %param.21) | copy-start | bytes 3145732
  137.7 8.8 %collective-permute-start.16 = (f32[1,1024,128]{2,1,0:T(8,128)S(1)}, f32[1,1024,128]{2,1,0:T(8,128)S(1)}, u32[]{:S(2)}, u32[]{:S(2)}) collective-permute-start(f32[1,1024,128]{2,1,0:T(8,128)S(1)} %dynamic-slice_bitcast_fusion), channel_id=1, source_target_pairs={{0,1},{1,0},{2,3},{3,2},{4,5},{5,4},{6,7},{7,6},{8,9},{9,8},{10,11... | collective-permute-start | bytes 1572872 | tf_op jit(solution)/shard_map/ppermute | solution.py:16
  137.9 8.6 %collective-permute-start.17 = (bf16[1024,128]{1,0:T(8,128)(2,1)S(1)}, bf16[1024,128]{1,0:T(8,128)(2,1)S(1)}, u32[]{:S(2)}, u32[]{:S(2)}) collective-permute-start(bf16[1024,128]{1,0:T(8,128)(2,1)S(1)} %fusion.19), channel_id=1, source_target_pairs={{0,2},{1,3},{2,0},{3,1},{4,6},{5,7},{6,4},{7,5},{8,10},{9,11},{10,... | collective-permute-start | bytes 786440 | tf_op jit(solution)/shard_map/ppermute | solution.py:16
  148.3 4.3 %collective-permute-start.18 = (f32[1026]{0:T(1024)S(1)}, f32[1026]{0:T(1024)S(1)}, u32[]{:S(2)}, u32[]{:S(2)}) collective-permute-start(f32[1026]{0:T(1024)S(1)} %concatenate.3), channel_id=1, source_target_pairs={{0,4},{4,0},{8,12},{12,8},{16,20},{20,16},{24,28},{28,24},{1,5},{5... | collective-permute-start | bytes 12320 | tf_op jit(solution)/shard_map/ppermute | solution.py:16
  152.5 3.7 %collective-permute-start.19 = (f32[1026]{0:T(1024)S(1)}, f32[1026]{0:T(1024)S(1)}, u32[]{:S(2)}, u32[]{:S(2)}) collective-permute-start(f32[1026]{0:T(1024)S(1)} %add.346), channel_id=1, source_target_pairs={{0,8},{4,12},{8,0},{12,4},{16,24},{20,28},{24,16},{28,20},{1,9},{5... | collective-permute-start | bytes 12320 | tf_op jit(solution)/shard_map/ppermute | solution.py:16
  152.5 1.1 collective-permute-start.21
  153.7 5.3 %collective-permute-start.22 = (f32[128]{0:T(128)S(1)}, f32[128]{0:T(128)S(1)}, u32[]{:S(2)}, u32[]{:S(2)}) collective-permute-start(f32[128]{0:T(128)S(1)} %add.349), channel_id=1, source_target_pairs={{0,2},{1,3},{2,0},{3,1},{4,6},{5,7},{6,4},{7,5},{8,10},{9,11},{10,... | collective-permute-start | bytes 1544 | tf_op jit(solution)/shard_map/ppermute | solution.py:16
  156.2 4.5 %collective-permute-start.20 = (f32[1026]{0:T(1024)S(1)}, f32[1026]{0:T(1024)S(1)}, u32[]{:S(2)}, u32[]{:S(2)}) collective-permute-start(f32[1026]{0:T(1024)S(1)} %add.347), channel_id=1, source_target_pairs={{0,16},{4,20},{8,24},{12,28},{16,0},{20,4},{24,8},{28,12},{1,17},{... | collective-permute-start | bytes 12320 | tf_op jit(solution)/shard_map/ppermute | solution.py:16

commit v6 on v3

--- a/solution.py
+++ b/solution.py
@@ -51,13 +51,23 @@
     return cur.reshape(head + (chunks * width,) + tail)
 
 
+def by_source(x, axis):
+    size = lax.axis_size(axis)
+    me = lax.axis_index(axis)
+    pieces = [x]
+    for shift in range(1, size):
+        pieces.append(lax.ppermute(x, axis, [(i, (i - shift) % size) for i in range(size)]))
+    stacked = jnp.stack(pieces)
+    order = (jnp.arange(size)[:, None] - me) % size == jnp.arange(size)[None, :]
+    hot = order.reshape((size, size) + (1,) * x.ndim)
+    return jnp.sum(jnp.where(hot, stacked[None], 0), 1)
+
+
 def sum_all(x, axis):
     size = lax.axis_size(axis)
-    if not is_power_of_two(size):
+    if size > 16:
         return lax.psum(x, axis)
-    for bit in range(size.bit_length() - 1):
-        x = x + exchange(x, axis, bit)
-    return x
+    return jnp.sum(by_source(x, axis), 0)
 
 
 def merge_totals(first_set, second_set):
@@ -70,10 +80,11 @@
 
 def merge_all(stats, axis):
     size = lax.axis_size(axis)
-    if is_power_of_two(size):
-        for bit in range(size.bit_length() - 1):
-            stats = merge_totals(stats, exchange(stats, axis, bit))
-        return stats
+    if size <= 16:
+        everything = by_source(stats, axis)
+        larger = jnp.max(everything[:, 0], 0)
+        combined = jnp.sum(everything[:, 1] * jnp.exp(everything[:, 0] - larger[None]), 0)
+        return jnp.stack([larger, combined, jnp.sum(everything[:, 2], 0)])
     everything = lax.all_gather(stats, axis)
     return lax.fori_loop(1, size, lambda k, so_far: merge_totals(so_far, everything[k]), everything[0])
 

time: 158 us -> 164 us (1.038)
  starting transfers between devices: 33.4 us -> 41.6 us
  waiting for transfers between devices: 41.4 us -> 35.7 us
  other arithmetic: 13.6 us -> 15.8 us
    ppermute x0 -> x16, starting transfers between devices: none -> 22.4 us  [by_source(): lax.ppermute(x, axis, [(i, (i - shift) % size) for i in range(size)])]
    ppermute x16 -> x7, starting transfers between devices: 19.2 us -> 4.99 us  [exchange(): return lax.ppermute(x, axis, [(i, i ^ 1 << bit) for i in range(size)])]
    ppermute x16 -> x7, waiting for transfers between devices: 34.9 us -> 24 us  [exchange(): return lax.ppermute(x, axis, [(i, i ^ 1 << bit) for i in range(size)])]
    ppermute x0 -> x16, waiting for transfers between devices: none -> 5.23 us  [by_source(): lax.ppermute(x, axis, [(i, (i - shift) % size) for i in range(size)])]
    unnamed x26 -> x28, local copies, waits for them, and re-layouts: 3.37 us -> 4.71 us
  transfers between devices with their start and end apart: 23 -> 30, of which waited for: 15 -> 13; matrix products, arithmetic and copies ran while one was open for 12% -> 13% of each run, Pallas kernels for 0% -> 0%
where the time goes in v6:
time: 164 us; the launch traced here: 163 us
  starting transfers between devices  41.6 us (25%)
  matrix products  39.4 us (24%)
  waiting for transfers between devices  35.7 us (22%)
  local copies, waits for them, and re-layouts  26.8 us (16%)
  other arithmetic  15.8 us (10%)
  between operations  3.91 us (2%)
    ppermute x7, waiting for transfers between devices, exchange(): return lax.ppermute(x, axis, [(i, i ^ 1 << bit) for i in range(size)])  24 us
    ppermute x16, starting transfers between devices, by_source(): lax.ppermute(x, axis, [(i, (i - shift) % size) for i in range(size)])  22.4 us
    ppermute x7, starting transfers between devices, body(): lax.ppermute(block, 'dp', [(i, (i - shift) % dp_count) for i in range(dp_...  14.2 us
    dot_general x1, matrix products, body(): jnp.dot(far_normed, far_rows, preferred_element_type=jnp.float32)  8.27 us
    dot_general x1, matrix products, body(): jnp.dot(near_normed, near_rows, preferred_element_type=jnp.float32)  8.13 us
    dot_general x1, matrix products, body(): lax.dot_general(far_rows, grad_logits, contract, preferred_element_type=j...  8.13 us
    dot_general x1, matrix products, body(): lax.dot_general(near_rows, near_logits, contract, preferred_element_type=...  8.13 us
    ppermute x7, waiting for transfers between devices, body(): lax.ppermute(block, 'dp', [(i, (i - shift) % dp_count) for i in range(dp_...  6.5 us
  transfers between devices with their start and end apart: 30, of which 13 were waited for; matrix products, arithmetic and copies ran while one was open for 13% of the time, Pallas kernels for 0%

profile of v6, /device:TPU:0, one launch (start us, length us, event | category | flops | bytes accessed | tf_op | source)
XLA Modules:
  0.0 163.2 jit_solution(9316204603553556294)
XLA Ops:
  4.8 1.7 %fusion.11 = bf16[8,2,80,512]{3,2,1,0:T(8,128)(2,1)S(1)} fusion(bf16[2,192,512]{2,1,0:T(8,128)(2,1)} %param.13, s32[8,80]{1,0:T(8,128)S(1)} %iota_add_fusion), kind=kOutput, calls=%fused_computation.14 | convolution fusion | flops 252436480 | bytes 1706496 | tf_op jit(solution)/shard_map/str,crf->sctf/dot_general | solution.py:142
  7.2 5.0 %collective-permute-start.1 = (bf16[2,80,512]{2,1,0:T(8,128)(2,1)S(1)}, bf16[2,80,512]{2,1,0:T(8,128)(2,1)}, u32[]{:S(2)}, u32[]{:S(2)}) collective-permute-start(bf16[2,80,512]{2,1,0:T(8,128)(2,1)S(1)} %get-tuple-element.29), channel_id=1, source_target_pairs={{0,24},{4,28},{8,0},{12,4},{16,8},{20,12},{24,16},{28,20},{1,25},{... | collective-permute-start | bytes 491528 | tf_op jit(solution)/shard_map/ppermute | solution.py:168
  12.3 1.5 collective-permute-start.6
  13.8 1.0 collective-permute-start.4
  14.8 2.8 %collective-permute-start.3 = (bf16[2,80,512]{2,1,0:T(8,128)(2,1)S(1)}, bf16[2,80,512]{2,1,0:T(8,128)(2,1)S(1)}, u32[]{:S(2)}, u32[]{:S(2)}) collective-permute-start(bf16[2,80,512]{2,1,0:T(8,128)(2,1)S(1)} %get-tuple-element.33), channel_id=1, source_target_pairs={{0,16},{4,20},{8,24},{12,28},{16,0},{20,4},{24,8},{28,12},{1,17},{... | collective-permute-start | bytes 491528 | tf_op jit(solution)/shard_map/ppermute | solution.py:168
  21.5 1.0 collective-permute-start.2
  23.7 2.9 %collective-permute-start = (bf16[2,80,512]{2,1,0:T(8,128)(2,1)S(1)}, bf16[2,80,512]{2,1,0:T(8,128)(2,1)}, u32[]{:S(2)}, u32[]{:S(2)}) collective-permute-start(bf16[2,80,512]{2,1,0:T(8,128)(2,1)S(1)} %get-tuple-element.35), channel_id=1, source_target_pairs={{0,28},{4,0},{8,4},{12,8},{16,12},{20,16},{24,20},{28,24},{1,29},{... | collective-permute-start | bytes 491528 | tf_op jit(solution)/shard_map/ppermute | solution.py:168
  27.8 0.9 fusion.95
  28.9 6.5 %collective-permute-done.4 = bf16[2,80,512]{2,1,0:T(8,128)(2,1)} collective-permute-done((bf16[2,80,512]{2,1,0:T(8,128)(2,1)S(1)}, bf16[2,80,512]{2,1,0:T(8,128)(2,1)}, u32[]{:S(2)}, u32[]{:S(2)}) %collective-permute-start.4) | collective-permute-done | bytes 163872 | tf_op jit(solution)/shard_map/ppermute | solution.py:168
  36.9 0.9 fusion.92
  38.1 0.9 fusion.91
  43.2 1.3 copy-done.4
  45.2 2.8 %reshape.612 = f32[128,2,2,1024]{3,2,1,0:T(2,128)} reshape(f32[128,4096]{1,0:T(8,128)S(1)} %fusion.100) | data formatting | bytes 4194304 | tf_op jit(solution)/shard_map/reshape | solution.py:26
  48.1 4.4 %constant_dynamic-slice_fusion.2 = (f32[128,2,1,1024]{3,2,1,0:T(1,128)S(1)}, f32[128,2,1,1024]{3,2,1,0:T(1,128)S(1)}) fusion(f32[128,2,2,1024]{3,2,1,0:T(2,128)} %reshape.612, s32[]{:T(128)S(6)} %select_n.265, s32[]{:T(128)S(6)} %select_n.266), kind=kLoop, calls=%fused_computation.150 | loop fusion | bytes 4194312 | tf_op jit(solution)/shard_map/jit(dynamic_index_in_dim)/dynamic_slice | solution.py:28
  52.5 2.0 %copy.90 = f32[128,2,1,1024]{0,3,1,2:T(8,128)} copy(f32[128,2,1,1024]{3,2,1,0:T(1,128)S(1)} %get-tuple-element.28) | data formatting | bytes 2097152 | tf_op jit(solution)/shard_map/jit(dynamic_index_in_dim)/dynamic_slice | solution.py:29
  55.2 2.2 %collective-permute-done.7 = f32[128,2,1024]{0,2,1:T(8,128)} collective-permute-done((f32[128,2,1024]{0,2,1:T(8,128)}, f32[128,2,1024]{0,2,1:T(8,128)}, u32[]{:S(2)}, u32[]{:S(2)}) %collective-permute-start.7) | collective-permute-done | bytes 1048608 | tf_op jit(solution)/shard_map/ppermute | solution.py:16
  57.4 1.3 bitcast_add_fusion
  58.8 1.0 copy-done.5
  59.8 1.6 collective-permute-start.8
  61.6 6.6 %collective-permute-done.8 = bf16[128,1,1024]{0,2,1:T(8,128)(2,1)S(1)} collective-permute-done((bf16[128,1,1024]{0,2,1:T(8,128)(2,1)S(1)}, bf16[128,1,1024]{0,2,1:T(8,128)(2,1)S(1)}, u32[]{:S(2)}, u32[]{:S(2)}) %collective-permute-start.8) | collective-permute-done | bytes 262176 | tf_op jit(solution)/shard_map/ppermute | solution.py:16
  68.2 1.2 multiply_reduce_fusion.1
  69.5 1.6 collective-permute-start.10
  71.0 1.4 collective-permute-start.9
  74.7 1.2 collective-permute-done.12
  76.1 1.6 collective-permute-start.13
  77.7 8.1 %fusion.6 = f32[128,4096]{1,0:T(8,128)S(1)} fusion(bf16[128,2048]{0,1:T(8,128)(2,1)S(1)} %bitcast.194, bf16[4096,4096]{1,0:T(8,128)(2,1)} %param.16, s32[]{:T(128)S(6)} %select_n.273), kind=kOutput, calls=%fused_computation.6 | convolution fusion | flops 2147483648 | bytes 19398660 | tf_op jit(solution)/shard_map/dot_general | solution.py:210
  85.8 4.5 %collective-permute-done.13 = bf16[128,2048]{0,1:T(8,128)(2,1)S(1)} collective-permute-done((bf16[128,2048]{0,1:T(8,128)(2,1)S(1)}, bf16[128,2048]{0,1:T(8,128)(2,1)S(1)}, u32[]{:S(2)}, u32[]{:S(2)}) %collective-permute-start.13) | collective-permute-done | bytes 524320 | tf_op jit(solution)/shard_map/ppermute | solution.py:16
  90.4 8.3 %fusion.99 = (f32[128]{0:T(128)S(1)}, f32[128,4096]{1,0:T(8,128)S(1)}) fusion(f32[128,4096]{1,0:T(8,128)S(1)} %fusion.6, bf16[128,2048]{0,1:T(8,128)(2,1)S(1)} %collective-permute-done.13, bf16[4096,4096]{1,0:T(8,128)(2,1)} %param.16, s32[]{:T(128)S(6)} %select_n.274), kind=kOutput, calls=%fused_computation.235 | convolution fusion | flops 2148532224 | bytes 21496324 | tf_op jit(solution)/shard_map/dot_general | solution.py:210
  98.7 1.3 copy-done.2
  100.7 1.6 collective-permute-start.15
  102.8 1.5 collective-permute-done.15
  104.4 0.9 collective-permute-done.16
  106.1 2.2 %multiply_convert_fusion = bf16[128,4096]{1,0:T(8,128)(2,1)S(1)} fusion(f32[128,4096]{1,0:T(8,128)} %copy-done.2, f32[128]{0:T(128)S(1)} %get-tuple-element.24, f32[128]{0:T(128)S(1)} %convert_element_type.66, s32[128]{0:T(128)S(1)} %broadcast_subtract_fusion), kind=kLoop, calls=%fused_computation.9 | loop fusion | flops 3145728 | bytes 3147264 | tf_op jit(solution)/shard_map/convert_element_type | solution.py:228
  108.4 8.1 %fusion = f32[2048,128]{1,0:T(8,128)S(1)} fusion(bf16[128,4096]{1,0:T(8,128)(2,1)S(1)} %multiply_convert_fusion, bf16[4096,4096]{1,0:T(8,128)(2,1)} %param.16, s32[]{:T(128)S(6)} %select_n.274), kind=kOutput, calls=%fused_computation | convolution fusion | flops 2147483648 | bytes 18874372 | tf_op jit(solution)/shard_map/dot_general | solution.py:231
  116.6 1.9 %collective-permute-done.17 = f32[1,1024,128]{2,1,0:T(8,128)S(1)} collective-permute-done((f32[1,1024,128]{2,1,0:T(8,128)S(1)}, f32[1,1024,128]{2,1,0:T(8,128)S(1)}, u32[]{:S(2)}, u32[]{:S(2)}) %collective-permute-start.17) | collective-permute-done | bytes 524320 | tf_op jit(solution)/shard_map/ppermute | solution.py:16
  118.6 8.1 %fusion.4 = f32[2048,128]{1,0:T(8,128)S(1)} fusion(bf16[128,4096]{1,0:T(8,128)(2,1)S(1)} %multiply_convert_fusion, bf16[4096,4096]{1,0:T(8,128)(2,1)} %param.16, s32[]{:T(128)S(6)} %select_n.273), kind=kOutput, calls=%fused_computation.4 | convolution fusion | flops 2147483648 | bytes 18874372 | tf_op jit(solution)/shard_map/dot_general | solution.py:240
  128.0 7.6 %collective-permute-done.19 = bf16[1024,128]{1,0:T(8,128)(2,1)S(1)} collective-permute-done((bf16[1024,128]{1,0:T(8,128)(2,1)S(1)}, bf16[1024,128]{1,0:T(8,128)(2,1)S(1)}, u32[]{:S(2)}, u32[]{:S(2)}) %collective-permute-start.19) | collective-permute-done | bytes 262176 | tf_op jit(solution)/shard_map/ppermute | solution.py:16
  136.0 1.0 collective-permute-start.28
  137.0 1.4 collective-permute-start.27
  138.4 1.4 concatenate.3
  139.8 3.3 %collective-permute-start.26 = (f32[1026]{0:T(1024)S(1)}, f32[1026]{0:T(1024)S(1)}, u32[]{:S(2)}, u32[]{:S(2)}) collective-permute-start(f32[1026]{0:T(1024)S(1)} %concatenate.3), channel_id=1, source_target_pairs={{0,4},{4,8},{8,12},{12,16},{16,20},{20,24},{24,28},{28,0},{1,5},{5... | collective-permute-start | bytes 12320 | tf_op jit(solution)/shard_map/ppermute | solution.py:59
  143.1 2.8 %collective-permute-start.25 = (f32[1026]{0:T(1024)S(1)}, f32[1026]{0:T(1024)S(1)}, u32[]{:S(2)}, u32[]{:S(2)}) collective-permute-start(f32[1026]{0:T(1024)S(1)} %concatenate.3), channel_id=1, source_target_pairs={{0,8},{4,12},{8,16},{12,20},{16,24},{20,28},{24,0},{28,4},{1,9},{5... | collective-permute-start | bytes 12320 | tf_op jit(solution)/shard_map/ppermute | solution.py:59
  145.8 2.4 %collective-permute-start.24 = (f32[1026]{0:T(1024)S(1)}, f32[1026]{0:T(1024)S(1)}, u32[]{:S(2)}, u32[]{:S(2)}) collective-permute-start(f32[1026]{0:T(1024)S(1)} %concatenate.3), channel_id=1, source_target_pairs={{0,12},{4,16},{8,20},{12,24},{16,28},{20,0},{24,4},{28,8},{1,13},{... | collective-permute-start | bytes 12320 | tf_op jit(solution)/shard_map/ppermute | solution.py:59
  148.2 2.5 %collective-permute-start.23 = (f32[1026]{0:T(1024)S(1)}, f32[1026]{0:T(1024)S(1)}, u32[]{:S(2)}, u32[]{:S(2)}) collective-permute-start(f32[1026]{0:T(1024)S(1)} %concatenate.3), channel_id=1, source_target_pairs={{0,16},{4,20},{8,24},{12,28},{16,0},{20,4},{24,8},{28,12},{1,17},{... | collective-permute-start | bytes 12320 | tf_op jit(solution)/shard_map/ppermute | solution.py:59
  150.7 2.3 %collective-permute-start.22 = (f32[1026]{0:T(1024)S(1)}, f32[1026]{0:T(1024)S(1)}, u32[]{:S(2)}, u32[]{:S(2)}) collective-permute-start(f32[1026]{0:T(1024)S(1)} %concatenate.3), channel_id=1, source_target_pairs={{0,20},{4,24},{8,28},{12,0},{16,4},{20,8},{24,12},{28,16},{1,21},{... | collective-permute-start | bytes 12320 | tf_op jit(solution)/shard_map/ppermute | solution.py:59
  153.3 1.4 collective-permute-start.20
  155.3 1.5 collective-permute-done.21
  157.7 1.3 slice_divide_fusion
  (177 shorter events, 28.4 us)
Async XLA Ops:
  0.6 17.8 %copy-start = (bf16[128,4096]{1,0:T(8,128)(2,1)S(1)}, bf16[128,4096]{1,0:T(8,128)(2,1)}, u32[]{:S(2)}) copy-start(bf16[128,4096]{1,0:T(8,128)(2,1)} %param.11) | copy-start | bytes 3145732
  4.8 13.1 %copy-start.11 = (s32[128]{0:T(128)S(1)}, s32[128]{0:T(128)}, u32[]{:S(2)}) copy-start(s32[128]{0:T(128)} %param.18) | copy-start | bytes 1540
  4.8 13.7 %copy-start.3 = (bf16[4096,512]{1,0:T(8,128)(2,1)S(1)}, bf16[4096,512]{1,0:T(8,128)(2,1)}, u32[]{:S(2)}) copy-start(bf16[4096,512]{1,0:T(8,128)(2,1)} %param.12) | copy-start | bytes 12582916
  7.2 14.2 %collective-permute-start.1 = (bf16[2,80,512]{2,1,0:T(8,128)(2,1)S(1)}, bf16[2,80,512]{2,1,0:T(8,128)(2,1)}, u32[]{:S(2)}, u32[]{:S(2)}) collective-permute-start(bf16[2,80,512]{2,1,0:T(8,128)(2,1)S(1)} %get-tuple-element.29), channel_id=1, source_target_pairs={{0,24},{4,28},{8,0},{12,4},{16,8},{20,12},{24,16},{28,20},{1,25},{... | collective-permute-start | bytes 491528 | tf_op jit(solution)/shard_map/ppermute | solution.py:168
  12.3 11.4 %collective-permute-start.6 = (bf16[2,80,512]{2,1,0:T(8,128)(2,1)S(1)}, bf16[2,80,512]{2,1,0:T(8,128)(2,1)}, u32[]{:S(2)}, u32[]{:S(2)}) collective-permute-start(bf16[2,80,512]{2,1,0:T(8,128)(2,1)S(1)} %get-tuple-element.30), channel_id=1, source_target_pairs={{0,4},{4,8},{8,12},{12,16},{16,20},{20,24},{24,28},{28,0},{1,5},{5... | collective-permute-start | bytes 491528 | tf_op jit(solution)/shard_map/ppermute | solution.py:168
  13.8 14.0 %collective-permute-start.5 = (bf16[2,80,512]{2,1,0:T(8,128)(2,1)S(1)}, bf16[2,80,512]{2,1,0:T(8,128)(2,1)}, u32[]{:S(2)}, u32[]{:S(2)}) collective-permute-start(bf16[2,80,512]{2,1,0:T(8,128)(2,1)S(1)} %get-tuple-element.31), channel_id=1, source_target_pairs={{0,8},{4,12},{8,16},{12,20},{16,24},{20,28},{24,0},{28,4},{1,9},{5... | collective-permute-start | bytes 491528 | tf_op jit(solution)/shard_map/ppermute | solution.py:168
  13.8 21.7 %collective-permute-start.4 = (bf16[2,80,512]{2,1,0:T(8,128)(2,1)S(1)}, bf16[2,80,512]{2,1,0:T(8,128)(2,1)}, u32[]{:S(2)}, u32[]{:S(2)}) collective-permute-start(bf16[2,80,512]{2,1,0:T(8,128)(2,1)S(1)} %get-tuple-element.32), channel_id=1, source_target_pairs={{0,12},{4,16},{8,20},{12,24},{16,28},{20,0},{24,4},{28,8},{1,13},{... | collective-permute-start | bytes 491528 | tf_op jit(solution)/shard_map/ppermute | solution.py:168
  14.8 21.9 %collective-permute-start.3 = (bf16[2,80,512]{2,1,0:T(8,128)(2,1)S(1)}, bf16[2,80,512]{2,1,0:T(8,128)(2,1)S(1)}, u32[]{:S(2)}, u32[]{:S(2)}) collective-permute-start(bf16[2,80,512]{2,1,0:T(8,128)(2,1)S(1)} %get-tuple-element.33), channel_id=1, source_target_pairs={{0,16},{4,20},{8,24},{12,28},{16,0},{20,4},{24,8},{28,12},{1,17},{... | collective-permute-start | bytes 491528 | tf_op jit(solution)/shard_map/ppermute | solution.py:168
  21.5 15.5 %collective-permute-start.2 = (bf16[2,80,512]{2,1,0:T(8,128)(2,1)}, bf16[2,80,512]{2,1,0:T(8,128)(2,1)}, u32[]{:S(2)}, u32[]{:S(2)}) collective-permute-start(bf16[2,80,512]{2,1,0:T(8,128)(2,1)} %get-tuple-element.34), channel_id=1, source_target_pairs={{0,20},{4,24},{8,28},{12,0},{16,4},{20,8},{24,12},{28,16},{1,21},{... | collective-permute-start | bytes 491528 | tf_op jit(solution)/shard_map/ppermute | solution.py:168
  23.7 14.5 %collective-permute-start = (bf16[2,80,512]{2,1,0:T(8,128)(2,1)S(1)}, bf16[2,80,512]{2,1,0:T(8,128)(2,1)}, u32[]{:S(2)}, u32[]{:S(2)}) collective-permute-start(bf16[2,80,512]{2,1,0:T(8,128)(2,1)S(1)} %get-tuple-element.35), channel_id=1, source_target_pairs={{0,28},{4,0},{8,4},{12,8},{16,12},{20,16},{24,20},{28,24},{1,29},{... | collective-permute-start | bytes 491528 | tf_op jit(solution)/shard_map/ppermute | solution.py:168
  27.5 11.9 %copy-start.8 = (pred[128,80]{0,1:T(8,128)(4,1)S(1)}, pred[128,80]{0,1:T(8,128)(4,1)}, u32[]{:S(2)}) copy-start(pred[128,80]{0,1:T(8,128)(4,1)} %get-tuple-element.71) | copy-start | bytes 30724
  36.5 3.4 %copy-start.7 = (pred[128,80]{0,1:T(8,128)(4,1)S(1)}, pred[128,80]{0,1:T(8,128)(4,1)}, u32[]{:S(2)}) copy-start(pred[128,80]{0,1:T(8,128)(4,1)} %get-tuple-element.72) | copy-start | bytes 30724
  38.1 2.3 %copy-start.6 = (pred[128,80]{0,1:T(8,128)(4,1)S(1)}, pred[128,80]{0,1:T(8,128)(4,1)}, u32[]{:S(2)}) copy-start(pred[128,80]{0,1:T(8,128)(4,1)} %get-tuple-element.73) | copy-start | bytes 30724
  41.8 1.2 copy-start.9
  42.3 2.2 %copy-start.4 = (bf16[512,4096]{1,0:T(8,128)(2,1)S(1)}, bf16[512,4096]{1,0:T(8,128)(2,1)}, u32[]{:S(2)}) copy-start(bf16[512,4096]{1,0:T(8,128)(2,1)} %param.14) | copy-start | bytes 12582916
  54.4 3.0 %collective-permute-start.7 = (f32[128,2,1024]{0,2,1:T(8,128)}, f32[128,2,1024]{0,2,1:T(8,128)}, u32[]{:S(2)}, u32[]{:S(2)}) collective-permute-start(f32[128,2,1024]{0,2,1:T(8,128)} %bitcast.181), channel_id=1, source_target_pairs={{0,1},{1,0},{2,3},{3,2},{4,5},{5,4},{6,7},{7,6},{8,9},{9,8},{10,11... | collective-permute-start | bytes 3145736 | tf_op jit(solution)/shard_map/ppermute | solution.py:16
  58.8 1.0 copy-start.5
  59.8 8.4 %collective-permute-start.8 = (bf16[128,1,1024]{0,2,1:T(8,128)(2,1)S(1)}, bf16[128,1,1024]{0,2,1:T(8,128)(2,1)S(1)}, u32[]{:S(2)}, u32[]{:S(2)}) collective-permute-start(bf16[128,1,1024]{0,2,1:T(8,128)(2,1)S(1)} %dynamic-slice_convert_fusion), channel_id=1, source_target_pairs={{0,2},{1,3},{2,0},{3,1},{4,6},{5,7},{6,4},{7,5},{8,10},{9,11},{10,... | collective-permute-start | bytes 786440 | tf_op jit(solution)/shard_map/ppermute | solution.py:16
  61.6 16.1 %copy-start.12 = (s32[128]{0:T(128)S(1)}, s32[128]{0:T(128)}, u32[]{:S(2)}) copy-start(s32[128]{0:T(128)} %param.20) | copy-start | bytes 1540
  69.4 3.8 %collective-permute-start.11 = (f32[128]{0:T(128)S(1)}, f32[128]{0:T(128)S(1)}, u32[]{:S(2)}, u32[]{:S(2)}) collective-permute-start(f32[128]{0:T(128)S(1)} %get-tuple-element.25), channel_id=1, source_target_pairs={{0,1},{1,2},{2,3},{3,0},{4,5},{5,6},{6,7},{7,4},{8,9},{9,10},{10,1... | collective-permute-start | bytes 1544 | tf_op jit(solution)/shard_map/ppermute | solution.py:59
  69.5 3.7 %collective-permute-start.10 = (f32[128]{0:T(128)S(1)}, f32[128]{0:T(128)S(1)}, u32[]{:S(2)}, u32[]{:S(2)}) collective-permute-start(f32[128]{0:T(128)S(1)} %get-tuple-element.25), channel_id=1, source_target_pairs={{0,2},{1,3},{2,0},{3,1},{4,6},{5,7},{6,4},{7,5},{8,10},{9,11},{10,... | collective-permute-start | bytes 1544 | tf_op jit(solution)/shard_map/ppermute | solution.py:59
  71.0 2.7 %collective-permute-start.9 = (f32[128]{0:T(128)S(1)}, f32[128]{0:T(128)S(1)}, u32[]{:S(2)}, u32[]{:S(2)}) collective-permute-start(f32[128]{0:T(128)S(1)} %get-tuple-element.25), channel_id=1, source_target_pairs={{0,3},{1,0},{2,1},{3,2},{4,7},{5,4},{6,5},{7,6},{8,11},{9,8},{10,9... | collective-permute-start | bytes 1544 | tf_op jit(solution)/shard_map/ppermute | solution.py:59
  74.1 1.8 %collective-permute-start.12 = (bf16[128,1,1024]{0,2,1:T(8,128)(2,1)S(1)}, bf16[128,1,1024]{0,2,1:T(8,128)(2,1)S(1)}, u32[]{:S(2)}, u32[]{:S(2)}) collective-permute-start(bf16[128,1,1024]{0,2,1:T(8,128)(2,1)S(1)} %fusion.40), channel_id=1, source_target_pairs={{0,1},{1,0},{2,3},{3,2},{4,5},{5,4},{6,7},{7,6},{8,9},{9,8},{10,11... | collective-permute-start | bytes 786440 | tf_op jit(solution)/shard_map/ppermute | solution.py:16
  76.1 14.3 %collective-permute-start.13 = (bf16[128,2048]{0,1:T(8,128)(2,1)S(1)}, bf16[128,2048]{0,1:T(8,128)(2,1)S(1)}, u32[]{:S(2)}, u32[]{:S(2)}) collective-permute-start(bf16[128,2048]{0,1:T(8,128)(2,1)S(1)} %bitcast.193), channel_id=1, source_target_pairs={{0,2},{1,3},{2,0},{3,1},{4,6},{5,7},{6,4},{7,5},{8,10},{9,11},{10,... | collective-permute-start | bytes 1572872 | tf_op jit(solution)/shard_map/ppermute | solution.py:16
  98.6 1.4 copy-start.2
  98.6 4.2 %copy-start.10 = (s32[128]{0:T(128)S(1)}, s32[128]{0:T(128)}, u32[]{:S(2)}) copy-start(s32[128]{0:T(128)} %param.21) | copy-start | bytes 1540
  100.7 3.7 %collective-permute-start.15 = (f32[3,128]{1,0:T(4,128)S(1)}, f32[3,128]{1,0:T(4,128)S(1)}, u32[]{:S(2)}, u32[]{:S(2)}) collective-permute-start(f32[3,128]{1,0:T(4,128)S(1)} %get-tuple-element.68), channel_id=1, source_target_pairs={{0,2},{1,3},{2,0},{3,1},{4,6},{5,7},{6,4},{7,5},{8,10},{9,11},{10,... | collective-permute-start | bytes 4616 | tf_op jit(solution)/shard_map/ppermute | solution.py:59
  102.3 2.1 %collective-permute-start.14 = (f32[3,128]{1,0:T(4,128)S(1)}, f32[3,128]{1,0:T(4,128)S(1)}, u32[]{:S(2)}, u32[]{:S(2)}) collective-permute-start(f32[3,128]{1,0:T(4,128)S(1)} %get-tuple-element.68), channel_id=1, source_target_pairs={{0,3},{1,0},{2,1},{3,2},{4,7},{5,4},{6,5},{7,6},{8,11},{9,8},{10,9... | collective-permute-start | bytes 4616 | tf_op jit(solution)/shard_map/ppermute | solution.py:59
  102.3 3.0 %collective-permute-start.16 = (f32[3,128]{1,0:T(4,128)S(1)}, f32[3,128]{1,0:T(4,128)S(1)}, u32[]{:S(2)}, u32[]{:S(2)}) collective-permute-start(f32[3,128]{1,0:T(4,128)S(1)} %get-tuple-element.68), channel_id=1, source_target_pairs={{0,1},{1,2},{2,3},{3,0},{4,5},{5,6},{6,7},{7,4},{8,9},{9,10},{10,1... | collective-permute-start | bytes 4616 | tf_op jit(solution)/shard_map/ppermute | solution.py:59
  116.5 2.0 %collective-permute-start.17 = (f32[1,1024,128]{2,1,0:T(8,128)S(1)}, f32[1,1024,128]{2,1,0:T(8,128)S(1)}, u32[]{:S(2)}, u32[]{:S(2)}) collective-permute-start(f32[1,1024,128]{2,1,0:T(8,128)S(1)} %dynamic-slice_bitcast_fusion.1), channel_id=1, source_target_pairs={{0,1},{1,0},{2,3},{3,2},{4,5},{5,4},{6,7},{7,6},{8,9},{9,8},{10,11... | collective-permute-start | bytes 1572872 | tf_op jit(solution)/shard_map/ppermute | solution.py:16
  126.8 8.8 %collective-permute-start.18 = (f32[1,1024,128]{2,1,0:T(8,128)S(1)}, f32[1,1024,128]{2,1,0:T(8,128)S(1)}, u32[]{:S(2)}, u32[]{:S(2)}) collective-permute-start(f32[1,1024,128]{2,1,0:T(8,128)S(1)} %dynamic-slice_bitcast_fusion), channel_id=1, source_target_pairs={{0,1},{1,0},{2,3},{3,2},{4,5},{5,4},{6,7},{7,6},{8,9},{9,8},{10,11... | collective-permute-start | bytes 1572872 | tf_op jit(solution)/shard_map/ppermute | solution.py:16
  127.0 8.6 %collective-permute-start.19 = (bf16[1024,128]{1,0:T(8,128)(2,1)S(1)}, bf16[1024,128]{1,0:T(8,128)(2,1)S(1)}, u32[]{:S(2)}, u32[]{:S(2)}) collective-permute-start(bf16[1024,128]{1,0:T(8,128)(2,1)S(1)} %fusion.23), channel_id=1, source_target_pairs={{0,2},{1,3},{2,0},{3,1},{4,6},{5,7},{6,4},{7,5},{8,10},{9,11},{10,... | collective-permute-start | bytes 786440 | tf_op jit(solution)/shard_map/ppermute | solution.py:16
  127.9 34.2 %copy-start.1 = (bf16[128,4096]{1,0:T(8,128)(2,1)S(1)}, bf16[128,4096]{1,0:T(8,128)(2,1)}, u32[]{:S(2)}) copy-start(bf16[128,4096]{1,0:T(8,128)(2,1)} %param.11) | copy-start | bytes 3145732
  136.0 9.9 %collective-permute-start.29 = (f32[128]{0:T(128)S(1)}, f32[128]{0:T(128)S(1)}, u32[]{:S(2)}, u32[]{:S(2)}) collective-permute-start(f32[128]{0:T(128)S(1)} %get-tuple-element.15), channel_id=1, source_target_pairs={{0,1},{1,2},{2,3},{3,0},{4,5},{5,6},{6,7},{7,4},{8,9},{9,10},{10,1... | collective-permute-start | bytes 1544 | tf_op jit(solution)/shard_map/ppermute | solution.py:59
  136.0 12.2 %collective-permute-start.28 = (f32[128]{0:T(128)S(1)}, f32[128]{0:T(128)S(1)}, u32[]{:S(2)}, u32[]{:S(2)}) collective-permute-start(f32[128]{0:T(128)S(1)} %get-tuple-element.15), channel_id=1, source_target_pairs={{0,2},{1,3},{2,0},{3,1},{4,6},{5,7},{6,4},{7,5},{8,10},{9,11},{10,... | collective-permute-start | bytes 1544 | tf_op jit(solution)/shard_map/ppermute | solution.py:59
  137.0 13.7 %collective-permute-start.27 = (f32[128]{0:T(128)S(1)}, f32[128]{0:T(128)S(1)}, u32[]{:S(2)}, u32[]{:S(2)}) collective-permute-start(f32[128]{0:T(128)S(1)} %get-tuple-element.15), channel_id=1, source_target_pairs={{0,3},{1,0},{2,1},{3,2},{4,7},{5,4},{6,5},{7,6},{8,11},{9,8},{10,9... | collective-permute-start | bytes 1544 | tf_op jit(solution)/shard_map/ppermute | solution.py:59
  139.8 13.3 %collective-permute-start.26 = (f32[1026]{0:T(1024)S(1)}, f32[1026]{0:T(1024)S(1)}, u32[]{:S(2)}, u32[]{:S(2)}) collective-permute-start(f32[1026]{0:T(1024)S(1)} %concatenate.3), channel_id=1, source_target_pairs={{0,4},{4,8},{8,12},{12,16},{16,20},{20,24},{24,28},{28,0},{1,5},{5... | collective-permute-start | bytes 12320 | tf_op jit(solution)/shard_map/ppermute | solution.py:59
  143.1 10.2 %collective-permute-start.25 = (f32[1026]{0:T(1024)S(1)}, f32[1026]{0:T(1024)S(1)}, u32[]{:S(2)}, u32[]{:S(2)}) collective-permute-start(f32[1026]{0:T(1024)S(1)} %concatenate.3), channel_id=1, source_target_pairs={{0,8},{4,12},{8,16},{12,20},{16,24},{20,28},{24,0},{28,4},{1,9},{5... | collective-permute-start | bytes 12320 | tf_op jit(solution)/shard_map/ppermute | solution.py:59
  145.8 8.9 %collective-permute-start.24 = (f32[1026]{0:T(1024)S(1)}, f32[1026]{0:T(1024)S(1)}, u32[]{:S(2)}, u32[]{:S(2)}) collective-permute-start(f32[1026]{0:T(1024)S(1)} %concatenate.3), channel_id=1, source_target_pairs={{0,12},{4,16},{8,20},{12,24},{16,28},{20,0},{24,4},{28,8},{1,13},{... | collective-permute-start | bytes 12320 | tf_op jit(solution)/shard_map/ppermute | solution.py:59
  148.2 6.6 %collective-permute-start.23 = (f32[1026]{0:T(1024)S(1)}, f32[1026]{0:T(1024)S(1)}, u32[]{:S(2)}, u32[]{:S(2)}) collective-permute-start(f32[1026]{0:T(1024)S(1)} %concatenate.3), channel_id=1, source_target_pairs={{0,16},{4,20},{8,24},{12,28},{16,0},{20,4},{24,8},{28,12},{1,17},{... | collective-permute-start | bytes 12320 | tf_op jit(solution)/shard_map/ppermute | solution.py:59
  150.7 4.6 %collective-permute-start.22 = (f32[1026]{0:T(1024)S(1)}, f32[1026]{0:T(1024)S(1)}, u32[]{:S(2)}, u32[]{:S(2)}) collective-permute-start(f32[1026]{0:T(1024)S(1)} %concatenate.3), channel_id=1, source_target_pairs={{0,20},{4,24},{8,28},{12,0},{16,4},{20,8},{24,12},{28,16},{1,21},{... | collective-permute-start | bytes 12320 | tf_op jit(solution)/shard_map/ppermute | solution.py:59
  153.1 3.7 %collective-permute-start.21 = (f32[1026]{0:T(1024)S(1)}, f32[1026]{0:T(1024)S(1)}, u32[]{:S(2)}, u32[]{:S(2)}) collective-permute-start(f32[1026]{0:T(1024)S(1)} %concatenate.3), channel_id=1, source_target_pairs={{0,24},{4,28},{8,0},{12,4},{16,8},{20,12},{24,16},{28,20},{1,25},{... | collective-permute-start | bytes 12320 | tf_op jit(solution)/shard_map/ppermute | solution.py:59
  153.3 3.7 %collective-permute-start.20 = (f32[1026]{0:T(1024)S(1)}, f32[1026]{0:T(1024)S(1)}, u32[]{:S(2)}, u32[]{:S(2)}) collective-permute-start(f32[1026]{0:T(1024)S(1)} %concatenate.3), channel_id=1, source_target_pairs={{0,28},{4,0},{8,4},{12,8},{16,12},{20,16},{24,20},{28,24},{1,29},{... | collective-permute-start | bytes 12320 | tf_op jit(solution)/shard_map/ppermute | solution.py:59

commit v7 on v3

--- a/solution.py
+++ b/solution.py
@@ -177,9 +177,7 @@
     feature_start = fsdp_index * feature_count
     gain_part = lax.dynamic_slice_in_dim(norm_gain, feature_start, feature_count, 0)
     hidden_part = lax.dynamic_slice_in_dim(dec_hidden, feature_start, feature_count, 1)
-    projected = lax.optimization_barrier(
-        jnp.dot(attended, w_out, preferred_element_type=jnp.float32)
-    )
+    projected = jnp.dot(attended, w_out, preferred_element_type=jnp.float32)
     if split_fsdp:
         projected = scatter_bits(projected, "fsdp", 1, levels, jnp.bfloat16)
     else:

time: 158 us -> 150 us (0.949)
  local copies, waits for them, and re-layouts: 25.5 us -> 16.8 us
  starting transfers between devices: 33.4 us -> 26 us
  waiting for transfers between devices: 41.4 us -> 47.9 us
    dot_general x0 -> x1, local copies, waits for them, and re-layouts: none -> 6.47 us  [body(): projected = jnp.dot(attended, w_out, preferred_element_type=jnp.float32)]
    ppermute x16, starting transfers between devices: 19.2 us -> 13.3 us  [exchange(): return lax.ppermute(x, axis, [(i, i ^ 1 << bit) for i in range(size)])]
    slice x8, local copies, waits for them, and re-layouts: 5.66 us -> 0.1 us  [body(): keys_here = block[0].reshape(window, heads_here, HEAD_DIM)]
    ppermute x7, waiting for transfers between devices: 6.5 us -> 11.2 us  [body(): lax.ppermute(block, 'dp', [(i, (i - shift) % dp_count) for i in range(dp_...]
    dynamic_slice x2 -> x4, local copies, waits for them, and re-layouts: 5.13 us -> 0.55 us  [scatter_bits(): keep = lax.dynamic_index_in_dim(cur, side, dim + 1, keepdims=False)]
    reshape x1 -> x0, local copies, waits for them, and re-layouts: 3.02 us -> none  [scatter_bits(): cur = cur.reshape(head + (chunks // 2, 2, width) + tail)]
    ppermute x16, waiting for transfers between devices: 34.9 us -> 36.8 us  [exchange(): return lax.ppermute(x, axis, [(i, i ^ 1 << bit) for i in range(size)])]
    dynamic_slice x1 -> x2, local copies, waits for them, and re-layouts: 1.98 us -> 0.39 us  [scatter_bits(): send = lax.dynamic_index_in_dim(cur, 1 - side, dim + 1, keepdims=False)]
  transfers between devices with their start and end apart: 23 -> 23, of which waited for: 15 -> 16; matrix products, arithmetic and copies ran while one was open for 12% -> 14% of each run, Pallas kernels for 0% -> 0%
where the time goes in v7:
time: 150 us; the launch traced here: 149 us
  waiting for transfers between devices  47.9 us (32%)
  matrix products  40.6 us (27%)
  starting transfers between devices  26 us (17%)
  local copies, waits for them, and re-layouts  16.8 us (11%)
  other arithmetic  14.2 us (9%)
  between operations  3.84 us (3%)
    ppermute x16, waiting for transfers between devices, exchange(): return lax.ppermute(x, axis, [(i, i ^ 1 << bit) for i in range(size)])  36.8 us
    ppermute x16, starting transfers between devices, exchange(): return lax.ppermute(x, axis, [(i, i ^ 1 << bit) for i in range(size)])  13.3 us
    ppermute x7, starting transfers between devices, body(): lax.ppermute(block, 'dp', [(i, (i - shift) % dp_count) for i in range(dp_...  12.7 us
    ppermute x7, waiting for transfers between devices, body(): lax.ppermute(block, 'dp', [(i, (i - shift) % dp_count) for i in range(dp_...  11.2 us
    dot_general x1, matrix products, body(): lax.dot_general(far_rows, grad_logits, contract, preferred_element_type=j...  8.36 us
    dot_general x1, matrix products, body(): jnp.dot(far_normed, far_rows, preferred_element_type=jnp.float32)  8.29 us
    dot_general x1, matrix products, body(): jnp.dot(near_normed, near_rows, preferred_element_type=jnp.float32)  8.14 us
    dot_general x1, matrix products, body(): lax.dot_general(near_rows, near_logits, contract, preferred_element_type=...  8.14 us
  transfers between devices with their start and end apart: 23, of which 16 were waited for; matrix products, arithmetic and copies ran while one was open for 14% of the time, Pallas kernels for 0%

profile of v7, /device:TPU:0, one launch (start us, length us, event | category | flops | bytes accessed | tf_op | source)
XLA Modules:
  0.0 149.4 jit_solution(14905320201686155140)
XLA Ops:
  0.7 0.8 lt.71
  1.7 0.8 fusion.71
  2.5 0.8 select_reduce_fusion.11
  3.4 0.8 select_reduce_fusion.19
  5.4 6.0 %collective-permute-start = (bf16[2,80,512]{2,1,0:T(8,128)(2,1)S(1)}, bf16[2,80,512]{2,1,0:T(8,128)(2,1)S(1)}, u32[]{:S(2)}, u32[]{:S(2)}) collective-permute-start(bf16[2,80,512]{2,1,0:T(8,128)(2,1)S(1)} %get-tuple-element.30), channel_id=1, source_target_pairs={{0,28},{4,0},{8,4},{12,8},{16,12},{20,16},{24,20},{28,24},{1,29},{... | collective-permute-start | bytes 491528 | tf_op jit(solution)/shard_map/ppermute | solution.py:157
  11.9 3.0 %collective-permute-start.3 = (bf16[2,80,512]{2,1,0:T(8,128)(2,1)S(1)}, bf16[2,80,512]{2,1,0:T(8,128)(2,1)S(1)}, u32[]{:S(2)}, u32[]{:S(2)}) collective-permute-start(bf16[2,80,512]{2,1,0:T(8,128)(2,1)S(1)} %get-tuple-element.28), channel_id=1, source_target_pairs={{0,16},{4,20},{8,24},{12,28},{16,0},{20,4},{24,8},{28,12},{1,17},{... | collective-permute-start | bytes 491528 | tf_op jit(solution)/shard_map/ppermute | solution.py:157
  15.7 2.0 %convolution_convert_fusion.1 = bf16[128,512]{1,0:T(8,128)(2,1)S(1)} fusion(bf16[128,4096]{1,0:T(8,128)(2,1)} %param.11, bf16[4096,512]{1,0:T(8,128)(2,1)S(1)} %copy-done.3), kind=kOutput, calls=%fused_computation.24 | convolution fusion | flops 536936448 | bytes 5373952 | tf_op jit(solution)/shard_map/dot_general | solution.py:148
  18.7 6.5 %copy.139 = bf16[4096,512]{1,0:T(8,128)(2,1)} copy(bf16[4096,512]{0,1:T(8,128)(2,1)} %bitcast.233) | data formatting | bytes 8388608 | tf_op jit(solution)/shard_map/dot_general | solution.py:180
  25.3 1.9 %collective-permute-start.5 = (bf16[2,80,512]{2,1,0:T(8,128)(2,1)S(1)}, bf16[2,80,512]{2,1,0:T(8,128)(2,1)S(1)}, u32[]{:S(2)}, u32[]{:S(2)}) collective-permute-start(bf16[2,80,512]{2,1,0:T(8,128)(2,1)S(1)} %get-tuple-element.26), channel_id=1, source_target_pairs={{0,8},{4,12},{8,16},{12,20},{16,24},{20,28},{24,0},{28,4},{1,9},{5... | collective-permute-start | bytes 491528 | tf_op jit(solution)/shard_map/ppermute | solution.py:157
  27.3 1.4 collective-permute-start.6
  28.9 10.4 %collective-permute-done.3 = bf16[2,80,512]{2,1,0:T(8,128)(2,1)S(1)} collective-permute-done((bf16[2,80,512]{2,1,0:T(8,128)(2,1)S(1)}, bf16[2,80,512]{2,1,0:T(8,128)(2,1)S(1)}, u32[]{:S(2)}, u32[]{:S(2)}) %collective-permute-start.3) | collective-permute-done | bytes 163872 | tf_op jit(solution)/shard_map/ppermute | solution.py:157
  39.5 0.7 collective-permute-done.4
  45.4 1.3 copy-done.2
  46.7 1.5 %fusion.112 = f32[128,2,2,1024]{3,0,2,1:T(8,128)S(1)} fusion(bf16[128,512,1,1]{0,1,3,2:T(8,128)(2,1)S(1)} %bitcast.236, bf16[2,2,1024,512]{3,2,1,0:T(8,128)(2,1)S(1)} %bitcast.224), kind=kOutput, calls=%fused_computation.241 | convolution fusion | flops 536870912 | bytes 6422528 | tf_op jit(solution)/shard_map/dot_general | solution.py:180
  48.2 1.1 dynamic-slice_bitcast_fusion
  49.3 3.0 %collective-permute-done.7 = f32[128,2,1024]{2,0,1:T(8,128)} collective-permute-done((f32[128,2,1024]{2,0,1:T(8,128)}, f32[128,2,1024]{2,0,1:T(8,128)}, u32[]{:S(2)}, u32[]{:S(2)}) %collective-permute-start.7) | collective-permute-done | bytes 1048608 | tf_op jit(solution)/shard_map/ppermute | solution.py:16
  52.3 1.4 bitcast_add_fusion
  53.7 1.0 copy-done.4
  54.8 1.6 %collective-permute-start.8 = (bf16[128,1,1024]{2,0,1:T(8,128)(2,1)S(1)}, bf16[128,1,1024]{2,0,1:T(8,128)(2,1)S(1)}, u32[]{:S(2)}, u32[]{:S(2)}) collective-permute-start(bf16[128,1,1024]{2,0,1:T(8,128)(2,1)S(1)} %dynamic-slice_convert_fusion), channel_id=1, source_target_pairs={{0,2},{1,3},{2,0},{3,1},{4,6},{5,7},{6,4},{7,5},{8,10},{9,11},{10,... | collective-permute-start | bytes 786440 | tf_op jit(solution)/shard_map/ppermute | solution.py:16
  56.3 6.8 %collective-permute-done.8 = bf16[128,1,1024]{2,0,1:T(8,128)(2,1)S(1)} collective-permute-done((bf16[128,1,1024]{2,0,1:T(8,128)(2,1)S(1)}, bf16[128,1,1024]{2,0,1:T(8,128)(2,1)S(1)}, u32[]{:S(2)}, u32[]{:S(2)}) %collective-permute-start.8) | collective-permute-done | bytes 262176 | tf_op jit(solution)/shard_map/ppermute | solution.py:16
  63.2 1.3 multiply_reduce_fusion.1
  64.6 1.1 collective-permute-done.9
  65.7 1.5 %collective-permute-start.10 = (f32[128]{0:T(128)S(1)}, f32[128]{0:T(128)S(1)}, u32[]{:S(2)}, u32[]{:S(2)}) collective-permute-start(f32[128]{0:T(128)S(1)} %add.329), channel_id=1, source_target_pairs={{0,2},{1,3},{2,0},{3,1},{4,6},{5,7},{6,4},{7,5},{8,10},{9,11},{10,... | collective-permute-start | bytes 1544 | tf_op jit(solution)/shard_map/ppermute | solution.py:16
  67.2 0.7 dynamic_slice.38
  67.9 1.3 collective-permute-done.10
  69.4 1.5 %collective-permute-done.11 = bf16[128,1,1024]{2,0,1:T(8,128)(2,1)S(1)} collective-permute-done((bf16[128,1,1024]{2,0,1:T(8,128)(2,1)S(1)}, bf16[128,1,1024]{2,0,1:T(8,128)(2,1)S(1)}, u32[]{:S(2)}, u32[]{:S(2)}) %collective-permute-start.11) | collective-permute-done | bytes 262176 | tf_op jit(solution)/shard_map/ppermute | solution.py:16
  71.5 1.6 %collective-permute-start.12 = (bf16[128,2048]{0,1:T(8,128)(2,1)S(1)}, bf16[128,2048]{0,1:T(8,128)(2,1)S(1)}, u32[]{:S(2)}, u32[]{:S(2)}) collective-permute-start(bf16[128,2048]{0,1:T(8,128)(2,1)S(1)} %bitcast.247), channel_id=1, source_target_pairs={{0,2},{1,3},{2,0},{3,1},{4,6},{5,7},{6,4},{7,5},{8,10},{9,11},{10,... | collective-permute-start | bytes 1572872 | tf_op jit(solution)/shard_map/ppermute | solution.py:16
  73.1 8.1 %fusion.6 = f32[128,4096]{1,0:T(8,128)S(1)} fusion(bf16[128,2048]{0,1:T(8,128)(2,1)S(1)} %bitcast.248, bf16[4096,4096]{1,0:T(8,128)(2,1)} %param.16, s32[]{:T(128)S(6)} %select_n.229), kind=kOutput, calls=%fused_computation.6 | convolution fusion | flops 2147483648 | bytes 19398660 | tf_op jit(solution)/shard_map/dot_general | solution.py:197
  81.2 4.3 %collective-permute-done.12 = bf16[128,2048]{0,1:T(8,128)(2,1)S(1)} collective-permute-done((bf16[128,2048]{0,1:T(8,128)(2,1)S(1)}, bf16[128,2048]{0,1:T(8,128)(2,1)S(1)}, u32[]{:S(2)}, u32[]{:S(2)}) %collective-permute-start.12) | collective-permute-done | bytes 524320 | tf_op jit(solution)/shard_map/ppermute | solution.py:16
  85.5 8.3 %fusion.111 = (f32[128]{0:T(128)S(1)}, f32[128,4096]{1,0:T(8,128)S(1)}) fusion(f32[128,4096]{1,0:T(8,128)S(1)} %fusion.6, bf16[128,2048]{0,1:T(8,128)(2,1)S(1)} %collective-permute-done.12, bf16[4096,4096]{1,0:T(8,128)(2,1)} %param.16, s32[]{:T(128)S(6)} %select_n.230), kind=kOutput, calls=%fused_computation.240 | convolution fusion | flops 2148532224 | bytes 21496324 | tf_op jit(solution)/shard_map/dot_general | solution.py:197
  93.8 0.7 select_reduce_fusion
  94.6 1.1 collective-permute-done.13
  95.8 1.6 %collective-permute-start.14 = (f32[3,128]{1,0:T(4,128)S(1)}, f32[3,128]{1,0:T(4,128)S(1)}, u32[]{:S(2)}, u32[]{:S(2)}) collective-permute-start(f32[3,128]{1,0:T(4,128)S(1)} %pad_maximum_fusion.2), channel_id=1, source_target_pairs={{0,2},{1,3},{2,0},{3,1},{4,6},{5,7},{6,4},{7,5},{8,10},{9,11},{10,... | collective-permute-start | bytes 4616 | tf_op jit(solution)/shard_map/ppermute | solution.py:16
  97.4 2.1 %collective-permute-done.14 = f32[3,128]{1,0:T(4,128)S(1)} collective-permute-done((f32[3,128]{1,0:T(4,128)S(1)}, f32[3,128]{1,0:T(4,128)S(1)}, u32[]{:S(2)}, u32[]{:S(2)}) %collective-permute-start.14) | collective-permute-done | bytes 1568 | tf_op jit(solution)/shard_map/ppermute | solution.py:16
  100.7 8.4 %fusion = f32[2048,128]{1,0:T(8,128)S(1)} fusion(bf16[128,4096]{1,0:T(8,128)(2,1)S(1)} %multiply_convert_fusion, bf16[4096,4096]{1,0:T(8,128)(2,1)} %param.16, s32[]{:T(128)S(6)} %select_n.230), kind=kOutput, calls=%fused_computation | convolution fusion | flops 2147483648 | bytes 18874372 | tf_op jit(solution)/shard_map/dot_general | solution.py:218
  109.6 1.8 %collective-permute-done.15 = f32[1,1024,128]{1,2,0:T(8,128)} collective-permute-done((f32[1,1024,128]{1,2,0:T(8,128)S(1)}, f32[1,1024,128]{1,2,0:T(8,128)}, u32[]{:S(2)}, u32[]{:S(2)}) %collective-permute-start.15) | collective-permute-done | bytes 524320 | tf_op jit(solution)/shard_map/ppermute | solution.py:16
  111.5 1.1 fusion.23
  112.6 8.1 %fusion.4 = f32[2048,128]{1,0:T(8,128)S(1)} fusion(bf16[128,4096]{1,0:T(8,128)(2,1)S(1)} %multiply_convert_fusion, bf16[4096,4096]{1,0:T(8,128)(2,1)} %param.16, s32[]{:T(128)S(6)} %select_n.229), kind=kOutput, calls=%fused_computation.4 | convolution fusion | flops 2147483648 | bytes 18874372 | tf_op jit(solution)/shard_map/dot_general | solution.py:227
  121.2 1.5 %collective-permute-start.17 = (bf16[1024,128]{0,1:T(8,128)(2,1)S(1)}, bf16[1024,128]{0,1:T(8,128)(2,1)S(1)}, u32[]{:S(2)}, u32[]{:S(2)}) collective-permute-start(bf16[1024,128]{0,1:T(8,128)(2,1)S(1)} %fusion.23), channel_id=1, source_target_pairs={{0,2},{1,3},{2,0},{3,1},{4,6},{5,7},{6,4},{7,5},{8,10},{9,11},{10,... | collective-permute-start | bytes 786440 | tf_op jit(solution)/shard_map/ppermute | solution.py:16
  123.0 6.8 %collective-permute-done.17 = bf16[1024,128]{0,1:T(8,128)(2,1)S(1)} collective-permute-done((bf16[1024,128]{0,1:T(8,128)(2,1)S(1)}, bf16[1024,128]{0,1:T(8,128)(2,1)S(1)}, u32[]{:S(2)}, u32[]{:S(2)}) %collective-permute-start.17) | collective-permute-done | bytes 262176 | tf_op jit(solution)/shard_map/ppermute | solution.py:16
  130.1 1.4 concatenate.3
  131.5 3.6 %collective-permute-done.18 = f32[1026]{0:T(1024)S(1)} collective-permute-done((f32[1026]{0:T(1024)S(1)}, f32[1026]{0:T(1024)S(1)}, u32[]{:S(2)}, u32[]{:S(2)}) %collective-permute-start.18) | collective-permute-done | bytes 4136 | tf_op jit(solution)/shard_map/ppermute | solution.py:16
  135.8 1.1 collective-permute-done.21
  136.9 1.5 %collective-permute-start.22 = (f32[128]{0:T(128)S(1)}, f32[128]{0:T(128)S(1)}, u32[]{:S(2)}, u32[]{:S(2)}) collective-permute-start(f32[128]{0:T(128)S(1)} %add.349), channel_id=1, source_target_pairs={{0,2},{1,3},{2,0},{3,1},{4,6},{5,7},{6,4},{7,5},{8,10},{9,11},{10,... | collective-permute-start | bytes 1544 | tf_op jit(solution)/shard_map/ppermute | solution.py:16
  138.8 2.9 %collective-permute-start.20 = (f32[1026]{0:T(1024)S(1)}, f32[1026]{0:T(1024)S(1)}, u32[]{:S(2)}, u32[]{:S(2)}) collective-permute-start(f32[1026]{0:T(1024)S(1)} %add.347), channel_id=1, source_target_pairs={{0,16},{4,20},{8,24},{12,28},{16,0},{20,4},{24,8},{28,12},{1,17},{... | collective-permute-start | bytes 12320 | tf_op jit(solution)/shard_map/ppermute | solution.py:16
  141.7 1.7 %collective-permute-done.20 = f32[1026]{0:T(1024)S(1)} collective-permute-done((f32[1026]{0:T(1024)S(1)}, f32[1026]{0:T(1024)S(1)}, u32[]{:S(2)}, u32[]{:S(2)}) %collective-permute-start.20) | collective-permute-done | bytes 4136 | tf_op jit(solution)/shard_map/ppermute | solution.py:16
  144.0 1.4 slice_divide_fusion
  146.7 1.6 %divide_convert_fusion = bf16[128,1024]{1,0:T(8,128)(2,1)} fusion(f32[1024,128]{0,1:T(8,128)S(1)} %get-tuple-element.20, f32[128,1024]{1,0:T(8,128)S(1)} %get-tuple-element.23, f32[]{:T(128)} %bitcast.70, f32[128]{0:T(128)S(1)} %add_multiply_fusion, f32[1024]{0:T(1024)S(1)} %dynamic_slice.38, f32[128]{0:T(128)S(1)} %add_rsqrt_fusion), kind=kLoop, calls=%fused_computation.41 | loop fusion | flops 917504 | bytes 1315844 | tf_op jit(solution)/shard_map/convert_element_type | solution.py:249
  (135 shorter events, 14.4 us)
Async XLA Ops:
  0.6 4.1 %copy-start = (bf16[2,192,512]{2,1,0:T(8,128)(2,1)S(1)}, bf16[2,192,512]{2,1,0:T(8,128)(2,1)}, u32[]{:S(2)}) copy-start(bf16[2,192,512]{2,1,0:T(8,128)(2,1)} %param.13) | copy-start | bytes 1179652
  4.7 10.9 %copy-start.6 = (s32[128]{0:T(128)S(1)}, s32[128]{0:T(128)}, u32[]{:S(2)}) copy-start(s32[128]{0:T(128)} %param.18) | copy-start | bytes 1540
  4.7 11.0 %copy-start.3 = (bf16[4096,512]{1,0:T(8,128)(2,1)S(1)}, bf16[4096,512]{1,0:T(8,128)(2,1)}, u32[]{:S(2)}) copy-start(bf16[4096,512]{1,0:T(8,128)(2,1)} %param.12) | copy-start | bytes 12582916
  5.4 19.9 %collective-permute-start = (bf16[2,80,512]{2,1,0:T(8,128)(2,1)S(1)}, bf16[2,80,512]{2,1,0:T(8,128)(2,1)S(1)}, u32[]{:S(2)}, u32[]{:S(2)}) collective-permute-start(bf16[2,80,512]{2,1,0:T(8,128)(2,1)S(1)} %get-tuple-element.30), channel_id=1, source_target_pairs={{0,28},{4,0},{8,4},{12,8},{16,12},{20,16},{24,20},{28,24},{1,29},{... | collective-permute-start | bytes 491528 | tf_op jit(solution)/shard_map/ppermute | solution.py:157
  11.4 15.9 %collective-permute-start.1 = (bf16[2,80,512]{2,1,0:T(8,128)(2,1)S(1)}, bf16[2,80,512]{2,1,0:T(8,128)(2,1)S(1)}, u32[]{:S(2)}, u32[]{:S(2)}) collective-permute-start(bf16[2,80,512]{2,1,0:T(8,128)(2,1)S(1)} %get-tuple-element.24), channel_id=1, source_target_pairs={{0,24},{4,28},{8,0},{12,4},{16,8},{20,12},{24,16},{28,20},{1,25},{... | collective-permute-start | bytes 491528 | tf_op jit(solution)/shard_map/ppermute | solution.py:157
  11.9 16.9 %collective-permute-start.2 = (bf16[2,80,512]{2,1,0:T(8,128)(2,1)S(1)}, bf16[2,80,512]{2,1,0:T(8,128)(2,1)S(1)}, u32[]{:S(2)}, u32[]{:S(2)}) collective-permute-start(bf16[2,80,512]{2,1,0:T(8,128)(2,1)S(1)} %get-tuple-element.29), channel_id=1, source_target_pairs={{0,20},{4,24},{8,28},{12,0},{16,4},{20,8},{24,12},{28,16},{1,21},{... | collective-permute-start | bytes 491528 | tf_op jit(solution)/shard_map/ppermute | solution.py:157
  11.9 27.5 %collective-permute-start.3 = (bf16[2,80,512]{2,1,0:T(8,128)(2,1)S(1)}, bf16[2,80,512]{2,1,0:T(8,128)(2,1)S(1)}, u32[]{:S(2)}, u32[]{:S(2)}) collective-permute-start(bf16[2,80,512]{2,1,0:T(8,128)(2,1)S(1)} %get-tuple-element.28), channel_id=1, source_target_pairs={{0,16},{4,20},{8,24},{12,28},{16,0},{20,4},{24,8},{28,12},{1,17},{... | collective-permute-start | bytes 491528 | tf_op jit(solution)/shard_map/ppermute | solution.py:157
  14.9 25.4 %collective-permute-start.4 = (bf16[2,80,512]{2,1,0:T(8,128)(2,1)S(1)}, bf16[2,80,512]{2,1,0:T(8,128)(2,1)S(1)}, u32[]{:S(2)}, u32[]{:S(2)}) collective-permute-start(bf16[2,80,512]{2,1,0:T(8,128)(2,1)S(1)} %get-tuple-element.27), channel_id=1, source_target_pairs={{0,12},{4,16},{8,20},{12,24},{16,28},{20,0},{24,4},{28,8},{1,13},{... | collective-permute-start | bytes 491528 | tf_op jit(solution)/shard_map/ppermute | solution.py:157
  25.3 15.1 %collective-permute-start.5 = (bf16[2,80,512]{2,1,0:T(8,128)(2,1)S(1)}, bf16[2,80,512]{2,1,0:T(8,128)(2,1)S(1)}, u32[]{:S(2)}, u32[]{:S(2)}) collective-permute-start(bf16[2,80,512]{2,1,0:T(8,128)(2,1)S(1)} %get-tuple-element.26), channel_id=1, source_target_pairs={{0,8},{4,12},{8,16},{12,20},{16,24},{20,28},{24,0},{28,4},{1,9},{5... | collective-permute-start | bytes 491528 | tf_op jit(solution)/shard_map/ppermute | solution.py:157
  27.3 13.2 %collective-permute-start.6 = (bf16[2,80,512]{2,1,0:T(8,128)(2,1)S(1)}, bf16[2,80,512]{2,1,0:T(8,128)(2,1)S(1)}, u32[]{:S(2)}, u32[]{:S(2)}) collective-permute-start(bf16[2,80,512]{2,1,0:T(8,128)(2,1)S(1)} %get-tuple-element.25), channel_id=1, source_target_pairs={{0,4},{4,8},{8,12},{12,16},{16,20},{20,24},{24,28},{28,0},{1,5},{5... | collective-permute-start | bytes 491528 | tf_op jit(solution)/shard_map/ppermute | solution.py:157
  44.5 2.2 %copy-start.2 = (bf16[4096,512]{1,0:T(8,128)(2,1)S(1)}, bf16[4096,512]{1,0:T(8,128)(2,1)}, u32[]{:S(2)}) copy-start(bf16[4096,512]{1,0:T(8,128)(2,1)} %copy.139) | copy-start | bytes 12582916
  49.3 3.0 %collective-permute-start.7 = (f32[128,2,1024]{2,0,1:T(8,128)}, f32[128,2,1024]{2,0,1:T(8,128)}, u32[]{:S(2)}, u32[]{:S(2)}) collective-permute-start(f32[128,2,1024]{2,0,1:T(8,128)} %dynamic-slice_bitcast_fusion), channel_id=1, source_target_pairs={{0,1},{1,0},{2,3},{3,2},{4,5},{5,4},{6,7},{7,6},{8,9},{9,8},{10,11... | collective-permute-start | bytes 3145736 | tf_op jit(solution)/shard_map/ppermute | solution.py:16
  53.7 1.0 copy-start.4
  54.8 8.4 %collective-permute-start.8 = (bf16[128,1,1024]{2,0,1:T(8,128)(2,1)S(1)}, bf16[128,1,1024]{2,0,1:T(8,128)(2,1)S(1)}, u32[]{:S(2)}, u32[]{:S(2)}) collective-permute-start(bf16[128,1,1024]{2,0,1:T(8,128)(2,1)S(1)} %dynamic-slice_convert_fusion), channel_id=1, source_target_pairs={{0,2},{1,3},{2,0},{3,1},{4,6},{5,7},{6,4},{7,5},{8,10},{9,11},{10,... | collective-permute-start | bytes 786440 | tf_op jit(solution)/shard_map/ppermute | solution.py:16
  64.5 1.2 collective-permute-start.9
  65.7 3.5 %collective-permute-start.10 = (f32[128]{0:T(128)S(1)}, f32[128]{0:T(128)S(1)}, u32[]{:S(2)}, u32[]{:S(2)}) collective-permute-start(f32[128]{0:T(128)S(1)} %add.329), channel_id=1, source_target_pairs={{0,2},{1,3},{2,0},{3,1},{4,6},{5,7},{6,4},{7,5},{8,10},{9,11},{10,... | collective-permute-start | bytes 1544 | tf_op jit(solution)/shard_map/ppermute | solution.py:16
  69.2 3.8 %copy-start.7 = (s32[128]{0:T(128)S(1)}, s32[128]{0:T(128)}, u32[]{:S(2)}) copy-start(s32[128]{0:T(128)} %param.20) | copy-start | bytes 1540
  69.3 1.6 %collective-permute-start.11 = (bf16[128,1,1024]{2,0,1:T(8,128)(2,1)S(1)}, bf16[128,1,1024]{2,0,1:T(8,128)(2,1)S(1)}, u32[]{:S(2)}, u32[]{:S(2)}) collective-permute-start(bf16[128,1,1024]{2,0,1:T(8,128)(2,1)S(1)} %fusion.40), channel_id=1, source_target_pairs={{0,1},{1,0},{2,3},{3,2},{4,5},{5,4},{6,7},{7,6},{8,9},{9,8},{10,11... | collective-permute-start | bytes 786440 | tf_op jit(solution)/shard_map/ppermute | solution.py:16
  71.5 14.0 %collective-permute-start.12 = (bf16[128,2048]{0,1:T(8,128)(2,1)S(1)}, bf16[128,2048]{0,1:T(8,128)(2,1)S(1)}, u32[]{:S(2)}, u32[]{:S(2)}) collective-permute-start(bf16[128,2048]{0,1:T(8,128)(2,1)S(1)} %bitcast.247), channel_id=1, source_target_pairs={{0,2},{1,3},{2,0},{3,1},{4,6},{5,7},{6,4},{7,5},{8,10},{9,11},{10,... | collective-permute-start | bytes 1572872 | tf_op jit(solution)/shard_map/ppermute | solution.py:16
  93.8 3.6 %copy-start.5 = (s32[128]{0:T(128)S(1)}, s32[128]{0:T(128)}, u32[]{:S(2)}) copy-start(s32[128]{0:T(128)} %param.21) | copy-start | bytes 1540
  94.5 1.2 collective-permute-start.13
  95.8 3.7 %collective-permute-start.14 = (f32[3,128]{1,0:T(4,128)S(1)}, f32[3,128]{1,0:T(4,128)S(1)}, u32[]{:S(2)}, u32[]{:S(2)}) collective-permute-start(f32[3,128]{1,0:T(4,128)S(1)} %pad_maximum_fusion.2), channel_id=1, source_target_pairs={{0,2},{1,3},{2,0},{3,1},{4,6},{5,7},{6,4},{7,5},{8,10},{9,11},{10,... | collective-permute-start | bytes 4616 | tf_op jit(solution)/shard_map/ppermute | solution.py:16
  109.4 2.1 %collective-permute-start.15 = (f32[1,1024,128]{1,2,0:T(8,128)S(1)}, f32[1,1024,128]{1,2,0:T(8,128)}, u32[]{:S(2)}, u32[]{:S(2)}) collective-permute-start(f32[1,1024,128]{1,2,0:T(8,128)S(1)} %bitcast.250), channel_id=1, source_target_pairs={{0,1},{1,0},{2,3},{3,2},{4,5},{5,4},{6,7},{7,6},{8,9},{9,8},{10,11... | collective-permute-start | bytes 1572872 | tf_op jit(solution)/shard_map/ppermute | solution.py:16
  121.0 8.8 %collective-permute-start.16 = (f32[1,1024,128]{1,2,0:T(8,128)S(1)}, f32[1,1024,128]{1,2,0:T(8,128)S(1)}, u32[]{:S(2)}, u32[]{:S(2)}) collective-permute-start(f32[1,1024,128]{1,2,0:T(8,128)S(1)} %bitcast.249), channel_id=1, source_target_pairs={{0,1},{1,0},{2,3},{3,2},{4,5},{5,4},{6,7},{7,6},{8,9},{9,8},{10,11... | collective-permute-start | bytes 1572872 | tf_op jit(solution)/shard_map/ppermute | solution.py:16
  121.2 8.6 %collective-permute-start.17 = (bf16[1024,128]{0,1:T(8,128)(2,1)S(1)}, bf16[1024,128]{0,1:T(8,128)(2,1)S(1)}, u32[]{:S(2)}, u32[]{:S(2)}) collective-permute-start(bf16[1024,128]{0,1:T(8,128)(2,1)S(1)} %fusion.23), channel_id=1, source_target_pairs={{0,2},{1,3},{2,0},{3,1},{4,6},{5,7},{6,4},{7,5},{8,10},{9,11},{10,... | collective-permute-start | bytes 786440 | tf_op jit(solution)/shard_map/ppermute | solution.py:16
  122.8 25.5 %copy-start.1 = (bf16[2,192,512]{2,1,0:T(8,128)(2,1)S(1)}, bf16[2,192,512]{2,1,0:T(8,128)(2,1)}, u32[]{:S(2)}) copy-start(bf16[2,192,512]{2,1,0:T(8,128)(2,1)} %param.13) | copy-start | bytes 1179652
  131.5 3.7 %collective-permute-start.18 = (f32[1026]{0:T(1024)S(1)}, f32[1026]{0:T(1024)S(1)}, u32[]{:S(2)}, u32[]{:S(2)}) collective-permute-start(f32[1026]{0:T(1024)S(1)} %concatenate.3), channel_id=1, source_target_pairs={{0,4},{4,0},{8,12},{12,8},{16,20},{20,16},{24,28},{28,24},{1,5},{5... | collective-permute-start | bytes 12320 | tf_op jit(solution)/shard_map/ppermute | solution.py:16
  135.2 3.7 %collective-permute-start.19 = (f32[1026]{0:T(1024)S(1)}, f32[1026]{0:T(1024)S(1)}, u32[]{:S(2)}, u32[]{:S(2)}) collective-permute-start(f32[1026]{0:T(1024)S(1)} %add.346), channel_id=1, source_target_pairs={{0,8},{4,12},{8,0},{12,4},{16,24},{20,28},{24,16},{28,20},{1,9},{5... | collective-permute-start | bytes 12320 | tf_op jit(solution)/shard_map/ppermute | solution.py:16
  135.8 1.1 collective-permute-start.21
  136.9 4.8 %collective-permute-start.22 = (f32[128]{0:T(128)S(1)}, f32[128]{0:T(128)S(1)}, u32[]{:S(2)}, u32[]{:S(2)}) collective-permute-start(f32[128]{0:T(128)S(1)} %add.349), channel_id=1, source_target_pairs={{0,2},{1,3},{2,0},{3,1},{4,6},{5,7},{6,4},{7,5},{8,10},{9,11},{10,... | collective-permute-start | bytes 1544 | tf_op jit(solution)/shard_map/ppermute | solution.py:16
  138.8 4.5 %collective-permute-start.20 = (f32[1026]{0:T(1024)S(1)}, f32[1026]{0:T(1024)S(1)}, u32[]{:S(2)}, u32[]{:S(2)}) collective-permute-start(f32[1026]{0:T(1024)S(1)} %add.347), channel_id=1, source_target_pairs={{0,16},{4,20},{8,24},{12,28},{16,0},{20,4},{24,8},{28,12},{1,17},{... | collective-permute-start | bytes 12320 | tf_op jit(solution)/shard_map/ppermute | solution.py:16

commit v8 on v7

--- a/solution.py
+++ b/solution.py
@@ -192,8 +192,9 @@
         top_side = (fsdp_index >> (levels - 1)) & 1
         near_rows = lax.dynamic_slice_in_dim(w_vocab, top_side * half, half, 0)
         far_rows = lax.dynamic_slice_in_dim(w_vocab, (1 - top_side) * half, half, 0)
+        crossed = exchange(normed_part, "fsdp", levels - 1)
         near_normed = gather_bits(normed_part, "fsdp", 1, levels - 1)
-        far_normed = exchange(near_normed, "fsdp", levels - 1)
+        far_normed = gather_bits(crossed, "fsdp", 1, levels - 1)
         logits = jnp.dot(near_normed, near_rows, preferred_element_type=jnp.float32) + jnp.dot(
             far_normed, far_rows, preferred_element_type=jnp.float32
         )

time: 150 us -> 151 us (level)
    ppermute x16 -> x17, waiting for transfers between devices: 36.8 us -> 37.3 us  [exchange(): return lax.ppermute(x, axis, [(i, i ^ 1 << bit) for i in range(size)])]
    ppermute x16 -> x17, starting transfers between devices: 13.3 us -> 13.4 us  [exchange(): return lax.ppermute(x, axis, [(i, i ^ 1 << bit) for i in range(size)])]
  transfers between devices with their start and end apart: 23 -> 24, of which waited for: 16 -> 16; matrix products, arithmetic and copies ran while one was open for 14% -> 8% of each run, Pallas kernels for 0% -> 0%
where the time goes in v8:
time: 151 us
  waiting for transfers between devices  48.5 us (32%)
  matrix products  40.4 us (27%)
  starting transfers between devices  26.2 us (17%)
  local copies, waits for them, and re-layouts  17.1 us (11%)
  other arithmetic  14.7 us (10%)
  between operations  3.88 us (3%)
    ppermute x17, waiting for transfers between devices, exchange(): return lax.ppermute(x, axis, [(i, i ^ 1 << bit) for i in range(size)])  37.3 us
    ppermute x17, starting transfers between devices, exchange(): return lax.ppermute(x, axis, [(i, i ^ 1 << bit) for i in range(size)])  13.4 us
    ppermute x7, starting transfers between devices, body(): lax.ppermute(block, 'dp', [(i, (i - shift) % dp_count) for i in range(dp_...  12.7 us
    ppermute x7, waiting for transfers between devices, body(): lax.ppermute(block, 'dp', [(i, (i - shift) % dp_count) for i in range(dp_...  11.2 us
    dot_general x1, matrix products, body(): jnp.dot(near_normed, near_rows, preferred_element_type=jnp.float32)  8.29 us
    dot_general x1, matrix products, body(): jnp.dot(far_normed, far_rows, preferred_element_type=jnp.float32)  8.15 us
    dot_general x1, matrix products, body(): lax.dot_general(far_rows, grad_logits, contract, preferred_element_type=j...  8.14 us
    dot_general x1, matrix products, body(): lax.dot_general(near_rows, near_logits, contract, preferred_element_type=...  8.13 us
  transfers between devices with their start and end apart: 24, of which 16 were waited for; matrix products, arithmetic and copies ran while one was open for 8% of the time, Pallas kernels for 0%

profile of v8, /device:TPU:0, one launch (start us, length us, event | category | flops | bytes accessed | tf_op | source)
XLA Modules:
  0.0 150.7 jit_solution(7769542592285053693)
XLA Ops:
  0.7 0.8 lt.71
  1.7 0.8 fusion.70
  2.5 0.8 select_reduce_fusion.11
  3.4 0.8 select_reduce_fusion.19
  5.4 6.0 %collective-permute-start = (bf16[2,80,512]{2,1,0:T(8,128)(2,1)S(1)}, bf16[2,80,512]{2,1,0:T(8,128)(2,1)S(1)}, u32[]{:S(2)}, u32[]{:S(2)}) collective-permute-start(bf16[2,80,512]{2,1,0:T(8,128)(2,1)S(1)} %get-tuple-element.30), channel_id=1, source_target_pairs={{0,28},{4,0},{8,4},{12,8},{16,12},{20,16},{24,20},{28,24},{1,29},{... | collective-permute-start | bytes 491528 | tf_op jit(solution)/shard_map/ppermute | solution.py:157
  11.9 3.0 %collective-permute-start.3 = (bf16[2,80,512]{2,1,0:T(8,128)(2,1)S(1)}, bf16[2,80,512]{2,1,0:T(8,128)(2,1)S(1)}, u32[]{:S(2)}, u32[]{:S(2)}) collective-permute-start(bf16[2,80,512]{2,1,0:T(8,128)(2,1)S(1)} %get-tuple-element.28), channel_id=1, source_target_pairs={{0,16},{4,20},{8,24},{12,28},{16,0},{20,4},{24,8},{28,12},{1,17},{... | collective-permute-start | bytes 491528 | tf_op jit(solution)/shard_map/ppermute | solution.py:157
  15.7 2.0 %convolution_convert_fusion.1 = bf16[128,512]{1,0:T(8,128)(2,1)S(1)} fusion(bf16[128,4096]{1,0:T(8,128)(2,1)} %param.11, bf16[4096,512]{1,0:T(8,128)(2,1)S(1)} %copy-done.3), kind=kOutput, calls=%fused_computation.24 | convolution fusion | flops 536936448 | bytes 5373952 | tf_op jit(solution)/shard_map/dot_general | solution.py:148
  18.7 6.5 %copy.141 = bf16[4096,512]{1,0:T(8,128)(2,1)} copy(bf16[4096,512]{0,1:T(8,128)(2,1)} %bitcast.241) | data formatting | bytes 8388608 | tf_op jit(solution)/shard_map/dot_general | solution.py:180
  25.3 1.9 %collective-permute-start.5 = (bf16[2,80,512]{2,1,0:T(8,128)(2,1)S(1)}, bf16[2,80,512]{2,1,0:T(8,128)(2,1)S(1)}, u32[]{:S(2)}, u32[]{:S(2)}) collective-permute-start(bf16[2,80,512]{2,1,0:T(8,128)(2,1)S(1)} %get-tuple-element.26), channel_id=1, source_target_pairs={{0,8},{4,12},{8,16},{12,20},{16,24},{20,28},{24,0},{28,4},{1,9},{5... | collective-permute-start | bytes 491528 | tf_op jit(solution)/shard_map/ppermute | solution.py:157
  27.3 1.4 collective-permute-start.6
  28.9 10.4 %collective-permute-done.3 = bf16[2,80,512]{2,1,0:T(8,128)(2,1)S(1)} collective-permute-done((bf16[2,80,512]{2,1,0:T(8,128)(2,1)S(1)}, bf16[2,80,512]{2,1,0:T(8,128)(2,1)S(1)}, u32[]{:S(2)}, u32[]{:S(2)}) %collective-permute-start.3) | collective-permute-done | bytes 163872 | tf_op jit(solution)/shard_map/ppermute | solution.py:157
  39.5 0.7 collective-permute-done.4
  45.4 1.3 copy-done.2
  46.7 1.5 %fusion.111 = f32[128,2,2,1024]{3,0,2,1:T(8,128)S(1)} fusion(bf16[128,512,1,1]{0,1,3,2:T(8,128)(2,1)S(1)} %bitcast.244, bf16[2,2,1024,512]{3,2,1,0:T(8,128)(2,1)S(1)} %bitcast.232), kind=kOutput, calls=%fused_computation.243 | convolution fusion | flops 536870912 | bytes 6422528 | tf_op jit(solution)/shard_map/dot_general | solution.py:180
  48.2 1.1 dynamic-slice_bitcast_fusion
  49.3 3.0 %collective-permute-done.7 = f32[128,2,1024]{2,0,1:T(8,128)} collective-permute-done((f32[128,2,1024]{2,0,1:T(8,128)}, f32[128,2,1024]{2,0,1:T(8,128)}, u32[]{:S(2)}, u32[]{:S(2)}) %collective-permute-start.7) | collective-permute-done | bytes 1048608 | tf_op jit(solution)/shard_map/ppermute | solution.py:16
  52.3 1.4 bitcast_add_fusion
  53.7 1.0 copy-done.4
  54.8 1.6 %collective-permute-start.8 = (bf16[128,1,1024]{2,0,1:T(8,128)(2,1)S(1)}, bf16[128,1,1024]{2,0,1:T(8,128)(2,1)S(1)}, u32[]{:S(2)}, u32[]{:S(2)}) collective-permute-start(bf16[128,1,1024]{2,0,1:T(8,128)(2,1)S(1)} %dynamic-slice_convert_fusion), channel_id=1, source_target_pairs={{0,2},{1,3},{2,0},{3,1},{4,6},{5,7},{6,4},{7,5},{8,10},{9,11},{10,... | collective-permute-start | bytes 786440 | tf_op jit(solution)/shard_map/ppermute | solution.py:16
  56.3 6.8 %collective-permute-done.8 = bf16[128,1,1024]{2,0,1:T(8,128)(2,1)S(1)} collective-permute-done((bf16[128,1,1024]{2,0,1:T(8,128)(2,1)S(1)}, bf16[128,1,1024]{2,0,1:T(8,128)(2,1)S(1)}, u32[]{:S(2)}, u32[]{:S(2)}) %collective-permute-start.8) | collective-permute-done | bytes 262176 | tf_op jit(solution)/shard_map/ppermute | solution.py:16
  63.2 1.3 multiply_reduce_fusion.1
  64.6 1.1 collective-permute-done.9
  65.7 1.5 %collective-permute-start.10 = (f32[128]{0:T(128)S(1)}, f32[128]{0:T(128)S(1)}, u32[]{:S(2)}, u32[]{:S(2)}) collective-permute-start(f32[128]{0:T(128)S(1)} %add.329), channel_id=1, source_target_pairs={{0,2},{1,3},{2,0},{3,1},{4,6},{5,7},{6,4},{7,5},{8,10},{9,11},{10,... | collective-permute-start | bytes 1544 | tf_op jit(solution)/shard_map/ppermute | solution.py:16
  67.9 1.3 collective-permute-done.10
  69.3 1.6 %collective-permute-start.12 = (bf16[128,1024]{1,0:T(8,128)(2,1)S(1)}, bf16[128,1024]{1,0:T(8,128)(2,1)S(1)}, u32[]{:S(2)}, u32[]{:S(2)}) collective-permute-start(bf16[128,1024]{1,0:T(8,128)(2,1)S(1)} %multiply_convert_fusion.1), channel_id=1, source_target_pairs={{0,2},{1,3},{2,0},{3,1},{4,6},{5,7},{6,4},{7,5},{8,10},{9,11},{10,... | collective-permute-start | bytes 786440 | tf_op jit(solution)/shard_map/ppermute | solution.py:16
  71.2 5.5 %collective-permute-done.12 = bf16[128,1024]{1,0:T(8,128)(2,1)S(1)} collective-permute-done((bf16[128,1024]{1,0:T(8,128)(2,1)S(1)}, bf16[128,1024]{1,0:T(8,128)(2,1)S(1)}, u32[]{:S(2)}, u32[]{:S(2)}) %collective-permute-start.12) | collective-permute-done | bytes 262176 | tf_op jit(solution)/shard_map/ppermute | solution.py:16
  77.2 1.0 collective-permute-done.13
  78.6 8.1 %fusion.2 = f32[128,4096]{1,0:T(8,128)S(1)} fusion(bf16[128,2048]{0,1:T(8,128)(2,1)S(1)} %bitcast.258, bf16[4096,4096]{1,0:T(8,128)(2,1)} %param.16, s32[]{:T(128)S(6)} %select_n.240), kind=kOutput, calls=%fused_computation.2 | convolution fusion | flops 2147483648 | bytes 19398660 | tf_op jit(solution)/shard_map/dot_general | solution.py:198
  86.8 8.3 %fusion.110 = (f32[128]{0:T(128)S(1)}, f32[128,4096]{1,0:T(8,128)S(1)}) fusion(f32[128,4096]{1,0:T(8,128)S(1)} %fusion.2, bf16[128,2048]{0,1:T(8,128)(2,1)S(1)} %bitcast.255, bf16[4096,4096]{1,0:T(8,128)(2,1)} %param.16, s32[]{:T(128)S(6)} %select_n.237), kind=kOutput, calls=%fused_computation.242 | convolution fusion | flops 2148532224 | bytes 21496324 | tf_op jit(solution)/shard_map/dot_general | solution.py:198
  95.1 0.7 select_reduce_fusion
  96.0 1.0 collective-permute-done.14
  97.0 1.6 %collective-permute-start.15 = (f32[3,128]{1,0:T(4,128)S(1)}, f32[3,128]{1,0:T(4,128)S(1)}, u32[]{:S(2)}, u32[]{:S(2)}) collective-permute-start(f32[3,128]{1,0:T(4,128)S(1)} %pad_maximum_fusion.3), channel_id=1, source_target_pairs={{0,2},{1,3},{2,0},{3,1},{4,6},{5,7},{6,4},{7,5},{8,10},{9,11},{10,... | collective-permute-start | bytes 4616 | tf_op jit(solution)/shard_map/ppermute | solution.py:16
  98.6 2.1 %collective-permute-done.15 = f32[3,128]{1,0:T(4,128)S(1)} collective-permute-done((f32[3,128]{1,0:T(4,128)S(1)}, f32[3,128]{1,0:T(4,128)S(1)}, u32[]{:S(2)}, u32[]{:S(2)}) %collective-permute-start.15) | collective-permute-done | bytes 1568 | tf_op jit(solution)/shard_map/ppermute | solution.py:16
  101.3 0.9 multiply_convert_fusion
  102.2 8.1 %fusion = f32[2048,128]{1,0:T(8,128)S(1)} fusion(bf16[128,4096]{1,0:T(8,128)(2,1)S(1)} %multiply_convert_fusion, bf16[4096,4096]{1,0:T(8,128)(2,1)} %param.16, s32[]{:T(128)S(6)} %select_n.240), kind=kOutput, calls=%fused_computation | convolution fusion | flops 2147483648 | bytes 18874372 | tf_op jit(solution)/shard_map/dot_general | solution.py:219
  110.9 1.8 %collective-permute-done.16 = f32[1,1024,128]{1,2,0:T(8,128)} collective-permute-done((f32[1,1024,128]{1,2,0:T(8,128)S(1)}, f32[1,1024,128]{1,2,0:T(8,128)}, u32[]{:S(2)}, u32[]{:S(2)}) %collective-permute-start.16) | collective-permute-done | bytes 524320 | tf_op jit(solution)/shard_map/ppermute | solution.py:16
  112.7 1.1 fusion.23
  113.9 8.1 %fusion.4 = f32[2048,128]{1,0:T(8,128)S(1)} fusion(bf16[128,4096]{1,0:T(8,128)(2,1)S(1)} %multiply_convert_fusion, bf16[4096,4096]{1,0:T(8,128)(2,1)} %param.16, s32[]{:T(128)S(6)} %select_n.237), kind=kOutput, calls=%fused_computation.4 | convolution fusion | flops 2147483648 | bytes 18874372 | tf_op jit(solution)/shard_map/dot_general | solution.py:228
  122.5 1.5 %collective-permute-start.18 = (bf16[1024,128]{0,1:T(8,128)(2,1)S(1)}, bf16[1024,128]{0,1:T(8,128)(2,1)S(1)}, u32[]{:S(2)}, u32[]{:S(2)}) collective-permute-start(bf16[1024,128]{0,1:T(8,128)(2,1)S(1)} %fusion.23), channel_id=1, source_target_pairs={{0,2},{1,3},{2,0},{3,1},{4,6},{5,7},{6,4},{7,5},{8,10},{9,11},{10,... | collective-permute-start | bytes 786440 | tf_op jit(solution)/shard_map/ppermute | solution.py:16
  124.2 6.8 %collective-permute-done.18 = bf16[1024,128]{0,1:T(8,128)(2,1)S(1)} collective-permute-done((bf16[1024,128]{0,1:T(8,128)(2,1)S(1)}, bf16[1024,128]{0,1:T(8,128)(2,1)S(1)}, u32[]{:S(2)}, u32[]{:S(2)}) %collective-permute-start.18) | collective-permute-done | bytes 262176 | tf_op jit(solution)/shard_map/ppermute | solution.py:16
  131.4 1.4 concatenate.3
  132.8 3.6 %collective-permute-done.19 = f32[1026]{0:T(1024)S(1)} collective-permute-done((f32[1026]{0:T(1024)S(1)}, f32[1026]{0:T(1024)S(1)}, u32[]{:S(2)}, u32[]{:S(2)}) %collective-permute-start.19) | collective-permute-done | bytes 4136 | tf_op jit(solution)/shard_map/ppermute | solution.py:16
  137.1 1.1 collective-permute-done.22
  138.2 1.5 %collective-permute-start.23 = (f32[128]{0:T(128)S(1)}, f32[128]{0:T(128)S(1)}, u32[]{:S(2)}, u32[]{:S(2)}) collective-permute-start(f32[128]{0:T(128)S(1)} %add.349), channel_id=1, source_target_pairs={{0,2},{1,3},{2,0},{3,1},{4,6},{5,7},{6,4},{7,5},{8,10},{9,11},{10,... | collective-permute-start | bytes 1544 | tf_op jit(solution)/shard_map/ppermute | solution.py:16
  140.1 2.9 %collective-permute-start.21 = (f32[1026]{0:T(1024)S(1)}, f32[1026]{0:T(1024)S(1)}, u32[]{:S(2)}, u32[]{:S(2)}) collective-permute-start(f32[1026]{0:T(1024)S(1)} %add.347), channel_id=1, source_target_pairs={{0,16},{4,20},{8,24},{12,28},{16,0},{20,4},{24,8},{28,12},{1,17},{... | collective-permute-start | bytes 12320 | tf_op jit(solution)/shard_map/ppermute | solution.py:16
  142.9 1.7 %collective-permute-done.21 = f32[1026]{0:T(1024)S(1)} collective-permute-done((f32[1026]{0:T(1024)S(1)}, f32[1026]{0:T(1024)S(1)}, u32[]{:S(2)}, u32[]{:S(2)}) %collective-permute-start.21) | collective-permute-done | bytes 4136 | tf_op jit(solution)/shard_map/ppermute | solution.py:16
  145.2 1.4 slice_divide_fusion
  148.0 1.6 %divide_convert_fusion = bf16[128,1024]{1,0:T(8,128)(2,1)} fusion(f32[1024,128]{0,1:T(8,128)S(1)} %get-tuple-element.20, f32[128,1024]{1,0:T(8,128)S(1)} %get-tuple-element.23, f32[]{:T(128)} %bitcast.74, f32[128]{0:T(128)S(1)} %add_multiply_fusion, f32[1024]{0:T(1024)S(1)} %dynamic_slice.38, f32[128]{0:T(128)S(1)} %add_rsqrt_fusion), kind=kLoop, calls=%fused_computation.42 | loop fusion | flops 917504 | bytes 1315844 | tf_op jit(solution)/shard_map/convert_element_type | solution.py:250
  (141 shorter events, 15.1 us)
Async XLA Ops:
  0.6 4.1 %copy-start = (bf16[2,192,512]{2,1,0:T(8,128)(2,1)S(1)}, bf16[2,192,512]{2,1,0:T(8,128)(2,1)}, u32[]{:S(2)}) copy-start(bf16[2,192,512]{2,1,0:T(8,128)(2,1)} %param.13) | copy-start | bytes 1179652
  4.7 10.9 %copy-start.6 = (s32[128]{0:T(128)S(1)}, s32[128]{0:T(128)}, u32[]{:S(2)}) copy-start(s32[128]{0:T(128)} %param.18) | copy-start | bytes 1540
  4.7 11.0 %copy-start.3 = (bf16[4096,512]{1,0:T(8,128)(2,1)S(1)}, bf16[4096,512]{1,0:T(8,128)(2,1)}, u32[]{:S(2)}) copy-start(bf16[4096,512]{1,0:T(8,128)(2,1)} %param.12) | copy-start | bytes 12582916
  5.4 19.9 %collective-permute-start = (bf16[2,80,512]{2,1,0:T(8,128)(2,1)S(1)}, bf16[2,80,512]{2,1,0:T(8,128)(2,1)S(1)}, u32[]{:S(2)}, u32[]{:S(2)}) collective-permute-start(bf16[2,80,512]{2,1,0:T(8,128)(2,1)S(1)} %get-tuple-element.30), channel_id=1, source_target_pairs={{0,28},{4,0},{8,4},{12,8},{16,12},{20,16},{24,20},{28,24},{1,29},{... | collective-permute-start | bytes 491528 | tf_op jit(solution)/shard_map/ppermute | solution.py:157
  11.4 15.9 %collective-permute-start.1 = (bf16[2,80,512]{2,1,0:T(8,128)(2,1)S(1)}, bf16[2,80,512]{2,1,0:T(8,128)(2,1)S(1)}, u32[]{:S(2)}, u32[]{:S(2)}) collective-permute-start(bf16[2,80,512]{2,1,0:T(8,128)(2,1)S(1)} %get-tuple-element.24), channel_id=1, source_target_pairs={{0,24},{4,28},{8,0},{12,4},{16,8},{20,12},{24,16},{28,20},{1,25},{... | collective-permute-start | bytes 491528 | tf_op jit(solution)/shard_map/ppermute | solution.py:157
  11.9 16.9 %collective-permute-start.2 = (bf16[2,80,512]{2,1,0:T(8,128)(2,1)S(1)}, bf16[2,80,512]{2,1,0:T(8,128)(2,1)S(1)}, u32[]{:S(2)}, u32[]{:S(2)}) collective-permute-start(bf16[2,80,512]{2,1,0:T(8,128)(2,1)S(1)} %get-tuple-element.29), channel_id=1, source_target_pairs={{0,20},{4,24},{8,28},{12,0},{16,4},{20,8},{24,12},{28,16},{1,21},{... | collective-permute-start | bytes 491528 | tf_op jit(solution)/shard_map/ppermute | solution.py:157
  11.9 27.5 %collective-permute-start.3 = (bf16[2,80,512]{2,1,0:T(8,128)(2,1)S(1)}, bf16[2,80,512]{2,1,0:T(8,128)(2,1)S(1)}, u32[]{:S(2)}, u32[]{:S(2)}) collective-permute-start(bf16[2,80,512]{2,1,0:T(8,128)(2,1)S(1)} %get-tuple-element.28), channel_id=1, source_target_pairs={{0,16},{4,20},{8,24},{12,28},{16,0},{20,4},{24,8},{28,12},{1,17},{... | collective-permute-start | bytes 491528 | tf_op jit(solution)/shard_map/ppermute | solution.py:157
  14.9 25.4 %collective-permute-start.4 = (bf16[2,80,512]{2,1,0:T(8,128)(2,1)S(1)}, bf16[2,80,512]{2,1,0:T(8,128)(2,1)S(1)}, u32[]{:S(2)}, u32[]{:S(2)}) collective-permute-start(bf16[2,80,512]{2,1,0:T(8,128)(2,1)S(1)} %get-tuple-element.27), channel_id=1, source_target_pairs={{0,12},{4,16},{8,20},{12,24},{16,28},{20,0},{24,4},{28,8},{1,13},{... | collective-permute-start | bytes 491528 | tf_op jit(solution)/shard_map/ppermute | solution.py:157
  25.3 15.1 %collective-permute-start.5 = (bf16[2,80,512]{2,1,0:T(8,128)(2,1)S(1)}, bf16[2,80,512]{2,1,0:T(8,128)(2,1)S(1)}, u32[]{:S(2)}, u32[]{:S(2)}) collective-permute-start(bf16[2,80,512]{2,1,0:T(8,128)(2,1)S(1)} %get-tuple-element.26), channel_id=1, source_target_pairs={{0,8},{4,12},{8,16},{12,20},{16,24},{20,28},{24,0},{28,4},{1,9},{5... | collective-permute-start | bytes 491528 | tf_op jit(solution)/shard_map/ppermute | solution.py:157
  27.3 13.2 %collective-permute-start.6 = (bf16[2,80,512]{2,1,0:T(8,128)(2,1)S(1)}, bf16[2,80,512]{2,1,0:T(8,128)(2,1)S(1)}, u32[]{:S(2)}, u32[]{:S(2)}) collective-permute-start(bf16[2,80,512]{2,1,0:T(8,128)(2,1)S(1)} %get-tuple-element.25), channel_id=1, source_target_pairs={{0,4},{4,8},{8,12},{12,16},{16,20},{20,24},{24,28},{28,0},{1,5},{5... | collective-permute-start | bytes 491528 | tf_op jit(solution)/shard_map/ppermute | solution.py:157
  44.5 2.2 %copy-start.2 = (bf16[4096,512]{1,0:T(8,128)(2,1)S(1)}, bf16[4096,512]{1,0:T(8,128)(2,1)}, u32[]{:S(2)}) copy-start(bf16[4096,512]{1,0:T(8,128)(2,1)} %copy.141) | copy-start | bytes 12582916
  49.3 3.0 %collective-permute-start.7 = (f32[128,2,1024]{2,0,1:T(8,128)}, f32[128,2,1024]{2,0,1:T(8,128)}, u32[]{:S(2)}, u32[]{:S(2)}) collective-permute-start(f32[128,2,1024]{2,0,1:T(8,128)} %dynamic-slice_bitcast_fusion), channel_id=1, source_target_pairs={{0,1},{1,0},{2,3},{3,2},{4,5},{5,4},{6,7},{7,6},{8,9},{9,8},{10,11... | collective-permute-start | bytes 3145736 | tf_op jit(solution)/shard_map/ppermute | solution.py:16
  53.7 1.0 copy-start.4
  54.7 16.4 %copy-start.7 = (s32[128]{0:T(128)S(1)}, s32[128]{0:T(128)}, u32[]{:S(2)}) copy-start(s32[128]{0:T(128)} %param.20) | copy-start | bytes 1540
  54.8 8.4 %collective-permute-start.8 = (bf16[128,1,1024]{2,0,1:T(8,128)(2,1)S(1)}, bf16[128,1,1024]{2,0,1:T(8,128)(2,1)S(1)}, u32[]{:S(2)}, u32[]{:S(2)}) collective-permute-start(bf16[128,1,1024]{2,0,1:T(8,128)(2,1)S(1)} %dynamic-slice_convert_fusion), channel_id=1, source_target_pairs={{0,2},{1,3},{2,0},{3,1},{4,6},{5,7},{6,4},{7,5},{8,10},{9,11},{10,... | collective-permute-start | bytes 786440 | tf_op jit(solution)/shard_map/ppermute | solution.py:16
  64.5 1.2 collective-permute-start.9
  65.7 3.5 %collective-permute-start.10 = (f32[128]{0:T(128)S(1)}, f32[128]{0:T(128)S(1)}, u32[]{:S(2)}, u32[]{:S(2)}) collective-permute-start(f32[128]{0:T(128)S(1)} %add.329), channel_id=1, source_target_pairs={{0,2},{1,3},{2,0},{3,1},{4,6},{5,7},{6,4},{7,5},{8,10},{9,11},{10,... | collective-permute-start | bytes 1544 | tf_op jit(solution)/shard_map/ppermute | solution.py:16
  69.3 7.3 %collective-permute-start.12 = (bf16[128,1024]{1,0:T(8,128)(2,1)S(1)}, bf16[128,1024]{1,0:T(8,128)(2,1)S(1)}, u32[]{:S(2)}, u32[]{:S(2)}) collective-permute-start(bf16[128,1024]{1,0:T(8,128)(2,1)S(1)} %multiply_convert_fusion.1), channel_id=1, source_target_pairs={{0,2},{1,3},{2,0},{3,1},{4,6},{5,7},{6,4},{7,5},{8,10},{9,11},{10,... | collective-permute-start | bytes 786440 | tf_op jit(solution)/shard_map/ppermute | solution.py:16
  71.0 5.6 %collective-permute-start.11 = (bf16[128,1,1024]{2,0,1:T(8,128)(2,1)S(1)}, bf16[128,1,1024]{2,0,1:T(8,128)(2,1)S(1)}, u32[]{:S(2)}, u32[]{:S(2)}) collective-permute-start(bf16[128,1,1024]{2,0,1:T(8,128)(2,1)S(1)} %fusion.144), channel_id=1, source_target_pairs={{0,1},{1,0},{2,3},{3,2},{4,5},{5,4},{6,7},{7,6},{8,9},{9,8},{10,11... | collective-permute-start | bytes 786440 | tf_op jit(solution)/shard_map/ppermute | solution.py:16
  76.7 1.5 %collective-permute-start.13 = (bf16[128,1,1024]{2,0,1:T(8,128)(2,1)S(1)}, bf16[128,1,1024]{2,0,1:T(8,128)(2,1)S(1)}, u32[]{:S(2)}, u32[]{:S(2)}) collective-permute-start(bf16[128,1,1024]{2,0,1:T(8,128)(2,1)S(1)} %bitcast.265), channel_id=1, source_target_pairs={{0,1},{1,0},{2,3},{3,2},{4,5},{5,4},{6,7},{7,6},{8,9},{9,8},{10,11... | collective-permute-start | bytes 786440 | tf_op jit(solution)/shard_map/ppermute | solution.py:16
  95.1 3.6 %copy-start.5 = (s32[128]{0:T(128)S(1)}, s32[128]{0:T(128)}, u32[]{:S(2)}) copy-start(s32[128]{0:T(128)} %param.21) | copy-start | bytes 1540
  95.8 1.2 collective-permute-start.14
  97.0 3.7 %collective-permute-start.15 = (f32[3,128]{1,0:T(4,128)S(1)}, f32[3,128]{1,0:T(4,128)S(1)}, u32[]{:S(2)}, u32[]{:S(2)}) collective-permute-start(f32[3,128]{1,0:T(4,128)S(1)} %pad_maximum_fusion.3), channel_id=1, source_target_pairs={{0,2},{1,3},{2,0},{3,1},{4,6},{5,7},{6,4},{7,5},{8,10},{9,11},{10,... | collective-permute-start | bytes 4616 | tf_op jit(solution)/shard_map/ppermute | solution.py:16
  110.6 2.1 %collective-permute-start.16 = (f32[1,1024,128]{1,2,0:T(8,128)S(1)}, f32[1,1024,128]{1,2,0:T(8,128)}, u32[]{:S(2)}, u32[]{:S(2)}) collective-permute-start(f32[1,1024,128]{1,2,0:T(8,128)S(1)} %bitcast.257), channel_id=1, source_target_pairs={{0,1},{1,0},{2,3},{3,2},{4,5},{5,4},{6,7},{7,6},{8,9},{9,8},{10,11... | collective-permute-start | bytes 1572872 | tf_op jit(solution)/shard_map/ppermute | solution.py:16
  122.3 8.8 %collective-permute-start.17 = (f32[1,1024,128]{1,2,0:T(8,128)S(1)}, f32[1,1024,128]{1,2,0:T(8,128)S(1)}, u32[]{:S(2)}, u32[]{:S(2)}) collective-permute-start(f32[1,1024,128]{1,2,0:T(8,128)S(1)} %bitcast.256), channel_id=1, source_target_pairs={{0,1},{1,0},{2,3},{3,2},{4,5},{5,4},{6,7},{7,6},{8,9},{9,8},{10,11... | collective-permute-start | bytes 1572872 | tf_op jit(solution)/shard_map/ppermute | solution.py:16
  122.5 8.6 %collective-permute-start.18 = (bf16[1024,128]{0,1:T(8,128)(2,1)S(1)}, bf16[1024,128]{0,1:T(8,128)(2,1)S(1)}, u32[]{:S(2)}, u32[]{:S(2)}) collective-permute-start(bf16[1024,128]{0,1:T(8,128)(2,1)S(1)} %fusion.23), channel_id=1, source_target_pairs={{0,2},{1,3},{2,0},{3,1},{4,6},{5,7},{6,4},{7,5},{8,10},{9,11},{10,... | collective-permute-start | bytes 786440 | tf_op jit(solution)/shard_map/ppermute | solution.py:16
  124.0 25.5 %copy-start.1 = (bf16[2,192,512]{2,1,0:T(8,128)(2,1)S(1)}, bf16[2,192,512]{2,1,0:T(8,128)(2,1)}, u32[]{:S(2)}) copy-start(bf16[2,192,512]{2,1,0:T(8,128)(2,1)} %param.13) | copy-start | bytes 1179652
  132.8 3.7 %collective-permute-start.19 = (f32[1026]{0:T(1024)S(1)}, f32[1026]{0:T(1024)S(1)}, u32[]{:S(2)}, u32[]{:S(2)}) collective-permute-start(f32[1026]{0:T(1024)S(1)} %concatenate.3), channel_id=1, source_target_pairs={{0,4},{4,0},{8,12},{12,8},{16,20},{20,16},{24,28},{28,24},{1,5},{5... | collective-permute-start | bytes 12320 | tf_op jit(solution)/shard_map/ppermute | solution.py:16
  136.4 3.7 %collective-permute-start.20 = (f32[1026]{0:T(1024)S(1)}, f32[1026]{0:T(1024)S(1)}, u32[]{:S(2)}, u32[]{:S(2)}) collective-permute-start(f32[1026]{0:T(1024)S(1)} %add.346), channel_id=1, source_target_pairs={{0,8},{4,12},{8,0},{12,4},{16,24},{20,28},{24,16},{28,20},{1,9},{5... | collective-permute-start | bytes 12320 | tf_op jit(solution)/shard_map/ppermute | solution.py:16
  137.1 1.1 collective-permute-start.22
  138.2 4.7 %collective-permute-start.23 = (f32[128]{0:T(128)S(1)}, f32[128]{0:T(128)S(1)}, u32[]{:S(2)}, u32[]{:S(2)}) collective-permute-start(f32[128]{0:T(128)S(1)} %add.349), channel_id=1, source_target_pairs={{0,2},{1,3},{2,0},{3,1},{4,6},{5,7},{6,4},{7,5},{8,10},{9,11},{10,... | collective-permute-start | bytes 1544 | tf_op jit(solution)/shard_map/ppermute | solution.py:16
  140.1 4.5 %collective-permute-start.21 = (f32[1026]{0:T(1024)S(1)}, f32[1026]{0:T(1024)S(1)}, u32[]{:S(2)}, u32[]{:S(2)}) collective-permute-start(f32[1026]{0:T(1024)S(1)} %add.347), channel_id=1, source_target_pairs={{0,16},{4,20},{8,24},{12,28},{16,0},{20,4},{24,8},{28,12},{1,17},{... | collective-permute-start | bytes 12320 | tf_op jit(solution)/shard_map/ppermute | solution.py:16

commit v9 on v7

--- a/solution.py
+++ b/solution.py
@@ -186,7 +186,7 @@
     square_total = sum_all(jnp.sum(summed_part * summed_part, 1), "fsdp")
     inv_root = lax.rsqrt(square_total / width + 1e-06)
     unit_part = summed_part * inv_root[:, None]
-    normed_part = (unit_part * gain_part).astype(jnp.bfloat16)
+    normed_part = (summed_part * gain_part).astype(jnp.bfloat16)
     if split_fsdp:
         half = width // 2
         top_side = (fsdp_index >> (levels - 1)) & 1
@@ -194,12 +194,13 @@
         far_rows = lax.dynamic_slice_in_dim(w_vocab, (1 - top_side) * half, half, 0)
         near_normed = gather_bits(normed_part, "fsdp", 1, levels - 1)
         far_normed = exchange(near_normed, "fsdp", levels - 1)
-        logits = jnp.dot(near_normed, near_rows, preferred_element_type=jnp.float32) + jnp.dot(
-            far_normed, far_rows, preferred_element_type=jnp.float32
-        )
+        logits = (
+            jnp.dot(near_normed, near_rows, preferred_element_type=jnp.float32)
+            + jnp.dot(far_normed, far_rows, preferred_element_type=jnp.float32)
+        ) * inv_root[:, None]
     else:
         normed_full = lax.all_gather(normed_part, "fsdp", axis=1, tiled=True)
-        logits = jnp.dot(normed_full, w_vocab, preferred_element_type=jnp.float32)
+        logits = jnp.dot(normed_full, w_vocab, preferred_element_type=jnp.float32) * inv_root[:, None]
     local_target = targets - fsdp_index * vocab_here
     picked = jnp.arange(vocab_here)[None, :] == local_target[:, None]
     local_top = jnp.max(logits, 1)

time: 150 us -> 147 us (0.980)
  starting transfers between devices: 26 us -> 22.1 us
    ppermute x16, starting transfers between devices: 13.3 us -> 9.4 us  [exchange(): return lax.ppermute(x, axis, [(i, i ^ 1 << bit) for i in range(size)])]
  transfers between devices with their start and end apart: 23 -> 23, of which waited for: 16 -> 15; matrix products, arithmetic and copies ran while one was open for 14% -> 14% of each run, Pallas kernels for 0% -> 0%
where the time goes in v9:
time: 147 us; the launch traced here: 146 us
  waiting for transfers between devices  48.4 us (33%)
  matrix products  40.6 us (28%)
  starting transfers between devices  22.1 us (15%)
  local copies, waits for them, and re-layouts  16.8 us (11%)
  other arithmetic  14 us (10%)
  between operations  3.85 us (3%)
    ppermute x16, waiting for transfers between devices, exchange(): return lax.ppermute(x, axis, [(i, i ^ 1 << bit) for i in range(size)])  37.2 us
    ppermute x7, starting transfers between devices, body(): lax.ppermute(block, 'dp', [(i, (i - shift) % dp_count) for i in range(dp_...  12.7 us
    ppermute x7, waiting for transfers between devices, body(): lax.ppermute(block, 'dp', [(i, (i - shift) % dp_count) for i in range(dp_...  11.2 us
    ppermute x16, starting transfers between devices, exchange(): return lax.ppermute(x, axis, [(i, i ^ 1 << bit) for i in range(size)])  9.4 us
    dot_general x1, matrix products, body(): jnp.dot(far_normed, far_rows, preferred_element_type=jnp.float32)  8.4 us
    dot_general x1, matrix products, body(): lax.dot_general(far_rows, grad_logits, contract, preferred_element_type=j...  8.36 us
    dot_general x1, matrix products, body(): jnp.dot(near_normed, near_rows, preferred_element_type=jnp.float32)  8.16 us
    dot_general x1, matrix products, body(): lax.dot_general(near_rows, near_logits, contract, preferred_element_type=...  8.13 us
  transfers between devices with their start and end apart: 23, of which 15 were waited for; matrix products, arithmetic and copies ran while one was open for 14% of the time, Pallas kernels for 0%

profile of v9, /device:TPU:0, one launch (start us, length us, event | category | flops | bytes accessed | tf_op | source)
XLA Modules:
  0.0 145.8 jit_solution(958973021961770783)
XLA Ops:
  0.7 0.8 lt.71
  1.7 0.8 fusion.74
  2.5 0.8 select_reduce_fusion.11
  3.4 0.8 select_reduce_fusion.19
  5.4 6.0 %collective-permute-start = (bf16[2,80,512]{2,1,0:T(8,128)(2,1)S(1)}, bf16[2,80,512]{2,1,0:T(8,128)(2,1)S(1)}, u32[]{:S(2)}, u32[]{:S(2)}) collective-permute-start(bf16[2,80,512]{2,1,0:T(8,128)(2,1)S(1)} %get-tuple-element.30), channel_id=1, source_target_pairs={{0,28},{4,0},{8,4},{12,8},{16,12},{20,16},{24,20},{28,24},{1,29},{... | collective-permute-start | bytes 491528 | tf_op jit(solution)/shard_map/ppermute | solution.py:157
  11.9 3.0 %collective-permute-start.3 = (bf16[2,80,512]{2,1,0:T(8,128)(2,1)S(1)}, bf16[2,80,512]{2,1,0:T(8,128)(2,1)S(1)}, u32[]{:S(2)}, u32[]{:S(2)}) collective-permute-start(bf16[2,80,512]{2,1,0:T(8,128)(2,1)S(1)} %get-tuple-element.28), channel_id=1, source_target_pairs={{0,16},{4,20},{8,24},{12,28},{16,0},{20,4},{24,8},{28,12},{1,17},{... | collective-permute-start | bytes 491528 | tf_op jit(solution)/shard_map/ppermute | solution.py:157
  15.7 1.9 %convolution_convert_fusion.1 = bf16[128,512]{1,0:T(8,128)(2,1)S(1)} fusion(bf16[128,4096]{1,0:T(8,128)(2,1)} %param.11, bf16[4096,512]{1,0:T(8,128)(2,1)S(1)} %copy-done.3), kind=kOutput, calls=%fused_computation.25 | convolution fusion | flops 536936448 | bytes 5373952 | tf_op jit(solution)/shard_map/dot_general | solution.py:148
  18.7 6.5 %copy.139 = bf16[4096,512]{1,0:T(8,128)(2,1)} copy(bf16[4096,512]{0,1:T(8,128)(2,1)} %bitcast.233) | data formatting | bytes 8388608 | tf_op jit(solution)/shard_map/dot_general | solution.py:180
  25.2 1.9 %collective-permute-start.5 = (bf16[2,80,512]{2,1,0:T(8,128)(2,1)S(1)}, bf16[2,80,512]{2,1,0:T(8,128)(2,1)S(1)}, u32[]{:S(2)}, u32[]{:S(2)}) collective-permute-start(bf16[2,80,512]{2,1,0:T(8,128)(2,1)S(1)} %get-tuple-element.26), channel_id=1, source_target_pairs={{0,8},{4,12},{8,16},{12,20},{16,24},{20,28},{24,0},{28,4},{1,9},{5... | collective-permute-start | bytes 491528 | tf_op jit(solution)/shard_map/ppermute | solution.py:157
  27.2 1.4 collective-permute-start.6
  28.9 10.5 %collective-permute-done.3 = bf16[2,80,512]{2,1,0:T(8,128)(2,1)S(1)} collective-permute-done((bf16[2,80,512]{2,1,0:T(8,128)(2,1)S(1)}, bf16[2,80,512]{2,1,0:T(8,128)(2,1)S(1)}, u32[]{:S(2)}, u32[]{:S(2)}) %collective-permute-start.3) | collective-permute-done | bytes 163872 | tf_op jit(solution)/shard_map/ppermute | solution.py:157
  39.5 0.7 collective-permute-done.4
  45.4 1.3 copy-done.2
  46.7 1.5 %fusion.115 = f32[128,2,2,1024]{3,0,2,1:T(8,128)S(1)} fusion(bf16[128,512,1,1]{0,1,3,2:T(8,128)(2,1)S(1)} %bitcast.236, bf16[2,2,1024,512]{3,2,1,0:T(8,128)(2,1)S(1)} %bitcast.224), kind=kOutput, calls=%fused_computation.242 | convolution fusion | flops 536870912 | bytes 6422528 | tf_op jit(solution)/shard_map/dot_general | solution.py:180
  48.2 1.1 dynamic-slice_bitcast_fusion
  49.3 3.0 %collective-permute-done.7 = f32[128,2,1024]{2,0,1:T(8,128)} collective-permute-done((f32[128,2,1024]{2,0,1:T(8,128)}, f32[128,2,1024]{2,0,1:T(8,128)}, u32[]{:S(2)}, u32[]{:S(2)}) %collective-permute-start.7) | collective-permute-done | bytes 1048608 | tf_op jit(solution)/shard_map/ppermute | solution.py:16
  52.3 1.4 bitcast_add_fusion
  53.7 1.0 copy-done.4
  54.7 1.6 %collective-permute-start.8 = (bf16[128,1,1024]{2,0,1:T(8,128)(2,1)S(1)}, bf16[128,1,1024]{2,0,1:T(8,128)(2,1)S(1)}, u32[]{:S(2)}, u32[]{:S(2)}) collective-permute-start(bf16[128,1,1024]{2,0,1:T(8,128)(2,1)S(1)} %dynamic-slice_convert_fusion), channel_id=1, source_target_pairs={{0,2},{1,3},{2,0},{3,1},{4,6},{5,7},{6,4},{7,5},{8,10},{9,11},{10,... | collective-permute-start | bytes 786440 | tf_op jit(solution)/shard_map/ppermute | solution.py:16
  56.3 0.7 dynamic_slice.38
  57.0 6.1 %collective-permute-done.8 = bf16[128,1,1024]{2,0,1:T(8,128)(2,1)S(1)} collective-permute-done((bf16[128,1,1024]{2,0,1:T(8,128)(2,1)S(1)}, bf16[128,1,1024]{2,0,1:T(8,128)(2,1)S(1)}, u32[]{:S(2)}, u32[]{:S(2)}) %collective-permute-start.8) | collective-permute-done | bytes 262176 | tf_op jit(solution)/shard_map/ppermute | solution.py:16
  63.1 1.3 multiply_reduce_fusion.1
  65.1 1.0 collective-permute-done.11
  66.1 1.5 %collective-permute-start.12 = (f32[128]{0:T(128)S(1)}, f32[128]{0:T(128)S(1)}, u32[]{:S(2)}, u32[]{:S(2)}) collective-permute-start(f32[128]{0:T(128)S(1)} %add.332), channel_id=1, source_target_pairs={{0,2},{1,3},{2,0},{3,1},{4,6},{5,7},{6,4},{7,5},{8,10},{9,11},{10,... | collective-permute-start | bytes 1544 | tf_op jit(solution)/shard_map/ppermute | solution.py:16
  68.6 1.0 collective-permute-done.12
  69.7 8.2 %fusion.6 = f32[128,4096]{1,0:T(8,128)S(1)} fusion(bf16[128,2048]{0,1:T(8,128)(2,1)S(1)} %bitcast.249, bf16[4096,4096]{1,0:T(8,128)(2,1)} %param.16, s32[]{:T(128)S(6)} %select_n.229), kind=kOutput, calls=%fused_computation.6 | convolution fusion | flops 2147483648 | bytes 19398660 | tf_op jit(solution)/shard_map/dot_general | solution.py:198
  77.8 4.0 %collective-permute-done.10 = bf16[128,2048]{0,1:T(8,128)(2,1)S(1)} collective-permute-done((bf16[128,2048]{0,1:T(8,128)(2,1)S(1)}, bf16[128,2048]{0,1:T(8,128)(2,1)S(1)}, u32[]{:S(2)}, u32[]{:S(2)}) %collective-permute-start.10) | collective-permute-done | bytes 524320 | tf_op jit(solution)/shard_map/ppermute | solution.py:16
  81.8 8.4 %fusion.114 = (f32[128]{0:T(128)S(1)}, f32[128,4096]{1,0:T(8,128)S(1)}) fusion(f32[128]{0:T(128)S(1)} %add_rsqrt_fusion, f32[128,4096]{1,0:T(8,128)S(1)} %fusion.6, bf16[128,2048]{0,1:T(8,128)(2,1)S(1)} %collective-permute-done.10, bf16[4096,4096]{1,0:T(8,128)(2,1)} %param.16, s32[]{:T(128)S(6)} %select_n.230), kind=kOutput, calls=%fused_computation.241 | convolution fusion | flops 2149056512 | bytes 21496836 | tf_op jit(solution)/shard_map/dot_general | solution.py:199
  90.2 0.7 select_reduce_fusion
  91.0 1.1 collective-permute-done.13
  92.8 3.1 %collective-permute-done.14 = f32[3,128]{1,0:T(4,128)S(1)} collective-permute-done((f32[3,128]{1,0:T(4,128)S(1)}, f32[3,128]{1,0:T(4,128)S(1)}, u32[]{:S(2)}, u32[]{:S(2)}) %collective-permute-start.14) | collective-permute-done | bytes 1568 | tf_op jit(solution)/shard_map/ppermute | solution.py:16
  95.8 0.6 fusion.95
  96.5 0.6 multiply_convert_fusion
  97.1 8.4 %fusion = f32[2048,128]{1,0:T(8,128)S(1)} fusion(bf16[128,4096]{1,0:T(8,128)(2,1)S(1)} %multiply_convert_fusion, bf16[4096,4096]{1,0:T(8,128)(2,1)} %param.16, s32[]{:T(128)S(6)} %select_n.230), kind=kOutput, calls=%fused_computation | convolution fusion | flops 2147483648 | bytes 18874372 | tf_op jit(solution)/shard_map/dot_general | solution.py:219
  106.0 1.8 %collective-permute-done.15 = f32[1,1024,128]{1,2,0:T(8,128)} collective-permute-done((f32[1,1024,128]{1,2,0:T(8,128)S(1)}, f32[1,1024,128]{1,2,0:T(8,128)}, u32[]{:S(2)}, u32[]{:S(2)}) %collective-permute-start.15) | collective-permute-done | bytes 524320 | tf_op jit(solution)/shard_map/ppermute | solution.py:16
  107.9 1.1 fusion.26
  109.0 8.1 %fusion.4 = f32[2048,128]{1,0:T(8,128)S(1)} fusion(bf16[128,4096]{1,0:T(8,128)(2,1)S(1)} %multiply_convert_fusion, bf16[4096,4096]{1,0:T(8,128)(2,1)} %param.16, s32[]{:T(128)S(6)} %select_n.229), kind=kOutput, calls=%fused_computation.4 | convolution fusion | flops 2147483648 | bytes 18874372 | tf_op jit(solution)/shard_map/dot_general | solution.py:228
  118.4 7.9 %collective-permute-done.17 = bf16[1024,128]{0,1:T(8,128)(2,1)S(1)} collective-permute-done((bf16[1024,128]{0,1:T(8,128)(2,1)S(1)}, bf16[1024,128]{0,1:T(8,128)(2,1)S(1)}, u32[]{:S(2)}, u32[]{:S(2)}) %collective-permute-start.17) | collective-permute-done | bytes 262176 | tf_op jit(solution)/shard_map/ppermute | solution.py:16
  126.5 1.4 concatenate.3
  127.9 3.6 %collective-permute-done.18 = f32[1026]{0:T(1024)S(1)} collective-permute-done((f32[1026]{0:T(1024)S(1)}, f32[1026]{0:T(1024)S(1)}, u32[]{:S(2)}, u32[]{:S(2)}) %collective-permute-start.18) | collective-permute-done | bytes 4136 | tf_op jit(solution)/shard_map/ppermute | solution.py:16
  131.6 0.6 collective-permute-start.19
  132.2 1.1 collective-permute-done.21
  133.8 1.4 collective-permute-done.19
  135.2 2.6 %collective-permute-start.20 = (f32[1026]{0:T(1024)S(1)}, f32[1026]{0:T(1024)S(1)}, u32[]{:S(2)}, u32[]{:S(2)}) collective-permute-start(f32[1026]{0:T(1024)S(1)} %add.347), channel_id=1, source_target_pairs={{0,16},{4,20},{8,24},{12,28},{16,0},{20,4},{24,8},{28,12},{1,17},{... | collective-permute-start | bytes 12320 | tf_op jit(solution)/shard_map/ppermute | solution.py:16
  137.8 2.0 %collective-permute-done.20 = f32[1026]{0:T(1024)S(1)} collective-permute-done((f32[1026]{0:T(1024)S(1)}, f32[1026]{0:T(1024)S(1)}, u32[]{:S(2)}, u32[]{:S(2)}) %collective-permute-start.20) | collective-permute-done | bytes 4136 | tf_op jit(solution)/shard_map/ppermute | solution.py:16
  139.8 0.6 fusion.113
  140.4 1.4 slice_divide_fusion
  143.1 1.6 %divide_convert_fusion = bf16[128,1024]{1,0:T(8,128)(2,1)} fusion(f32[1024,128]{0,1:T(8,128)S(1)} %get-tuple-element.20, f32[128,1024]{1,0:T(8,128)S(1)} %get-tuple-element.23, f32[]{:T(128)} %bitcast.70, f32[128]{0:T(128)S(1)} %add_multiply_fusion, f32[128]{0:T(128)S(1)} %add_rsqrt_fusion, f32[1024]{0:T(1024)S(1)} %dynamic_slice.38), kind=kLoop, calls=%fused_computation.42 | loop fusion | flops 917504 | bytes 1315844 | tf_op jit(solution)/shard_map/convert_element_type | solution.py:250
  (135 shorter events, 14.0 us)
Async XLA Ops:
  0.6 4.1 %copy-start = (bf16[2,192,512]{2,1,0:T(8,128)(2,1)S(1)}, bf16[2,192,512]{2,1,0:T(8,128)(2,1)}, u32[]{:S(2)}) copy-start(bf16[2,192,512]{2,1,0:T(8,128)(2,1)} %param.13) | copy-start | bytes 1179652
  4.7 10.9 %copy-start.6 = (s32[128]{0:T(128)S(1)}, s32[128]{0:T(128)}, u32[]{:S(2)}) copy-start(s32[128]{0:T(128)} %param.18) | copy-start | bytes 1540
  4.7 11.0 %copy-start.3 = (bf16[4096,512]{1,0:T(8,128)(2,1)S(1)}, bf16[4096,512]{1,0:T(8,128)(2,1)}, u32[]{:S(2)}) copy-start(bf16[4096,512]{1,0:T(8,128)(2,1)} %param.12) | copy-start | bytes 12582916
  5.4 19.8 %collective-permute-start = (bf16[2,80,512]{2,1,0:T(8,128)(2,1)S(1)}, bf16[2,80,512]{2,1,0:T(8,128)(2,1)S(1)}, u32[]{:S(2)}, u32[]{:S(2)}) collective-permute-start(bf16[2,80,512]{2,1,0:T(8,128)(2,1)S(1)} %get-tuple-element.30), channel_id=1, source_target_pairs={{0,28},{4,0},{8,4},{12,8},{16,12},{20,16},{24,20},{28,24},{1,29},{... | collective-permute-start | bytes 491528 | tf_op jit(solution)/shard_map/ppermute | solution.py:157
  11.4 15.8 %collective-permute-start.1 = (bf16[2,80,512]{2,1,0:T(8,128)(2,1)S(1)}, bf16[2,80,512]{2,1,0:T(8,128)(2,1)S(1)}, u32[]{:S(2)}, u32[]{:S(2)}) collective-permute-start(bf16[2,80,512]{2,1,0:T(8,128)(2,1)S(1)} %get-tuple-element.24), channel_id=1, source_target_pairs={{0,24},{4,28},{8,0},{12,4},{16,8},{20,12},{24,16},{28,20},{1,25},{... | collective-permute-start | bytes 491528 | tf_op jit(solution)/shard_map/ppermute | solution.py:157
  11.9 16.9 %collective-permute-start.2 = (bf16[2,80,512]{2,1,0:T(8,128)(2,1)S(1)}, bf16[2,80,512]{2,1,0:T(8,128)(2,1)S(1)}, u32[]{:S(2)}, u32[]{:S(2)}) collective-permute-start(bf16[2,80,512]{2,1,0:T(8,128)(2,1)S(1)} %get-tuple-element.29), channel_id=1, source_target_pairs={{0,20},{4,24},{8,28},{12,0},{16,4},{20,8},{24,12},{28,16},{1,21},{... | collective-permute-start | bytes 491528 | tf_op jit(solution)/shard_map/ppermute | solution.py:157
  11.9 27.5 %collective-permute-start.3 = (bf16[2,80,512]{2,1,0:T(8,128)(2,1)S(1)}, bf16[2,80,512]{2,1,0:T(8,128)(2,1)S(1)}, u32[]{:S(2)}, u32[]{:S(2)}) collective-permute-start(bf16[2,80,512]{2,1,0:T(8,128)(2,1)S(1)} %get-tuple-element.28), channel_id=1, source_target_pairs={{0,16},{4,20},{8,24},{12,28},{16,0},{20,4},{24,8},{28,12},{1,17},{... | collective-permute-start | bytes 491528 | tf_op jit(solution)/shard_map/ppermute | solution.py:157
  14.9 25.3 %collective-permute-start.4 = (bf16[2,80,512]{2,1,0:T(8,128)(2,1)S(1)}, bf16[2,80,512]{2,1,0:T(8,128)(2,1)S(1)}, u32[]{:S(2)}, u32[]{:S(2)}) collective-permute-start(bf16[2,80,512]{2,1,0:T(8,128)(2,1)S(1)} %get-tuple-element.27), channel_id=1, source_target_pairs={{0,12},{4,16},{8,20},{12,24},{16,28},{20,0},{24,4},{28,8},{1,13},{... | collective-permute-start | bytes 491528 | tf_op jit(solution)/shard_map/ppermute | solution.py:157
  25.2 15.2 %collective-permute-start.5 = (bf16[2,80,512]{2,1,0:T(8,128)(2,1)S(1)}, bf16[2,80,512]{2,1,0:T(8,128)(2,1)S(1)}, u32[]{:S(2)}, u32[]{:S(2)}) collective-permute-start(bf16[2,80,512]{2,1,0:T(8,128)(2,1)S(1)} %get-tuple-element.26), channel_id=1, source_target_pairs={{0,8},{4,12},{8,16},{12,20},{16,24},{20,28},{24,0},{28,4},{1,9},{5... | collective-permute-start | bytes 491528 | tf_op jit(solution)/shard_map/ppermute | solution.py:157
  27.2 13.3 %collective-permute-start.6 = (bf16[2,80,512]{2,1,0:T(8,128)(2,1)S(1)}, bf16[2,80,512]{2,1,0:T(8,128)(2,1)S(1)}, u32[]{:S(2)}, u32[]{:S(2)}) collective-permute-start(bf16[2,80,512]{2,1,0:T(8,128)(2,1)S(1)} %get-tuple-element.25), channel_id=1, source_target_pairs={{0,4},{4,8},{8,12},{12,16},{16,20},{20,24},{24,28},{28,0},{1,5},{5... | collective-permute-start | bytes 491528 | tf_op jit(solution)/shard_map/ppermute | solution.py:157
  44.5 2.2 %copy-start.2 = (bf16[4096,512]{1,0:T(8,128)(2,1)S(1)}, bf16[4096,512]{1,0:T(8,128)(2,1)}, u32[]{:S(2)}) copy-start(bf16[4096,512]{1,0:T(8,128)(2,1)} %copy.139) | copy-start | bytes 12582916
  49.3 3.0 %collective-permute-start.7 = (f32[128,2,1024]{2,0,1:T(8,128)}, f32[128,2,1024]{2,0,1:T(8,128)}, u32[]{:S(2)}, u32[]{:S(2)}) collective-permute-start(f32[128,2,1024]{2,0,1:T(8,128)} %dynamic-slice_bitcast_fusion), channel_id=1, source_target_pairs={{0,1},{1,0},{2,3},{3,2},{4,5},{5,4},{6,7},{7,6},{8,9},{9,8},{10,11... | collective-permute-start | bytes 3145736 | tf_op jit(solution)/shard_map/ppermute | solution.py:16
  53.7 1.0 copy-start.4
  54.7 9.9 %copy-start.7 = (s32[128]{0:T(128)S(1)}, s32[128]{0:T(128)}, u32[]{:S(2)}) copy-start(s32[128]{0:T(128)} %param.20) | copy-start | bytes 1540
  54.7 8.4 %collective-permute-start.8 = (bf16[128,1,1024]{2,0,1:T(8,128)(2,1)S(1)}, bf16[128,1,1024]{2,0,1:T(8,128)(2,1)S(1)}, u32[]{:S(2)}, u32[]{:S(2)}) collective-permute-start(bf16[128,1,1024]{2,0,1:T(8,128)(2,1)S(1)} %dynamic-slice_convert_fusion), channel_id=1, source_target_pairs={{0,2},{1,3},{2,0},{3,1},{4,6},{5,7},{6,4},{7,5},{8,10},{9,11},{10,... | collective-permute-start | bytes 786440 | tf_op jit(solution)/shard_map/ppermute | solution.py:16
  64.5 3.1 %collective-permute-start.9 = (bf16[128,1,1024]{2,0,1:T(8,128)(2,1)S(1)}, bf16[128,1,1024]{2,0,1:T(8,128)(2,1)S(1)}, u32[]{:S(2)}, u32[]{:S(2)}) collective-permute-start(bf16[128,1,1024]{2,0,1:T(8,128)(2,1)S(1)} %fusion.43), channel_id=1, source_target_pairs={{0,1},{1,0},{2,3},{3,2},{4,5},{5,4},{6,7},{7,6},{8,9},{9,8},{10,11... | collective-permute-start | bytes 786440 | tf_op jit(solution)/shard_map/ppermute | solution.py:16
  64.6 1.5 %collective-permute-start.11 = (f32[128]{0:T(128)S(1)}, f32[128]{0:T(128)S(1)}, u32[]{:S(2)}, u32[]{:S(2)}) collective-permute-start(f32[128]{0:T(128)S(1)} %get-tuple-element.22), channel_id=1, source_target_pairs={{0,1},{1,0},{2,3},{3,2},{4,5},{5,4},{6,7},{7,6},{8,9},{9,8},{10,11... | collective-permute-start | bytes 1544 | tf_op jit(solution)/shard_map/ppermute | solution.py:16
  66.1 3.5 %collective-permute-start.12 = (f32[128]{0:T(128)S(1)}, f32[128]{0:T(128)S(1)}, u32[]{:S(2)}, u32[]{:S(2)}) collective-permute-start(f32[128]{0:T(128)S(1)} %add.332), channel_id=1, source_target_pairs={{0,2},{1,3},{2,0},{3,1},{4,6},{5,7},{6,4},{7,5},{8,10},{9,11},{10,... | collective-permute-start | bytes 1544 | tf_op jit(solution)/shard_map/ppermute | solution.py:16
  68.0 13.8 %collective-permute-start.10 = (bf16[128,2048]{0,1:T(8,128)(2,1)S(1)}, bf16[128,2048]{0,1:T(8,128)(2,1)S(1)}, u32[]{:S(2)}, u32[]{:S(2)}) collective-permute-start(bf16[128,2048]{0,1:T(8,128)(2,1)S(1)} %bitcast.248), channel_id=1, source_target_pairs={{0,2},{1,3},{2,0},{3,1},{4,6},{5,7},{6,4},{7,5},{8,10},{9,11},{10,... | collective-permute-start | bytes 1572872 | tf_op jit(solution)/shard_map/ppermute | solution.py:16
  90.2 2.6 %copy-start.5 = (s32[128]{0:T(128)S(1)}, s32[128]{0:T(128)}, u32[]{:S(2)}) copy-start(s32[128]{0:T(128)} %param.21) | copy-start | bytes 1540
  90.9 1.2 collective-permute-start.13
  92.2 3.7 %collective-permute-start.14 = (f32[3,128]{1,0:T(4,128)S(1)}, f32[3,128]{1,0:T(4,128)S(1)}, u32[]{:S(2)}, u32[]{:S(2)}) collective-permute-start(f32[3,128]{1,0:T(4,128)S(1)} %pad_maximum_fusion.2), channel_id=1, source_target_pairs={{0,2},{1,3},{2,0},{3,1},{4,6},{5,7},{6,4},{7,5},{8,10},{9,11},{10,... | collective-permute-start | bytes 4616 | tf_op jit(solution)/shard_map/ppermute | solution.py:16
  105.8 2.1 %collective-permute-start.15 = (f32[1,1024,128]{1,2,0:T(8,128)S(1)}, f32[1,1024,128]{1,2,0:T(8,128)}, u32[]{:S(2)}, u32[]{:S(2)}) collective-permute-start(f32[1,1024,128]{1,2,0:T(8,128)S(1)} %bitcast.250), channel_id=1, source_target_pairs={{0,1},{1,0},{2,3},{3,2},{4,5},{5,4},{6,7},{7,6},{8,9},{9,8},{10,11... | collective-permute-start | bytes 1572872 | tf_op jit(solution)/shard_map/ppermute | solution.py:16
  117.4 8.8 %collective-permute-start.16 = (f32[1,1024,128]{1,2,0:T(8,128)S(1)}, f32[1,1024,128]{1,2,0:T(8,128)S(1)}, u32[]{:S(2)}, u32[]{:S(2)}) collective-permute-start(f32[1,1024,128]{1,2,0:T(8,128)S(1)} %bitcast.247), channel_id=1, source_target_pairs={{0,1},{1,0},{2,3},{3,2},{4,5},{5,4},{6,7},{7,6},{8,9},{9,8},{10,11... | collective-permute-start | bytes 1572872 | tf_op jit(solution)/shard_map/ppermute | solution.py:16
  117.6 8.6 %collective-permute-start.17 = (bf16[1024,128]{0,1:T(8,128)(2,1)S(1)}, bf16[1024,128]{0,1:T(8,128)(2,1)S(1)}, u32[]{:S(2)}, u32[]{:S(2)}) collective-permute-start(bf16[1024,128]{0,1:T(8,128)(2,1)S(1)} %fusion.26), channel_id=1, source_target_pairs={{0,2},{1,3},{2,0},{3,1},{4,6},{5,7},{6,4},{7,5},{8,10},{9,11},{10,... | collective-permute-start | bytes 786440 | tf_op jit(solution)/shard_map/ppermute | solution.py:16
  118.2 26.5 %copy-start.1 = (bf16[2,192,512]{2,1,0:T(8,128)(2,1)S(1)}, bf16[2,192,512]{2,1,0:T(8,128)(2,1)}, u32[]{:S(2)}) copy-start(bf16[2,192,512]{2,1,0:T(8,128)(2,1)} %param.13) | copy-start | bytes 1179652
  127.9 3.7 %collective-permute-start.18 = (f32[1026]{0:T(1024)S(1)}, f32[1026]{0:T(1024)S(1)}, u32[]{:S(2)}, u32[]{:S(2)}) collective-permute-start(f32[1026]{0:T(1024)S(1)} %concatenate.3), channel_id=1, source_target_pairs={{0,4},{4,0},{8,12},{12,8},{16,20},{20,16},{24,28},{28,24},{1,5},{5... | collective-permute-start | bytes 12320 | tf_op jit(solution)/shard_map/ppermute | solution.py:16
  131.6 3.7 %collective-permute-start.19 = (f32[1026]{0:T(1024)S(1)}, f32[1026]{0:T(1024)S(1)}, u32[]{:S(2)}, u32[]{:S(2)}) collective-permute-start(f32[1026]{0:T(1024)S(1)} %add.346), channel_id=1, source_target_pairs={{0,8},{4,12},{8,0},{12,4},{16,24},{20,28},{24,16},{28,20},{1,9},{5... | collective-permute-start | bytes 12320 | tf_op jit(solution)/shard_map/ppermute | solution.py:16
  132.2 1.1 collective-permute-start.21
  133.3 4.5 %collective-permute-start.22 = (f32[128]{0:T(128)S(1)}, f32[128]{0:T(128)S(1)}, u32[]{:S(2)}, u32[]{:S(2)}) collective-permute-start(f32[128]{0:T(128)S(1)} %add.349), channel_id=1, source_target_pairs={{0,2},{1,3},{2,0},{3,1},{4,6},{5,7},{6,4},{7,5},{8,10},{9,11},{10,... | collective-permute-start | bytes 1544 | tf_op jit(solution)/shard_map/ppermute | solution.py:16
  135.2 4.5 %collective-permute-start.20 = (f32[1026]{0:T(1024)S(1)}, f32[1026]{0:T(1024)S(1)}, u32[]{:S(2)}, u32[]{:S(2)}) collective-permute-start(f32[1026]{0:T(1024)S(1)} %add.347), channel_id=1, source_target_pairs={{0,16},{4,20},{8,24},{12,28},{16,0},{20,4},{24,8},{28,12},{1,17},{... | collective-permute-start | bytes 12320 | tf_op jit(solution)/shard_map/ppermute | solution.py:16

commit v10 on v9

--- a/solution.py
+++ b/solution.py
@@ -148,31 +148,30 @@
     query_proj = jnp.dot(dec_hidden, w_query, preferred_element_type=jnp.float32).astype(
         jnp.bfloat16
     )
-    queries = lax.optimization_barrier(query_proj).reshape(dec_len, heads_here, HEAD_DIM)
-    run_sum = jnp.zeros((heads_here, dec_len), jnp.float32)
-    run_acc = jnp.zeros((heads_here, dec_len, HEAD_DIM), jnp.float32)
+    queries = lax.optimization_barrier(query_proj)
+    head_mask = jnp.arange(heads_here)[:, None] == jnp.arange(heads_here * HEAD_DIM)[None, :] // HEAD_DIM
+    spread = jnp.where(head_mask[:, None, :], queries[None], jnp.zeros((), queries.dtype)).reshape(
+        heads_here * dec_len, heads_here * HEAD_DIM
+    )
+    spread_sources = jnp.tile(sources, heads_here)
+    run_sum = jnp.zeros((heads_here * dec_len,), jnp.float32)
+    run_acc = jnp.zeros((heads_here * dec_len, heads_here * HEAD_DIM), jnp.float32)
     for shift in range(dp_count):
         block = windows[shift]
         if shift:
             block = lax.ppermute(
                 block, "dp", [(i, (i - shift) % dp_count) for i in range(dp_count)]
             )
-        keys_here = block[0].reshape(window, heads_here, HEAD_DIM)
-        values_here = block[1].astype(jnp.float32).reshape(window, heads_here, HEAD_DIM)
-        scores = jnp.einsum(
-            "ihd,jhd->hij", queries, keys_here, preferred_element_type=jnp.float32
-        )
-        allowed = (sources[:, None] == key_ids[shift][None, :])[None]
-        top = jnp.max(jnp.where(allowed, scores, jnp.float32(-1e30)), 2)
-        weights = jnp.where(allowed, jnp.exp(scores - top[:, :, None]), 0.0)
-        run_sum = run_sum + jnp.sum(weights, 2)
-        run_acc = run_acc + jnp.einsum("hij,jhd->hid", weights, values_here)
-    attended = (
-        (run_acc / run_sum[:, :, None])
-        .transpose(1, 0, 2)
-        .reshape(dec_len, heads_here * HEAD_DIM)
-        .astype(jnp.bfloat16)
-    )
+        scores = lax.dot_general(
+            spread, block[0], (((1,), (1,)), ((), ())), preferred_element_type=jnp.float32
+        )
+        allowed = spread_sources[:, None] == key_ids[shift][None, :]
+        top = jnp.max(jnp.where(allowed, scores, jnp.float32(-1e30)), 1)
+        weights = jnp.where(allowed, jnp.exp(scores - top[:, None]), 0.0)
+        run_sum = run_sum + jnp.sum(weights, 1)
+        run_acc = run_acc + jnp.dot(weights, block[1].astype(jnp.float32))
+    spread_out = (run_acc / run_sum[:, None]).reshape(heads_here, dec_len, heads_here * HEAD_DIM)
+    attended = jnp.sum(jnp.where(head_mask[:, None, :], spread_out, 0.0), 0).astype(jnp.bfloat16)
 
     feature_start = fsdp_index * feature_count
     gain_part = lax.dynamic_slice_in_dim(norm_gain, feature_start, feature_count, 0)

time: 147 us -> 160 us (1.088)
  matrix products: 40.6 us -> 57.3 us
  waiting for transfers between devices: 48.4 us -> 38.9 us
  starting transfers between devices: 22.1 us -> 29.4 us
    dot_general x16, matrix products: 3.61 us -> 19.1 us  [the longest x8 10.2 us: body(): run_acc = run_acc + jnp.dot(weights, block[1].astype(jnp.float32))]
    ppermute x7, waiting for transfers between devices: 11.2 us -> 4.4 us  [body(): lax.ppermute(block, 'dp', [(i, (i - shift) % dp_count) for i in range(dp_...]
    dot_general x1 -> x0, local copies, waits for them, and re-layouts: 6.47 us -> none  [body(): projected = jnp.dot(attended, w_out, preferred_element_type=jnp.float32)]
    ppermute x16, starting transfers between devices: 9.4 us -> 15.1 us  [exchange(): return lax.ppermute(x, axis, [(i, i ^ 1 << bit) for i in range(size)])]
    dynamic_slice x4 -> x2, local copies, waits for them, and re-layouts: 0.55 us -> 5.13 us  [scatter_bits(): keep = lax.dynamic_index_in_dim(cur, side, dim + 1, keepdims=False)]
    ppermute x16, waiting for transfers between devices: 37.2 us -> 34.5 us  [exchange(): return lax.ppermute(x, axis, [(i, i ^ 1 << bit) for i in range(size)])]
    reshape x8 -> x1, local copies, waits for them, and re-layouts: 0.95 us -> 3.02 us  [scatter_bits(): cur = cur.reshape(head + (chunks // 2, 2, width) + tail)]
  transfers between devices with their start and end apart: 23 -> 23, of which waited for: 15 -> 15; matrix products, arithmetic and copies ran while one was open for 14% -> 15% of each run, Pallas kernels for 0% -> 0%
where the time goes in v10:
time: 160 us; the launch traced here: 159 us
  matrix products  57.3 us (36%)
  waiting for transfers between devices  38.9 us (24%)
  starting transfers between devices  29.4 us (18%)
  local copies, waits for them, and re-layouts  16.9 us (11%)
  other arithmetic  12.5 us (8%)
  between operations  3.59 us (2%)
    ppermute x16, waiting for transfers between devices, exchange(): return lax.ppermute(x, axis, [(i, i ^ 1 << bit) for i in range(size)])  34.5 us
    ppermute x16, starting transfers between devices, exchange(): return lax.ppermute(x, axis, [(i, i ^ 1 << bit) for i in range(size)])  15.1 us
    ppermute x7, starting transfers between devices, body(): lax.ppermute(block, 'dp', [(i, (i - shift) % dp_count) for i in range(dp_...  14.3 us
    dot_general x8, matrix products, body(): run_acc = run_acc + jnp.dot(weights, block[1].astype(jnp.float32))  10.2 us
    dot_general x8, matrix products, body(): lax.dot_general(spread, block[0], (((1,), (1,)), ((), ())), preferred_ele...  8.96 us
    dot_general x1, matrix products, body(): jnp.dot(far_normed, far_rows, preferred_element_type=jnp.float32)  8.39 us
    dot_general x1, matrix products, body(): lax.dot_general(far_rows, grad_logits, contract, preferred_element_type=j...  8.35 us
    dot_general x1, matrix products, body(): jnp.dot(near_normed, near_rows, preferred_element_type=jnp.float32)  8.13 us
  transfers between devices with their start and end apart: 23, of which 15 were waited for; matrix products, arithmetic and copies ran while one was open for 15% of the time, Pallas kernels for 0%

profile of v10, /device:TPU:0, one launch (start us, length us, event | category | flops | bytes accessed | tf_op | source)
XLA Modules:
  0.0 158.7 jit_solution(8822358135575179353)
XLA Ops:
  4.7 1.5 fusion.14
  7.3 6.0 %collective-permute-start = (bf16[2,80,512]{2,1,0:T(8,128)(2,1)}, bf16[2,80,512]{2,1,0:T(8,128)(2,1)}, u32[]{:S(2)}, u32[]{:S(2)}) collective-permute-start(bf16[2,80,512]{2,1,0:T(8,128)(2,1)} %get-tuple-element.51), channel_id=1, source_target_pairs={{0,28},{4,0},{8,4},{12,8},{16,12},{20,16},{24,20},{28,24},{1,29},{... | collective-permute-start | bytes 491528 | tf_op jit(solution)/shard_map/ppermute | solution.py:162
  13.3 2.5 %collective-permute-start.4 = (bf16[2,80,512]{2,1,0:T(8,128)(2,1)}, bf16[2,80,512]{2,1,0:T(8,128)(2,1)}, u32[]{:S(2)}, u32[]{:S(2)}) collective-permute-start(bf16[2,80,512]{2,1,0:T(8,128)(2,1)} %get-tuple-element.47), channel_id=1, source_target_pairs={{0,12},{4,16},{8,20},{12,24},{16,28},{20,0},{24,4},{28,8},{1,13},{... | collective-permute-start | bytes 491528 | tf_op jit(solution)/shard_map/ppermute | solution.py:162
  15.8 2.8 %collective-permute-start.3 = (bf16[2,80,512]{2,1,0:T(8,128)(2,1)}, bf16[2,80,512]{2,1,0:T(8,128)(2,1)}, u32[]{:S(2)}, u32[]{:S(2)}) collective-permute-start(bf16[2,80,512]{2,1,0:T(8,128)(2,1)} %get-tuple-element.48), channel_id=1, source_target_pairs={{0,16},{4,20},{8,24},{12,28},{16,0},{20,4},{24,8},{28,12},{1,17},{... | collective-permute-start | bytes 491528 | tf_op jit(solution)/shard_map/ppermute | solution.py:162
  19.3 2.9 %convolution_convert_fusion.1 = bf16[128,512]{1,0:T(8,128)(2,1)S(1)} fusion(bf16[128,4096]{1,0:T(8,128)(2,1)S(1)} %copy-done, bf16[4096,512]{1,0:T(8,128)(2,1)} %param.12), kind=kOutput, calls=%fused_computation.18 | convolution fusion | flops 536936448 | bytes 5373952 | tf_op jit(solution)/shard_map/dot_general | solution.py:148
  22.3 1.2 fusion.87
  23.8 1.5 fusion.21
  25.3 1.5 fusion.31
  26.8 2.8 %collective-permute-start.1 = (bf16[2,80,512]{2,1,0:T(8,128)(2,1)S(1)}, bf16[2,80,512]{2,1,0:T(8,128)(2,1)S(1)}, u32[]{:S(2)}, u32[]{:S(2)}) collective-permute-start(bf16[2,80,512]{2,1,0:T(8,128)(2,1)S(1)} %copy-done.5), channel_id=1, source_target_pairs={{0,24},{4,28},{8,0},{12,4},{16,8},{20,12},{24,16},{28,20},{1,25},{... | collective-permute-start | bytes 491528 | tf_op jit(solution)/shard_map/ppermute | solution.py:162
  29.6 1.3 fusion.80
  31.0 1.3 fusion.81
  32.3 3.9 %collective-permute-done.4 = bf16[2,80,512]{2,1,0:T(8,128)(2,1)} collective-permute-done((bf16[2,80,512]{2,1,0:T(8,128)(2,1)}, bf16[2,80,512]{2,1,0:T(8,128)(2,1)}, u32[]{:S(2)}, u32[]{:S(2)}) %collective-permute-start.4) | collective-permute-done | bytes 163872 | tf_op jit(solution)/shard_map/ppermute | solution.py:162
  36.2 1.3 fusion.82
  37.5 1.3 fusion.83
  42.0 1.4 fusion.33
  43.4 1.4 fusion.39
  44.8 1.4 fusion.41
  46.2 1.4 fusion.43
  47.7 2.0 %add_divide_fusion = f32[1024,512]{1,0:T(8,128)S(1)} fusion(f32[1024,512]{1,0:T(8,128)S(1)} %fusion.43, f32[1024,512]{1,0:T(8,128)S(1)} %fusion.41, f32[1024,512]{1,0:T(8,128)S(1)} %fusion.39, f32[1024,512]{1,0:T(8,128)S(1)} %fusion.37, f32[1024,512]{1,0:T(8,128)S(1)} %fusion.35, f32[1024,512]{1,0:T(8,128)S(1)} %fusion.31, f32[1024,512]{1,0:T(8,128)S(1)} %fusion.33, ...), kind=kOutput, calls=%fused_computation.15 | convolution fusion | flops 88326144 | bytes 17199424 | tf_op jit(solution)/shard_map/dot_general | solution.py:172
  50.6 3.0 %reshape.381 = f32[128,2,2,1024]{3,2,1,0:T(2,128)} reshape(f32[128,4096]{1,0:T(8,128)S(1)} %fusion.130) | data formatting | bytes 4194304 | tf_op jit(solution)/shard_map/reshape | solution.py:26
  53.7 4.4 %constant_dynamic-slice_fusion.2 = (f32[128,2,1,1024]{3,2,1,0:T(1,128)S(1)}, f32[128,2,1,1024]{3,2,1,0:T(1,128)S(1)}) fusion(f32[128,2,2,1024]{3,2,1,0:T(2,128)} %reshape.381, s32[]{:T(128)S(6)} %select_n.284, s32[]{:T(128)S(6)} %select_n.285), kind=kLoop, calls=%fused_computation.179 | loop fusion | bytes 4194312 | tf_op jit(solution)/shard_map/jit(dynamic_index_in_dim)/dynamic_slice | solution.py:28
  58.0 2.0 %copy.30 = f32[128,2,1,1024]{0,3,1,2:T(8,128)} copy(f32[128,2,1,1024]{3,2,1,0:T(1,128)S(1)} %get-tuple-element.44) | data formatting | bytes 2097152 | tf_op jit(solution)/shard_map/jit(dynamic_index_in_dim)/dynamic_slice | solution.py:29
  60.8 2.2 %collective-permute-done.7 = f32[128,2,1024]{0,2,1:T(8,128)} collective-permute-done((f32[128,2,1024]{0,2,1:T(8,128)}, f32[128,2,1024]{0,2,1:T(8,128)}, u32[]{:S(2)}, u32[]{:S(2)}) %collective-permute-start.7) | collective-permute-done | bytes 1048608 | tf_op jit(solution)/shard_map/ppermute | solution.py:16
  63.0 1.3 bitcast_add_fusion
  65.4 1.6 collective-permute-start.8
  67.9 5.9 %collective-permute-done.8 = bf16[128,1,1024]{0,2,1:T(8,128)(2,1)S(1)} collective-permute-done((bf16[128,1,1024]{0,2,1:T(8,128)(2,1)S(1)}, bf16[128,1,1024]{0,2,1:T(8,128)(2,1)S(1)}, u32[]{:S(2)}, u32[]{:S(2)}) %collective-permute-start.8) | collective-permute-done | bytes 262176 | tf_op jit(solution)/shard_map/ppermute | solution.py:16
  73.8 1.2 multiply_reduce_fusion.1
  75.8 1.0 collective-permute-done.11
  76.8 1.5 collective-permute-start.12
  79.2 1.2 collective-permute-done.12
  80.3 8.1 %fusion.6 = f32[128,4096]{1,0:T(8,128)S(1)} fusion(bf16[128,2048]{0,1:T(8,128)(2,1)S(1)} %bitcast.252, bf16[4096,4096]{1,0:T(8,128)(2,1)} %param.16, s32[]{:T(128)S(6)} %select_n.291), kind=kOutput, calls=%fused_computation.6 | convolution fusion | flops 2147483648 | bytes 19398660 | tf_op jit(solution)/shard_map/dot_general | solution.py:197
  88.5 3.9 %collective-permute-done.10 = bf16[128,2048]{0,1:T(8,128)(2,1)S(1)} collective-permute-done((bf16[128,2048]{0,1:T(8,128)(2,1)S(1)}, bf16[128,2048]{0,1:T(8,128)(2,1)S(1)}, u32[]{:S(2)}, u32[]{:S(2)}) %collective-permute-start.10) | collective-permute-done | bytes 524320 | tf_op jit(solution)/shard_map/ppermute | solution.py:16
  92.3 8.4 %fusion.129 = (f32[128]{0:T(128)S(1)}, f32[128,4096]{1,0:T(8,128)S(1)}) fusion(f32[128]{0:T(128)S(1)} %add_rsqrt_fusion, f32[128,4096]{1,0:T(8,128)S(1)} %fusion.6, bf16[128,2048]{0,1:T(8,128)(2,1)S(1)} %collective-permute-done.10, bf16[4096,4096]{1,0:T(8,128)(2,1)} %param.16, s32[]{:T(128)S(6)} %select_n.292), kind=kOutput, calls=%fused_computation.271 | convolution fusion | flops 2149056512 | bytes 21496836 | tf_op jit(solution)/shard_map/dot_general | solution.py:198
  101.5 1.1 collective-permute-done.13
  103.3 3.1 %collective-permute-done.14 = f32[3,128]{1,0:T(4,128)S(1)} collective-permute-done((f32[3,128]{1,0:T(4,128)S(1)}, f32[3,128]{1,0:T(4,128)S(1)}, u32[]{:S(2)}, u32[]{:S(2)}) %collective-permute-start.14) | collective-permute-done | bytes 1568 | tf_op jit(solution)/shard_map/ppermute | solution.py:16
  107.6 8.4 %fusion = f32[2048,128]{1,0:T(8,128)S(1)} fusion(bf16[128,4096]{1,0:T(8,128)(2,1)S(1)} %multiply_convert_fusion, bf16[4096,4096]{1,0:T(8,128)(2,1)} %param.16, s32[]{:T(128)S(6)} %select_n.292), kind=kOutput, calls=%fused_computation | convolution fusion | flops 2147483648 | bytes 18874372 | tf_op jit(solution)/shard_map/dot_general | solution.py:218
  116.1 1.9 %collective-permute-done.15 = f32[1,1024,128]{2,1,0:T(8,128)S(1)} collective-permute-done((f32[1,1024,128]{2,1,0:T(8,128)S(1)}, f32[1,1024,128]{2,1,0:T(8,128)S(1)}, u32[]{:S(2)}, u32[]{:S(2)}) %collective-permute-start.15) | collective-permute-done | bytes 524320 | tf_op jit(solution)/shard_map/ppermute | solution.py:16
  118.1 8.1 %fusion.4 = f32[2048,128]{1,0:T(8,128)S(1)} fusion(bf16[128,4096]{1,0:T(8,128)(2,1)S(1)} %multiply_convert_fusion, bf16[4096,4096]{1,0:T(8,128)(2,1)} %param.16, s32[]{:T(128)S(6)} %select_n.291), kind=kOutput, calls=%fused_computation.4 | convolution fusion | flops 2147483648 | bytes 18874372 | tf_op jit(solution)/shard_map/dot_general | solution.py:227
  127.1 8.1 %collective-permute-done.17 = bf16[1024,128]{1,0:T(8,128)(2,1)S(1)} collective-permute-done((bf16[1024,128]{1,0:T(8,128)(2,1)S(1)}, bf16[1024,128]{1,0:T(8,128)(2,1)S(1)}, u32[]{:S(2)}, u32[]{:S(2)}) %collective-permute-start.17) | collective-permute-done | bytes 262176 | tf_op jit(solution)/shard_map/ppermute | solution.py:16
  135.5 1.4 concatenate.3
  136.9 2.4 %collective-permute-start.18 = (f32[1026]{0:T(1024)S(1)}, f32[1026]{0:T(1024)S(1)}, u32[]{:S(2)}, u32[]{:S(2)}) collective-permute-start(f32[1026]{0:T(1024)S(1)} %concatenate.3), channel_id=1, source_target_pairs={{0,4},{4,0},{8,12},{12,8},{16,20},{20,16},{24,28},{28,24},{1,5},{5... | collective-permute-start | bytes 12320 | tf_op jit(solution)/shard_map/ppermute | solution.py:16
  139.3 1.6 %collective-permute-done.18 = f32[1026]{0:T(1024)S(1)} collective-permute-done((f32[1026]{0:T(1024)S(1)}, f32[1026]{0:T(1024)S(1)}, u32[]{:S(2)}, u32[]{:S(2)}) %collective-permute-start.18) | collective-permute-done | bytes 4136 | tf_op jit(solution)/shard_map/ppermute | solution.py:16
  140.9 5.4 %collective-permute-start.19 = (f32[1026]{0:T(1024)S(1)}, f32[1026]{0:T(1024)S(1)}, u32[]{:S(2)}, u32[]{:S(2)}) collective-permute-start(f32[1026]{0:T(1024)S(1)} %add.324), channel_id=1, source_target_pairs={{0,8},{4,12},{8,0},{12,4},{16,24},{20,28},{24,16},{28,20},{1,9},{5... | collective-permute-start | bytes 12320 | tf_op jit(solution)/shard_map/ppermute | solution.py:16
  146.3 1.1 collective-permute-done.21
  147.9 1.2 collective-permute-start.20
  149.1 1.9 %collective-permute-done.22 = f32[128]{0:T(128)S(1)} collective-permute-done((f32[128]{0:T(128)S(1)}, f32[128]{0:T(128)S(1)}, u32[]{:S(2)}, u32[]{:S(2)}) %collective-permute-start.22) | collective-permute-done | bytes 544 | tf_op jit(solution)/shard_map/ppermute | solution.py:16
  151.0 1.5 collective-permute-done.20
  153.2 1.3 slice_divide_fusion
  (109 shorter events, 21.5 us)
Async XLA Ops:
  0.6 18.7 %copy-start = (bf16[128,4096]{1,0:T(8,128)(2,1)S(1)}, bf16[128,4096]{1,0:T(8,128)(2,1)}, u32[]{:S(2)}) copy-start(bf16[128,4096]{1,0:T(8,128)(2,1)} %param.11) | copy-start | bytes 3145732
  7.3 16.3 %collective-permute-start = (bf16[2,80,512]{2,1,0:T(8,128)(2,1)}, bf16[2,80,512]{2,1,0:T(8,128)(2,1)}, u32[]{:S(2)}, u32[]{:S(2)}) collective-permute-start(bf16[2,80,512]{2,1,0:T(8,128)(2,1)} %get-tuple-element.51), channel_id=1, source_target_pairs={{0,28},{4,0},{8,4},{12,8},{16,12},{20,16},{24,20},{28,24},{1,29},{... | collective-permute-start | bytes 491528 | tf_op jit(solution)/shard_map/ppermute | solution.py:162
  13.3 13.5 %collective-permute-start.6 = (bf16[2,80,512]{2,1,0:T(8,128)(2,1)}, bf16[2,80,512]{2,1,0:T(8,128)(2,1)}, u32[]{:S(2)}, u32[]{:S(2)}) collective-permute-start(bf16[2,80,512]{2,1,0:T(8,128)(2,1)} %get-tuple-element.45), channel_id=1, source_target_pairs={{0,4},{4,8},{8,12},{12,16},{16,20},{20,24},{24,28},{28,0},{1,5},{5... | collective-permute-start | bytes 491528 | tf_op jit(solution)/shard_map/ppermute | solution.py:162
  13.3 17.7 %collective-permute-start.5 = (bf16[2,80,512]{2,1,0:T(8,128)(2,1)}, bf16[2,80,512]{2,1,0:T(8,128)(2,1)}, u32[]{:S(2)}, u32[]{:S(2)}) collective-permute-start(bf16[2,80,512]{2,1,0:T(8,128)(2,1)} %get-tuple-element.46), channel_id=1, source_target_pairs={{0,8},{4,12},{8,16},{12,20},{16,24},{20,28},{24,0},{28,4},{1,9},{5... | collective-permute-start | bytes 491528 | tf_op jit(solution)/shard_map/ppermute | solution.py:162
  13.3 22.9 %collective-permute-start.4 = (bf16[2,80,512]{2,1,0:T(8,128)(2,1)}, bf16[2,80,512]{2,1,0:T(8,128)(2,1)}, u32[]{:S(2)}, u32[]{:S(2)}) collective-permute-start(bf16[2,80,512]{2,1,0:T(8,128)(2,1)} %get-tuple-element.47), channel_id=1, source_target_pairs={{0,12},{4,16},{8,20},{12,24},{16,28},{20,0},{24,4},{28,8},{1,13},{... | collective-permute-start | bytes 491528 | tf_op jit(solution)/shard_map/ppermute | solution.py:162
  15.8 21.8 %collective-permute-start.3 = (bf16[2,80,512]{2,1,0:T(8,128)(2,1)}, bf16[2,80,512]{2,1,0:T(8,128)(2,1)}, u32[]{:S(2)}, u32[]{:S(2)}) collective-permute-start(bf16[2,80,512]{2,1,0:T(8,128)(2,1)} %get-tuple-element.48), channel_id=1, source_target_pairs={{0,16},{4,20},{8,24},{12,28},{16,0},{20,4},{24,8},{28,12},{1,17},{... | collective-permute-start | bytes 491528 | tf_op jit(solution)/shard_map/ppermute | solution.py:162
  22.2 1.3 copy-start.7
  23.6 15.3 %collective-permute-start.2 = (bf16[2,80,512]{2,1,0:T(8,128)(2,1)}, bf16[2,80,512]{2,1,0:T(8,128)(2,1)S(1)}, u32[]{:S(2)}, u32[]{:S(2)}) collective-permute-start(bf16[2,80,512]{2,1,0:T(8,128)(2,1)} %get-tuple-element.49), channel_id=1, source_target_pairs={{0,20},{4,24},{8,28},{12,0},{16,4},{20,8},{24,12},{28,16},{1,21},{... | collective-permute-start | bytes 491528 | tf_op jit(solution)/shard_map/ppermute | solution.py:162
  23.8 3.0 %copy-start.5 = (bf16[2,80,512]{2,1,0:T(8,128)(2,1)S(1)}, bf16[2,80,512]{2,1,0:T(8,128)(2,1)}, u32[]{:S(2)}) copy-start(bf16[2,80,512]{2,1,0:T(8,128)(2,1)} %get-tuple-element.50) | copy-start | bytes 491524
  26.8 13.0 %collective-permute-start.1 = (bf16[2,80,512]{2,1,0:T(8,128)(2,1)S(1)}, bf16[2,80,512]{2,1,0:T(8,128)(2,1)S(1)}, u32[]{:S(2)}, u32[]{:S(2)}) collective-permute-start(bf16[2,80,512]{2,1,0:T(8,128)(2,1)S(1)} %copy-done.5), channel_id=1, source_target_pairs={{0,24},{4,28},{8,0},{12,4},{16,8},{20,12},{24,16},{28,20},{1,25},{... | collective-permute-start | bytes 491528 | tf_op jit(solution)/shard_map/ppermute | solution.py:162
  32.3 7.5 %copy-start.4 = (f32[1024,80]{0,1:T(8,128)S(1)}, f32[1024,80]{0,1:T(8,128)}, u32[]{:S(2)}) copy-start(f32[1024,80]{0,1:T(8,128)} %fusion.87) | copy-start | bytes 983044
  47.7 2.2 %copy-start.2 = (bf16[512,4096]{1,0:T(8,128)(2,1)S(1)}, bf16[512,4096]{1,0:T(8,128)(2,1)}, u32[]{:S(2)}) copy-start(bf16[512,4096]{1,0:T(8,128)(2,1)} %param.14) | copy-start | bytes 12582916
  60.0 3.0 %collective-permute-start.7 = (f32[128,2,1024]{0,2,1:T(8,128)}, f32[128,2,1024]{0,2,1:T(8,128)}, u32[]{:S(2)}, u32[]{:S(2)}) collective-permute-start(f32[128,2,1024]{0,2,1:T(8,128)} %bitcast.250), channel_id=1, source_target_pairs={{0,1},{1,0},{2,3},{3,2},{4,5},{5,4},{6,7},{7,6},{8,9},{9,8},{10,11... | collective-permute-start | bytes 3145736 | tf_op jit(solution)/shard_map/ppermute | solution.py:16
  64.4 1.0 copy-start.3
  65.3 9.9 %copy-start.8 = (s32[128]{0:T(128)S(1)}, s32[128]{0:T(128)}, u32[]{:S(2)}) copy-start(s32[128]{0:T(128)} %param.20) | copy-start | bytes 1540
  65.4 8.4 %collective-permute-start.8 = (bf16[128,1,1024]{0,2,1:T(8,128)(2,1)S(1)}, bf16[128,1,1024]{0,2,1:T(8,128)(2,1)S(1)}, u32[]{:S(2)}, u32[]{:S(2)}) collective-permute-start(bf16[128,1,1024]{0,2,1:T(8,128)(2,1)S(1)} %dynamic-slice_convert_fusion), channel_id=1, source_target_pairs={{0,2},{1,3},{2,0},{3,1},{4,6},{5,7},{6,4},{7,5},{8,10},{9,11},{10,... | collective-permute-start | bytes 786440 | tf_op jit(solution)/shard_map/ppermute | solution.py:16
  75.2 3.1 %collective-permute-start.9 = (bf16[128,1,1024]{0,2,1:T(8,128)(2,1)S(1)}, bf16[128,1,1024]{0,2,1:T(8,128)(2,1)S(1)}, u32[]{:S(2)}, u32[]{:S(2)}) collective-permute-start(bf16[128,1,1024]{0,2,1:T(8,128)(2,1)S(1)} %fusion.29), channel_id=1, source_target_pairs={{0,1},{1,0},{2,3},{3,2},{4,5},{5,4},{6,7},{7,6},{8,9},{9,8},{10,11... | collective-permute-start | bytes 786440 | tf_op jit(solution)/shard_map/ppermute | solution.py:16
  75.3 1.5 collective-permute-start.11
  76.8 3.5 %collective-permute-start.12 = (f32[128]{0:T(128)S(1)}, f32[128]{0:T(128)S(1)}, u32[]{:S(2)}, u32[]{:S(2)}) collective-permute-start(f32[128]{0:T(128)S(1)} %add.310), channel_id=1, source_target_pairs={{0,2},{1,3},{2,0},{3,1},{4,6},{5,7},{6,4},{7,5},{8,10},{9,11},{10,... | collective-permute-start | bytes 1544 | tf_op jit(solution)/shard_map/ppermute | solution.py:16
  78.6 13.8 %collective-permute-start.10 = (bf16[128,2048]{0,1:T(8,128)(2,1)S(1)}, bf16[128,2048]{0,1:T(8,128)(2,1)S(1)}, u32[]{:S(2)}, u32[]{:S(2)}) collective-permute-start(bf16[128,2048]{0,1:T(8,128)(2,1)S(1)} %bitcast.251), channel_id=1, source_target_pairs={{0,2},{1,3},{2,0},{3,1},{4,6},{5,7},{6,4},{7,5},{8,10},{9,11},{10,... | collective-permute-start | bytes 1572872 | tf_op jit(solution)/shard_map/ppermute | solution.py:16
  100.7 2.6 %copy-start.6 = (s32[128]{0:T(128)S(1)}, s32[128]{0:T(128)}, u32[]{:S(2)}) copy-start(s32[128]{0:T(128)} %param.21) | copy-start | bytes 1540
  101.5 1.2 collective-permute-start.13
  102.7 3.7 %collective-permute-start.14 = (f32[3,128]{1,0:T(4,128)S(1)}, f32[3,128]{1,0:T(4,128)S(1)}, u32[]{:S(2)}, u32[]{:S(2)}) collective-permute-start(f32[3,128]{1,0:T(4,128)S(1)} %pad_maximum_fusion.2), channel_id=1, source_target_pairs={{0,2},{1,3},{2,0},{3,1},{4,6},{5,7},{6,4},{7,5},{8,10},{9,11},{10,... | collective-permute-start | bytes 4616 | tf_op jit(solution)/shard_map/ppermute | solution.py:16
  116.1 2.0 %collective-permute-start.15 = (f32[1,1024,128]{2,1,0:T(8,128)S(1)}, f32[1,1024,128]{2,1,0:T(8,128)S(1)}, u32[]{:S(2)}, u32[]{:S(2)}) collective-permute-start(f32[1,1024,128]{2,1,0:T(8,128)S(1)} %dynamic-slice_bitcast_fusion.1), channel_id=1, source_target_pairs={{0,1},{1,0},{2,3},{3,2},{4,5},{5,4},{6,7},{7,6},{8,9},{9,8},{10,11... | collective-permute-start | bytes 1572872 | tf_op jit(solution)/shard_map/ppermute | solution.py:16
  126.3 31.3 %copy-start.1 = (bf16[128,4096]{1,0:T(8,128)(2,1)S(1)}, bf16[128,4096]{1,0:T(8,128)(2,1)}, u32[]{:S(2)}) copy-start(bf16[128,4096]{1,0:T(8,128)(2,1)} %param.11) | copy-start | bytes 3145732
  126.3 8.8 %collective-permute-start.16 = (f32[1,1024,128]{2,1,0:T(8,128)S(1)}, f32[1,1024,128]{2,1,0:T(8,128)S(1)}, u32[]{:S(2)}, u32[]{:S(2)}) collective-permute-start(f32[1,1024,128]{2,1,0:T(8,128)S(1)} %dynamic-slice_bitcast_fusion), channel_id=1, source_target_pairs={{0,1},{1,0},{2,3},{3,2},{4,5},{5,4},{6,7},{7,6},{8,9},{9,8},{10,11... | collective-permute-start | bytes 1572872 | tf_op jit(solution)/shard_map/ppermute | solution.py:16
  126.5 8.6 %collective-permute-start.17 = (bf16[1024,128]{1,0:T(8,128)(2,1)S(1)}, bf16[1024,128]{1,0:T(8,128)(2,1)S(1)}, u32[]{:S(2)}, u32[]{:S(2)}) collective-permute-start(bf16[1024,128]{1,0:T(8,128)(2,1)S(1)} %fusion.18), channel_id=1, source_target_pairs={{0,2},{1,3},{2,0},{3,1},{4,6},{5,7},{6,4},{7,5},{8,10},{9,11},{10,... | collective-permute-start | bytes 786440 | tf_op jit(solution)/shard_map/ppermute | solution.py:16
  136.9 4.0 %collective-permute-start.18 = (f32[1026]{0:T(1024)S(1)}, f32[1026]{0:T(1024)S(1)}, u32[]{:S(2)}, u32[]{:S(2)}) collective-permute-start(f32[1026]{0:T(1024)S(1)} %concatenate.3), channel_id=1, source_target_pairs={{0,4},{4,0},{8,12},{12,8},{16,20},{20,16},{24,28},{28,24},{1,5},{5... | collective-permute-start | bytes 12320 | tf_op jit(solution)/shard_map/ppermute | solution.py:16
  140.9 7.1 %collective-permute-start.19 = (f32[1026]{0:T(1024)S(1)}, f32[1026]{0:T(1024)S(1)}, u32[]{:S(2)}, u32[]{:S(2)}) collective-permute-start(f32[1026]{0:T(1024)S(1)} %add.324), channel_id=1, source_target_pairs={{0,8},{4,12},{8,0},{12,4},{16,24},{20,28},{24,16},{28,20},{1,9},{5... | collective-permute-start | bytes 12320 | tf_op jit(solution)/shard_map/ppermute | solution.py:16
  146.3 1.1 collective-permute-start.21
  147.4 3.5 %collective-permute-start.22 = (f32[128]{0:T(128)S(1)}, f32[128]{0:T(128)S(1)}, u32[]{:S(2)}, u32[]{:S(2)}) collective-permute-start(f32[128]{0:T(128)S(1)} %add.327), channel_id=1, source_target_pairs={{0,2},{1,3},{2,0},{3,1},{4,6},{5,7},{6,4},{7,5},{8,10},{9,11},{10,... | collective-permute-start | bytes 1544 | tf_op jit(solution)/shard_map/ppermute | solution.py:16
  147.9 4.6 %collective-permute-start.20 = (f32[1026]{0:T(1024)S(1)}, f32[1026]{0:T(1024)S(1)}, u32[]{:S(2)}, u32[]{:S(2)}) collective-permute-start(f32[1026]{0:T(1024)S(1)} %add.325), channel_id=1, source_target_pairs={{0,16},{4,20},{8,24},{12,28},{16,0},{20,4},{24,8},{28,12},{1,17},{... | collective-permute-start | bytes 12320 | tf_op jit(solution)/shard_map/ppermute | solution.py:16

commit v11 on v9

--- a/solution.py
+++ b/solution.py
@@ -177,10 +177,25 @@
     feature_start = fsdp_index * feature_count
     gain_part = lax.dynamic_slice_in_dim(norm_gain, feature_start, feature_count, 0)
     hidden_part = lax.dynamic_slice_in_dim(dec_hidden, feature_start, feature_count, 1)
-    projected = jnp.dot(attended, w_out, preferred_element_type=jnp.float32)
-    if split_fsdp:
+    if levels == 2:
+        quarter = width // 4
+        low_bit, high_bit = fsdp_index & 1, fsdp_index >> 1
+
+        def chunk_product(chunk):
+            columns = lax.dynamic_slice_in_dim(w_out, chunk * quarter, quarter, 1)
+            return jnp.dot(attended, columns, preferred_element_type=jnp.float32)
+
+        sent = jnp.stack([chunk_product(1 - low_bit), chunk_product(3 - low_bit)])
+        kept = jnp.stack([chunk_product(low_bit), chunk_product(2 + low_bit)])
+        kept = kept + exchange(sent, "fsdp", 0)
+        mine = lax.dynamic_index_in_dim(kept, high_bit, 0, keepdims=False)
+        other = lax.dynamic_index_in_dim(kept, 1 - high_bit, 0, keepdims=False)
+        projected = mine + exchange(other.astype(jnp.bfloat16), "fsdp", 1).astype(jnp.float32)
+    elif split_fsdp:
+        projected = jnp.dot(attended, w_out, preferred_element_type=jnp.float32)
         projected = scatter_bits(projected, "fsdp", 1, levels, jnp.bfloat16)
     else:
+        projected = jnp.dot(attended, w_out, preferred_element_type=jnp.float32)
         projected = lax.psum_scatter(projected, "fsdp", scatter_dimension=1, tiled=True)
     summed_part = projected + hidden_part.astype(jnp.float32)
     square_total = sum_all(jnp.sum(summed_part * summed_part, 1), "fsdp")

time: 147 us -> 141 us (0.959)
  starting transfers between devices: 22.1 us -> 31.2 us
  local copies, waits for them, and re-layouts: 16.8 us -> 8.95 us
  waiting for transfers between devices: 48.4 us -> 40.8 us
  matrix products: 40.6 us -> 43 us
    ppermute x16, starting transfers between devices: 9.4 us -> 16.7 us  [exchange(): return lax.ppermute(x, axis, [(i, i ^ 1 << bit) for i in range(size)])]
    dot_general x1 -> x0, local copies, waits for them, and re-layouts: 6.47 us -> none  [body(): projected = jnp.dot(attended, w_out, preferred_element_type=jnp.float32)]
    ppermute x16, waiting for transfers between devices: 37.2 us -> 32 us  [exchange(): return lax.ppermute(x, axis, [(i, i ^ 1 << bit) for i in range(size)])]
    ppermute x7, waiting for transfers between devices: 11.2 us -> 8.82 us  [body(): lax.ppermute(block, 'dp', [(i, (i - shift) % dp_count) for i in range(dp_...]
    dot_general x1 -> x4, matrix products: 1.49 us -> 3.77 us  [chunk_product(): return jnp.dot(attended, columns, preferred_element_type=jnp.float32)]
    ppermute x7, starting transfers between devices: 12.7 us -> 14.5 us  [body(): lax.ppermute(block, 'dp', [(i, (i - shift) % dp_count) for i in range(dp_...]
  transfers between devices with their start and end apart: 23 -> 23, of which waited for: 15 -> 13; matrix products, arithmetic and copies ran while one was open for 14% -> 13% of each run, Pallas kernels for 0% -> 0%
where the time goes in v11:
time: 141 us
  matrix products  43 us (30%)
  waiting for transfers between devices  40.8 us (29%)
  starting transfers between devices  31.2 us (22%)
  other arithmetic  12.7 us (9%)
  local copies, waits for them, and re-layouts  8.95 us (6%)
  between operations  3.99 us (3%)
    ppermute x16, waiting for transfers between devices, exchange(): return lax.ppermute(x, axis, [(i, i ^ 1 << bit) for i in range(size)])  32 us
    ppermute x16, starting transfers between devices, exchange(): return lax.ppermute(x, axis, [(i, i ^ 1 << bit) for i in range(size)])  16.7 us
    ppermute x7, starting transfers between devices, body(): lax.ppermute(block, 'dp', [(i, (i - shift) % dp_count) for i in range(dp_...  14.5 us
    ppermute x7, waiting for transfers between devices, body(): lax.ppermute(block, 'dp', [(i, (i - shift) % dp_count) for i in range(dp_...  8.82 us
    dot_general x1, matrix products, body(): lax.dot_general(far_rows, grad_logits, contract, preferred_element_type=j...  8.48 us
    dot_general x1, matrix products, body(): jnp.dot(far_normed, far_rows, preferred_element_type=jnp.float32)  8.39 us
    dot_general x1, matrix products, body(): lax.dot_general(near_rows, near_logits, contract, preferred_element_type=...  8.13 us
    dot_general x1, matrix products, body(): jnp.dot(near_normed, near_rows, preferred_element_type=jnp.float32)  8.13 us
  transfers between devices with their start and end apart: 23, of which 13 were waited for; matrix products, arithmetic and copies ran while one was open for 13% of the time, Pallas kernels for 0%

profile of v11, /device:TPU:0, one launch (start us, length us, event | category | flops | bytes accessed | tf_op | source)
XLA Modules:
  0.0 140.8 jit_solution(10164244305356378451)
XLA Ops:
  0.7 0.8 fusion.84
  1.7 0.8 select_reduce_fusion.11
  2.5 0.8 lt.80
  3.4 1.0 select_reduce_fusion.19
  5.5 5.1 %collective-permute-start.1 = (bf16[2,80,512]{2,1,0:T(8,128)(2,1)S(1)}, bf16[2,80,512]{2,1,0:T(8,128)(2,1)S(1)}, u32[]{:S(2)}, u32[]{:S(2)}) collective-permute-start(bf16[2,80,512]{2,1,0:T(8,128)(2,1)S(1)} %get-tuple-element.21), channel_id=1, source_target_pairs={{0,24},{4,28},{8,0},{12,4},{16,8},{20,12},{24,16},{28,20},{1,25},{... | collective-permute-start | bytes 491528 | tf_op jit(solution)/shard_map/ppermute | solution.py:157
  10.6 1.5 %collective-permute-start.6 = (bf16[2,80,512]{2,1,0:T(8,128)(2,1)S(1)}, bf16[2,80,512]{2,1,0:T(8,128)(2,1)S(1)}, u32[]{:S(2)}, u32[]{:S(2)}) collective-permute-start(bf16[2,80,512]{2,1,0:T(8,128)(2,1)S(1)} %get-tuple-element.22), channel_id=1, source_target_pairs={{0,4},{4,8},{8,12},{12,16},{16,20},{20,24},{24,28},{28,0},{1,5},{5... | collective-permute-start | bytes 491528 | tf_op jit(solution)/shard_map/ppermute | solution.py:157
  12.1 1.0 collective-permute-start.4
  13.1 2.8 %collective-permute-start.3 = (bf16[2,80,512]{2,1,0:T(8,128)(2,1)S(1)}, bf16[2,80,512]{2,1,0:T(8,128)(2,1)S(1)}, u32[]{:S(2)}, u32[]{:S(2)}) collective-permute-start(bf16[2,80,512]{2,1,0:T(8,128)(2,1)S(1)} %get-tuple-element.25), channel_id=1, source_target_pairs={{0,16},{4,20},{8,24},{12,28},{16,0},{20,4},{24,8},{28,12},{1,17},{... | collective-permute-start | bytes 491528 | tf_op jit(solution)/shard_map/ppermute | solution.py:157
  16.8 2.0 %convolution_convert_fusion.1 = bf16[128,512]{1,0:T(8,128)(2,1)S(1)} fusion(bf16[128,4096]{1,0:T(8,128)(2,1)} %param.11, bf16[4096,512]{1,0:T(8,128)(2,1)S(1)} %copy-done.3), kind=kOutput, calls=%fused_computation.29 | convolution fusion | flops 536936448 | bytes 5373952 | tf_op jit(solution)/shard_map/dot_general | solution.py:148
  19.9 1.1 collective-permute-start.2
  21.2 3.1 %collective-permute-start = (bf16[2,80,512]{2,1,0:T(8,128)(2,1)S(1)}, bf16[2,80,512]{2,1,0:T(8,128)(2,1)S(1)}, u32[]{:S(2)}, u32[]{:S(2)}) collective-permute-start(bf16[2,80,512]{2,1,0:T(8,128)(2,1)S(1)} %get-tuple-element.27), channel_id=1, source_target_pairs={{0,28},{4,0},{8,4},{12,8},{16,12},{20,16},{24,20},{28,24},{1,29},{... | collective-permute-start | bytes 491528 | tf_op jit(solution)/shard_map/ppermute | solution.py:157
  24.8 8.8 %collective-permute-done.4 = bf16[2,80,512]{2,1,0:T(8,128)(2,1)S(1)} collective-permute-done((bf16[2,80,512]{2,1,0:T(8,128)(2,1)S(1)}, bf16[2,80,512]{2,1,0:T(8,128)(2,1)S(1)}, u32[]{:S(2)}, u32[]{:S(2)}) %collective-permute-start.4) | collective-permute-done | bytes 163872 | tf_op jit(solution)/shard_map/ppermute | solution.py:157
  34.2 0.9 fusion.119
  39.5 1.1 copy-done.2
  41.4 1.6 %convolution_bitcast_fusion.2 = f32[1,128,1024]{2,1,0:T(8,128)S(1)} fusion(bf16[128,512]{0,1:T(8,128)(2,1)S(1)} %bitcast.240, bf16[512,4096]{1,0:T(8,128)(2,1)} %param.14, s32[]{:T(128)S(6)} %select_n.232), kind=kOutput, calls=%fused_computation.18 | convolution fusion | flops 134217728 | bytes 1703940 | tf_op jit(solution)/shard_map/dot_general | solution.py:186
  42.9 1.6 %convolution_bitcast_fusion.3 = f32[1,128,1024]{2,1,0:T(8,128)S(1)} fusion(bf16[128,512]{0,1:T(8,128)(2,1)S(1)} %bitcast.241, bf16[512,4096]{1,0:T(8,128)(2,1)} %param.14, s32[]{:T(128)S(6)} %select_n.231), kind=kOutput, calls=%fused_computation.19 | convolution fusion | flops 134217728 | bytes 1703940 | tf_op jit(solution)/shard_map/dot_general | solution.py:186
  44.7 1.6 %collective-permute-start.8 = (bf16[128,1024]{1,0:T(8,128)(2,1)S(1)}, bf16[128,1024]{1,0:T(8,128)(2,1)S(1)}, u32[]{:S(2)}, u32[]{:S(2)}) collective-permute-start(bf16[128,1024]{1,0:T(8,128)(2,1)S(1)} %fusion.48), channel_id=1, source_target_pairs={{0,2},{1,3},{2,0},{3,1},{4,6},{5,7},{6,4},{7,5},{8,10},{9,11},{10,... | collective-permute-start | bytes 786440 | tf_op jit(solution)/shard_map/ppermute | solution.py:16
  46.3 0.7 dynamic_slice.51
  47.0 6.5 %collective-permute-done.8 = bf16[128,1024]{1,0:T(8,128)(2,1)S(1)} collective-permute-done((bf16[128,1024]{1,0:T(8,128)(2,1)S(1)}, bf16[128,1024]{1,0:T(8,128)(2,1)S(1)}, u32[]{:S(2)}, u32[]{:S(2)}) %collective-permute-start.8) | collective-permute-done | bytes 262176 | tf_op jit(solution)/shard_map/ppermute | solution.py:16
  53.5 1.1 multiply_reduce_fusion.1
  55.3 1.0 collective-permute-done.11
  56.3 1.5 %collective-permute-start.12 = (f32[128]{0:T(128)S(1)}, f32[128]{0:T(128)S(1)}, u32[]{:S(2)}, u32[]{:S(2)}) collective-permute-start(f32[128]{0:T(128)S(1)} %add.343), channel_id=1, source_target_pairs={{0,2},{1,3},{2,0},{3,1},{4,6},{5,7},{6,4},{7,5},{8,10},{9,11},{10,... | collective-permute-start | bytes 1544 | tf_op jit(solution)/shard_map/ppermute | solution.py:16
  58.8 1.1 collective-permute-done.12
  59.8 8.1 %fusion.6 = f32[128,4096]{1,0:T(8,128)S(1)} fusion(bf16[128,2048]{0,1:T(8,128)(2,1)S(1)} %bitcast.256, bf16[4096,4096]{1,0:T(8,128)(2,1)} %param.16, s32[]{:T(128)S(6)} %select_n.240), kind=kOutput, calls=%fused_computation.6 | convolution fusion | flops 2147483648 | bytes 19398660 | tf_op jit(solution)/shard_map/dot_general | solution.py:213
  68.0 4.0 %collective-permute-done.10 = bf16[128,2048]{0,1:T(8,128)(2,1)S(1)} collective-permute-done((bf16[128,2048]{0,1:T(8,128)(2,1)S(1)}, bf16[128,2048]{0,1:T(8,128)(2,1)S(1)}, u32[]{:S(2)}, u32[]{:S(2)}) %collective-permute-start.10) | collective-permute-done | bytes 524320 | tf_op jit(solution)/shard_map/ppermute | solution.py:16
  72.0 8.4 %fusion.125 = (f32[128]{0:T(128)S(1)}, f32[128,4096]{1,0:T(8,128)S(1)}) fusion(f32[128]{0:T(128)S(1)} %add_rsqrt_fusion, f32[128,4096]{1,0:T(8,128)S(1)} %fusion.6, bf16[128,2048]{0,1:T(8,128)(2,1)S(1)} %collective-permute-done.10, bf16[4096,4096]{1,0:T(8,128)(2,1)} %param.16, s32[]{:T(128)S(6)} %select_n.241), kind=kOutput, calls=%fused_computation.255 | convolution fusion | flops 2149056512 | bytes 21496836 | tf_op jit(solution)/shard_map/dot_general | solution.py:214
  80.3 0.7 select_reduce_fusion
  81.1 1.1 collective-permute-done.13
  82.3 0.6 collective-permute-start.14
  82.9 3.1 %collective-permute-done.14 = f32[3,128]{1,0:T(4,128)S(1)} collective-permute-done((f32[3,128]{1,0:T(4,128)S(1)}, f32[3,128]{1,0:T(4,128)S(1)}, u32[]{:S(2)}, u32[]{:S(2)}) %collective-permute-start.14) | collective-permute-done | bytes 1568 | tf_op jit(solution)/shard_map/ppermute | solution.py:16
  86.0 0.6 fusion.105
  86.6 0.6 multiply_convert_fusion
  87.3 8.5 %fusion = f32[2048,128]{1,0:T(8,128)S(1)} fusion(bf16[128,4096]{1,0:T(8,128)(2,1)S(1)} %multiply_convert_fusion, bf16[4096,4096]{1,0:T(8,128)(2,1)} %param.16, s32[]{:T(128)S(6)} %select_n.241), kind=kOutput, calls=%fused_computation | convolution fusion | flops 2147483648 | bytes 18874372 | tf_op jit(solution)/shard_map/dot_general | solution.py:234
  96.3 1.8 %collective-permute-done.15 = f32[1,1024,128]{1,2,0:T(8,128)} collective-permute-done((f32[1,1024,128]{1,2,0:T(8,128)S(1)}, f32[1,1024,128]{1,2,0:T(8,128)}, u32[]{:S(2)}, u32[]{:S(2)}) %collective-permute-start.15) | collective-permute-done | bytes 524320 | tf_op jit(solution)/shard_map/ppermute | solution.py:16
  98.2 1.1 fusion.30
  99.3 8.1 %fusion.4 = f32[2048,128]{1,0:T(8,128)S(1)} fusion(bf16[128,4096]{1,0:T(8,128)(2,1)S(1)} %copy-done.5, bf16[4096,4096]{1,0:T(8,128)(2,1)} %param.16, s32[]{:T(128)S(6)} %select_n.240), kind=kOutput, calls=%fused_computation.4 | convolution fusion | flops 2147483648 | bytes 18874372 | tf_op jit(solution)/shard_map/dot_general | solution.py:243
  108.6 7.9 %collective-permute-done.17 = bf16[1024,128]{0,1:T(8,128)(2,1)S(1)} collective-permute-done((bf16[1024,128]{0,1:T(8,128)(2,1)S(1)}, bf16[1024,128]{0,1:T(8,128)(2,1)S(1)}, u32[]{:S(2)}, u32[]{:S(2)}) %collective-permute-start.17) | collective-permute-done | bytes 262176 | tf_op jit(solution)/shard_map/ppermute | solution.py:16
  116.8 1.4 concatenate.3
  118.2 4.3 %collective-permute-start.18 = (f32[1026]{0:T(1024)S(1)}, f32[1026]{0:T(1024)S(1)}, u32[]{:S(2)}, u32[]{:S(2)}) collective-permute-start(f32[1026]{0:T(1024)S(1)} %concatenate.3), channel_id=1, source_target_pairs={{0,4},{4,0},{8,12},{12,8},{16,20},{20,16},{24,28},{28,24},{1,5},{5... | collective-permute-start | bytes 12320 | tf_op jit(solution)/shard_map/ppermute | solution.py:16
  122.5 1.6 %collective-permute-done.18 = f32[1026]{0:T(1024)S(1)} collective-permute-done((f32[1026]{0:T(1024)S(1)}, f32[1026]{0:T(1024)S(1)}, u32[]{:S(2)}, u32[]{:S(2)}) %collective-permute-start.18) | collective-permute-done | bytes 4136 | tf_op jit(solution)/shard_map/ppermute | solution.py:16
  124.1 4.4 %collective-permute-start.19 = (f32[1026]{0:T(1024)S(1)}, f32[1026]{0:T(1024)S(1)}, u32[]{:S(2)}, u32[]{:S(2)}) collective-permute-start(f32[1026]{0:T(1024)S(1)} %add.359), channel_id=1, source_target_pairs={{0,8},{4,12},{8,0},{12,4},{16,24},{20,28},{24,16},{28,20},{1,9},{5... | collective-permute-start | bytes 12320 | tf_op jit(solution)/shard_map/ppermute | solution.py:16
  128.5 1.1 collective-permute-done.21
  130.2 1.7 %collective-permute-start.20 = (f32[1026]{0:T(1024)S(1)}, f32[1026]{0:T(1024)S(1)}, u32[]{:S(2)}, u32[]{:S(2)}) collective-permute-start(f32[1026]{0:T(1024)S(1)} %add.360), channel_id=1, source_target_pairs={{0,16},{4,20},{8,24},{12,28},{16,0},{20,4},{24,8},{28,12},{1,17},{... | collective-permute-start | bytes 12320 | tf_op jit(solution)/shard_map/ppermute | solution.py:16
  131.9 1.3 collective-permute-done.22
  133.2 1.5 %collective-permute-done.20 = f32[1026]{0:T(1024)S(1)} collective-permute-done((f32[1026]{0:T(1024)S(1)}, f32[1026]{0:T(1024)S(1)}, u32[]{:S(2)}, u32[]{:S(2)}) %collective-permute-start.20) | collective-permute-done | bytes 4136 | tf_op jit(solution)/shard_map/ppermute | solution.py:16
  134.7 0.6 fusion.124
  135.3 1.4 slice_divide_fusion
  138.1 1.6 %divide_convert_fusion = bf16[128,1024]{1,0:T(8,128)(2,1)} fusion(f32[1024,128]{0,1:T(8,128)S(1)} %get-tuple-element.17, f32[128,1024]{1,0:T(8,128)S(1)} %get-tuple-element.20, f32[]{:T(128)} %bitcast.70, f32[128]{0:T(128)S(1)} %add_multiply_fusion, f32[128]{0:T(128)S(1)} %add_rsqrt_fusion, f32[1024]{0:T(1024)S(1)} %dynamic_slice.51), kind=kLoop, calls=%fused_computation.51 | loop fusion | flops 917504 | bytes 1315844 | tf_op jit(solution)/shard_map/convert_element_type | solution.py:265
  (139 shorter events, 13.8 us)
Async XLA Ops:
  0.6 4.2 %copy-start = (bf16[2,192,512]{2,1,0:T(8,128)(2,1)S(1)}, bf16[2,192,512]{2,1,0:T(8,128)(2,1)}, u32[]{:S(2)}) copy-start(bf16[2,192,512]{2,1,0:T(8,128)(2,1)} %param.13) | copy-start | bytes 1179652
  0.6 15.5 %copy-start.7 = (s32[128]{0:T(128)S(1)}, s32[128]{0:T(128)}, u32[]{:S(2)}) copy-start(s32[128]{0:T(128)} %param.18) | copy-start | bytes 1540
  3.3 13.5 %copy-start.3 = (bf16[4096,512]{1,0:T(8,128)(2,1)S(1)}, bf16[4096,512]{1,0:T(8,128)(2,1)}, u32[]{:S(2)}) copy-start(bf16[4096,512]{1,0:T(8,128)(2,1)} %param.12) | copy-start | bytes 12582916
  5.5 14.3 %collective-permute-start.1 = (bf16[2,80,512]{2,1,0:T(8,128)(2,1)S(1)}, bf16[2,80,512]{2,1,0:T(8,128)(2,1)S(1)}, u32[]{:S(2)}, u32[]{:S(2)}) collective-permute-start(bf16[2,80,512]{2,1,0:T(8,128)(2,1)S(1)} %get-tuple-element.21), channel_id=1, source_target_pairs={{0,24},{4,28},{8,0},{12,4},{16,8},{20,12},{24,16},{28,20},{1,25},{... | collective-permute-start | bytes 491528 | tf_op jit(solution)/shard_map/ppermute | solution.py:157
  10.6 10.6 %collective-permute-start.6 = (bf16[2,80,512]{2,1,0:T(8,128)(2,1)S(1)}, bf16[2,80,512]{2,1,0:T(8,128)(2,1)S(1)}, u32[]{:S(2)}, u32[]{:S(2)}) collective-permute-start(bf16[2,80,512]{2,1,0:T(8,128)(2,1)S(1)} %get-tuple-element.22), channel_id=1, source_target_pairs={{0,4},{4,8},{8,12},{12,16},{16,20},{20,24},{24,28},{28,0},{1,5},{5... | collective-permute-start | bytes 491528 | tf_op jit(solution)/shard_map/ppermute | solution.py:157
  12.1 12.4 %collective-permute-start.5 = (bf16[2,80,512]{2,1,0:T(8,128)(2,1)S(1)}, bf16[2,80,512]{2,1,0:T(8,128)(2,1)S(1)}, u32[]{:S(2)}, u32[]{:S(2)}) collective-permute-start(bf16[2,80,512]{2,1,0:T(8,128)(2,1)S(1)} %get-tuple-element.23), channel_id=1, source_target_pairs={{0,8},{4,12},{8,16},{12,20},{16,24},{20,28},{24,0},{28,4},{1,9},{5... | collective-permute-start | bytes 491528 | tf_op jit(solution)/shard_map/ppermute | solution.py:157
  12.1 21.5 %collective-permute-start.4 = (bf16[2,80,512]{2,1,0:T(8,128)(2,1)S(1)}, bf16[2,80,512]{2,1,0:T(8,128)(2,1)S(1)}, u32[]{:S(2)}, u32[]{:S(2)}) collective-permute-start(bf16[2,80,512]{2,1,0:T(8,128)(2,1)S(1)} %get-tuple-element.24), channel_id=1, source_target_pairs={{0,12},{4,16},{8,20},{12,24},{16,28},{20,0},{24,4},{28,8},{1,13},{... | collective-permute-start | bytes 491528 | tf_op jit(solution)/shard_map/ppermute | solution.py:157
  13.1 20.8 %collective-permute-start.3 = (bf16[2,80,512]{2,1,0:T(8,128)(2,1)S(1)}, bf16[2,80,512]{2,1,0:T(8,128)(2,1)S(1)}, u32[]{:S(2)}, u32[]{:S(2)}) collective-permute-start(bf16[2,80,512]{2,1,0:T(8,128)(2,1)S(1)} %get-tuple-element.25), channel_id=1, source_target_pairs={{0,16},{4,20},{8,24},{12,28},{16,0},{20,4},{24,8},{28,12},{1,17},{... | collective-permute-start | bytes 491528 | tf_op jit(solution)/shard_map/ppermute | solution.py:157
  19.9 14.3 %collective-permute-start.2 = (bf16[2,80,512]{2,1,0:T(8,128)(2,1)S(1)}, bf16[2,80,512]{2,1,0:T(8,128)(2,1)}, u32[]{:S(2)}, u32[]{:S(2)}) collective-permute-start(bf16[2,80,512]{2,1,0:T(8,128)(2,1)S(1)} %get-tuple-element.26), channel_id=1, source_target_pairs={{0,20},{4,24},{8,28},{12,0},{16,4},{20,8},{24,12},{28,16},{1,21},{... | collective-permute-start | bytes 491528 | tf_op jit(solution)/shard_map/ppermute | solution.py:157
  21.2 14.2 %collective-permute-start = (bf16[2,80,512]{2,1,0:T(8,128)(2,1)S(1)}, bf16[2,80,512]{2,1,0:T(8,128)(2,1)S(1)}, u32[]{:S(2)}, u32[]{:S(2)}) collective-permute-start(bf16[2,80,512]{2,1,0:T(8,128)(2,1)S(1)} %get-tuple-element.27), channel_id=1, source_target_pairs={{0,28},{4,0},{8,4},{12,8},{16,12},{20,16},{24,20},{28,24},{1,29},{... | collective-permute-start | bytes 491528 | tf_op jit(solution)/shard_map/ppermute | solution.py:157
  38.3 2.2 %copy-start.2 = (bf16[512,4096]{1,0:T(8,128)(2,1)S(1)}, bf16[512,4096]{1,0:T(8,128)(2,1)}, u32[]{:S(2)}) copy-start(bf16[512,4096]{1,0:T(8,128)(2,1)} %param.14) | copy-start | bytes 12582916
  41.3 3.2 %collective-permute-start.7 = (f32[2,128,1024]{2,1,0:T(8,128)S(1)}, f32[2,128,1024]{2,1,0:T(8,128)S(1)}, u32[]{:S(2)}, u32[]{:S(2)}) collective-permute-start(f32[2,128,1024]{2,1,0:T(8,128)S(1)} %pad_maximum_fusion), channel_id=1, source_target_pairs={{0,1},{1,0},{2,3},{3,2},{4,5},{5,4},{6,7},{7,6},{8,9},{9,8},{10,11... | collective-permute-start | bytes 3145736 | tf_op jit(solution)/shard_map/ppermute | solution.py:16
  44.5 10.3 %copy-start.8 = (s32[128]{0:T(128)S(1)}, s32[128]{0:T(128)}, u32[]{:S(2)}) copy-start(s32[128]{0:T(128)} %param.20) | copy-start | bytes 1540
  44.7 8.8 %collective-permute-start.8 = (bf16[128,1024]{1,0:T(8,128)(2,1)S(1)}, bf16[128,1024]{1,0:T(8,128)(2,1)S(1)}, u32[]{:S(2)}, u32[]{:S(2)}) collective-permute-start(bf16[128,1024]{1,0:T(8,128)(2,1)S(1)} %fusion.48), channel_id=1, source_target_pairs={{0,2},{1,3},{2,0},{3,1},{4,6},{5,7},{6,4},{7,5},{8,10},{9,11},{10,... | collective-permute-start | bytes 786440 | tf_op jit(solution)/shard_map/ppermute | solution.py:16
  54.7 3.1 %collective-permute-start.9 = (bf16[128,1,1024]{2,0,1:T(8,128)(2,1)S(1)}, bf16[128,1,1024]{2,0,1:T(8,128)(2,1)S(1)}, u32[]{:S(2)}, u32[]{:S(2)}) collective-permute-start(bf16[128,1,1024]{2,0,1:T(8,128)(2,1)S(1)} %fusion.49), channel_id=1, source_target_pairs={{0,1},{1,0},{2,3},{3,2},{4,5},{5,4},{6,7},{7,6},{8,9},{9,8},{10,11... | collective-permute-start | bytes 786440 | tf_op jit(solution)/shard_map/ppermute | solution.py:16
  54.8 1.5 %collective-permute-start.11 = (f32[128]{0:T(128)S(1)}, f32[128]{0:T(128)S(1)}, u32[]{:S(2)}, u32[]{:S(2)}) collective-permute-start(f32[128]{0:T(128)S(1)} %get-tuple-element.19), channel_id=1, source_target_pairs={{0,1},{1,0},{2,3},{3,2},{4,5},{5,4},{6,7},{7,6},{8,9},{9,8},{10,11... | collective-permute-start | bytes 1544 | tf_op jit(solution)/shard_map/ppermute | solution.py:16
  56.3 3.5 %collective-permute-start.12 = (f32[128]{0:T(128)S(1)}, f32[128]{0:T(128)S(1)}, u32[]{:S(2)}, u32[]{:S(2)}) collective-permute-start(f32[128]{0:T(128)S(1)} %add.343), channel_id=1, source_target_pairs={{0,2},{1,3},{2,0},{3,1},{4,6},{5,7},{6,4},{7,5},{8,10},{9,11},{10,... | collective-permute-start | bytes 1544 | tf_op jit(solution)/shard_map/ppermute | solution.py:16
  58.2 13.8 %collective-permute-start.10 = (bf16[128,2048]{0,1:T(8,128)(2,1)S(1)}, bf16[128,2048]{0,1:T(8,128)(2,1)S(1)}, u32[]{:S(2)}, u32[]{:S(2)}) collective-permute-start(bf16[128,2048]{0,1:T(8,128)(2,1)S(1)} %bitcast.255), channel_id=1, source_target_pairs={{0,2},{1,3},{2,0},{3,1},{4,6},{5,7},{6,4},{7,5},{8,10},{9,11},{10,... | collective-permute-start | bytes 1572872 | tf_op jit(solution)/shard_map/ppermute | solution.py:16
  68.0 14.9 %copy-start.6 = (s32[128]{0:T(128)S(1)}, s32[128]{0:T(128)}, u32[]{:S(2)}) copy-start(s32[128]{0:T(128)} %param.21) | copy-start | bytes 1540
  81.1 1.2 collective-permute-start.13
  82.3 3.7 %collective-permute-start.14 = (f32[3,128]{1,0:T(4,128)S(1)}, f32[3,128]{1,0:T(4,128)S(1)}, u32[]{:S(2)}, u32[]{:S(2)}) collective-permute-start(f32[3,128]{1,0:T(4,128)S(1)} %pad_maximum_fusion.3), channel_id=1, source_target_pairs={{0,2},{1,3},{2,0},{3,1},{4,6},{5,7},{6,4},{7,5},{8,10},{9,11},{10,... | collective-permute-start | bytes 4616 | tf_op jit(solution)/shard_map/ppermute | solution.py:16
  87.2 8.5 %copy-start.4 = (bf16[128,4096]{1,0:T(8,128)(2,1)}, bf16[128,4096]{1,0:T(8,128)(2,1)S(1)}, u32[]{:S(2)}) copy-start(bf16[128,4096]{1,0:T(8,128)(2,1)S(1)} %multiply_convert_fusion) | copy-start | bytes 3145732
  95.8 3.5 %copy-start.5 = (bf16[128,4096]{1,0:T(8,128)(2,1)S(1)}, bf16[128,4096]{1,0:T(8,128)(2,1)}, u32[]{:S(2)}) copy-start(bf16[128,4096]{1,0:T(8,128)(2,1)} %copy-done.4) | copy-start | bytes 3145732
  96.1 2.1 %collective-permute-start.15 = (f32[1,1024,128]{1,2,0:T(8,128)S(1)}, f32[1,1024,128]{1,2,0:T(8,128)}, u32[]{:S(2)}, u32[]{:S(2)}) collective-permute-start(f32[1,1024,128]{1,2,0:T(8,128)S(1)} %bitcast.257), channel_id=1, source_target_pairs={{0,1},{1,0},{2,3},{3,2},{4,5},{5,4},{6,7},{7,6},{8,9},{9,8},{10,11... | collective-permute-start | bytes 1572872 | tf_op jit(solution)/shard_map/ppermute | solution.py:16
  107.5 32.1 %copy-start.1 = (bf16[2,192,512]{2,1,0:T(8,128)(2,1)S(1)}, bf16[2,192,512]{2,1,0:T(8,128)(2,1)}, u32[]{:S(2)}) copy-start(bf16[2,192,512]{2,1,0:T(8,128)(2,1)} %param.13) | copy-start | bytes 1179652
  107.7 8.8 %collective-permute-start.16 = (f32[1,1024,128]{1,2,0:T(8,128)S(1)}, f32[1,1024,128]{1,2,0:T(8,128)S(1)}, u32[]{:S(2)}, u32[]{:S(2)}) collective-permute-start(f32[1,1024,128]{1,2,0:T(8,128)S(1)} %bitcast.254), channel_id=1, source_target_pairs={{0,1},{1,0},{2,3},{3,2},{4,5},{5,4},{6,7},{7,6},{8,9},{9,8},{10,11... | collective-permute-start | bytes 1572872 | tf_op jit(solution)/shard_map/ppermute | solution.py:16
  107.9 8.6 %collective-permute-start.17 = (bf16[1024,128]{0,1:T(8,128)(2,1)S(1)}, bf16[1024,128]{0,1:T(8,128)(2,1)S(1)}, u32[]{:S(2)}, u32[]{:S(2)}) collective-permute-start(bf16[1024,128]{0,1:T(8,128)(2,1)S(1)} %fusion.30), channel_id=1, source_target_pairs={{0,2},{1,3},{2,0},{3,1},{4,6},{5,7},{6,4},{7,5},{8,10},{9,11},{10,... | collective-permute-start | bytes 786440 | tf_op jit(solution)/shard_map/ppermute | solution.py:16
  118.2 5.9 %collective-permute-start.18 = (f32[1026]{0:T(1024)S(1)}, f32[1026]{0:T(1024)S(1)}, u32[]{:S(2)}, u32[]{:S(2)}) collective-permute-start(f32[1026]{0:T(1024)S(1)} %concatenate.3), channel_id=1, source_target_pairs={{0,4},{4,0},{8,12},{12,8},{16,20},{20,16},{24,28},{28,24},{1,5},{5... | collective-permute-start | bytes 12320 | tf_op jit(solution)/shard_map/ppermute | solution.py:16
  124.1 6.1 %collective-permute-start.19 = (f32[1026]{0:T(1024)S(1)}, f32[1026]{0:T(1024)S(1)}, u32[]{:S(2)}, u32[]{:S(2)}) collective-permute-start(f32[1026]{0:T(1024)S(1)} %add.359), channel_id=1, source_target_pairs={{0,8},{4,12},{8,0},{12,4},{16,24},{20,28},{24,16},{28,20},{1,9},{5... | collective-permute-start | bytes 12320 | tf_op jit(solution)/shard_map/ppermute | solution.py:16
  128.5 1.1 collective-permute-start.21
  129.7 3.5 %collective-permute-start.22 = (f32[128]{0:T(128)S(1)}, f32[128]{0:T(128)S(1)}, u32[]{:S(2)}, u32[]{:S(2)}) collective-permute-start(f32[128]{0:T(128)S(1)} %add.362), channel_id=1, source_target_pairs={{0,2},{1,3},{2,0},{3,1},{4,6},{5,7},{6,4},{7,5},{8,10},{9,11},{10,... | collective-permute-start | bytes 1544 | tf_op jit(solution)/shard_map/ppermute | solution.py:16
  130.2 4.6 %collective-permute-start.20 = (f32[1026]{0:T(1024)S(1)}, f32[1026]{0:T(1024)S(1)}, u32[]{:S(2)}, u32[]{:S(2)}) collective-permute-start(f32[1026]{0:T(1024)S(1)} %add.360), channel_id=1, source_target_pairs={{0,16},{4,20},{8,24},{12,28},{16,0},{20,4},{24,8},{28,12},{1,17},{... | collective-permute-start | bytes 12320 | tf_op jit(solution)/shard_map/ppermute | solution.py:16

commit v12 on v11

--- a/solution.py
+++ b/solution.py
@@ -230,7 +230,25 @@
         mask_float[:, None] * (jnp.exp(logits - log_total[:, None]) - picked.astype(jnp.float32))
     ).astype(jnp.bfloat16)
     contract = (((1,), (1,)), ((), ()))
-    if split_fsdp:
+    if levels == 2:
+
+        def grad_chunk(chunk, logits_in):
+            rows_here = lax.dynamic_slice_in_dim(w_vocab, chunk * quarter, quarter, 0)
+            return lax.dot_general(rows_here, logits_in, contract, preferred_element_type=jnp.float32)
+
+        far_base = 2 * (1 - high_bit)
+        far_kept = grad_chunk(far_base + low_bit, grad_logits) + exchange(
+            grad_chunk(far_base + 1 - low_bit, grad_logits), "fsdp", 0
+        )
+        far_wire, rest_logits = lax.optimization_barrier(
+            (far_kept.astype(jnp.bfloat16), grad_logits)
+        )
+        far_got = exchange(far_wire, "fsdp", 1).astype(jnp.float32)
+        near_base = 2 * high_bit
+        near_got = exchange(grad_chunk(near_base + 1 - low_bit, rest_logits), "fsdp", 0)
+        own = grad_chunk(near_base + low_bit, rest_logits)
+        grad_normed = (own + near_got + far_got).T
+    elif split_fsdp:
         far_grad = lax.dot_general(
             far_rows, grad_logits, contract, preferred_element_type=jnp.float32
         )

time: 141 us -> 148 us (1.050)
  matrix products: 43 us -> 52.6 us
  local copies, waits for them, and re-layouts: 8.95 us -> 6.96 us
    dot_general x2 -> x4, matrix products: 16.6 us -> 26.2 us  [grad_chunk(): lax.dot_general(rows_here, logits_in, contract, preferred_element_type=jn...]
    unnamed x22 -> x18, local copies, waits for them, and re-layouts: 1.89 us -> 0.05 us
where the time goes in v12:
time: 148 us; the launch traced here: 147 us
  matrix products  52.6 us (36%)
  waiting for transfers between devices  41 us (28%)
  starting transfers between devices  31.3 us (21%)
  other arithmetic  11.4 us (8%)
  local copies, waits for them, and re-layouts  6.96 us (5%)
  between operations  3.96 us (3%)
    ppermute x16, waiting for transfers between devices, exchange(): return lax.ppermute(x, axis, [(i, i ^ 1 << bit) for i in range(size)])  32.2 us
    dot_general x4, matrix products, grad_chunk(): lax.dot_general(rows_here, logits_in, contract, preferred_element_type=jn...  26.2 us
    ppermute x16, starting transfers between devices, exchange(): return lax.ppermute(x, axis, [(i, i ^ 1 << bit) for i in range(size)])  16.7 us
    ppermute x7, starting transfers between devices, body(): lax.ppermute(block, 'dp', [(i, (i - shift) % dp_count) for i in range(dp_...  14.6 us
    ppermute x7, waiting for transfers between devices, body(): lax.ppermute(block, 'dp', [(i, (i - shift) % dp_count) for i in range(dp_...  8.81 us
    dot_general x1, matrix products, body(): jnp.dot(far_normed, far_rows, preferred_element_type=jnp.float32)  8.4 us
    dot_general x1, matrix products, body(): jnp.dot(near_normed, near_rows, preferred_element_type=jnp.float32)  8.16 us
    dot_general x4, matrix products, chunk_product(): return jnp.dot(attended, columns, preferred_element_type=jnp.float32)  3.77 us
  transfers between devices with their start and end apart: 23, of which 13 were waited for; matrix products, arithmetic and copies ran while one was open for 13% of the time, Pallas kernels for 0%

profile of v12, /device:TPU:0, one launch (start us, length us, event | category | flops | bytes accessed | tf_op | source)
XLA Modules:
  0.0 147.2 jit_solution(5536687239736549034)
XLA Ops:
  0.7 0.8 fusion.103
  1.7 0.8 select_reduce_fusion.11
  2.5 0.8 lt.83
  3.4 1.0 select_reduce_fusion.19
  5.5 5.1 %collective-permute-start.1 = (bf16[2,80,512]{2,1,0:T(8,128)(2,1)S(1)}, bf16[2,80,512]{2,1,0:T(8,128)(2,1)S(1)}, u32[]{:S(2)}, u32[]{:S(2)}) collective-permute-start(bf16[2,80,512]{2,1,0:T(8,128)(2,1)S(1)} %get-tuple-element.20), channel_id=1, source_target_pairs={{0,24},{4,28},{8,0},{12,4},{16,8},{20,12},{24,16},{28,20},{1,25},{... | collective-permute-start | bytes 491528 | tf_op jit(solution)/shard_map/ppermute | solution.py:157
  10.6 1.5 %collective-permute-start.6 = (bf16[2,80,512]{2,1,0:T(8,128)(2,1)S(1)}, bf16[2,80,512]{2,1,0:T(8,128)(2,1)S(1)}, u32[]{:S(2)}, u32[]{:S(2)}) collective-permute-start(bf16[2,80,512]{2,1,0:T(8,128)(2,1)S(1)} %get-tuple-element.21), channel_id=1, source_target_pairs={{0,4},{4,8},{8,12},{12,16},{16,20},{20,24},{24,28},{28,0},{1,5},{5... | collective-permute-start | bytes 491528 | tf_op jit(solution)/shard_map/ppermute | solution.py:157
  12.1 1.0 collective-permute-start.4
  13.1 2.8 %collective-permute-start.3 = (bf16[2,80,512]{2,1,0:T(8,128)(2,1)S(1)}, bf16[2,80,512]{2,1,0:T(8,128)(2,1)S(1)}, u32[]{:S(2)}, u32[]{:S(2)}) collective-permute-start(bf16[2,80,512]{2,1,0:T(8,128)(2,1)S(1)} %get-tuple-element.24), channel_id=1, source_target_pairs={{0,16},{4,20},{8,24},{12,28},{16,0},{20,4},{24,8},{28,12},{1,17},{... | collective-permute-start | bytes 491528 | tf_op jit(solution)/shard_map/ppermute | solution.py:157
  16.8 2.0 %convolution_convert_fusion.1 = bf16[128,512]{1,0:T(8,128)(2,1)S(1)} fusion(bf16[128,4096]{1,0:T(8,128)(2,1)} %param.11, bf16[4096,512]{1,0:T(8,128)(2,1)S(1)} %copy-done.3), kind=kOutput, calls=%fused_computation.38 | convolution fusion | flops 536936448 | bytes 5373952 | tf_op jit(solution)/shard_map/dot_general | solution.py:148
  19.9 1.1 collective-permute-start.2
  21.2 3.1 %collective-permute-start = (bf16[2,80,512]{2,1,0:T(8,128)(2,1)S(1)}, bf16[2,80,512]{2,1,0:T(8,128)(2,1)S(1)}, u32[]{:S(2)}, u32[]{:S(2)}) collective-permute-start(bf16[2,80,512]{2,1,0:T(8,128)(2,1)S(1)} %get-tuple-element.26), channel_id=1, source_target_pairs={{0,28},{4,0},{8,4},{12,8},{16,12},{20,16},{24,20},{28,24},{1,29},{... | collective-permute-start | bytes 491528 | tf_op jit(solution)/shard_map/ppermute | solution.py:157
  24.8 8.8 %collective-permute-done.4 = bf16[2,80,512]{2,1,0:T(8,128)(2,1)S(1)} collective-permute-done((bf16[2,80,512]{2,1,0:T(8,128)(2,1)S(1)}, bf16[2,80,512]{2,1,0:T(8,128)(2,1)S(1)}, u32[]{:S(2)}, u32[]{:S(2)}) %collective-permute-start.4) | collective-permute-done | bytes 163872 | tf_op jit(solution)/shard_map/ppermute | solution.py:157
  34.2 0.9 fusion.138
  40.3 1.6 %convolution_bitcast_fusion.2 = f32[1,128,1024]{2,1,0:T(8,128)S(1)} fusion(bf16[128,512]{0,1:T(8,128)(2,1)S(1)} %bitcast.217, bf16[512,4096]{1,0:T(8,128)(2,1)} %param.14, s32[]{:T(128)S(6)} %select_n.235), kind=kOutput, calls=%fused_computation.22 | convolution fusion | flops 134217728 | bytes 1703940 | tf_op jit(solution)/shard_map/dot_general | solution.py:186
  41.9 1.6 %convolution_bitcast_fusion.3 = f32[1,128,1024]{2,1,0:T(8,128)S(1)} fusion(bf16[128,512]{0,1:T(8,128)(2,1)S(1)} %bitcast.218, bf16[512,4096]{1,0:T(8,128)(2,1)} %param.14, s32[]{:T(128)S(6)} %select_n.234), kind=kOutput, calls=%fused_computation.23 | convolution fusion | flops 134217728 | bytes 1703940 | tf_op jit(solution)/shard_map/dot_general | solution.py:186
  43.7 1.6 %collective-permute-start.8 = (bf16[128,1024]{1,0:T(8,128)(2,1)S(1)}, bf16[128,1024]{1,0:T(8,128)(2,1)S(1)}, u32[]{:S(2)}, u32[]{:S(2)}) collective-permute-start(bf16[128,1024]{1,0:T(8,128)(2,1)S(1)} %fusion.65), channel_id=1, source_target_pairs={{0,2},{1,3},{2,0},{3,1},{4,6},{5,7},{6,4},{7,5},{8,10},{9,11},{10,... | collective-permute-start | bytes 786440 | tf_op jit(solution)/shard_map/ppermute | solution.py:16
  45.3 0.7 dynamic_slice.50
  46.0 6.5 %collective-permute-done.8 = bf16[128,1024]{1,0:T(8,128)(2,1)S(1)} collective-permute-done((bf16[128,1024]{1,0:T(8,128)(2,1)S(1)}, bf16[128,1024]{1,0:T(8,128)(2,1)S(1)}, u32[]{:S(2)}, u32[]{:S(2)}) %collective-permute-start.8) | collective-permute-done | bytes 262176 | tf_op jit(solution)/shard_map/ppermute | solution.py:16
  52.5 1.1 multiply_reduce_fusion.2
  54.2 1.0 collective-permute-done.11
  55.2 1.5 %collective-permute-start.12 = (f32[128]{0:T(128)S(1)}, f32[128]{0:T(128)S(1)}, u32[]{:S(2)}, u32[]{:S(2)}) collective-permute-start(f32[128]{0:T(128)S(1)} %add.361), channel_id=1, source_target_pairs={{0,2},{1,3},{2,0},{3,1},{4,6},{5,7},{6,4},{7,5},{8,10},{9,11},{10,... | collective-permute-start | bytes 1544 | tf_op jit(solution)/shard_map/ppermute | solution.py:16
  57.7 1.0 collective-permute-done.12
  58.8 8.2 %fusion.2 = f32[128,4096]{1,0:T(8,128)S(1)} fusion(bf16[128,2048]{0,1:T(8,128)(2,1)S(1)} %bitcast.230, bf16[4096,4096]{1,0:T(8,128)(2,1)} %param.16, s32[]{:T(128)S(6)} %select_n.243), kind=kOutput, calls=%fused_computation.2 | convolution fusion | flops 2147483648 | bytes 19398660 | tf_op jit(solution)/shard_map/dot_general | solution.py:213
  67.0 3.9 %collective-permute-done.10 = bf16[128,2048]{0,1:T(8,128)(2,1)S(1)} collective-permute-done((bf16[128,2048]{0,1:T(8,128)(2,1)S(1)}, bf16[128,2048]{0,1:T(8,128)(2,1)S(1)}, u32[]{:S(2)}, u32[]{:S(2)}) %collective-permute-start.10) | collective-permute-done | bytes 524320 | tf_op jit(solution)/shard_map/ppermute | solution.py:16
  70.9 8.4 %fusion.144 = (f32[128]{0:T(128)S(1)}, f32[128,4096]{1,0:T(8,128)S(1)}) fusion(f32[128]{0:T(128)S(1)} %add_rsqrt_fusion, f32[128,4096]{1,0:T(8,128)S(1)} %fusion.2, bf16[128,2048]{0,1:T(8,128)(2,1)S(1)} %collective-permute-done.10, bf16[4096,4096]{1,0:T(8,128)(2,1)} %param.16, s32[]{:T(128)S(6)} %select_n.244), kind=kOutput, calls=%fused_computation.256 | convolution fusion | flops 2149056512 | bytes 21496836 | tf_op jit(solution)/shard_map/dot_general | solution.py:214
  79.3 0.7 select_reduce_fusion
  80.1 1.1 collective-permute-done.13
  81.3 0.6 collective-permute-start.14
  81.9 3.1 %collective-permute-done.14 = f32[3,128]{1,0:T(4,128)S(1)} collective-permute-done((f32[3,128]{1,0:T(4,128)S(1)}, f32[3,128]{1,0:T(4,128)S(1)}, u32[]{:S(2)}, u32[]{:S(2)}) %collective-permute-start.14) | collective-permute-done | bytes 1568 | tf_op jit(solution)/shard_map/ppermute | solution.py:16
  84.9 0.6 fusion.124
  85.6 0.7 multiply_convert_fusion
  86.2 6.9 %fusion.6 = f32[1024,128]{0,1:T(8,128)S(1)} fusion(bf16[128,4096]{1,0:T(8,128)(2,1)S(1)} %multiply_convert_fusion, bf16[4096,4096]{1,0:T(8,128)(2,1)} %param.16, s32[]{:T(128)S(6)} %select_n.248), kind=kOutput, calls=%fused_computation.6 | convolution fusion | flops 1073741824 | bytes 9961476 | tf_op jit(solution)/shard_map/dot_general | solution.py:237
  93.2 1.9 %collective-permute-done.15 = f32[1024,128]{0,1:T(8,128)S(1)} collective-permute-done((f32[1024,128]{0,1:T(8,128)S(1)}, f32[1024,128]{0,1:T(8,128)S(1)}, u32[]{:S(2)}, u32[]{:S(2)}) %collective-permute-start.15) | collective-permute-done | bytes 524320 | tf_op jit(solution)/shard_map/ppermute | solution.py:16
  95.1 6.5 %fusion.31 = bf16[1024,128]{0,1:T(8,128)(2,1)S(1)} fusion(f32[1024,128]{0,1:T(8,128)S(1)} %collective-permute-done.15, bf16[128,4096]{1,0:T(8,128)(2,1)} %copy-done.4, bf16[4096,4096]{1,0:T(8,128)(2,1)} %param.16, s32[]{:T(128)S(6)} %select_n.247), kind=kOutput, calls=%fused_computation.28 | convolution fusion | flops 1074003968 | bytes 10223620 | tf_op jit(solution)/shard_map/dot_general | solution.py:237
  101.6 6.3 %fusion.4 = f32[1024,128]{0,1:T(8,128)S(1)} fusion(bf16[128,4096]{1,0:T(8,128)(2,1)S(1)} %copy-done.5, bf16[4096,4096]{1,0:T(8,128)(2,1)} %param.16, s32[]{:T(128)S(6)} %select_n.249), kind=kOutput, calls=%fused_computation.4 | convolution fusion | flops 1073741824 | bytes 9961476 | tf_op jit(solution)/shard_map/dot_general | solution.py:237
  108.6 8.1 %collective-permute-done.17 = bf16[1024,128]{0,1:T(8,128)(2,1)S(1)} collective-permute-done((bf16[1024,128]{0,1:T(8,128)(2,1)S(1)}, bf16[1024,128]{0,1:T(8,128)(2,1)S(1)}, u32[]{:S(2)}, u32[]{:S(2)}) %collective-permute-start.17) | collective-permute-done | bytes 262176 | tf_op jit(solution)/shard_map/ppermute | solution.py:16
  116.7 6.5 %multiply_reduce_fusion = (f32[128]{0:T(128)S(1)}, f32[1024]{0:T(1024)S(1)}, f32[128,1024]{1,0:T(8,128)S(1)}) fusion(f32[128,1024]{1,0:T(8,128)S(1)} %get-tuple-element.19, f32[128]{0:T(128)S(1)} %add_rsqrt_fusion, f32[1024]{0:T(1024)S(1)} %dynamic_slice.50, bf16[1024,128]{0,1:T(8,128)(2,1)S(1)} %collective-permute-done.17, ...), kind=kOutput, calls=%fused_computation.54 | convolution fusion | flops 1074920320 | bytes 11281412 | tf_op jit(solution)/shard_map/dot_general | solution.py:237
  123.2 1.4 concatenate.3
  124.6 4.3 %collective-permute-start.18 = (f32[1026]{0:T(1024)S(1)}, f32[1026]{0:T(1024)S(1)}, u32[]{:S(2)}, u32[]{:S(2)}) collective-permute-start(f32[1026]{0:T(1024)S(1)} %concatenate.3), channel_id=1, source_target_pairs={{0,4},{4,0},{8,12},{12,8},{16,20},{20,16},{24,28},{28,24},{1,5},{5... | collective-permute-start | bytes 12320 | tf_op jit(solution)/shard_map/ppermute | solution.py:16
  128.9 1.6 %collective-permute-done.18 = f32[1026]{0:T(1024)S(1)} collective-permute-done((f32[1026]{0:T(1024)S(1)}, f32[1026]{0:T(1024)S(1)}, u32[]{:S(2)}, u32[]{:S(2)}) %collective-permute-start.18) | collective-permute-done | bytes 4136 | tf_op jit(solution)/shard_map/ppermute | solution.py:16
  130.5 4.4 %collective-permute-start.19 = (f32[1026]{0:T(1024)S(1)}, f32[1026]{0:T(1024)S(1)}, u32[]{:S(2)}, u32[]{:S(2)}) collective-permute-start(f32[1026]{0:T(1024)S(1)} %add.383), channel_id=1, source_target_pairs={{0,8},{4,12},{8,0},{12,4},{16,24},{20,28},{24,16},{28,20},{1,9},{5... | collective-permute-start | bytes 12320 | tf_op jit(solution)/shard_map/ppermute | solution.py:16
  135.0 1.1 collective-permute-done.21
  136.6 1.7 %collective-permute-start.20 = (f32[1026]{0:T(1024)S(1)}, f32[1026]{0:T(1024)S(1)}, u32[]{:S(2)}, u32[]{:S(2)}) collective-permute-start(f32[1026]{0:T(1024)S(1)} %add.384), channel_id=1, source_target_pairs={{0,16},{4,20},{8,24},{12,28},{16,0},{20,4},{24,8},{28,12},{1,17},{... | collective-permute-start | bytes 12320 | tf_op jit(solution)/shard_map/ppermute | solution.py:16
  138.3 1.3 collective-permute-done.22
  139.6 1.5 %collective-permute-done.20 = f32[1026]{0:T(1024)S(1)} collective-permute-done((f32[1026]{0:T(1024)S(1)}, f32[1026]{0:T(1024)S(1)}, u32[]{:S(2)}, u32[]{:S(2)}) %collective-permute-start.20) | collective-permute-done | bytes 4136 | tf_op jit(solution)/shard_map/ppermute | solution.py:16
  141.1 0.6 fusion.143
  141.7 1.4 slice_divide_fusion
  144.5 1.6 %divide_convert_fusion = bf16[128,1024]{1,0:T(8,128)(2,1)} fusion(f32[128,1024]{1,0:T(8,128)S(1)} %get-tuple-element.84, f32[128,1024]{1,0:T(8,128)S(1)} %get-tuple-element.19, f32[]{:T(128)} %bitcast.62, f32[128]{0:T(128)S(1)} %add_multiply_fusion, f32[128]{0:T(128)S(1)} %add_rsqrt_fusion, f32[1024]{0:T(1024)S(1)} %dynamic_slice.50), kind=kLoop, calls=%fused_computation.53 | loop fusion | flops 917504 | bytes 1315844 | tf_op jit(solution)/shard_map/convert_element_type | solution.py:283
  (133 shorter events, 12.6 us)
Async XLA Ops:
  0.6 4.2 %copy-start = (bf16[2,192,512]{2,1,0:T(8,128)(2,1)S(1)}, bf16[2,192,512]{2,1,0:T(8,128)(2,1)}, u32[]{:S(2)}) copy-start(bf16[2,192,512]{2,1,0:T(8,128)(2,1)} %param.13) | copy-start | bytes 1179652
  0.6 15.5 %copy-start.7 = (s32[128]{0:T(128)S(1)}, s32[128]{0:T(128)}, u32[]{:S(2)}) copy-start(s32[128]{0:T(128)} %param.18) | copy-start | bytes 1540
  3.3 13.4 %copy-start.3 = (bf16[4096,512]{1,0:T(8,128)(2,1)S(1)}, bf16[4096,512]{1,0:T(8,128)(2,1)}, u32[]{:S(2)}) copy-start(bf16[4096,512]{1,0:T(8,128)(2,1)} %param.12) | copy-start | bytes 12582916
  5.5 14.3 %collective-permute-start.1 = (bf16[2,80,512]{2,1,0:T(8,128)(2,1)S(1)}, bf16[2,80,512]{2,1,0:T(8,128)(2,1)S(1)}, u32[]{:S(2)}, u32[]{:S(2)}) collective-permute-start(bf16[2,80,512]{2,1,0:T(8,128)(2,1)S(1)} %get-tuple-element.20), channel_id=1, source_target_pairs={{0,24},{4,28},{8,0},{12,4},{16,8},{20,12},{24,16},{28,20},{1,25},{... | collective-permute-start | bytes 491528 | tf_op jit(solution)/shard_map/ppermute | solution.py:157
  10.6 10.6 %collective-permute-start.6 = (bf16[2,80,512]{2,1,0:T(8,128)(2,1)S(1)}, bf16[2,80,512]{2,1,0:T(8,128)(2,1)S(1)}, u32[]{:S(2)}, u32[]{:S(2)}) collective-permute-start(bf16[2,80,512]{2,1,0:T(8,128)(2,1)S(1)} %get-tuple-element.21), channel_id=1, source_target_pairs={{0,4},{4,8},{8,12},{12,16},{16,20},{20,24},{24,28},{28,0},{1,5},{5... | collective-permute-start | bytes 491528 | tf_op jit(solution)/shard_map/ppermute | solution.py:157
  12.1 12.4 %collective-permute-start.5 = (bf16[2,80,512]{2,1,0:T(8,128)(2,1)S(1)}, bf16[2,80,512]{2,1,0:T(8,128)(2,1)S(1)}, u32[]{:S(2)}, u32[]{:S(2)}) collective-permute-start(bf16[2,80,512]{2,1,0:T(8,128)(2,1)S(1)} %get-tuple-element.22), channel_id=1, source_target_pairs={{0,8},{4,12},{8,16},{12,20},{16,24},{20,28},{24,0},{28,4},{1,9},{5... | collective-permute-start | bytes 491528 | tf_op jit(solution)/shard_map/ppermute | solution.py:157
  12.1 21.5 %collective-permute-start.4 = (bf16[2,80,512]{2,1,0:T(8,128)(2,1)S(1)}, bf16[2,80,512]{2,1,0:T(8,128)(2,1)S(1)}, u32[]{:S(2)}, u32[]{:S(2)}) collective-permute-start(bf16[2,80,512]{2,1,0:T(8,128)(2,1)S(1)} %get-tuple-element.23), channel_id=1, source_target_pairs={{0,12},{4,16},{8,20},{12,24},{16,28},{20,0},{24,4},{28,8},{1,13},{... | collective-permute-start | bytes 491528 | tf_op jit(solution)/shard_map/ppermute | solution.py:157
  13.1 20.8 %collective-permute-start.3 = (bf16[2,80,512]{2,1,0:T(8,128)(2,1)S(1)}, bf16[2,80,512]{2,1,0:T(8,128)(2,1)S(1)}, u32[]{:S(2)}, u32[]{:S(2)}) collective-permute-start(bf16[2,80,512]{2,1,0:T(8,128)(2,1)S(1)} %get-tuple-element.24), channel_id=1, source_target_pairs={{0,16},{4,20},{8,24},{12,28},{16,0},{20,4},{24,8},{28,12},{1,17},{... | collective-permute-start | bytes 491528 | tf_op jit(solution)/shard_map/ppermute | solution.py:157
  19.9 14.3 %collective-permute-start.2 = (bf16[2,80,512]{2,1,0:T(8,128)(2,1)S(1)}, bf16[2,80,512]{2,1,0:T(8,128)(2,1)}, u32[]{:S(2)}, u32[]{:S(2)}) collective-permute-start(bf16[2,80,512]{2,1,0:T(8,128)(2,1)S(1)} %get-tuple-element.25), channel_id=1, source_target_pairs={{0,20},{4,24},{8,28},{12,0},{16,4},{20,8},{24,12},{28,16},{1,21},{... | collective-permute-start | bytes 491528 | tf_op jit(solution)/shard_map/ppermute | solution.py:157
  21.2 14.2 %collective-permute-start = (bf16[2,80,512]{2,1,0:T(8,128)(2,1)S(1)}, bf16[2,80,512]{2,1,0:T(8,128)(2,1)S(1)}, u32[]{:S(2)}, u32[]{:S(2)}) collective-permute-start(bf16[2,80,512]{2,1,0:T(8,128)(2,1)S(1)} %get-tuple-element.26), channel_id=1, source_target_pairs={{0,28},{4,0},{8,4},{12,8},{16,12},{20,16},{24,20},{28,24},{1,29},{... | collective-permute-start | bytes 491528 | tf_op jit(solution)/shard_map/ppermute | solution.py:157
  37.3 2.2 %copy-start.2 = (bf16[512,4096]{1,0:T(8,128)(2,1)S(1)}, bf16[512,4096]{1,0:T(8,128)(2,1)}, u32[]{:S(2)}) copy-start(bf16[512,4096]{1,0:T(8,128)(2,1)} %param.14) | copy-start | bytes 12582916
  40.2 3.2 %collective-permute-start.7 = (f32[2,128,1024]{2,1,0:T(8,128)S(1)}, f32[2,128,1024]{2,1,0:T(8,128)S(1)}, u32[]{:S(2)}, u32[]{:S(2)}) collective-permute-start(f32[2,128,1024]{2,1,0:T(8,128)S(1)} %pad_maximum_fusion), channel_id=1, source_target_pairs={{0,1},{1,0},{2,3},{3,2},{4,5},{5,4},{6,7},{7,6},{8,9},{9,8},{10,11... | collective-permute-start | bytes 3145736 | tf_op jit(solution)/shard_map/ppermute | solution.py:16
  41.9 11.9 %copy-start.8 = (s32[128]{0:T(128)S(1)}, s32[128]{0:T(128)}, u32[]{:S(2)}) copy-start(s32[128]{0:T(128)} %param.20) | copy-start | bytes 1540
  43.7 8.8 %collective-permute-start.8 = (bf16[128,1024]{1,0:T(8,128)(2,1)S(1)}, bf16[128,1024]{1,0:T(8,128)(2,1)S(1)}, u32[]{:S(2)}, u32[]{:S(2)}) collective-permute-start(bf16[128,1024]{1,0:T(8,128)(2,1)S(1)} %fusion.65), channel_id=1, source_target_pairs={{0,2},{1,3},{2,0},{3,1},{4,6},{5,7},{6,4},{7,5},{8,10},{9,11},{10,... | collective-permute-start | bytes 786440 | tf_op jit(solution)/shard_map/ppermute | solution.py:16
  53.6 3.1 %collective-permute-start.9 = (bf16[128,1,1024]{2,0,1:T(8,128)(2,1)S(1)}, bf16[128,1,1024]{2,0,1:T(8,128)(2,1)S(1)}, u32[]{:S(2)}, u32[]{:S(2)}) collective-permute-start(bf16[128,1,1024]{2,0,1:T(8,128)(2,1)S(1)} %fusion.66), channel_id=1, source_target_pairs={{0,1},{1,0},{2,3},{3,2},{4,5},{5,4},{6,7},{7,6},{8,9},{9,8},{10,11... | collective-permute-start | bytes 786440 | tf_op jit(solution)/shard_map/ppermute | solution.py:16
  53.7 1.5 %collective-permute-start.11 = (f32[128]{0:T(128)S(1)}, f32[128]{0:T(128)S(1)}, u32[]{:S(2)}, u32[]{:S(2)}) collective-permute-start(f32[128]{0:T(128)S(1)} %get-tuple-element.18), channel_id=1, source_target_pairs={{0,1},{1,0},{2,3},{3,2},{4,5},{5,4},{6,7},{7,6},{8,9},{9,8},{10,11... | collective-permute-start | bytes 1544 | tf_op jit(solution)/shard_map/ppermute | solution.py:16
  55.2 3.5 %collective-permute-start.12 = (f32[128]{0:T(128)S(1)}, f32[128]{0:T(128)S(1)}, u32[]{:S(2)}, u32[]{:S(2)}) collective-permute-start(f32[128]{0:T(128)S(1)} %add.361), channel_id=1, source_target_pairs={{0,2},{1,3},{2,0},{3,1},{4,6},{5,7},{6,4},{7,5},{8,10},{9,11},{10,... | collective-permute-start | bytes 1544 | tf_op jit(solution)/shard_map/ppermute | solution.py:16
  57.2 13.8 %collective-permute-start.10 = (bf16[128,2048]{0,1:T(8,128)(2,1)S(1)}, bf16[128,2048]{0,1:T(8,128)(2,1)S(1)}, u32[]{:S(2)}, u32[]{:S(2)}) collective-permute-start(bf16[128,2048]{0,1:T(8,128)(2,1)S(1)} %bitcast.229), channel_id=1, source_target_pairs={{0,2},{1,3},{2,0},{3,1},{4,6},{5,7},{6,4},{7,5},{8,10},{9,11},{10,... | collective-permute-start | bytes 1572872 | tf_op jit(solution)/shard_map/ppermute | solution.py:16
  67.0 14.9 %copy-start.6 = (s32[128]{0:T(128)S(1)}, s32[128]{0:T(128)}, u32[]{:S(2)}) copy-start(s32[128]{0:T(128)} %param.21) | copy-start | bytes 1540
  80.0 1.2 collective-permute-start.13
  81.3 3.7 %collective-permute-start.14 = (f32[3,128]{1,0:T(4,128)S(1)}, f32[3,128]{1,0:T(4,128)S(1)}, u32[]{:S(2)}, u32[]{:S(2)}) collective-permute-start(f32[3,128]{1,0:T(4,128)S(1)} %pad_maximum_fusion.3), channel_id=1, source_target_pairs={{0,2},{1,3},{2,0},{3,1},{4,6},{5,7},{6,4},{7,5},{8,10},{9,11},{10,... | collective-permute-start | bytes 4616 | tf_op jit(solution)/shard_map/ppermute | solution.py:16
  86.2 6.9 %copy-start.4 = (bf16[128,4096]{1,0:T(8,128)(2,1)}, bf16[128,4096]{1,0:T(8,128)(2,1)S(1)}, u32[]{:S(2)}) copy-start(bf16[128,4096]{1,0:T(8,128)(2,1)S(1)} %multiply_convert_fusion) | copy-start | bytes 3145732
  93.1 2.0 %collective-permute-start.15 = (f32[1024,128]{0,1:T(8,128)S(1)}, f32[1024,128]{0,1:T(8,128)S(1)}, u32[]{:S(2)}, u32[]{:S(2)}) collective-permute-start(f32[1024,128]{0,1:T(8,128)S(1)} %fusion.6), channel_id=1, source_target_pairs={{0,1},{1,0},{2,3},{3,2},{4,5},{5,4},{6,7},{7,6},{8,9},{9,8},{10,11... | collective-permute-start | bytes 1572872 | tf_op jit(solution)/shard_map/ppermute | solution.py:16
  93.2 8.4 %copy-start.5 = (bf16[128,4096]{1,0:T(8,128)(2,1)S(1)}, bf16[128,4096]{1,0:T(8,128)(2,1)}, u32[]{:S(2)}) copy-start(bf16[128,4096]{1,0:T(8,128)(2,1)} %copy-done.4) | copy-start | bytes 3145732
  107.9 8.8 %collective-permute-start.16 = (f32[1024,128]{0,1:T(8,128)S(1)}, f32[1024,128]{0,1:T(8,128)S(1)}, u32[]{:S(2)}, u32[]{:S(2)}) collective-permute-start(f32[1024,128]{0,1:T(8,128)S(1)} %fusion.4), channel_id=1, source_target_pairs={{0,1},{1,0},{2,3},{3,2},{4,5},{5,4},{6,7},{7,6},{8,9},{9,8},{10,11... | collective-permute-start | bytes 1572872 | tf_op jit(solution)/shard_map/ppermute | solution.py:16
  108.1 8.6 %collective-permute-start.17 = (bf16[1024,128]{0,1:T(8,128)(2,1)S(1)}, bf16[1024,128]{0,1:T(8,128)(2,1)S(1)}, u32[]{:S(2)}, u32[]{:S(2)}) collective-permute-start(bf16[1024,128]{0,1:T(8,128)(2,1)S(1)} %fusion.31), channel_id=1, source_target_pairs={{0,2},{1,3},{2,0},{3,1},{4,6},{5,7},{6,4},{7,5},{8,10},{9,11},{10,... | collective-permute-start | bytes 786440 | tf_op jit(solution)/shard_map/ppermute | solution.py:16
  108.6 37.4 %copy-start.1 = (bf16[2,192,512]{2,1,0:T(8,128)(2,1)S(1)}, bf16[2,192,512]{2,1,0:T(8,128)(2,1)}, u32[]{:S(2)}) copy-start(bf16[2,192,512]{2,1,0:T(8,128)(2,1)} %param.13) | copy-start | bytes 1179652
  124.6 5.9 %collective-permute-start.18 = (f32[1026]{0:T(1024)S(1)}, f32[1026]{0:T(1024)S(1)}, u32[]{:S(2)}, u32[]{:S(2)}) collective-permute-start(f32[1026]{0:T(1024)S(1)} %concatenate.3), channel_id=1, source_target_pairs={{0,4},{4,0},{8,12},{12,8},{16,20},{20,16},{24,28},{28,24},{1,5},{5... | collective-permute-start | bytes 12320 | tf_op jit(solution)/shard_map/ppermute | solution.py:16
  130.5 6.0 %collective-permute-start.19 = (f32[1026]{0:T(1024)S(1)}, f32[1026]{0:T(1024)S(1)}, u32[]{:S(2)}, u32[]{:S(2)}) collective-permute-start(f32[1026]{0:T(1024)S(1)} %add.383), channel_id=1, source_target_pairs={{0,8},{4,12},{8,0},{12,4},{16,24},{20,28},{24,16},{28,20},{1,9},{5... | collective-permute-start | bytes 12320 | tf_op jit(solution)/shard_map/ppermute | solution.py:16
  135.0 1.1 collective-permute-start.21
  136.1 3.5 %collective-permute-start.22 = (f32[128]{0:T(128)S(1)}, f32[128]{0:T(128)S(1)}, u32[]{:S(2)}, u32[]{:S(2)}) collective-permute-start(f32[128]{0:T(128)S(1)} %add.386), channel_id=1, source_target_pairs={{0,2},{1,3},{2,0},{3,1},{4,6},{5,7},{6,4},{7,5},{8,10},{9,11},{10,... | collective-permute-start | bytes 1544 | tf_op jit(solution)/shard_map/ppermute | solution.py:16
  136.6 4.6 %collective-permute-start.20 = (f32[1026]{0:T(1024)S(1)}, f32[1026]{0:T(1024)S(1)}, u32[]{:S(2)}, u32[]{:S(2)}) collective-permute-start(f32[1026]{0:T(1024)S(1)} %add.384), channel_id=1, source_target_pairs={{0,16},{4,20},{8,24},{12,28},{16,0},{20,4},{24,8},{28,12},{1,17},{... | collective-permute-start | bytes 12320 | tf_op jit(solution)/shard_map/ppermute | solution.py:16

commit v13 on v11

--- a/solution.py
+++ b/solution.py
@@ -234,9 +234,8 @@
         far_grad = lax.dot_general(
             far_rows, grad_logits, contract, preferred_element_type=jnp.float32
         )
-        far_grad, near_logits = lax.optimization_barrier(
-            (scatter_bits(far_grad, "fsdp", 0, levels - 1), grad_logits)
-        )
+        far_grad = scatter_bits(far_grad, "fsdp", 0, levels - 1)
+        near_logits = grad_logits
         far_grad = exchange(far_grad.astype(jnp.bfloat16), "fsdp", levels - 1).astype(
             jnp.float32
         )

time: 141 us -> 141 us (level)
  waiting for transfers between devices: 40.8 us -> 38.7 us
  local copies, waits for them, and re-layouts: 8.95 us -> 10.9 us
    ppermute x16, waiting for transfers between devices: 32 us -> 29.8 us  [exchange(): return lax.ppermute(x, axis, [(i, i ^ 1 << bit) for i in range(size)])]
    unnamed x22 -> x18, local copies, waits for them, and re-layouts: 1.89 us -> 3.97 us
  transfers between devices with their start and end apart: 23 -> 23, of which waited for: 13 -> 12; matrix products, arithmetic and copies ran while one was open for 13% -> 20% of each run, Pallas kernels for 0% -> 0%
where the time goes in v13:
time: 141 us; the launch traced here: 140 us
  matrix products  43.1 us (31%)
  waiting for transfers between devices  38.7 us (27%)
  starting transfers between devices  31.5 us (22%)
  other arithmetic  12 us (9%)
  local copies, waits for them, and re-layouts  10.9 us (8%)
  between operations  3.93 us (3%)
    ppermute x16, waiting for transfers between devices, exchange(): return lax.ppermute(x, axis, [(i, i ^ 1 << bit) for i in range(size)])  29.8 us
    ppermute x16, starting transfers between devices, exchange(): return lax.ppermute(x, axis, [(i, i ^ 1 << bit) for i in range(size)])  17 us
    ppermute x7, starting transfers between devices, body(): lax.ppermute(block, 'dp', [(i, (i - shift) % dp_count) for i in range(dp_...  14.5 us
    ppermute x7, waiting for transfers between devices, body(): lax.ppermute(block, 'dp', [(i, (i - shift) % dp_count) for i in range(dp_...  8.81 us
    dot_general x1, matrix products, body(): jnp.dot(far_normed, far_rows, preferred_element_type=jnp.float32)  8.39 us
    dot_general x1, matrix products, body(): lax.dot_general(far_rows, grad_logits, contract, preferred_element_type=j...  8.36 us
    dot_general x1, matrix products, body(): lax.dot_general(near_rows, near_logits, contract, preferred_element_type=...  8.36 us
    dot_general x1, matrix products, body(): jnp.dot(near_normed, near_rows, preferred_element_type=jnp.float32)  8.13 us
  transfers between devices with their start and end apart: 23, of which 12 were waited for; matrix products, arithmetic and copies ran while one was open for 20% of the time, Pallas kernels for 0%

profile of v13, /device:TPU:0, one launch (start us, length us, event | category | flops | bytes accessed | tf_op | source)
XLA Modules:
  0.0 140.1 jit_solution(1758216927405170987)
XLA Ops:
  0.7 0.8 fusion.85
  1.7 0.8 select_reduce_fusion.11
  2.5 0.8 lt.80
  3.4 0.8 select_reduce_fusion.19
  5.4 5.1 %collective-permute-start.1 = (bf16[2,80,512]{2,1,0:T(8,128)(2,1)S(1)}, bf16[2,80,512]{2,1,0:T(8,128)(2,1)S(1)}, u32[]{:S(2)}, u32[]{:S(2)}) collective-permute-start(bf16[2,80,512]{2,1,0:T(8,128)(2,1)S(1)} %get-tuple-element.17), channel_id=1, source_target_pairs={{0,24},{4,28},{8,0},{12,4},{16,8},{20,12},{24,16},{28,20},{1,25},{... | collective-permute-start | bytes 491528 | tf_op jit(solution)/shard_map/ppermute | solution.py:157
  10.5 1.5 %collective-permute-start.6 = (bf16[2,80,512]{2,1,0:T(8,128)(2,1)S(1)}, bf16[2,80,512]{2,1,0:T(8,128)(2,1)S(1)}, u32[]{:S(2)}, u32[]{:S(2)}) collective-permute-start(bf16[2,80,512]{2,1,0:T(8,128)(2,1)S(1)} %get-tuple-element.18), channel_id=1, source_target_pairs={{0,4},{4,8},{8,12},{12,16},{16,20},{20,24},{24,28},{28,0},{1,5},{5... | collective-permute-start | bytes 491528 | tf_op jit(solution)/shard_map/ppermute | solution.py:157
  12.0 1.0 collective-permute-start.4
  12.9 2.8 %collective-permute-start.3 = (bf16[2,80,512]{2,1,0:T(8,128)(2,1)S(1)}, bf16[2,80,512]{2,1,0:T(8,128)(2,1)S(1)}, u32[]{:S(2)}, u32[]{:S(2)}) collective-permute-start(bf16[2,80,512]{2,1,0:T(8,128)(2,1)S(1)} %get-tuple-element.21), channel_id=1, source_target_pairs={{0,16},{4,20},{8,24},{12,28},{16,0},{20,4},{24,8},{28,12},{1,17},{... | collective-permute-start | bytes 491528 | tf_op jit(solution)/shard_map/ppermute | solution.py:157
  16.6 2.0 %convolution_convert_fusion.1 = bf16[128,512]{1,0:T(8,128)(2,1)S(1)} fusion(bf16[128,4096]{1,0:T(8,128)(2,1)} %param.11, bf16[4096,512]{1,0:T(8,128)(2,1)S(1)} %copy-done.3), kind=kOutput, calls=%fused_computation.29 | convolution fusion | flops 536936448 | bytes 5373952 | tf_op jit(solution)/shard_map/dot_general | solution.py:148
  19.7 1.1 collective-permute-start.2
  21.1 3.1 %collective-permute-start = (bf16[2,80,512]{2,1,0:T(8,128)(2,1)S(1)}, bf16[2,80,512]{2,1,0:T(8,128)(2,1)S(1)}, u32[]{:S(2)}, u32[]{:S(2)}) collective-permute-start(bf16[2,80,512]{2,1,0:T(8,128)(2,1)S(1)} %get-tuple-element.23), channel_id=1, source_target_pairs={{0,28},{4,0},{8,4},{12,8},{16,12},{20,16},{24,20},{28,24},{1,29},{... | collective-permute-start | bytes 491528 | tf_op jit(solution)/shard_map/ppermute | solution.py:157
  24.7 8.8 %collective-permute-done.4 = bf16[2,80,512]{2,1,0:T(8,128)(2,1)S(1)} collective-permute-done((bf16[2,80,512]{2,1,0:T(8,128)(2,1)S(1)}, bf16[2,80,512]{2,1,0:T(8,128)(2,1)S(1)}, u32[]{:S(2)}, u32[]{:S(2)}) %collective-permute-start.4) | collective-permute-done | bytes 163872 | tf_op jit(solution)/shard_map/ppermute | solution.py:157
  38.4 1.3 copy-done.2
  40.6 1.6 %convolution_bitcast_fusion.2 = f32[1,128,1024]{2,1,0:T(8,128)S(1)} fusion(bf16[128,512]{0,1:T(8,128)(2,1)S(1)} %bitcast.240, bf16[512,4096]{1,0:T(8,128)(2,1)} %param.14, s32[]{:T(128)S(6)} %select_n.232), kind=kOutput, calls=%fused_computation.18 | convolution fusion | flops 134217728 | bytes 1703940 | tf_op jit(solution)/shard_map/dot_general | solution.py:186
  42.1 1.6 %convolution_bitcast_fusion.3 = f32[1,128,1024]{2,1,0:T(8,128)S(1)} fusion(bf16[128,512]{0,1:T(8,128)(2,1)S(1)} %bitcast.241, bf16[512,4096]{1,0:T(8,128)(2,1)} %param.14, s32[]{:T(128)S(6)} %select_n.231), kind=kOutput, calls=%fused_computation.19 | convolution fusion | flops 134217728 | bytes 1703940 | tf_op jit(solution)/shard_map/dot_general | solution.py:186
  43.9 1.6 %collective-permute-start.8 = (bf16[128,1024]{1,0:T(8,128)(2,1)S(1)}, bf16[128,1024]{1,0:T(8,128)(2,1)S(1)}, u32[]{:S(2)}, u32[]{:S(2)}) collective-permute-start(bf16[128,1024]{1,0:T(8,128)(2,1)S(1)} %fusion.48), channel_id=1, source_target_pairs={{0,2},{1,3},{2,0},{3,1},{4,6},{5,7},{6,4},{7,5},{8,10},{9,11},{10,... | collective-permute-start | bytes 786440 | tf_op jit(solution)/shard_map/ppermute | solution.py:16
  45.5 0.7 dynamic_slice.51
  46.2 6.5 %collective-permute-done.8 = bf16[128,1024]{1,0:T(8,128)(2,1)S(1)} collective-permute-done((bf16[128,1024]{1,0:T(8,128)(2,1)S(1)}, bf16[128,1024]{1,0:T(8,128)(2,1)S(1)}, u32[]{:S(2)}, u32[]{:S(2)}) %collective-permute-start.8) | collective-permute-done | bytes 262176 | tf_op jit(solution)/shard_map/ppermute | solution.py:16
  52.7 1.1 multiply_reduce_fusion.1
  54.5 1.0 collective-permute-done.11
  55.5 1.5 %collective-permute-start.12 = (f32[128]{0:T(128)S(1)}, f32[128]{0:T(128)S(1)}, u32[]{:S(2)}, u32[]{:S(2)}) collective-permute-start(f32[128]{0:T(128)S(1)} %add.343), channel_id=1, source_target_pairs={{0,2},{1,3},{2,0},{3,1},{4,6},{5,7},{6,4},{7,5},{8,10},{9,11},{10,... | collective-permute-start | bytes 1544 | tf_op jit(solution)/shard_map/ppermute | solution.py:16
  58.0 1.1 collective-permute-done.12
  59.0 8.1 %fusion.6 = f32[128,4096]{1,0:T(8,128)S(1)} fusion(bf16[128,2048]{0,1:T(8,128)(2,1)S(1)} %bitcast.257, bf16[4096,4096]{1,0:T(8,128)(2,1)} %param.16, s32[]{:T(128)S(6)} %select_n.240), kind=kOutput, calls=%fused_computation.6 | convolution fusion | flops 2147483648 | bytes 19398660 | tf_op jit(solution)/shard_map/dot_general | solution.py:213
  67.2 4.0 %collective-permute-done.10 = bf16[128,2048]{0,1:T(8,128)(2,1)S(1)} collective-permute-done((bf16[128,2048]{0,1:T(8,128)(2,1)S(1)}, bf16[128,2048]{0,1:T(8,128)(2,1)S(1)}, u32[]{:S(2)}, u32[]{:S(2)}) %collective-permute-start.10) | collective-permute-done | bytes 524320 | tf_op jit(solution)/shard_map/ppermute | solution.py:16
  71.1 8.4 %fusion.126 = (f32[128]{0:T(128)S(1)}, f32[128,4096]{1,0:T(8,128)S(1)}) fusion(f32[128]{0:T(128)S(1)} %add_rsqrt_fusion, f32[128,4096]{1,0:T(8,128)S(1)} %fusion.6, bf16[128,2048]{0,1:T(8,128)(2,1)S(1)} %collective-permute-done.10, bf16[4096,4096]{1,0:T(8,128)(2,1)} %param.16, s32[]{:T(128)S(6)} %select_n.241), kind=kOutput, calls=%fused_computation.256 | convolution fusion | flops 2149056512 | bytes 21496836 | tf_op jit(solution)/shard_map/dot_general | solution.py:214
  79.6 0.7 select_reduce_fusion
  80.3 1.1 collective-permute-done.13
  81.5 0.6 collective-permute-start.14
  82.1 3.1 %collective-permute-done.14 = f32[3,128]{1,0:T(4,128)S(1)} collective-permute-done((f32[3,128]{1,0:T(4,128)S(1)}, f32[3,128]{1,0:T(4,128)S(1)}, u32[]{:S(2)}, u32[]{:S(2)}) %collective-permute-start.14) | collective-permute-done | bytes 1568 | tf_op jit(solution)/shard_map/ppermute | solution.py:16
  85.2 0.6 fusion.106
  85.8 8.4 %fusion = f32[2048,128]{1,0:T(8,128)S(1)} fusion(bf16[4096,4096]{1,0:T(8,128)(2,1)} %param.16, s32[]{:T(128)S(6)} %select_n.241, f32[128,4096]{1,0:T(8,128)S(1)} %get-tuple-element.84, f32[128]{0:T(128)S(1)} %get-tuple-element.14, f32[128]{0:T(128)S(1)} %convert_element_type.63, s32[128]{0:T(128)S(1)} %broadcast_subtract_fusion), kind=kOutput, calls=%fused_computation | convolution fusion | flops 2150629376 | bytes 19924484 | tf_op jit(solution)/shard_map/dot_general | solution.py:234
  94.2 0.9 constant_dynamic-slice_fusion
  95.1 2.0 %copy.110 = f32[1,1,1024,128]{2,3,1,0:T(8,128)} copy(f32[1,1,1024,128]{3,2,1,0:T(8,128)} %get-tuple-element.29) | data formatting | bytes 1048576
  97.1 8.4 %fusion.4 = f32[2048,128]{1,0:T(8,128)S(1)} fusion(bf16[4096,4096]{1,0:T(8,128)(2,1)} %param.16, s32[]{:T(128)S(6)} %select_n.240, f32[128,4096]{1,0:T(8,128)S(1)} %get-tuple-element.84, f32[128]{0:T(128)S(1)} %get-tuple-element.14, f32[128]{0:T(128)S(1)} %convert_element_type.63, s32[128]{0:T(128)S(1)} %broadcast_subtract_fusion), kind=kOutput, calls=%fused_computation.4 | convolution fusion | flops 2150629376 | bytes 19924484 | tf_op jit(solution)/shard_map/dot_general | solution.py:242
  106.5 1.1 fusion.50
  107.6 0.6 collective-permute-start.17
  108.4 7.5 %collective-permute-done.17 = bf16[1024,128]{0,1:T(8,128)(2,1)S(1)} collective-permute-done((bf16[1024,128]{0,1:T(8,128)(2,1)S(1)}, bf16[1024,128]{0,1:T(8,128)(2,1)S(1)}, u32[]{:S(2)}, u32[]{:S(2)}) %collective-permute-start.17) | collective-permute-done | bytes 262176 | tf_op jit(solution)/shard_map/ppermute | solution.py:16
  116.2 1.4 concatenate.3
  117.6 4.2 %collective-permute-start.18 = (f32[1026]{0:T(1024)S(1)}, f32[1026]{0:T(1024)S(1)}, u32[]{:S(2)}, u32[]{:S(2)}) collective-permute-start(f32[1026]{0:T(1024)S(1)} %concatenate.3), channel_id=1, source_target_pairs={{0,4},{4,0},{8,12},{12,8},{16,20},{20,16},{24,28},{28,24},{1,5},{5... | collective-permute-start | bytes 12320 | tf_op jit(solution)/shard_map/ppermute | solution.py:16
  121.8 1.6 %collective-permute-done.18 = f32[1026]{0:T(1024)S(1)} collective-permute-done((f32[1026]{0:T(1024)S(1)}, f32[1026]{0:T(1024)S(1)}, u32[]{:S(2)}, u32[]{:S(2)}) %collective-permute-start.18) | collective-permute-done | bytes 4136 | tf_op jit(solution)/shard_map/ppermute | solution.py:16
  123.4 4.4 %collective-permute-start.19 = (f32[1026]{0:T(1024)S(1)}, f32[1026]{0:T(1024)S(1)}, u32[]{:S(2)}, u32[]{:S(2)}) collective-permute-start(f32[1026]{0:T(1024)S(1)} %add.359), channel_id=1, source_target_pairs={{0,8},{4,12},{8,0},{12,4},{16,24},{20,28},{24,16},{28,20},{1,9},{5... | collective-permute-start | bytes 12320 | tf_op jit(solution)/shard_map/ppermute | solution.py:16
  127.8 1.1 collective-permute-done.21
  129.5 1.7 %collective-permute-start.20 = (f32[1026]{0:T(1024)S(1)}, f32[1026]{0:T(1024)S(1)}, u32[]{:S(2)}, u32[]{:S(2)}) collective-permute-start(f32[1026]{0:T(1024)S(1)} %add.360), channel_id=1, source_target_pairs={{0,16},{4,20},{8,24},{12,28},{16,0},{20,4},{24,8},{28,12},{1,17},{... | collective-permute-start | bytes 12320 | tf_op jit(solution)/shard_map/ppermute | solution.py:16
  131.2 1.3 collective-permute-done.22
  132.5 1.5 %collective-permute-done.20 = f32[1026]{0:T(1024)S(1)} collective-permute-done((f32[1026]{0:T(1024)S(1)}, f32[1026]{0:T(1024)S(1)}, u32[]{:S(2)}, u32[]{:S(2)}) %collective-permute-start.20) | collective-permute-done | bytes 4136 | tf_op jit(solution)/shard_map/ppermute | solution.py:16
  134.0 0.6 fusion.125
  134.6 1.4 slice_divide_fusion
  137.4 1.6 %divide_convert_fusion = bf16[128,1024]{1,0:T(8,128)(2,1)} fusion(f32[1024,128]{0,1:T(8,128)S(1)} %get-tuple-element.13, f32[128,1024]{1,0:T(8,128)S(1)} %get-tuple-element.16, f32[]{:T(128)} %bitcast.70, f32[128]{0:T(128)S(1)} %add_multiply_fusion, f32[128]{0:T(128)S(1)} %add_rsqrt_fusion, f32[1024]{0:T(1024)S(1)} %dynamic_slice.51), kind=kLoop, calls=%fused_computation.51 | loop fusion | flops 917504 | bytes 1315844 | tf_op jit(solution)/shard_map/convert_element_type | solution.py:264
  (134 shorter events, 13.3 us)
Async XLA Ops:
  0.6 4.1 %copy-start = (bf16[2,192,512]{2,1,0:T(8,128)(2,1)S(1)}, bf16[2,192,512]{2,1,0:T(8,128)(2,1)}, u32[]{:S(2)}) copy-start(bf16[2,192,512]{2,1,0:T(8,128)(2,1)} %param.13) | copy-start | bytes 1179652
  4.7 11.3 %copy-start.5 = (s32[128]{0:T(128)S(1)}, s32[128]{0:T(128)}, u32[]{:S(2)}) copy-start(s32[128]{0:T(128)} %param.18) | copy-start | bytes 1540
  4.7 11.9 %copy-start.3 = (bf16[4096,512]{1,0:T(8,128)(2,1)S(1)}, bf16[4096,512]{1,0:T(8,128)(2,1)}, u32[]{:S(2)}) copy-start(bf16[4096,512]{1,0:T(8,128)(2,1)} %param.12) | copy-start | bytes 12582916
  5.4 14.3 %collective-permute-start.1 = (bf16[2,80,512]{2,1,0:T(8,128)(2,1)S(1)}, bf16[2,80,512]{2,1,0:T(8,128)(2,1)S(1)}, u32[]{:S(2)}, u32[]{:S(2)}) collective-permute-start(bf16[2,80,512]{2,1,0:T(8,128)(2,1)S(1)} %get-tuple-element.17), channel_id=1, source_target_pairs={{0,24},{4,28},{8,0},{12,4},{16,8},{20,12},{24,16},{28,20},{1,25},{... | collective-permute-start | bytes 491528 | tf_op jit(solution)/shard_map/ppermute | solution.py:157
  10.5 10.6 %collective-permute-start.6 = (bf16[2,80,512]{2,1,0:T(8,128)(2,1)S(1)}, bf16[2,80,512]{2,1,0:T(8,128)(2,1)S(1)}, u32[]{:S(2)}, u32[]{:S(2)}) collective-permute-start(bf16[2,80,512]{2,1,0:T(8,128)(2,1)S(1)} %get-tuple-element.18), channel_id=1, source_target_pairs={{0,4},{4,8},{8,12},{12,16},{16,20},{20,24},{24,28},{28,0},{1,5},{5... | collective-permute-start | bytes 491528 | tf_op jit(solution)/shard_map/ppermute | solution.py:157
  12.0 12.4 %collective-permute-start.5 = (bf16[2,80,512]{2,1,0:T(8,128)(2,1)S(1)}, bf16[2,80,512]{2,1,0:T(8,128)(2,1)S(1)}, u32[]{:S(2)}, u32[]{:S(2)}) collective-permute-start(bf16[2,80,512]{2,1,0:T(8,128)(2,1)S(1)} %get-tuple-element.19), channel_id=1, source_target_pairs={{0,8},{4,12},{8,16},{12,20},{16,24},{20,28},{24,0},{28,4},{1,9},{5... | collective-permute-start | bytes 491528 | tf_op jit(solution)/shard_map/ppermute | solution.py:157
  12.0 21.5 %collective-permute-start.4 = (bf16[2,80,512]{2,1,0:T(8,128)(2,1)S(1)}, bf16[2,80,512]{2,1,0:T(8,128)(2,1)S(1)}, u32[]{:S(2)}, u32[]{:S(2)}) collective-permute-start(bf16[2,80,512]{2,1,0:T(8,128)(2,1)S(1)} %get-tuple-element.20), channel_id=1, source_target_pairs={{0,12},{4,16},{8,20},{12,24},{16,28},{20,0},{24,4},{28,8},{1,13},{... | collective-permute-start | bytes 491528 | tf_op jit(solution)/shard_map/ppermute | solution.py:157
  12.9 20.8 %collective-permute-start.3 = (bf16[2,80,512]{2,1,0:T(8,128)(2,1)S(1)}, bf16[2,80,512]{2,1,0:T(8,128)(2,1)S(1)}, u32[]{:S(2)}, u32[]{:S(2)}) collective-permute-start(bf16[2,80,512]{2,1,0:T(8,128)(2,1)S(1)} %get-tuple-element.21), channel_id=1, source_target_pairs={{0,16},{4,20},{8,24},{12,28},{16,0},{20,4},{24,8},{28,12},{1,17},{... | collective-permute-start | bytes 491528 | tf_op jit(solution)/shard_map/ppermute | solution.py:157
  19.7 14.3 %collective-permute-start.2 = (bf16[2,80,512]{2,1,0:T(8,128)(2,1)S(1)}, bf16[2,80,512]{2,1,0:T(8,128)(2,1)S(1)}, u32[]{:S(2)}, u32[]{:S(2)}) collective-permute-start(bf16[2,80,512]{2,1,0:T(8,128)(2,1)S(1)} %get-tuple-element.22), channel_id=1, source_target_pairs={{0,20},{4,24},{8,28},{12,0},{16,4},{20,8},{24,12},{28,16},{1,21},{... | collective-permute-start | bytes 491528 | tf_op jit(solution)/shard_map/ppermute | solution.py:157
  21.1 13.2 %collective-permute-start = (bf16[2,80,512]{2,1,0:T(8,128)(2,1)S(1)}, bf16[2,80,512]{2,1,0:T(8,128)(2,1)S(1)}, u32[]{:S(2)}, u32[]{:S(2)}) collective-permute-start(bf16[2,80,512]{2,1,0:T(8,128)(2,1)S(1)} %get-tuple-element.23), channel_id=1, source_target_pairs={{0,28},{4,0},{8,4},{12,8},{16,12},{20,16},{24,20},{28,24},{1,29},{... | collective-permute-start | bytes 491528 | tf_op jit(solution)/shard_map/ppermute | solution.py:157
  37.5 2.2 %copy-start.2 = (bf16[512,4096]{1,0:T(8,128)(2,1)S(1)}, bf16[512,4096]{1,0:T(8,128)(2,1)}, u32[]{:S(2)}) copy-start(bf16[512,4096]{1,0:T(8,128)(2,1)} %param.14) | copy-start | bytes 12582916
  40.5 3.2 %collective-permute-start.7 = (f32[2,128,1024]{2,1,0:T(8,128)S(1)}, f32[2,128,1024]{2,1,0:T(8,128)S(1)}, u32[]{:S(2)}, u32[]{:S(2)}) collective-permute-start(f32[2,128,1024]{2,1,0:T(8,128)S(1)} %pad_maximum_fusion), channel_id=1, source_target_pairs={{0,1},{1,0},{2,3},{3,2},{4,5},{5,4},{6,7},{7,6},{8,9},{9,8},{10,11... | collective-permute-start | bytes 3145736 | tf_op jit(solution)/shard_map/ppermute | solution.py:16
  43.9 10.1 %copy-start.6 = (s32[128]{0:T(128)S(1)}, s32[128]{0:T(128)}, u32[]{:S(2)}) copy-start(s32[128]{0:T(128)} %param.20) | copy-start | bytes 1540
  43.9 8.8 %collective-permute-start.8 = (bf16[128,1024]{1,0:T(8,128)(2,1)S(1)}, bf16[128,1024]{1,0:T(8,128)(2,1)S(1)}, u32[]{:S(2)}, u32[]{:S(2)}) collective-permute-start(bf16[128,1024]{1,0:T(8,128)(2,1)S(1)} %fusion.48), channel_id=1, source_target_pairs={{0,2},{1,3},{2,0},{3,1},{4,6},{5,7},{6,4},{7,5},{8,10},{9,11},{10,... | collective-permute-start | bytes 786440 | tf_op jit(solution)/shard_map/ppermute | solution.py:16
  53.9 3.1 %collective-permute-start.9 = (bf16[128,1,1024]{2,0,1:T(8,128)(2,1)S(1)}, bf16[128,1,1024]{2,0,1:T(8,128)(2,1)S(1)}, u32[]{:S(2)}, u32[]{:S(2)}) collective-permute-start(bf16[128,1,1024]{2,0,1:T(8,128)(2,1)S(1)} %fusion.49), channel_id=1, source_target_pairs={{0,1},{1,0},{2,3},{3,2},{4,5},{5,4},{6,7},{7,6},{8,9},{9,8},{10,11... | collective-permute-start | bytes 786440 | tf_op jit(solution)/shard_map/ppermute | solution.py:16
  54.0 1.5 %collective-permute-start.11 = (f32[128]{0:T(128)S(1)}, f32[128]{0:T(128)S(1)}, u32[]{:S(2)}, u32[]{:S(2)}) collective-permute-start(f32[128]{0:T(128)S(1)} %get-tuple-element.15), channel_id=1, source_target_pairs={{0,1},{1,0},{2,3},{3,2},{4,5},{5,4},{6,7},{7,6},{8,9},{9,8},{10,11... | collective-permute-start | bytes 1544 | tf_op jit(solution)/shard_map/ppermute | solution.py:16
  55.5 3.5 %collective-permute-start.12 = (f32[128]{0:T(128)S(1)}, f32[128]{0:T(128)S(1)}, u32[]{:S(2)}, u32[]{:S(2)}) collective-permute-start(f32[128]{0:T(128)S(1)} %add.343), channel_id=1, source_target_pairs={{0,2},{1,3},{2,0},{3,1},{4,6},{5,7},{6,4},{7,5},{8,10},{9,11},{10,... | collective-permute-start | bytes 1544 | tf_op jit(solution)/shard_map/ppermute | solution.py:16
  57.4 13.8 %collective-permute-start.10 = (bf16[128,2048]{0,1:T(8,128)(2,1)S(1)}, bf16[128,2048]{0,1:T(8,128)(2,1)S(1)}, u32[]{:S(2)}, u32[]{:S(2)}) collective-permute-start(bf16[128,2048]{0,1:T(8,128)(2,1)S(1)} %bitcast.256), channel_id=1, source_target_pairs={{0,2},{1,3},{2,0},{3,1},{4,6},{5,7},{6,4},{7,5},{8,10},{9,11},{10,... | collective-permute-start | bytes 1572872 | tf_op jit(solution)/shard_map/ppermute | solution.py:16
  79.5 2.6 %copy-start.4 = (s32[128]{0:T(128)S(1)}, s32[128]{0:T(128)}, u32[]{:S(2)}) copy-start(s32[128]{0:T(128)} %param.21) | copy-start | bytes 1540
  80.3 1.2 collective-permute-start.13
  81.5 3.7 %collective-permute-start.14 = (f32[3,128]{1,0:T(4,128)S(1)}, f32[3,128]{1,0:T(4,128)S(1)}, u32[]{:S(2)}, u32[]{:S(2)}) collective-permute-start(f32[3,128]{1,0:T(4,128)S(1)} %pad_maximum_fusion.3), channel_id=1, source_target_pairs={{0,2},{1,3},{2,0},{3,1},{4,6},{5,7},{6,4},{7,5},{8,10},{9,11},{10,... | collective-permute-start | bytes 4616 | tf_op jit(solution)/shard_map/ppermute | solution.py:16
  97.1 9.4 %collective-permute-start.16 = (f32[1,1024,128]{1,2,0:T(8,128)}, f32[1,1024,128]{1,2,0:T(8,128)}, u32[]{:S(2)}, u32[]{:S(2)}) collective-permute-start(f32[1,1024,128]{1,2,0:T(8,128)} %bitcast.254), channel_id=1, source_target_pairs={{0,1},{1,0},{2,3},{3,2},{4,5},{5,4},{6,7},{7,6},{8,9},{9,8},{10,11... | collective-permute-start | bytes 1572872 | tf_op jit(solution)/shard_map/ppermute | solution.py:16
  105.7 2.7 %collective-permute-start.15 = (f32[1,1024,128]{1,2,0:T(8,128)S(1)}, f32[1,1024,128]{1,2,0:T(8,128)S(1)}, u32[]{:S(2)}, u32[]{:S(2)}) collective-permute-start(f32[1,1024,128]{1,2,0:T(8,128)S(1)} %bitcast.255), channel_id=1, source_target_pairs={{0,1},{1,0},{2,3},{3,2},{4,5},{5,4},{6,7},{7,6},{8,9},{9,8},{10,11... | collective-permute-start | bytes 1572872 | tf_op jit(solution)/shard_map/ppermute | solution.py:16
  107.6 8.3 %collective-permute-start.17 = (bf16[1024,128]{0,1:T(8,128)(2,1)S(1)}, bf16[1024,128]{0,1:T(8,128)(2,1)S(1)}, u32[]{:S(2)}, u32[]{:S(2)}) collective-permute-start(bf16[1024,128]{0,1:T(8,128)(2,1)S(1)} %fusion.50), channel_id=1, source_target_pairs={{0,2},{1,3},{2,0},{3,1},{4,6},{5,7},{6,4},{7,5},{8,10},{9,11},{10,... | collective-permute-start | bytes 786440 | tf_op jit(solution)/shard_map/ppermute | solution.py:16
  108.2 30.7 %copy-start.1 = (bf16[2,192,512]{2,1,0:T(8,128)(2,1)S(1)}, bf16[2,192,512]{2,1,0:T(8,128)(2,1)}, u32[]{:S(2)}) copy-start(bf16[2,192,512]{2,1,0:T(8,128)(2,1)} %param.13) | copy-start | bytes 1179652
  117.6 5.8 %collective-permute-start.18 = (f32[1026]{0:T(1024)S(1)}, f32[1026]{0:T(1024)S(1)}, u32[]{:S(2)}, u32[]{:S(2)}) collective-permute-start(f32[1026]{0:T(1024)S(1)} %concatenate.3), channel_id=1, source_target_pairs={{0,4},{4,0},{8,12},{12,8},{16,20},{20,16},{24,28},{28,24},{1,5},{5... | collective-permute-start | bytes 12320 | tf_op jit(solution)/shard_map/ppermute | solution.py:16
  123.4 6.1 %collective-permute-start.19 = (f32[1026]{0:T(1024)S(1)}, f32[1026]{0:T(1024)S(1)}, u32[]{:S(2)}, u32[]{:S(2)}) collective-permute-start(f32[1026]{0:T(1024)S(1)} %add.359), channel_id=1, source_target_pairs={{0,8},{4,12},{8,0},{12,4},{16,24},{20,28},{24,16},{28,20},{1,9},{5... | collective-permute-start | bytes 12320 | tf_op jit(solution)/shard_map/ppermute | solution.py:16
  127.8 1.1 collective-permute-start.21
  129.0 3.5 %collective-permute-start.22 = (f32[128]{0:T(128)S(1)}, f32[128]{0:T(128)S(1)}, u32[]{:S(2)}, u32[]{:S(2)}) collective-permute-start(f32[128]{0:T(128)S(1)} %add.362), channel_id=1, source_target_pairs={{0,2},{1,3},{2,0},{3,1},{4,6},{5,7},{6,4},{7,5},{8,10},{9,11},{10,... | collective-permute-start | bytes 1544 | tf_op jit(solution)/shard_map/ppermute | solution.py:16
  129.5 4.6 %collective-permute-start.20 = (f32[1026]{0:T(1024)S(1)}, f32[1026]{0:T(1024)S(1)}, u32[]{:S(2)}, u32[]{:S(2)}) collective-permute-start(f32[1026]{0:T(1024)S(1)} %add.360), channel_id=1, source_target_pairs={{0,16},{4,20},{8,24},{12,28},{16,0},{20,4},{24,8},{28,12},{1,17},{... | collective-permute-start | bytes 12320 | tf_op jit(solution)/shard_map/ppermute | solution.py:16

commit v14 on v13

--- a/solution.py
+++ b/solution.py
@@ -207,7 +207,15 @@
         top_side = (fsdp_index >> (levels - 1)) & 1
         near_rows = lax.dynamic_slice_in_dim(w_vocab, top_side * half, half, 0)
         far_rows = lax.dynamic_slice_in_dim(w_vocab, (1 - top_side) * half, half, 0)
-        near_normed = gather_bits(normed_part, "fsdp", 1, levels - 1)
+        if levels == 2:
+            pair_normed = exchange(normed_part, "fsdp", 0)
+            near_normed = jnp.where(
+                low_bit == 0,
+                jnp.concatenate([normed_part, pair_normed], 1),
+                jnp.concatenate([pair_normed, normed_part], 1),
+            )
+        else:
+            near_normed = gather_bits(normed_part, "fsdp", 1, levels - 1)
         far_normed = exchange(near_normed, "fsdp", levels - 1)
         logits = (
             jnp.dot(near_normed, near_rows, preferred_element_type=jnp.float32)

time: 141 us -> 148 us (1.050)
  waiting for transfers between devices: 38.7 us -> 44.1 us
  starting transfers between devices: 31.5 us -> 34.1 us
    ppermute x16, waiting for transfers between devices: 29.8 us -> 35.3 us  [exchange(): return lax.ppermute(x, axis, [(i, i ^ 1 << bit) for i in range(size)])]
    ppermute x16, starting transfers between devices: 17 us -> 19.5 us  [exchange(): return lax.ppermute(x, axis, [(i, i ^ 1 << bit) for i in range(size)])]
  transfers between devices with their start and end apart: 23 -> 23, of which waited for: 12 -> 12; matrix products, arithmetic and copies ran while one was open for 20% -> 13% of each run, Pallas kernels for 0% -> 0%
where the time goes in v14:
time: 148 us
  waiting for transfers between devices  44.1 us (30%)
  matrix products  43.1 us (29%)
  starting transfers between devices  34.1 us (23%)
  other arithmetic  11.9 us (8%)
  local copies, waits for them, and re-layouts  10.7 us (7%)
  between operations  3.91 us (3%)
    ppermute x16, waiting for transfers between devices, exchange(): return lax.ppermute(x, axis, [(i, i ^ 1 << bit) for i in range(size)])  35.3 us
    ppermute x16, starting transfers between devices, exchange(): return lax.ppermute(x, axis, [(i, i ^ 1 << bit) for i in range(size)])  19.5 us
    ppermute x7, starting transfers between devices, body(): lax.ppermute(block, 'dp', [(i, (i - shift) % dp_count) for i in range(dp_...  14.6 us
    ppermute x7, waiting for transfers between devices, body(): lax.ppermute(block, 'dp', [(i, (i - shift) % dp_count) for i in range(dp_...  8.81 us
    dot_general x1, matrix products, body(): jnp.dot(near_normed, near_rows, preferred_element_type=jnp.float32)  8.43 us
    dot_general x1, matrix products, body(): lax.dot_general(far_rows, grad_logits, contract, preferred_element_type=j...  8.36 us
    dot_general x1, matrix products, body(): lax.dot_general(near_rows, near_logits, contract, preferred_element_type=...  8.36 us
    dot_general x1, matrix products, body(): jnp.dot(far_normed, far_rows, preferred_element_type=jnp.float32)  8.11 us
  transfers between devices with their start and end apart: 23, of which 12 were waited for; matrix products, arithmetic and copies ran while one was open for 13% of the time, Pallas kernels for 0%

profile of v14, /device:TPU:0, one launch (start us, length us, event | category | flops | bytes accessed | tf_op | source)
XLA Modules:
  0.0 147.8 jit_solution(8066298566467465664)
XLA Ops:
  0.7 0.8 fusion.84
  1.7 0.8 select_reduce_fusion.11
  2.5 0.8 lt.80
  3.4 0.8 select_reduce_fusion.19
  5.4 5.1 %collective-permute-start.1 = (bf16[2,80,512]{2,1,0:T(8,128)(2,1)S(1)}, bf16[2,80,512]{2,1,0:T(8,128)(2,1)S(1)}, u32[]{:S(2)}, u32[]{:S(2)}) collective-permute-start(bf16[2,80,512]{2,1,0:T(8,128)(2,1)S(1)} %get-tuple-element.17), channel_id=1, source_target_pairs={{0,24},{4,28},{8,0},{12,4},{16,8},{20,12},{24,16},{28,20},{1,25},{... | collective-permute-start | bytes 491528 | tf_op jit(solution)/shard_map/ppermute | solution.py:157
  10.5 1.5 %collective-permute-start.6 = (bf16[2,80,512]{2,1,0:T(8,128)(2,1)S(1)}, bf16[2,80,512]{2,1,0:T(8,128)(2,1)S(1)}, u32[]{:S(2)}, u32[]{:S(2)}) collective-permute-start(bf16[2,80,512]{2,1,0:T(8,128)(2,1)S(1)} %get-tuple-element.18), channel_id=1, source_target_pairs={{0,4},{4,8},{8,12},{12,16},{16,20},{20,24},{24,28},{28,0},{1,5},{5... | collective-permute-start | bytes 491528 | tf_op jit(solution)/shard_map/ppermute | solution.py:157
  12.0 1.0 collective-permute-start.4
  12.9 2.8 %collective-permute-start.3 = (bf16[2,80,512]{2,1,0:T(8,128)(2,1)S(1)}, bf16[2,80,512]{2,1,0:T(8,128)(2,1)S(1)}, u32[]{:S(2)}, u32[]{:S(2)}) collective-permute-start(bf16[2,80,512]{2,1,0:T(8,128)(2,1)S(1)} %get-tuple-element.21), channel_id=1, source_target_pairs={{0,16},{4,20},{8,24},{12,28},{16,0},{20,4},{24,8},{28,12},{1,17},{... | collective-permute-start | bytes 491528 | tf_op jit(solution)/shard_map/ppermute | solution.py:157
  16.6 2.0 %convolution_convert_fusion.1 = bf16[128,512]{1,0:T(8,128)(2,1)S(1)} fusion(bf16[128,4096]{1,0:T(8,128)(2,1)} %param.11, bf16[4096,512]{1,0:T(8,128)(2,1)S(1)} %copy-done.3), kind=kOutput, calls=%fused_computation.29 | convolution fusion | flops 536936448 | bytes 5373952 | tf_op jit(solution)/shard_map/dot_general | solution.py:148
  19.7 1.1 collective-permute-start.2
  21.1 3.1 %collective-permute-start = (bf16[2,80,512]{2,1,0:T(8,128)(2,1)S(1)}, bf16[2,80,512]{2,1,0:T(8,128)(2,1)S(1)}, u32[]{:S(2)}, u32[]{:S(2)}) collective-permute-start(bf16[2,80,512]{2,1,0:T(8,128)(2,1)S(1)} %get-tuple-element.23), channel_id=1, source_target_pairs={{0,28},{4,0},{8,4},{12,8},{16,12},{20,16},{24,20},{28,24},{1,29},{... | collective-permute-start | bytes 491528 | tf_op jit(solution)/shard_map/ppermute | solution.py:157
  24.7 8.8 %collective-permute-done.4 = bf16[2,80,512]{2,1,0:T(8,128)(2,1)S(1)} collective-permute-done((bf16[2,80,512]{2,1,0:T(8,128)(2,1)S(1)}, bf16[2,80,512]{2,1,0:T(8,128)(2,1)S(1)}, u32[]{:S(2)}, u32[]{:S(2)}) %collective-permute-start.4) | collective-permute-done | bytes 163872 | tf_op jit(solution)/shard_map/ppermute | solution.py:157
  38.4 1.3 copy-done.2
  40.6 1.6 %convolution_bitcast_fusion.2 = f32[1,128,1024]{2,1,0:T(8,128)S(1)} fusion(bf16[128,512]{0,1:T(8,128)(2,1)S(1)} %bitcast.231, bf16[512,4096]{1,0:T(8,128)(2,1)} %param.14, s32[]{:T(128)S(6)} %select_n.228), kind=kOutput, calls=%fused_computation.18 | convolution fusion | flops 134217728 | bytes 1703940 | tf_op jit(solution)/shard_map/dot_general | solution.py:186
  42.1 1.6 %convolution_bitcast_fusion.3 = f32[1,128,1024]{2,1,0:T(8,128)S(1)} fusion(bf16[128,512]{0,1:T(8,128)(2,1)S(1)} %bitcast.232, bf16[512,4096]{1,0:T(8,128)(2,1)} %param.14, s32[]{:T(128)S(6)} %select_n.227), kind=kOutput, calls=%fused_computation.19 | convolution fusion | flops 134217728 | bytes 1703940 | tf_op jit(solution)/shard_map/dot_general | solution.py:186
  43.9 1.6 %collective-permute-start.8 = (bf16[128,1024]{1,0:T(8,128)(2,1)S(1)}, bf16[128,1024]{1,0:T(8,128)(2,1)S(1)}, u32[]{:S(2)}, u32[]{:S(2)}) collective-permute-start(bf16[128,1024]{1,0:T(8,128)(2,1)S(1)} %fusion.48), channel_id=1, source_target_pairs={{0,2},{1,3},{2,0},{3,1},{4,6},{5,7},{6,4},{7,5},{8,10},{9,11},{10,... | collective-permute-start | bytes 786440 | tf_op jit(solution)/shard_map/ppermute | solution.py:16
  45.5 0.7 dynamic_slice.51
  46.2 6.5 %collective-permute-done.8 = bf16[128,1024]{1,0:T(8,128)(2,1)S(1)} collective-permute-done((bf16[128,1024]{1,0:T(8,128)(2,1)S(1)}, bf16[128,1024]{1,0:T(8,128)(2,1)S(1)}, u32[]{:S(2)}, u32[]{:S(2)}) %collective-permute-start.8) | collective-permute-done | bytes 262176 | tf_op jit(solution)/shard_map/ppermute | solution.py:16
  52.7 1.1 multiply_reduce_fusion.1
  53.9 1.5 %collective-permute-done.9 = bf16[128,1024]{1,0:T(8,128)(2,1)S(1)} collective-permute-done((bf16[128,1024]{1,0:T(8,128)(2,1)S(1)}, bf16[128,1024]{1,0:T(8,128)(2,1)S(1)}, u32[]{:S(2)}, u32[]{:S(2)}) %collective-permute-start.9) | collective-permute-done | bytes 262176 | tf_op jit(solution)/shard_map/ppermute | solution.py:16
  55.6 1.6 %collective-permute-start.10 = (bf16[128,2048]{1,0:T(8,128)(2,1)S(1)}, bf16[128,2048]{1,0:T(8,128)(2,1)S(1)}, u32[]{:S(2)}, u32[]{:S(2)}) collective-permute-start(bf16[128,2048]{1,0:T(8,128)(2,1)S(1)} %maximum_select_fusion), channel_id=1, source_target_pairs={{0,2},{1,3},{2,0},{3,1},{4,6},{5,7},{6,4},{7,5},{8,10},{9,11},{10,... | collective-permute-start | bytes 1572872 | tf_op jit(solution)/shard_map/ppermute | solution.py:16
  57.2 1.1 collective-permute-done.11
  58.8 10.9 %collective-permute-done.12 = f32[128]{0:T(128)S(1)} collective-permute-done((f32[128]{0:T(128)S(1)}, f32[128]{0:T(128)S(1)}, u32[]{:S(2)}, u32[]{:S(2)}) %collective-permute-start.12) | collective-permute-done | bytes 544 | tf_op jit(solution)/shard_map/ppermute | solution.py:16
  69.7 8.1 %fusion.2 = f32[128,4096]{1,0:T(8,128)S(1)} fusion(bf16[128,2048]{1,0:T(8,128)(2,1)S(1)} %collective-permute-done.10, bf16[4096,4096]{1,0:T(8,128)(2,1)} %param.16, s32[]{:T(128)S(6)} %select_n.236), kind=kOutput, calls=%fused_computation.2 | convolution fusion | flops 2147483648 | bytes 19398660 | tf_op jit(solution)/shard_map/dot_general | solution.py:222
  77.8 8.4 %fusion.125 = (f32[128]{0:T(128)S(1)}, f32[128,4096]{1,0:T(8,128)S(1)}) fusion(f32[128]{0:T(128)S(1)} %add_rsqrt_fusion, f32[128,4096]{1,0:T(8,128)S(1)} %fusion.2, bf16[128,2048]{1,0:T(8,128)(2,1)S(1)} %maximum_select_fusion, bf16[4096,4096]{1,0:T(8,128)(2,1)} %param.16, s32[]{:T(128)S(6)} %select_n.235), kind=kOutput, calls=%fused_computation.253 | convolution fusion | flops 2149056512 | bytes 21496836 | tf_op jit(solution)/shard_map/dot_general | solution.py:221
  86.3 0.7 select_reduce_fusion
  87.0 1.1 collective-permute-done.13
  88.2 1.6 %collective-permute-start.14 = (f32[3,128]{1,0:T(4,128)S(1)}, f32[3,128]{1,0:T(4,128)S(1)}, u32[]{:S(2)}, u32[]{:S(2)}) collective-permute-start(f32[3,128]{1,0:T(4,128)S(1)} %pad_maximum_fusion.2), channel_id=1, source_target_pairs={{0,2},{1,3},{2,0},{3,1},{4,6},{5,7},{6,4},{7,5},{8,10},{9,11},{10,... | collective-permute-start | bytes 4616 | tf_op jit(solution)/shard_map/ppermute | solution.py:16
  89.8 2.1 %collective-permute-done.14 = f32[3,128]{1,0:T(4,128)S(1)} collective-permute-done((f32[3,128]{1,0:T(4,128)S(1)}, f32[3,128]{1,0:T(4,128)S(1)}, u32[]{:S(2)}, u32[]{:S(2)}) %collective-permute-start.14) | collective-permute-done | bytes 1568 | tf_op jit(solution)/shard_map/ppermute | solution.py:16
  91.9 0.6 fusion.105
  92.5 8.4 %fusion = f32[2048,128]{1,0:T(8,128)S(1)} fusion(bf16[4096,4096]{1,0:T(8,128)(2,1)} %param.16, s32[]{:T(128)S(6)} %select_n.236, f32[128,4096]{1,0:T(8,128)S(1)} %get-tuple-element.82, f32[128]{0:T(128)S(1)} %get-tuple-element.14, f32[128]{0:T(128)S(1)} %convert_element_type.63, s32[128]{0:T(128)S(1)} %broadcast_subtract_fusion), kind=kOutput, calls=%fused_computation | convolution fusion | flops 2150629376 | bytes 19924484 | tf_op jit(solution)/shard_map/dot_general | solution.py:242
  100.9 0.9 constant_dynamic-slice_fusion
  101.8 2.0 %copy.108 = f32[1,1,1024,128]{2,3,1,0:T(8,128)} copy(f32[1,1,1024,128]{3,2,1,0:T(8,128)} %get-tuple-element.29) | data formatting | bytes 1048576
  103.8 8.4 %fusion.4 = f32[2048,128]{1,0:T(8,128)S(1)} fusion(bf16[4096,4096]{1,0:T(8,128)(2,1)} %param.16, s32[]{:T(128)S(6)} %select_n.235, f32[128,4096]{1,0:T(8,128)S(1)} %get-tuple-element.82, f32[128]{0:T(128)S(1)} %get-tuple-element.14, f32[128]{0:T(128)S(1)} %convert_element_type.63, s32[128]{0:T(128)S(1)} %broadcast_subtract_fusion), kind=kOutput, calls=%fused_computation.4 | convolution fusion | flops 2150629376 | bytes 19924484 | tf_op jit(solution)/shard_map/dot_general | solution.py:250
  113.2 1.1 fusion.49
  114.3 1.6 %collective-permute-start.17 = (bf16[1024,128]{0,1:T(8,128)(2,1)S(1)}, bf16[1024,128]{0,1:T(8,128)(2,1)S(1)}, u32[]{:S(2)}, u32[]{:S(2)}) collective-permute-start(bf16[1024,128]{0,1:T(8,128)(2,1)S(1)} %fusion.49), channel_id=1, source_target_pairs={{0,2},{1,3},{2,0},{3,1},{4,6},{5,7},{6,4},{7,5},{8,10},{9,11},{10,... | collective-permute-start | bytes 786440 | tf_op jit(solution)/shard_map/ppermute | solution.py:16
  116.1 6.5 %collective-permute-done.17 = bf16[1024,128]{0,1:T(8,128)(2,1)S(1)} collective-permute-done((bf16[1024,128]{0,1:T(8,128)(2,1)S(1)}, bf16[1024,128]{0,1:T(8,128)(2,1)S(1)}, u32[]{:S(2)}, u32[]{:S(2)}) %collective-permute-start.17) | collective-permute-done | bytes 262176 | tf_op jit(solution)/shard_map/ppermute | solution.py:16
  122.9 1.4 concatenate.11
  124.3 4.2 %collective-permute-start.18 = (f32[1026]{0:T(1024)S(1)}, f32[1026]{0:T(1024)S(1)}, u32[]{:S(2)}, u32[]{:S(2)}) collective-permute-start(f32[1026]{0:T(1024)S(1)} %concatenate.11), channel_id=1, source_target_pairs={{0,4},{4,0},{8,12},{12,8},{16,20},{20,16},{24,28},{28,24},{1,5},{5... | collective-permute-start | bytes 12320 | tf_op jit(solution)/shard_map/ppermute | solution.py:16
  128.5 1.6 %collective-permute-done.18 = f32[1026]{0:T(1024)S(1)} collective-permute-done((f32[1026]{0:T(1024)S(1)}, f32[1026]{0:T(1024)S(1)}, u32[]{:S(2)}, u32[]{:S(2)}) %collective-permute-start.18) | collective-permute-done | bytes 4136 | tf_op jit(solution)/shard_map/ppermute | solution.py:16
  130.1 4.4 %collective-permute-start.19 = (f32[1026]{0:T(1024)S(1)}, f32[1026]{0:T(1024)S(1)}, u32[]{:S(2)}, u32[]{:S(2)}) collective-permute-start(f32[1026]{0:T(1024)S(1)} %add.359), channel_id=1, source_target_pairs={{0,8},{4,12},{8,0},{12,4},{16,24},{20,28},{24,16},{28,20},{1,9},{5... | collective-permute-start | bytes 12320 | tf_op jit(solution)/shard_map/ppermute | solution.py:16
  134.5 1.1 collective-permute-done.21
  135.7 1.5 %collective-permute-start.22 = (f32[128]{0:T(128)S(1)}, f32[128]{0:T(128)S(1)}, u32[]{:S(2)}, u32[]{:S(2)}) collective-permute-start(f32[128]{0:T(128)S(1)} %add.362), channel_id=1, source_target_pairs={{0,2},{1,3},{2,0},{3,1},{4,6},{5,7},{6,4},{7,5},{8,10},{9,11},{10,... | collective-permute-start | bytes 1544 | tf_op jit(solution)/shard_map/ppermute | solution.py:16
  137.2 1.7 %collective-permute-start.20 = (f32[1026]{0:T(1024)S(1)}, f32[1026]{0:T(1024)S(1)}, u32[]{:S(2)}, u32[]{:S(2)}) collective-permute-start(f32[1026]{0:T(1024)S(1)} %add.360), channel_id=1, source_target_pairs={{0,16},{4,20},{8,24},{12,28},{16,0},{20,4},{24,8},{28,12},{1,17},{... | collective-permute-start | bytes 12320 | tf_op jit(solution)/shard_map/ppermute | solution.py:16
  139.2 2.5 %collective-permute-done.20 = f32[1026]{0:T(1024)S(1)} collective-permute-done((f32[1026]{0:T(1024)S(1)}, f32[1026]{0:T(1024)S(1)}, u32[]{:S(2)}, u32[]{:S(2)}) %collective-permute-start.20) | collective-permute-done | bytes 4136 | tf_op jit(solution)/shard_map/ppermute | solution.py:16
  141.7 0.6 fusion.124
  142.3 1.4 slice_divide_fusion
  145.1 1.6 %divide_convert_fusion = bf16[128,1024]{1,0:T(8,128)(2,1)} fusion(f32[1024,128]{0,1:T(8,128)S(1)} %get-tuple-element.13, f32[128,1024]{1,0:T(8,128)S(1)} %get-tuple-element.16, f32[]{:T(128)} %bitcast.66, f32[128]{0:T(128)S(1)} %add_multiply_fusion, f32[128]{0:T(128)S(1)} %add_rsqrt_fusion, f32[1024]{0:T(1024)S(1)} %dynamic_slice.51), kind=kLoop, calls=%fused_computation.51 | loop fusion | flops 917504 | bytes 1315844 | tf_op jit(solution)/shard_map/convert_element_type | solution.py:272
  (132 shorter events, 12.3 us)
Async XLA Ops:
  0.6 4.1 %copy-start = (bf16[2,192,512]{2,1,0:T(8,128)(2,1)S(1)}, bf16[2,192,512]{2,1,0:T(8,128)(2,1)}, u32[]{:S(2)}) copy-start(bf16[2,192,512]{2,1,0:T(8,128)(2,1)} %param.13) | copy-start | bytes 1179652
  4.7 11.3 %copy-start.5 = (s32[128]{0:T(128)S(1)}, s32[128]{0:T(128)}, u32[]{:S(2)}) copy-start(s32[128]{0:T(128)} %param.18) | copy-start | bytes 1540
  4.7 11.9 %copy-start.3 = (bf16[4096,512]{1,0:T(8,128)(2,1)S(1)}, bf16[4096,512]{1,0:T(8,128)(2,1)}, u32[]{:S(2)}) copy-start(bf16[4096,512]{1,0:T(8,128)(2,1)} %param.12) | copy-start | bytes 12582916
  5.4 14.3 %collective-permute-start.1 = (bf16[2,80,512]{2,1,0:T(8,128)(2,1)S(1)}, bf16[2,80,512]{2,1,0:T(8,128)(2,1)S(1)}, u32[]{:S(2)}, u32[]{:S(2)}) collective-permute-start(bf16[2,80,512]{2,1,0:T(8,128)(2,1)S(1)} %get-tuple-element.17), channel_id=1, source_target_pairs={{0,24},{4,28},{8,0},{12,4},{16,8},{20,12},{24,16},{28,20},{1,25},{... | collective-permute-start | bytes 491528 | tf_op jit(solution)/shard_map/ppermute | solution.py:157
  10.5 10.6 %collective-permute-start.6 = (bf16[2,80,512]{2,1,0:T(8,128)(2,1)S(1)}, bf16[2,80,512]{2,1,0:T(8,128)(2,1)S(1)}, u32[]{:S(2)}, u32[]{:S(2)}) collective-permute-start(bf16[2,80,512]{2,1,0:T(8,128)(2,1)S(1)} %get-tuple-element.18), channel_id=1, source_target_pairs={{0,4},{4,8},{8,12},{12,16},{16,20},{20,24},{24,28},{28,0},{1,5},{5... | collective-permute-start | bytes 491528 | tf_op jit(solution)/shard_map/ppermute | solution.py:157
  12.0 12.4 %collective-permute-start.5 = (bf16[2,80,512]{2,1,0:T(8,128)(2,1)S(1)}, bf16[2,80,512]{2,1,0:T(8,128)(2,1)S(1)}, u32[]{:S(2)}, u32[]{:S(2)}) collective-permute-start(bf16[2,80,512]{2,1,0:T(8,128)(2,1)S(1)} %get-tuple-element.19), channel_id=1, source_target_pairs={{0,8},{4,12},{8,16},{12,20},{16,24},{20,28},{24,0},{28,4},{1,9},{5... | collective-permute-start | bytes 491528 | tf_op jit(solution)/shard_map/ppermute | solution.py:157
  12.0 21.5 %collective-permute-start.4 = (bf16[2,80,512]{2,1,0:T(8,128)(2,1)S(1)}, bf16[2,80,512]{2,1,0:T(8,128)(2,1)S(1)}, u32[]{:S(2)}, u32[]{:S(2)}) collective-permute-start(bf16[2,80,512]{2,1,0:T(8,128)(2,1)S(1)} %get-tuple-element.20), channel_id=1, source_target_pairs={{0,12},{4,16},{8,20},{12,24},{16,28},{20,0},{24,4},{28,8},{1,13},{... | collective-permute-start | bytes 491528 | tf_op jit(solution)/shard_map/ppermute | solution.py:157
  12.9 20.8 %collective-permute-start.3 = (bf16[2,80,512]{2,1,0:T(8,128)(2,1)S(1)}, bf16[2,80,512]{2,1,0:T(8,128)(2,1)S(1)}, u32[]{:S(2)}, u32[]{:S(2)}) collective-permute-start(bf16[2,80,512]{2,1,0:T(8,128)(2,1)S(1)} %get-tuple-element.21), channel_id=1, source_target_pairs={{0,16},{4,20},{8,24},{12,28},{16,0},{20,4},{24,8},{28,12},{1,17},{... | collective-permute-start | bytes 491528 | tf_op jit(solution)/shard_map/ppermute | solution.py:157
  19.7 14.3 %collective-permute-start.2 = (bf16[2,80,512]{2,1,0:T(8,128)(2,1)S(1)}, bf16[2,80,512]{2,1,0:T(8,128)(2,1)S(1)}, u32[]{:S(2)}, u32[]{:S(2)}) collective-permute-start(bf16[2,80,512]{2,1,0:T(8,128)(2,1)S(1)} %get-tuple-element.22), channel_id=1, source_target_pairs={{0,20},{4,24},{8,28},{12,0},{16,4},{20,8},{24,12},{28,16},{1,21},{... | collective-permute-start | bytes 491528 | tf_op jit(solution)/shard_map/ppermute | solution.py:157
  21.1 13.3 %collective-permute-start = (bf16[2,80,512]{2,1,0:T(8,128)(2,1)S(1)}, bf16[2,80,512]{2,1,0:T(8,128)(2,1)S(1)}, u32[]{:S(2)}, u32[]{:S(2)}) collective-permute-start(bf16[2,80,512]{2,1,0:T(8,128)(2,1)S(1)} %get-tuple-element.23), channel_id=1, source_target_pairs={{0,28},{4,0},{8,4},{12,8},{16,12},{20,16},{24,20},{28,24},{1,29},{... | collective-permute-start | bytes 491528 | tf_op jit(solution)/shard_map/ppermute | solution.py:157
  37.5 2.2 %copy-start.2 = (bf16[512,4096]{1,0:T(8,128)(2,1)S(1)}, bf16[512,4096]{1,0:T(8,128)(2,1)}, u32[]{:S(2)}) copy-start(bf16[512,4096]{1,0:T(8,128)(2,1)} %param.14) | copy-start | bytes 12582916
  40.5 3.2 %collective-permute-start.7 = (f32[2,128,1024]{2,1,0:T(8,128)S(1)}, f32[2,128,1024]{2,1,0:T(8,128)S(1)}, u32[]{:S(2)}, u32[]{:S(2)}) collective-permute-start(f32[2,128,1024]{2,1,0:T(8,128)S(1)} %pad_maximum_fusion), channel_id=1, source_target_pairs={{0,1},{1,0},{2,3},{3,2},{4,5},{5,4},{6,7},{7,6},{8,9},{9,8},{10,11... | collective-permute-start | bytes 3145736 | tf_op jit(solution)/shard_map/ppermute | solution.py:16
  43.8 13.3 %copy-start.6 = (s32[128]{0:T(128)S(1)}, s32[128]{0:T(128)}, u32[]{:S(2)}) copy-start(s32[128]{0:T(128)} %param.20) | copy-start | bytes 1540
  43.9 8.8 %collective-permute-start.8 = (bf16[128,1024]{1,0:T(8,128)(2,1)S(1)}, bf16[128,1024]{1,0:T(8,128)(2,1)S(1)}, u32[]{:S(2)}, u32[]{:S(2)}) collective-permute-start(bf16[128,1024]{1,0:T(8,128)(2,1)S(1)} %fusion.48), channel_id=1, source_target_pairs={{0,2},{1,3},{2,0},{3,1},{4,6},{5,7},{6,4},{7,5},{8,10},{9,11},{10,... | collective-permute-start | bytes 786440 | tf_op jit(solution)/shard_map/ppermute | solution.py:16
  53.8 1.6 %collective-permute-start.9 = (bf16[128,1024]{1,0:T(8,128)(2,1)S(1)}, bf16[128,1024]{1,0:T(8,128)(2,1)S(1)}, u32[]{:S(2)}, u32[]{:S(2)}) collective-permute-start(bf16[128,1024]{1,0:T(8,128)(2,1)S(1)} %multiply_convert_fusion.1), channel_id=1, source_target_pairs={{0,1},{1,0},{2,3},{3,2},{4,5},{5,4},{6,7},{7,6},{8,9},{9,8},{10,11... | collective-permute-start | bytes 786440 | tf_op jit(solution)/shard_map/ppermute | solution.py:16
  55.6 14.1 %collective-permute-start.10 = (bf16[128,2048]{1,0:T(8,128)(2,1)S(1)}, bf16[128,2048]{1,0:T(8,128)(2,1)S(1)}, u32[]{:S(2)}, u32[]{:S(2)}) collective-permute-start(bf16[128,2048]{1,0:T(8,128)(2,1)S(1)} %maximum_select_fusion), channel_id=1, source_target_pairs={{0,2},{1,3},{2,0},{3,1},{4,6},{5,7},{6,4},{7,5},{8,10},{9,11},{10,... | collective-permute-start | bytes 1572872 | tf_op jit(solution)/shard_map/ppermute | solution.py:16
  57.2 1.1 collective-permute-start.11
  58.3 11.4 %collective-permute-start.12 = (f32[128]{0:T(128)S(1)}, f32[128]{0:T(128)S(1)}, u32[]{:S(2)}, u32[]{:S(2)}) collective-permute-start(f32[128]{0:T(128)S(1)} %add.343), channel_id=1, source_target_pairs={{0,2},{1,3},{2,0},{3,1},{4,6},{5,7},{6,4},{7,5},{8,10},{9,11},{10,... | collective-permute-start | bytes 1544 | tf_op jit(solution)/shard_map/ppermute | solution.py:16
  86.2 3.6 %copy-start.4 = (s32[128]{0:T(128)S(1)}, s32[128]{0:T(128)}, u32[]{:S(2)}) copy-start(s32[128]{0:T(128)} %param.21) | copy-start | bytes 1540
  87.0 1.2 collective-permute-start.13
  88.2 3.7 %collective-permute-start.14 = (f32[3,128]{1,0:T(4,128)S(1)}, f32[3,128]{1,0:T(4,128)S(1)}, u32[]{:S(2)}, u32[]{:S(2)}) collective-permute-start(f32[3,128]{1,0:T(4,128)S(1)} %pad_maximum_fusion.2), channel_id=1, source_target_pairs={{0,2},{1,3},{2,0},{3,1},{4,6},{5,7},{6,4},{7,5},{8,10},{9,11},{10,... | collective-permute-start | bytes 4616 | tf_op jit(solution)/shard_map/ppermute | solution.py:16
  103.8 9.4 %collective-permute-start.16 = (f32[1,1024,128]{1,2,0:T(8,128)}, f32[1,1024,128]{1,2,0:T(8,128)}, u32[]{:S(2)}, u32[]{:S(2)}) collective-permute-start(f32[1,1024,128]{1,2,0:T(8,128)} %bitcast.245), channel_id=1, source_target_pairs={{0,1},{1,0},{2,3},{3,2},{4,5},{5,4},{6,7},{7,6},{8,9},{9,8},{10,11... | collective-permute-start | bytes 1572872 | tf_op jit(solution)/shard_map/ppermute | solution.py:16
  112.4 3.7 %collective-permute-start.15 = (f32[1,1024,128]{1,2,0:T(8,128)S(1)}, f32[1,1024,128]{1,2,0:T(8,128)S(1)}, u32[]{:S(2)}, u32[]{:S(2)}) collective-permute-start(f32[1,1024,128]{1,2,0:T(8,128)S(1)} %bitcast.246), channel_id=1, source_target_pairs={{0,1},{1,0},{2,3},{3,2},{4,5},{5,4},{6,7},{7,6},{8,9},{9,8},{10,11... | collective-permute-start | bytes 1572872 | tf_op jit(solution)/shard_map/ppermute | solution.py:16
  114.3 8.3 %collective-permute-start.17 = (bf16[1024,128]{0,1:T(8,128)(2,1)S(1)}, bf16[1024,128]{0,1:T(8,128)(2,1)S(1)}, u32[]{:S(2)}, u32[]{:S(2)}) collective-permute-start(bf16[1024,128]{0,1:T(8,128)(2,1)S(1)} %fusion.49), channel_id=1, source_target_pairs={{0,2},{1,3},{2,0},{3,1},{4,6},{5,7},{6,4},{7,5},{8,10},{9,11},{10,... | collective-permute-start | bytes 786440 | tf_op jit(solution)/shard_map/ppermute | solution.py:16
  115.9 30.7 %copy-start.1 = (bf16[2,192,512]{2,1,0:T(8,128)(2,1)S(1)}, bf16[2,192,512]{2,1,0:T(8,128)(2,1)}, u32[]{:S(2)}) copy-start(bf16[2,192,512]{2,1,0:T(8,128)(2,1)} %param.13) | copy-start | bytes 1179652
  124.3 5.8 %collective-permute-start.18 = (f32[1026]{0:T(1024)S(1)}, f32[1026]{0:T(1024)S(1)}, u32[]{:S(2)}, u32[]{:S(2)}) collective-permute-start(f32[1026]{0:T(1024)S(1)} %concatenate.11), channel_id=1, source_target_pairs={{0,4},{4,0},{8,12},{12,8},{16,20},{20,16},{24,28},{28,24},{1,5},{5... | collective-permute-start | bytes 12320 | tf_op jit(solution)/shard_map/ppermute | solution.py:16
  130.1 7.1 %collective-permute-start.19 = (f32[1026]{0:T(1024)S(1)}, f32[1026]{0:T(1024)S(1)}, u32[]{:S(2)}, u32[]{:S(2)}) collective-permute-start(f32[1026]{0:T(1024)S(1)} %add.359), channel_id=1, source_target_pairs={{0,8},{4,12},{8,0},{12,4},{16,24},{20,28},{24,16},{28,20},{1,9},{5... | collective-permute-start | bytes 12320 | tf_op jit(solution)/shard_map/ppermute | solution.py:16
  134.5 1.1 collective-permute-start.21
  135.7 3.5 %collective-permute-start.22 = (f32[128]{0:T(128)S(1)}, f32[128]{0:T(128)S(1)}, u32[]{:S(2)}, u32[]{:S(2)}) collective-permute-start(f32[128]{0:T(128)S(1)} %add.362), channel_id=1, source_target_pairs={{0,2},{1,3},{2,0},{3,1},{4,6},{5,7},{6,4},{7,5},{8,10},{9,11},{10,... | collective-permute-start | bytes 1544 | tf_op jit(solution)/shard_map/ppermute | solution.py:16
  137.2 4.6 %collective-permute-start.20 = (f32[1026]{0:T(1024)S(1)}, f32[1026]{0:T(1024)S(1)}, u32[]{:S(2)}, u32[]{:S(2)}) collective-permute-start(f32[1026]{0:T(1024)S(1)} %add.360), channel_id=1, source_target_pairs={{0,16},{4,20},{8,24},{12,28},{16,0},{20,4},{24,8},{28,12},{1,17},{... | collective-permute-start | bytes 12320 | tf_op jit(solution)/shard_map/ppermute | solution.py:16
